TPU v7x, 32 devices: a whole 2x2x4 slice. The times are simulated.
32 devices in a mesh: seq: 8 (over z, core), head: 4 (over y, x).
Axes of the slice: x: 2, y: 2, z: 4, core: 2. Of those that a mesh axis runs over, the one named last changes fastest.
Arguments:
- conv_output: bfloat16 [1024, 2048], P('seq', 'head'), may hold values from -6 to 6
- output_grad: bfloat16 [1024, 2048], P('seq', 'head'), may hold values from -6 to 6
- write_keys: bfloat16 [1024, 512], P('seq', 'head'), may hold values from -1.5 to 1.5
- read_queries: bfloat16 [1024, 512], P('seq', 'head'), may hold values from -1.5 to 1.5
- log_decay: float32 [1024, 32], P('seq', 'head'), may hold values from -0.7 to 0
- step_size: float32 [1024, 32], P('seq', 'head'), may hold values from 0.005 to 0.05
- skip_gain: float32 [32], P('head'), may hold values from 0.5 to 1.5
- conv_weight: float32 [4, 2048], P(None, 'head'), may hold values from -3 to 3
Outputs:
- input_grad: bfloat16 [1024, 2048], P('seq', 'head')
- keys_grad: float32 [1024, 512], P('seq', 'head')
- queries_grad: float32 [1024, 512], P('seq', 'head')
- decay_grad: float32 [1024, 32], P('seq', 'head')
- step_grad: float32 [1024, 32], P('seq', 'head')
All inputs are finite; a program needn't handle non-finite values.
Results may differ from a plain program's by a relative error of at most 0.0055.
Values may be sent and summed in bfloat16 or wider, within the bound.
No kernel may reach another device: no remote copies, remote signals or barrier semaphores. Data moves between devices by JAX's collectives and lax.ppermute only.
A program may use at most 64 MiB of HBM per device.

v0:
```python
import jax
import jax.numpy as jnp
from jax import lax
from jax.sharding import PartitionSpec as P

precise = lax.Precision.HIGHEST


def swapped(block, axis, bit):
    count = lax.axis_size(axis)
    route = []
    for low in range(count):
        high = low | 1 << bit
        if high != low and high < count:
            route += [(low, high), (high, low)]
    return lax.ppermute(block, axis, route)


def carried_in(shard, axis, combine, identity, reverse):
    peers, place = (lax.axis_size(axis), lax.axis_index(axis))
    everything = jax.tree.map(lambda part: lax.all_gather(part, axis), shard)
    start = jax.tree.map(
        lambda part, zero: jnp.broadcast_to(jnp.asarray(zero, part.dtype), part.shape),
        shard,
        identity,
    )

    def lap(k, before):
        at = peers - 1 - k if reverse else k
        reached = at > place if reverse else at < place
        new = combine(before, jax.tree.map(lambda part: part[at], everything))
        return jax.tree.map(lambda a, b: jnp.where(reached, a, b), new, before)

    return lax.fori_loop(0, peers, lap, start)


def shifted(block, axis, distance):
    devices = range(lax.axis_size(axis))
    route = [(i - distance, i) for i in devices if i - distance in devices]
    return lax.ppermute(block, axis, route)


def product(left, right):
    return jnp.dot(left, right, preferred_element_type=jnp.float32, precision=precise)


def forward_combine(earlier, latter):
    return (earlier[0] * latter[0], latter[0][:, None, None] * earlier[1] + latter[1])


def backward_combine(earlier, latter):
    return (latter[0] * earlier[0], latter[1] + latter[0][:, None, None] * earlier[1])


def body(
    conv_output, output_grad, write_keys, read_queries, log_decay, step_size, skip_gain, conv_weight
):
    length = conv_output.shape[0]
    head_count = log_decay.shape[1]
    head_width = conv_output.shape[1] // head_count
    parity = lax.axis_index("head") % 2
    own_first = parity == 0
    partner = swapped((write_keys, read_queries), "head", 0)
    keys_full = jnp.where(
        own_first,
        jnp.concatenate([write_keys, partner[0]], 1),
        jnp.concatenate([partner[0], write_keys], 1),
    ).astype(jnp.float32)
    queries_full = jnp.where(
        own_first,
        jnp.concatenate([read_queries, partner[1]], 1),
        jnp.concatenate([partner[1], read_queries], 1),
    ).astype(jnp.float32)
    state_count = keys_full.shape[1]
    preact = conv_output.astype(jnp.float32)
    values = jax.nn.silu(preact)
    upstream = output_grad.astype(jnp.float32)
    values3 = values.reshape(length, head_count, head_width)
    upstream3 = upstream.reshape(length, head_count, head_width)
    cumulative = jnp.cumsum(log_decay, axis=0)
    totals = cumulative[-1]
    to_end = jnp.exp(totals[None, :] - cumulative)
    from_start = jnp.exp(cumulative)
    weighted = values3 * (to_end * step_size)[:, :, None]
    seeded = upstream3 * from_start[:, :, None]
    local_state = jnp.einsum("ln,lhp->hnp", keys_full, weighted, precision=precise)
    local_grad = jnp.einsum("ln,lhp->hnp", queries_full, seeded, precision=precise)
    decay_total = jnp.exp(totals)
    identity = (jnp.ones_like(decay_total), jnp.zeros_like(local_state))
    entering = carried_in((decay_total, local_state), "seq", forward_combine, identity, False)[1]
    arriving = carried_in((decay_total, local_grad), "seq", backward_combine, identity, True)[1]
    scores = product(queries_full, keys_full.T)
    row_ids = lax.broadcasted_iota(jnp.int32, (length, length), 0)
    col_ids = lax.broadcasted_iota(jnp.int32, (length, length), 1)
    causal = row_ids >= col_ids
    cum_heads = cumulative.T
    step_heads = step_size.T
    log_gap = jnp.where(causal[None], cum_heads[:, :, None] - cum_heads[:, None, :], -1e30)
    decay_mask = jnp.exp(log_gap)
    pair_dots = jnp.einsum("thp,shp->hts", upstream3, values3, precision=precise)
    masked_scores = decay_mask * scores[None]
    weight_sum = jnp.einsum("hts,hs->ts", decay_mask * pair_dots, step_heads, precision=precise)
    within = jnp.einsum(
        "hts,thp->shp", masked_scores * step_heads[:, None, :], upstream3, precision=precise
    )
    effect = masked_scores * pair_dots
    row_sums = jnp.einsum("hts,hs->th", effect, step_heads, precision=precise)
    col_sums = jnp.sum(effect, 1).T
    from_state = jnp.einsum("ln,hnp->lhp", queries_full, entering, precision=precise)
    into_state = jnp.einsum("ln,hnp->lhp", keys_full, arriving, precision=precise)
    carried = jnp.sum(values3 * into_state, 2)
    step_grad = col_sums + to_end * carried
    value_grad = (
        within
        + skip_gain[None, :, None] * upstream3
        + (to_end * step_size)[:, :, None] * into_state
    )
    leaving = decay_total[:, None, None] * entering + local_state
    decay_terms = (
        row_sums
        - col_sums * step_size
        + from_start * jnp.sum(upstream3 * from_state, 2)
        - to_end * step_size * carried
    )
    last_row = (lax.broadcasted_iota(jnp.int32, (length, 1), 0) == length - 1).astype(jnp.float32)
    decay_terms = decay_terms + last_row * jnp.sum(arriving * leaving, (1, 2))[None, :]
    decay_grad = jnp.flip(jnp.cumsum(jnp.flip(decay_terms, 0), 0), 0)
    query_part = product(weight_sum, keys_full) + jnp.einsum(
        "lhp,hnp->ln", seeded, entering, precision=precise
    )
    key_part = lax.dot_general(
        weight_sum,
        queries_full,
        (((0,), (0,)), ((), ())),
        preferred_element_type=jnp.float32,
        precision=precise,
    )
    key_part = key_part + jnp.einsum("lhp,hnp->ln", weighted, arriving, precision=precise)
    half_width = state_count // 2
    key_mine = jnp.where(own_first, key_part[:, :half_width], key_part[:, half_width:])
    key_other = jnp.where(own_first, key_part[:, half_width:], key_part[:, :half_width])
    query_mine = jnp.where(own_first, query_part[:, :half_width], query_part[:, half_width:])
    query_other = jnp.where(own_first, query_part[:, half_width:], query_part[:, :half_width])
    received = (
        swapped(key_other.astype(jnp.bfloat16), "head", 0).astype(key_other.dtype),
        swapped(query_other.astype(jnp.bfloat16), "head", 0).astype(query_other.dtype),
    )
    keys_grad = key_mine + received[0]
    queries_grad = query_mine + received[1]
    logistic = jax.nn.sigmoid(preact)
    conv_grad = value_grad.reshape(length, -1) * logistic * (1.0 + preact * (1.0 - logistic))
    following = shifted(conv_grad[:3], "seq", -1)
    extended = jnp.concatenate([conv_grad, following], 0)
    input_grad = jnp.zeros_like(conv_grad)
    for offset in range(4):
        input_grad = (
            input_grad + conv_weight[offset][None, :] * extended[3 - offset : 3 - offset + length]
        )
    return (input_grad.astype(jnp.bfloat16), keys_grad, queries_grad, decay_grad, step_grad)


def solution(mesh):
    return jax.shard_map(
        body,
        mesh=mesh,
        in_specs=(
            P("seq", "head"),
            P("seq", "head"),
            P("seq", "head"),
            P("seq", "head"),
            P("seq", "head"),
            P("seq", "head"),
            P("head"),
            P(None, "head"),
        ),
        out_specs=(
            P("seq", "head"),
            P("seq", "head"),
            P("seq", "head"),
            P("seq", "head"),
            P("seq", "head"),
        ),
        check_vma=False,
    )
```

profile of v0, /device:TPU:0, one launch (start us, length us, event | category | flops | bytes accessed | tf_op | source)
XLA Modules:
  0.0 168.4 jit_solution(5960335788928022852)
XLA Ops:
  7.2 3.0 %collective-permute-start = (bf16[128,128]{1,0:T(8,128)(2,1)}, bf16[128,128]{1,0:T(8,128)(2,1)S(1)}, u32[]{:S(2)}, u32[]{:S(2)}) collective-permute-start(bf16[128,128]{1,0:T(8,128)(2,1)} %param.15), channel_id=1, source_target_pairs={{0,1},{1,0},{2,3},{3,2},{4,5},{5,4},{6,7},{7,6},{8,9},{9,8},{10,11... | collective-permute-start | bytes 98312 | tf_op jit(solution)/shard_map/ppermute | solution.py:16
  10.2 0.8 copy.37
  11.0 0.8 copy.33
  12.6 1.0 copy.36
  13.7 2.0 %convolution_bitcast_fusion.2 = f32[8,256,64]{1,2,0:T(8,128)} fusion(bf16[128,8,64]{0,2,1:T(8,128)(2,1)S(1)} %bitcast.110, f32[128,8]{0,1:T(8,128)S(1)} %copy.39, bf16[128,128]{1,0:T(8,128)(2,1)S(1)} %collective-permute-done, bf16[128,128]{1,0:T(8,128)(2,1)} %param.15, pred[]{:T(512)S(6)} %eq.16), kind=kOutput, calls=%fused_computation.10 | convolution fusion | flops 201752576 | bytes 724993 | tf_op jit(solution)/shard_map/ln,lhp->hnp/dot_general | solution.py:87
  15.8 0.7 collective-permute-start.1
  16.6 12.2 %all-gather.2 = f32[8,1,8]{2,1,0:T(1,128)} all-gather(f32[1,1,8]{2,1,0:T(1,128)S(1)} %get-tuple-element.326), channel_id=1, replica_groups=mesh['seq'=8,'head'=4] {'seq'}, dimensions={0}, use_global_device_ids=true | all-gather | bytes 288 | tf_op jit(solution)/shard_map/all_gather | solution.py:21
  28.9 1.0 fusion.53
  29.9 33.6 %all-gather.6.cloned.1.call-done = f32[64,256,64]{1,2,0:T(8,128)} async-done(((f32[8,256,64]{1,2,0:T(8,128)}), f32[64,256,64]{1,2,0:T(8,128)}) %all-gather.6.cloned.1.call-update) | async-done | bytes 4194320 | tf_op jit(solution)/shard_map/all_gather | solution.py:21
  63.5 20.1 %while.30 = (s32[]{:T(128)}, f32[8,256,64]{2,1,0:T(8,128)S(1)}, s32[]{:T(128)}, f32[8,8,256,64]{2,3,1,0:T(8,128)}, f32[8,8]{1,0:T(8,128)}, /*index=5*/s32[]{:T(128)}, s32[]{:T(128)}, s32[]{:T(128)}, s32[]{:T(128)}) while((s32[]{:T(128)}, f32[8,256,64]{2,1,0:T(8,128)S(1)}, s32[]{:T(128)}, f32[8,8,256,64]{2,3,1,0:T(8,128)}, ...), condition=%wide.region_2.3_spmd.clone, body=%wide.region_1.2_spmd.clone.sunk | while | flops 524296 | bytes 3670287 | solution.py:34
  63.5 0.7 dynamic-slice_bitcast_fusion.4
  64.2 1.1 constant_dynamic-slice_fusion.4
  66.7 1.1 constant_dynamic-slice_fusion.4
  68.5 0.7 dynamic-slice_bitcast_fusion.4
  69.2 1.1 constant_dynamic-slice_fusion.4
  71.7 1.1 constant_dynamic-slice_fusion.4
  73.5 0.7 dynamic-slice_bitcast_fusion.4
  74.2 1.1 constant_dynamic-slice_fusion.4
  76.0 0.7 dynamic-slice_bitcast_fusion.4
  76.7 1.1 constant_dynamic-slice_fusion.4
  79.2 1.1 constant_dynamic-slice_fusion.4
  81.7 1.1 constant_dynamic-slice_fusion.4
  85.3 2.0 %convolution_bitcast_fusion = f32[8,256,64]{1,2,0:T(8,128)} fusion(f32[128,8,64]{0,2,1:T(8,128)S(1)} %bitcast.107, f32[128,8]{0,1:T(8,128)} %copy-done.21, bf16[128,128]{1,0:T(8,128)(2,1)} %copy-done.12, bf16[128,128]{1,0:T(8,128)(2,1)S(1)} %copy-done.8, pred[]{:T(512)S(6)} %eq.16), kind=kOutput, calls=%fused_computation.8 | convolution fusion | flops 201687040 | bytes 856065 | tf_op jit(solution)/shard_map/ln,lhp->hnp/dot_general | solution.py:86
  87.9 1.3 fusion.51
  89.2 1.4 fusion.55
  91.3 1.3 collective-permute-start.2
  92.5 1.3 multiply_reduce_fusion
  93.8 1.7 %fusion.8 = f32[8,128]{1,0:T(8,128)} fusion(f32[8,128,128]{2,1,0:T(8,128)S(1)} %get-tuple-element.332, f32[128,128]{1,0:T(8,128)} %copy-done.17, f32[8,128]{1,0:T(8,128)} %copy-done.20, pred[128,128]{1,0:T(8,128)(4,1)S(1)} %iota_compare_fusion), kind=kLoop, calls=%fused_computation.32 | loop fusion | flops 654336 | bytes 614400 | tf_op jit(solution)/shard_map/reduce_sum | solution.py:108
  95.5 1.7 %convolution_bitcast_fusion.5 = f32[128,256]{1,0:T(8,128)S(1)} fusion(f32[8,256,64]{2,1,0:T(8,128)S(1)} %get-tuple-element.231, f32[128,8,64]{0,2,1:T(8,128)S(1)} %bitcast.109, f32[128,8]{0,1:T(8,128)} %copy-done.21), kind=kOutput, calls=%fused_computation.16 | convolution fusion | flops 201392128 | bytes 921600 | tf_op jit(solution)/shard_map/lhp,hnp->ln/dot_general | solution.py:138
  97.3 1.1 convolution_add_fusion.1
  98.4 1.9 %fusion.9 = f32[8,1,128]{2,1,0:T(1,128)S(1)} fusion(f32[8,128,1]{1,2,0:T(1,128)} %bitcast.123, f32[8,128,128]{2,1,0:T(8,128)S(1)} %get-tuple-element.332, f32[128,128]{1,0:T(8,128)} %copy-done.17, f32[8,128]{1,0:T(8,128)} %copy-done.20, pred[128,128]{1,0:T(8,128)(4,1)S(1)} %iota_compare_fusion), kind=kOutput, calls=%fused_computation.33 | convolution fusion | flops 2097152 | bytes 618496 | tf_op jit(solution)/shard_map/hts,hs->th/dot_general | solution.py:107
  100.5 1.5 collective-permute-start.3
  102.0 0.8 copy.47
  102.9 1.6 fusion.16
  105.3 28.1 %all-gather.8.cloned.1.call-done = f32[64,256,64]{1,2,0:T(8,128)} async-done(((f32[8,256,64]{1,2,0:T(8,128)}), f32[64,256,64]{1,2,0:T(8,128)}) %all-gather.8.cloned.1.call-update) | async-done | bytes 4194320 | tf_op jit(solution)/shard_map/all_gather | solution.py:21
  133.4 20.0 %while.31 = (s32[]{:T(128)}, f32[8,256,64]{2,1,0:T(8,128)S(1)}, s32[]{:T(128)}, f32[8,8]{1,0:T(8,128)}, f32[8,8,256,64]{2,3,1,0:T(8,128)}, /*index=5*/s32[]{:T(128)}, s32[]{:T(128)}) while((s32[]{:T(128)}, f32[8,256,64]{2,1,0:T(8,128)S(1)}, s32[]{:T(128)}, f32[8,8]{1,0:T(8,128)}, f32[8,8,256,64]{2,3,1,0:T(8,128)}, ...), condition=%wide.region_4.5_spmd.clone, body=%wide.region_3.4_spmd.clone.sunk | while | flops 524292 | bytes 3670225 | solution.py:34
  134.1 1.1 constant_dynamic-slice_fusion.5
  136.6 1.1 constant_dynamic-slice_fusion.5
  139.1 1.1 constant_dynamic-slice_fusion.5
  141.6 1.1 constant_dynamic-slice_fusion.5
  144.1 1.1 constant_dynamic-slice_fusion.5
  146.6 1.1 constant_dynamic-slice_fusion.5
  149.1 1.1 constant_dynamic-slice_fusion.5
  151.6 1.1 constant_dynamic-slice_fusion.5
  153.5 1.0 convolution_bitcast_fusion.4
  154.9 1.3 multiply_reduce_fusion.1
  156.9 1.5 collective-permute-start.4
  160.1 0.8 collective-permute-done.4
  (142 shorter events, 27.5 us)
Async XLA Ops:
  7.2 56.3 %all-gather.6.cloned.1.call-start = ((), (), s32[]{:S(2)}) async-start(), calls=%async_computation | async-start | bytes 4718592 | tf_op jit(solution)/shard_map/all_gather | solution.py:21
  7.2 6.5 %collective-permute-start = (bf16[128,128]{1,0:T(8,128)(2,1)}, bf16[128,128]{1,0:T(8,128)(2,1)S(1)}, u32[]{:S(2)}, u32[]{:S(2)}) collective-permute-start(bf16[128,128]{1,0:T(8,128)(2,1)} %param.15), channel_id=1, source_target_pairs={{0,1},{1,0},{2,3},{3,2},{4,5},{5,4},{6,7},{7,6},{8,9},{9,8},{10,11... | collective-permute-start | bytes 98312 | tf_op jit(solution)/shard_map/ppermute | solution.py:16
  11.0 1.1 copy-start.2
  12.0 51.5 %copy-start = (f32[128,8]{1,0:T(8,128)}, f32[128,8]{1,0:T(8,128)S(1)}, u32[]{:S(2)}) copy-start(f32[128,8]{1,0:T(8,128)S(1)} %reduce_window_sum.18) | copy-start | bytes 12292
  12.0 0.6 copy-start.23
  12.0 51.4 %copy-start.4 = (f32[128,8]{1,0:T(8,128)}, f32[128,8]{1,0:T(8,128)S(1)}, u32[]{:S(2)}) copy-start(f32[128,8]{1,0:T(8,128)S(1)} %get-tuple-element.323) | copy-start | bytes 12292
  13.7 49.8 %copy-start.18 = (f32[128,8]{0,1:T(8,128)}, f32[128,8]{0,1:T(8,128)S(1)}, u32[]{:S(2)}) copy-start(f32[128,8]{0,1:T(8,128)S(1)} %copy.39) | copy-start | bytes 12292
  13.7 49.8 %copy-start.10 = (bf16[128,128]{1,0:T(8,128)(2,1)}, bf16[128,128]{1,0:T(8,128)(2,1)S(1)}, u32[]{:S(2)}) copy-start(bf16[128,128]{1,0:T(8,128)(2,1)S(1)} %collective-permute-done) | copy-start | bytes 98308
  15.7 117.6 %all-gather.8.cloned.1.call-start = ((), (), s32[]{:S(2)}) async-start(), calls=%async_computation.1 | async-start | bytes 4718592 | tf_op jit(solution)/shard_map/all_gather | solution.py:21
  15.8 13.1 %collective-permute-start.1 = (bf16[128,128]{1,0:T(8,128)(2,1)}, bf16[128,128]{1,0:T(8,128)(2,1)S(1)}, u32[]{:S(2)}, u32[]{:S(2)}) collective-permute-start(bf16[128,128]{1,0:T(8,128)(2,1)} %param.14), channel_id=1, source_target_pairs={{0,1},{1,0},{2,3},{3,2},{4,5},{5,4},{6,7},{7,6},{8,9},{9,8},{10,11... | collective-permute-start | bytes 98312 | tf_op jit(solution)/shard_map/ppermute | solution.py:16
  16.6 67.7 %copy-start.20 = (f32[8,128]{1,0:T(8,128)}, f32[8,128]{1,0:T(8,128)S(1)}, u32[]{:S(2)}) copy-start(f32[8,128]{1,0:T(8,128)S(1)} %copy.34) | copy-start | bytes 12292
  16.6 67.7 %copy-start.21 = (f32[128,8]{0,1:T(8,128)}, f32[128,8]{0,1:T(8,128)S(1)}, u32[]{:S(2)}) copy-start(f32[128,8]{0,1:T(8,128)S(1)} %copy.38) | copy-start | bytes 12292
  28.9 55.0 %copy-start.12 = (bf16[128,128]{1,0:T(8,128)(2,1)}, bf16[128,128]{1,0:T(8,128)(2,1)S(1)}, u32[]{:S(2)}) copy-start(bf16[128,128]{1,0:T(8,128)(2,1)S(1)} %collective-permute-done.1) | copy-start | bytes 98308
  29.9 54.5 %copy-start.17 = (f32[128,128]{1,0:T(8,128)}, f32[128,128]{1,0:T(8,128)S(1)}, u32[]{:S(2)}) copy-start(f32[128,128]{1,0:T(8,128)S(1)} %fusion.53) | copy-start | bytes 196612
  63.4 20.5 %copy-start.7 = (bf16[128,128]{1,0:T(8,128)(2,1)S(1)}, bf16[128,128]{1,0:T(8,128)(2,1)}, u32[]{:S(2)}) copy-start(bf16[128,128]{1,0:T(8,128)(2,1)} %param.14) | copy-start | bytes 98308
  63.4 20.9 %copy-start.22 = (f32[128,8]{0,1:T(8,128)S(1)}, f32[128,8]{0,1:T(8,128)}, u32[]{:S(2)}) copy-start(f32[128,8]{0,1:T(8,128)} %param.17) | copy-start | bytes 12292
  63.4 20.9 %copy-start.27 = (f32[8]{0:T(128)S(1)}, f32[8]{0:T(128)}, u32[]{:S(2)}) copy-start(f32[8]{0:T(128)} %param.18) | copy-start | bytes 100
  83.5 1.5 copy-start.16
  83.6 1.8 %copy-start.8 = (bf16[128,128]{1,0:T(8,128)(2,1)S(1)}, bf16[128,128]{1,0:T(8,128)(2,1)}, u32[]{:S(2)}) copy-start(bf16[128,128]{1,0:T(8,128)(2,1)} %param.14) | copy-start | bytes 98308
  91.3 11.6 %collective-permute-start.2 = (f32[3,512]{1,0:T(4,128)}, f32[3,512]{1,0:T(4,128)}, u32[]{:S(2)}, u32[]{:S(2)}) collective-permute-start(f32[3,512]{1,0:T(4,128)} %slice.57), channel_id=1, source_target_pairs={{4,0},{8,4},{12,8},{16,12},{20,16},{24,20},{28,24},{5,1},{9,5},{13... | collective-permute-start | bytes 18440 | tf_op jit(solution)/shard_map/ppermute | solution.py:40
  93.8 6.5 %copy-start.14 = (f32[128,128]{0,1:T(8,128)}, f32[128,128]{0,1:T(8,128)S(1)}, u32[]{:S(2)}) copy-start(f32[128,128]{0,1:T(8,128)S(1)} %get-tuple-element.331) | copy-start | bytes 196612
  100.5 4.2 %collective-permute-start.3 = (bf16[128,128]{1,0:T(8,128)(2,1)S(1)}, bf16[128,128]{1,0:T(8,128)(2,1)S(1)}, u32[]{:S(2)}, u32[]{:S(2)}) collective-permute-start(bf16[128,128]{1,0:T(8,128)(2,1)S(1)} %select_convert_fusion.1), channel_id=1, source_target_pairs={{0,1},{1,0},{2,3},{3,2},{4,5},{5,4},{6,7},{7,6},{8,9},{9,8},{10,11... | collective-permute-start | bytes 98312 | tf_op jit(solution)/shard_map/ppermute | solution.py:16
  133.4 20.1 %copy-start.19 = (f32[128,8]{0,1:T(8,128)S(1)}, f32[128,8]{0,1:T(8,128)}, u32[]{:S(2)}) copy-start(f32[128,8]{0,1:T(8,128)} %copy-done.18) | copy-start | bytes 12292
  133.4 21.5 %copy-start.25 = (f32[8]{0:T(128)S(1)}, f32[8]{0:T(128)}, u32[]{:S(2)}) copy-start(f32[8]{0:T(128)} %fusion.51) | copy-start | bytes 100
  153.4 2.8 %copy-start.6 = (bf16[128,128]{1,0:T(8,128)(2,1)S(1)}, bf16[128,128]{1,0:T(8,128)(2,1)}, u32[]{:S(2)}) copy-start(bf16[128,128]{1,0:T(8,128)(2,1)} %param.15) | copy-start | bytes 98308
  153.4 2.8 %copy-start.11 = (bf16[128,128]{1,0:T(8,128)(2,1)S(1)}, bf16[128,128]{1,0:T(8,128)(2,1)}, u32[]{:S(2)}) copy-start(bf16[128,128]{1,0:T(8,128)(2,1)} %copy-done.10) | copy-start | bytes 98308
  153.4 3.2 %copy-start.9 = (bf16[128,128]{1,0:T(8,128)(2,1)S(1)}, bf16[128,128]{1,0:T(8,128)(2,1)}, u32[]{:S(2)}) copy-start(bf16[128,128]{1,0:T(8,128)(2,1)} %param.14) | copy-start | bytes 98308
  153.4 3.2 %copy-start.13 = (bf16[128,128]{1,0:T(8,128)(2,1)S(1)}, bf16[128,128]{1,0:T(8,128)(2,1)}, u32[]{:S(2)}) copy-start(bf16[128,128]{1,0:T(8,128)(2,1)} %copy-done.12) | copy-start | bytes 98308
  153.4 3.2 %copy-start.15 = (f32[128,128]{0,1:T(8,128)S(1)}, f32[128,128]{0,1:T(8,128)}, u32[]{:S(2)}) copy-start(f32[128,128]{0,1:T(8,128)} %copy-done.14) | copy-start | bytes 196612
  153.4 5.0 %copy-start.1 = (f32[128,8]{1,0:T(8,128)S(1)}, f32[128,8]{1,0:T(8,128)}, u32[]{:S(2)}) copy-start(f32[128,8]{1,0:T(8,128)} %copy-done) | copy-start | bytes 12292
  153.4 5.0 %copy-start.3 = (f32[128,8]{1,0:T(8,128)S(1)}, f32[128,8]{1,0:T(8,128)}, u32[]{:S(2)}) copy-start(f32[128,8]{1,0:T(8,128)} %copy-done.2) | copy-start | bytes 12292
  153.4 5.0 %copy-start.5 = (f32[128,8]{1,0:T(8,128)S(1)}, f32[128,8]{1,0:T(8,128)}, u32[]{:S(2)}) copy-start(f32[128,8]{1,0:T(8,128)} %copy-done.4) | copy-start | bytes 12292
  153.5 5.0 %copy-start.24 = (f32[8]{0:T(128)S(1)}, f32[8]{0:T(128)}, u32[]{:S(2)}) copy-start(f32[8]{0:T(128)} %copy-done.23) | copy-start | bytes 100
  153.5 5.0 %copy-start.26 = (f32[128]{0:T(128)S(1)}, f32[128]{0:T(128)}, u32[]{:S(2)}) copy-start(f32[128]{0:T(128)} %compare_convert_fusion) | copy-start | bytes 1540
  156.9 4.0 %collective-permute-start.4 = (bf16[128,128]{1,0:T(8,128)(2,1)S(1)}, bf16[128,128]{1,0:T(8,128)(2,1)S(1)}, u32[]{:S(2)}, u32[]{:S(2)}) collective-permute-start(bf16[128,128]{1,0:T(8,128)(2,1)S(1)} %select_convert_fusion), channel_id=1, source_target_pairs={{0,1},{1,0},{2,3},{3,2},{4,5},{5,4},{6,7},{7,6},{8,9},{9,8},{10,11... | collective-permute-start | bytes 98312 | tf_op jit(solution)/shard_map/ppermute | solution.py:16
Sparse Core Ops, SparseCore 0:
  15.9 47.5 all-gather.5
  87.5 45.8 all-gather.7
where the time goes:
time: 171 us; the launch traced here: 168 us
  waiting for transfers between devices  62.7 us (37%)
  local copies, waits for them, and re-layouts  43.7 us (26%)
  between operations  14.6 us (9%)
  matrix products  13.6 us (8%)
  other arithmetic  12.8 us (7%)
  blocking collectives  12.2 us (7%)
  starting transfers between devices  8.13 us (5%)
    all_gather x2, waiting for transfers between devices, carried_in(): everything = jax.tree.map(lambda part: lax.all_gather(part, axis), shard)  61.7 us
    dynamic_slice x32, local copies, waits for them, and re-layouts, lap(): new = combine(before, jax.tree.map(lambda part: part[at], everything))  22.6 us
    all_gather x1, blocking collectives, carried_in(): everything = jax.tree.map(lambda part: lax.all_gather(part, axis), shard)  12.2 us
    ppermute x4, starting transfers between devices, swapped(): return lax.ppermute(block, axis, route)  6.77 us
    select_n x16, other arithmetic, lap(): return jax.tree.map(lambda a, b: jnp.where(reached, a, b), new, before)  5.63 us
    mul x8, local copies, waits for them, and re-layouts, backward_combine(): latter[0][:, None, None] * earlier[1]  5.53 us
    mul x8, local copies, waits for them, and re-layouts, forward_combine(): latter[0][:, None, None] * earlier[1] + latter[1]  5.52 us
    unnamed x61, local copies, waits for them, and re-layouts  4.59 us
  transfers between devices with their start and end apart: 7, of which 4 were waited for; matrix products, arithmetic and copies ran while one was open for 12% of the time, Pallas kernels for 0%

commit v1 on v0

--- a/solution.py
+++ b/solution.py
@@ -16,22 +16,26 @@
     return lax.ppermute(block, axis, route)
 
 
-def carried_in(shard, axis, combine, identity, reverse):
-    peers, place = (lax.axis_size(axis), lax.axis_index(axis))
-    everything = jax.tree.map(lambda part: lax.all_gather(part, axis), shard)
-    start = jax.tree.map(
-        lambda part, zero: jnp.broadcast_to(jnp.asarray(zero, part.dtype), part.shape),
-        shard,
-        identity,
-    )
-
-    def lap(k, before):
-        at = peers - 1 - k if reverse else k
-        reached = at > place if reverse else at < place
-        new = combine(before, jax.tree.map(lambda part: part[at], everything))
-        return jax.tree.map(lambda a, b: jnp.where(reached, a, b), new, before)
-
-    return lax.fori_loop(0, peers, lap, start)
+def scanned_in(shards, axis):
+    peers = lax.axis_size(axis)
+    near = [(jnp.ones_like(a), jnp.zeros_like(s)) for a, s, _ in shards]
+    window = [(a, s) for a, s, _ in shards]
+    distance = 1
+    while distance < peers:
+        routes = []
+        for _, _, reverse in shards:
+            step = -distance if reverse else distance
+            routes.append([(i, i + step) for i in range(peers) if 0 <= i + step < peers])
+        received = [lax.ppermute(w, axis, r) for w, r in zip(window, routes)]
+        more = 2 * distance < peers
+        for k, (far_a, far_s) in enumerate(received):
+            near_a, near_s = near[k]
+            near[k] = (near_a * far_a, near_s + near_a[:, None, None] * far_s)
+            if more:
+                win_a, win_s = window[k]
+                window[k] = (win_a * far_a, win_s + win_a[:, None, None] * far_s)
+        distance *= 2
+    return [s for _, s in near]
 
 
 def shifted(block, axis, distance):
@@ -42,14 +46,6 @@
 
 def product(left, right):
     return jnp.dot(left, right, preferred_element_type=jnp.float32, precision=precise)
-
-
-def forward_combine(earlier, latter):
-    return (earlier[0] * latter[0], latter[0][:, None, None] * earlier[1] + latter[1])
-
-
-def backward_combine(earlier, latter):
-    return (latter[0] * earlier[0], latter[1] + latter[0][:, None, None] * earlier[1])
 
 
 def body(
@@ -86,9 +82,9 @@
     local_state = jnp.einsum("ln,lhp->hnp", keys_full, weighted, precision=precise)
     local_grad = jnp.einsum("ln,lhp->hnp", queries_full, seeded, precision=precise)
     decay_total = jnp.exp(totals)
-    identity = (jnp.ones_like(decay_total), jnp.zeros_like(local_state))
-    entering = carried_in((decay_total, local_state), "seq", forward_combine, identity, False)[1]
-    arriving = carried_in((decay_total, local_grad), "seq", backward_combine, identity, True)[1]
+    entering, arriving = scanned_in(
+        [(decay_total, local_state, False), (decay_total, local_grad, True)], "seq"
+    )
     scores = product(queries_full, keys_full.T)
     row_ids = lax.broadcasted_iota(jnp.int32, (length, length), 0)
     col_ids = lax.broadcasted_iota(jnp.int32, (length, length), 1)

time: 171 us -> 99.2 us (0.58)
  the two profiles are of different devices: /device:TPU:0 before, /device:TPU:1 now
where the time goes in v1:
time: 99.2 us; the launch traced here: 97.8 us
  starting transfers between devices  37 us (37%)
  waiting for transfers between devices  27.2 us (27%)
  local copies, waits for them, and re-layouts  14.6 us (15%)
  other arithmetic  10 us (10%)
  matrix products  7.77 us (8%)
  between operations  1.23 us (1%)
    ppermute x10, starting transfers between devices, scanned_in(): received = [lax.ppermute(w, axis, r) for w, r in zip(window, routes)]  30.2 us
    ppermute x10, waiting for transfers between devices, scanned_in(): received = [lax.ppermute(w, axis, r) for w, r in zip(window, routes)]  14.3 us
    ppermute x1, waiting for transfers between devices, shifted(): return lax.ppermute(block, axis, route)  12.9 us
    unnamed x111, local copies, waits for them, and re-layouts  10.5 us
    ppermute x4, starting transfers between devices, swapped(): return lax.ppermute(block, axis, route)  3.78 us
    ppermute x1, starting transfers between devices, shifted(): return lax.ppermute(block, axis, route)  3.05 us
    dot_general x1, matrix products, body(): row_sums = jnp.einsum('hts,hs->th', effect, step_heads, precision=precise)  2.75 us
    reduce_sum x1, other arithmetic, body(): jnp.sum(arriving * leaving, (1, 2))[None, :]  2.1 us
  transfers between devices with their start and end apart: 15, of which 6 were waited for; matrix products, arithmetic and copies ran while one was open for 18% of the time, Pallas kernels for 0%

profile of v1, /device:TPU:1, one launch (start us, length us, event | category | flops | bytes accessed | tf_op | source)
XLA Modules:
  0.0 97.8 jit_solution(1048917996969682707)
XLA Ops:
  0.6 2.1 %collective-permute-start.1 = (bf16[128,128]{1,0:T(8,128)(2,1)}, bf16[128,128]{1,0:T(8,128)(2,1)S(1)}, u32[]{:S(2)}, u32[]{:S(2)}) collective-permute-start(bf16[128,128]{1,0:T(8,128)(2,1)} %param.10), channel_id=1, source_target_pairs={{0,1},{1,0},{2,3},{3,2},{4,5},{5,4},{6,7},{7,6},{8,9},{9,8},{10,11... | collective-permute-start | bytes 98312 | tf_op jit(solution)/shard_map/ppermute | solution.py:16
  2.8 0.8 copy.25
  6.2 0.6 copy-done.10
  7.2 4.5 %collective-permute-start.9 = (f32[8,256,64]{1,2,0:T(8,128)S(1)}, f32[8,256,64]{1,2,0:T(8,128)S(1)}, u32[]{:S(2)}, u32[]{:S(2)}) collective-permute-start(f32[8,256,64]{1,2,0:T(8,128)S(1)} %convolution_bitcast_fusion), channel_id=1, source_target_pairs={{0,4},{4,8},{8,12},{12,16},{16,20},{20,24},{24,28},{1,5},{5,9},{9,... | collective-permute-start | bytes 1572872 | tf_op jit(solution)/shard_map/ppermute | solution.py:29
  11.7 0.6 copy-done.16
  12.7 1.9 %collective-permute-start.2 = (f32[8,256,64]{1,2,0:T(8,128)S(1)}, f32[8,256,64]{1,2,0:T(8,128)S(1)}, u32[]{:S(2)}, u32[]{:S(2)}) collective-permute-start(f32[8,256,64]{1,2,0:T(8,128)S(1)} %convolution_bitcast_fusion.2), channel_id=1, source_target_pairs={{4,0},{8,4},{12,8},{16,12},{20,16},{24,20},{28,24},{5,1},{9,5},{13... | collective-permute-start | bytes 1572872 | tf_op jit(solution)/shard_map/ppermute | solution.py:29
  14.7 3.6 %collective-permute-start.10 = (f32[8]{0:T(128)S(1)}, f32[8]{0:T(128)S(1)}, u32[]{:S(2)}, u32[]{:S(2)}) collective-permute-start(f32[8]{0:T(128)S(1)} %fusion.49), channel_id=1, source_target_pairs={{0,4},{4,8},{8,12},{12,16},{16,20},{20,24},{24,28},{1,5},{5,9},{9,... | collective-permute-start | bytes 104 | tf_op jit(solution)/shard_map/ppermute | solution.py:29
  18.3 1.9 %collective-permute-start.3 = (f32[8]{0:T(128)S(1)}, f32[8]{0:T(128)S(1)}, u32[]{:S(2)}, u32[]{:S(2)}) collective-permute-start(f32[8]{0:T(128)S(1)} %fusion.49), channel_id=1, source_target_pairs={{4,0},{8,4},{12,8},{16,12},{20,16},{24,20},{28,24},{5,1},{9,5},{13... | collective-permute-start | bytes 104 | tf_op jit(solution)/shard_map/ppermute | solution.py:29
  20.4 2.9 %collective-permute-done.2 = f32[8,256,64]{1,2,0:T(8,128)S(1)} collective-permute-done((f32[8,256,64]{1,2,0:T(8,128)S(1)}, f32[8,256,64]{1,2,0:T(8,128)S(1)}, u32[]{:S(2)}, u32[]{:S(2)}) %collective-permute-start.2) | collective-permute-done | bytes 524320 | tf_op jit(solution)/shard_map/ppermute | solution.py:29
  23.5 1.3 %collective-permute-start.4 = (f32[8,256,64]{1,2,0:T(8,128)S(1)}, f32[8,256,64]{1,2,0:T(8,128)S(1)}, u32[]{:S(2)}, u32[]{:S(2)}) collective-permute-start(f32[8,256,64]{1,2,0:T(8,128)S(1)} %get-tuple-element.28), channel_id=1, source_target_pairs={{8,0},{12,4},{16,8},{20,12},{24,16},{28,20},{9,1},{13,5},{17,9},{2... | collective-permute-start | bytes 1572872 | tf_op jit(solution)/shard_map/ppermute | solution.py:29
  24.8 1.1 %multiply_reduce_fusion = (f32[128,128]{0,1:T(8,128)}, f32[8,128,128]{2,1,0:T(8,128)S(1)}) fusion(f32[128,8]{0,1:T(8,128)S(1)} %copy-done.41, f32[8,128]{1,0:T(8,128)S(1)} %copy.26, pred[128,128]{1,0:T(8,128)(4,1)S(1)} %iota_compare_fusion, f32[128,8,64]{0,2,1:T(8,128)S(1)} %bitcast.87, bf16[128,8,64]{0,2,1:T(8,128)(2,1)S(1)} %bitcast.90), kind=kOutput, calls=%fused_computation.10 | convolution fusion | flops 101302272 | bytes 1007616 | tf_op jit(solution)/shard_map/thp,shp->hts/dot_general | solution.py:96
  25.9 4.0 %collective-permute-start.11 = (f32[8,256,64]{1,2,0:T(8,128)S(1)}, f32[8,256,64]{1,2,0:T(8,128)S(1)}, u32[]{:S(2)}, u32[]{:S(2)}) collective-permute-start(f32[8,256,64]{1,2,0:T(8,128)S(1)} %get-tuple-element.29), channel_id=1, source_target_pairs={{0,8},{4,12},{8,16},{12,20},{16,24},{20,28},{1,9},{5,13},{9,17},{1... | collective-permute-start | bytes 1572872 | tf_op jit(solution)/shard_map/ppermute | solution.py:29
  29.9 0.6 fusion.56
  30.5 0.7 fusion.51
  31.2 6.4 %collective-permute-done.4 = f32[8,256,64]{1,2,0:T(8,128)S(1)} collective-permute-done((f32[8,256,64]{1,2,0:T(8,128)S(1)}, f32[8,256,64]{1,2,0:T(8,128)S(1)}, u32[]{:S(2)}, u32[]{:S(2)}) %collective-permute-start.4) | collective-permute-done | bytes 524320 | tf_op jit(solution)/shard_map/ppermute | solution.py:29
  37.7 0.9 multiply_add_fusion.4
  38.6 1.3 %collective-permute-start.6 = (f32[8,256,64]{1,2,0:T(8,128)}, f32[8,256,64]{1,2,0:T(8,128)S(1)}, u32[]{:S(2)}, u32[]{:S(2)}) collective-permute-start(f32[8,256,64]{1,2,0:T(8,128)} %multiply_add_fusion.4), channel_id=1, source_target_pairs={{16,0},{20,4},{24,8},{28,12},{17,1},{21,5},{25,9},{29,13},{18,2},{... | collective-permute-start | bytes 1572872 | tf_op jit(solution)/shard_map/ppermute | solution.py:29
  39.9 0.7 collective-permute-done.11
  40.6 0.9 multiply_add_fusion.1
  41.5 6.2 %collective-permute-start.13 = (f32[8,256,64]{1,2,0:T(8,128)}, f32[8,256,64]{1,2,0:T(8,128)}, u32[]{:S(2)}, u32[]{:S(2)}) collective-permute-start(f32[8,256,64]{1,2,0:T(8,128)} %multiply_add_fusion.1), channel_id=1, source_target_pairs={{0,16},{4,20},{8,24},{12,28},{1,17},{5,21},{9,25},{13,29},{2,18},{... | collective-permute-start | bytes 1572872 | tf_op jit(solution)/shard_map/ppermute | solution.py:29
  47.7 0.6 compare_convert_fusion
  48.3 1.4 %collective-permute-start.5 = (f32[8]{0:T(128)S(1)}, f32[8]{0:T(128)S(1)}, u32[]{:S(2)}, u32[]{:S(2)}) collective-permute-start(f32[8]{0:T(128)S(1)} %get-tuple-element.20), channel_id=1, source_target_pairs={{8,0},{12,4},{16,8},{20,12},{24,16},{28,20},{9,1},{13,5},{17,9},{2... | collective-permute-start | bytes 104 | tf_op jit(solution)/shard_map/ppermute | solution.py:29
  49.7 4.0 %collective-permute-start.12 = (f32[8]{0:T(128)S(1)}, f32[8]{0:T(128)S(1)}, u32[]{:S(2)}, u32[]{:S(2)}) collective-permute-start(f32[8]{0:T(128)S(1)} %get-tuple-element.21), channel_id=1, source_target_pairs={{0,8},{4,12},{8,16},{12,20},{16,24},{20,28},{1,9},{5,13},{9,17},{1... | collective-permute-start | bytes 104 | tf_op jit(solution)/shard_map/ppermute | solution.py:29
  53.7 0.5 mul.241
  54.2 4.2 %collective-permute-done.12 = f32[8]{0:T(128)S(1)} collective-permute-done((f32[8]{0:T(128)S(1)}, f32[8]{0:T(128)S(1)}, u32[]{:S(2)}, u32[]{:S(2)}) %collective-permute-start.12) | collective-permute-done | bytes 64 | tf_op jit(solution)/shard_map/ppermute | solution.py:29
  58.4 0.5 mul.267
  59.1 0.6 copy-done.26
  59.8 0.8 fusion.6
  60.6 1.4 %copy.34 = f32[8,128]{0,1:T(8,128)} copy(f32[8,128]{1,0:T(8,128)} %fusion.6) | data formatting | bytes 8192 | tf_op jit(solution)/shard_map/reduce_sum | solution.py:104
  62.0 2.7 %fusion.7 = f32[8,1,128]{2,1,0:T(1,128)} fusion(f32[8,128,1]{1,2,0:T(1,128)} %bitcast.100, f32[8,128,128]{2,1,0:T(8,128)} %copy-done.9, f32[128,128]{1,0:T(8,128)} %copy-done.26, f32[8,128]{1,0:T(8,128)} %copy-done.31, pred[128,128]{1,0:T(8,128)(4,1)S(1)} %iota_compare_fusion), kind=kOutput, calls=%fused_computation.31 | convolution fusion | flops 2097152 | bytes 618496 | tf_op jit(solution)/shard_map/hts,hs->th/dot_general | solution.py:103
  64.7 1.4 %copy.50 = f32[8,1,128]{0,2,1:T(8,128)} copy(f32[8,1,128]{2,1,0:T(1,128)} %fusion.7) | data formatting | bytes 8192 | tf_op jit(solution)/shard_map/hts,hs->th/dot_general | solution.py:103
  66.3 0.8 copy-done.6
  67.1 2.1 %multiply_reduce_fusion.1 = (f32[8]{0:T(128)}, f32[8,256,64]{1,2,0:T(8,128)S(1)}, f32[8,256,64]{1,2,0:T(8,128)S(1)}) fusion(f32[8,256,64]{1,2,0:T(8,128)S(1)} %convolution_bitcast_fusion, f32[8]{0:T(128)} %copy-done.50, f32[8,256,64]{1,2,0:T(8,128)} %collective-permute-done.13, f32[8]{0:T(128)} %mul.267, f32[8,256,64]{1,2,0:T(8,128)S(1)} %collective-permute-done.9, ...), kind=kLoop, calls=%fused_computation.11 | loop fusion | flops 1572856 | bytes 4718784 | tf_op jit(solution)/shard_map/reduce_sum | solution.py:122
  69.2 0.6 convolution_bitcast_fusion.5
  70.4 0.6 copy-done.35
  71.0 0.6 convolution_bitcast_fusion.4
  73.4 0.7 copy.39
  74.0 0.7 copy.40
  75.0 1.3 %collective-permute-start.14 = (bf16[128,128]{1,0:T(8,128)(2,1)S(1)}, bf16[128,128]{1,0:T(8,128)(2,1)S(1)}, u32[]{:S(2)}, u32[]{:S(2)}) collective-permute-start(bf16[128,128]{1,0:T(8,128)(2,1)S(1)} %select_convert_fusion), channel_id=1, source_target_pairs={{0,1},{1,0},{2,3},{3,2},{4,5},{5,4},{6,7},{7,6},{8,9},{9,8},{10,11... | collective-permute-start | bytes 98312 | tf_op jit(solution)/shard_map/ppermute | solution.py:16
  76.3 0.6 copy-done.52
  76.9 0.5 fusion.1
  77.6 0.8 copy-done.8
  78.5 3.1 %collective-permute-start.7 = (f32[3,512]{1,0:T(4,128)S(1)}, f32[3,512]{1,0:T(4,128)S(1)}, u32[]{:S(2)}, u32[]{:S(2)}) collective-permute-start(f32[3,512]{1,0:T(4,128)S(1)} %slice.57), channel_id=1, source_target_pairs={{4,0},{8,4},{12,8},{16,12},{20,16},{24,20},{28,24},{5,1},{9,5},{13... | collective-permute-start | bytes 18440 | tf_op jit(solution)/shard_map/ppermute | solution.py:44
  82.2 12.9 %collective-permute-done.7 = f32[3,512]{1,0:T(4,128)S(1)} collective-permute-done((f32[3,512]{1,0:T(4,128)S(1)}, f32[3,512]{1,0:T(4,128)S(1)}, u32[]{:S(2)}, u32[]{:S(2)}) %collective-permute-start.7) | collective-permute-done | bytes 6176 | tf_op jit(solution)/shard_map/ppermute | solution.py:44
  95.1 0.6 copy-done.37
  95.8 0.8 fusion.14
  96.6 0.6 convert_add_fusion
  97.2 0.6 convert_add_fusion.1
  (141 shorter events, 7.4 us)
Async XLA Ops:
  0.6 3.8 %copy-start.7 = (bf16[128,512]{1,0:T(8,128)(2,1)S(1)}, bf16[128,512]{1,0:T(8,128)(2,1)}, u32[]{:S(2)}) copy-start(bf16[128,512]{1,0:T(8,128)(2,1)} %param.8) | copy-start | bytes 393220
  0.6 5.5 %collective-permute-start.1 = (bf16[128,128]{1,0:T(8,128)(2,1)}, bf16[128,128]{1,0:T(8,128)(2,1)S(1)}, u32[]{:S(2)}, u32[]{:S(2)}) collective-permute-start(bf16[128,128]{1,0:T(8,128)(2,1)} %param.10), channel_id=1, source_target_pairs={{0,1},{1,0},{2,3},{3,2},{4,5},{5,4},{6,7},{7,6},{8,9},{9,8},{10,11... | collective-permute-start | bytes 98312 | tf_op jit(solution)/shard_map/ppermute | solution.py:16
  2.7 9.0 %collective-permute-start = (bf16[128,128]{1,0:T(8,128)(2,1)}, bf16[128,128]{1,0:T(8,128)(2,1)S(1)}, u32[]{:S(2)}, u32[]{:S(2)}) collective-permute-start(bf16[128,128]{1,0:T(8,128)(2,1)} %param.11), channel_id=1, source_target_pairs={{0,1},{1,0},{2,3},{3,2},{4,5},{5,4},{6,7},{7,6},{8,9},{9,8},{10,11... | collective-permute-start | bytes 98312 | tf_op jit(solution)/shard_map/ppermute | solution.py:16
  3.8 16.4 %copy-start = (f32[128,8]{1,0:T(8,128)}, f32[128,8]{1,0:T(8,128)S(1)}, u32[]{:S(2)}) copy-start(f32[128,8]{1,0:T(8,128)S(1)} %reduce_window_sum.18) | copy-start | bytes 12292
  5.1 1.1 %copy-start.28 = (f32[128,8]{0,1:T(8,128)}, f32[128,8]{0,1:T(8,128)S(1)}, u32[]{:S(2)}) copy-start(f32[128,8]{0,1:T(8,128)S(1)} %copy.30) | copy-start | bytes 12292
  5.1 0.9 copy-start.25
  6.1 5.7 %copy-start.34 = (f32[128,8]{0,1:T(8,128)}, f32[128,8]{0,1:T(8,128)S(1)}, u32[]{:S(2)}) copy-start(f32[128,8]{0,1:T(8,128)S(1)} %copy.31) | copy-start | bytes 12292
  6.2 1.0 %copy-start.19 = (bf16[128,128]{1,0:T(8,128)(2,1)}, bf16[128,128]{1,0:T(8,128)(2,1)S(1)}, u32[]{:S(2)}) copy-start(bf16[128,128]{1,0:T(8,128)(2,1)S(1)} %collective-permute-done.1) | copy-start | bytes 98308
  6.8 5.5 %copy-start.13 = (bf16[128,128]{1,0:T(8,128)(2,1)S(1)}, bf16[128,128]{1,0:T(8,128)(2,1)}, u32[]{:S(2)}) copy-start(bf16[128,128]{1,0:T(8,128)(2,1)} %param.11) | copy-start | bytes 98308
  7.2 13.1 %collective-permute-start.9 = (f32[8,256,64]{1,2,0:T(8,128)S(1)}, f32[8,256,64]{1,2,0:T(8,128)S(1)}, u32[]{:S(2)}, u32[]{:S(2)}) collective-permute-start(f32[8,256,64]{1,2,0:T(8,128)S(1)} %convolution_bitcast_fusion), channel_id=1, source_target_pairs={{0,4},{4,8},{8,12},{12,16},{16,20},{20,24},{24,28},{1,5},{5,9},{9,... | collective-permute-start | bytes 1572872 | tf_op jit(solution)/shard_map/ppermute | solution.py:29
  12.7 10.5 %collective-permute-start.2 = (f32[8,256,64]{1,2,0:T(8,128)S(1)}, f32[8,256,64]{1,2,0:T(8,128)S(1)}, u32[]{:S(2)}, u32[]{:S(2)}) collective-permute-start(f32[8,256,64]{1,2,0:T(8,128)S(1)} %convolution_bitcast_fusion.2), channel_id=1, source_target_pairs={{4,0},{8,4},{12,8},{16,12},{20,16},{24,20},{28,24},{5,1},{9,5},{13... | collective-permute-start | bytes 1572872 | tf_op jit(solution)/shard_map/ppermute | solution.py:29
  14.6 8.6 %copy-start.50 = (f32[8]{0:T(128)}, f32[8]{0:T(128)S(1)}, u32[]{:S(2)}) copy-start(f32[8]{0:T(128)S(1)} %fusion.49) | copy-start | bytes 100
  14.7 15.9 %collective-permute-start.10 = (f32[8]{0:T(128)S(1)}, f32[8]{0:T(128)S(1)}, u32[]{:S(2)}, u32[]{:S(2)}) collective-permute-start(f32[8]{0:T(128)S(1)} %fusion.49), channel_id=1, source_target_pairs={{0,4},{4,8},{8,12},{12,16},{16,20},{20,24},{24,28},{1,5},{5,9},{9,... | collective-permute-start | bytes 104 | tf_op jit(solution)/shard_map/ppermute | solution.py:29
  18.3 12.2 %collective-permute-start.3 = (f32[8]{0:T(128)S(1)}, f32[8]{0:T(128)S(1)}, u32[]{:S(2)}, u32[]{:S(2)}) collective-permute-start(f32[8]{0:T(128)S(1)} %fusion.49), channel_id=1, source_target_pairs={{4,0},{8,4},{12,8},{16,12},{20,16},{24,20},{28,24},{5,1},{9,5},{13... | collective-permute-start | bytes 104 | tf_op jit(solution)/shard_map/ppermute | solution.py:29
  20.3 4.5 %copy-start.31 = (f32[8,128]{1,0:T(8,128)}, f32[8,128]{1,0:T(8,128)S(1)}, u32[]{:S(2)}) copy-start(f32[8,128]{1,0:T(8,128)S(1)} %copy.26) | copy-start | bytes 12292
  23.4 6.5 %copy-start.40 = (f32[4,512]{1,0:T(4,128)S(1)}, f32[4,512]{1,0:T(4,128)}, u32[]{:S(2)}) copy-start(f32[4,512]{1,0:T(4,128)} %param.15) | copy-start | bytes 24580
  23.5 14.2 %collective-permute-start.4 = (f32[8,256,64]{1,2,0:T(8,128)S(1)}, f32[8,256,64]{1,2,0:T(8,128)S(1)}, u32[]{:S(2)}, u32[]{:S(2)}) collective-permute-start(f32[8,256,64]{1,2,0:T(8,128)S(1)} %get-tuple-element.28), channel_id=1, source_target_pairs={{8,0},{12,4},{16,8},{20,12},{24,16},{28,20},{9,1},{13,5},{17,9},{2... | collective-permute-start | bytes 1572872 | tf_op jit(solution)/shard_map/ppermute | solution.py:29
  25.9 33.2 %copy-start.9 = (f32[8,128,128]{2,1,0:T(8,128)}, f32[8,128,128]{2,1,0:T(8,128)S(1)}, u32[]{:S(2)}) copy-start(f32[8,128,128]{2,1,0:T(8,128)S(1)} %get-tuple-element.31) | copy-start | bytes 1572868
  25.9 14.7 %collective-permute-start.11 = (f32[8,256,64]{1,2,0:T(8,128)S(1)}, f32[8,256,64]{1,2,0:T(8,128)S(1)}, u32[]{:S(2)}, u32[]{:S(2)}) collective-permute-start(f32[8,256,64]{1,2,0:T(8,128)S(1)} %get-tuple-element.29), channel_id=1, source_target_pairs={{0,8},{4,12},{8,16},{12,20},{16,24},{20,28},{1,9},{5,13},{9,17},{1... | collective-permute-start | bytes 1572872 | tf_op jit(solution)/shard_map/ppermute | solution.py:29
  30.5 7.1 %copy-start.43 = (f32[8]{0:T(128)}, f32[8]{0:T(128)S(1)}, u32[]{:S(2)}) copy-start(f32[8]{0:T(128)S(1)} %collective-permute-done.10) | copy-start | bytes 100
  30.5 7.1 %copy-start.45 = (f32[8]{0:T(128)}, f32[8]{0:T(128)S(1)}, u32[]{:S(2)}) copy-start(f32[8]{0:T(128)S(1)} %collective-permute-done.3) | copy-start | bytes 100
  38.6 27.7 %collective-permute-start.6 = (f32[8,256,64]{1,2,0:T(8,128)}, f32[8,256,64]{1,2,0:T(8,128)S(1)}, u32[]{:S(2)}, u32[]{:S(2)}) collective-permute-start(f32[8,256,64]{1,2,0:T(8,128)} %multiply_add_fusion.4), channel_id=1, source_target_pairs={{16,0},{20,4},{24,8},{28,12},{17,1},{21,5},{25,9},{29,13},{18,2},{... | collective-permute-start | bytes 1572872 | tf_op jit(solution)/shard_map/ppermute | solution.py:29
  40.6 18.4 %copy-start.11 = (bf16[128,128]{1,0:T(8,128)(2,1)S(1)}, bf16[128,128]{1,0:T(8,128)(2,1)}, u32[]{:S(2)}) copy-start(bf16[128,128]{1,0:T(8,128)(2,1)} %param.10) | copy-start | bytes 98308
  40.6 18.4 %copy-start.14 = (bf16[128,128]{1,0:T(8,128)(2,1)S(1)}, bf16[128,128]{1,0:T(8,128)(2,1)}, u32[]{:S(2)}) copy-start(bf16[128,128]{1,0:T(8,128)(2,1)} %param.11) | copy-start | bytes 98308
  40.6 18.4 %copy-start.17 = (bf16[128,128]{1,0:T(8,128)(2,1)S(1)}, bf16[128,128]{1,0:T(8,128)(2,1)}, u32[]{:S(2)}) copy-start(bf16[128,128]{1,0:T(8,128)(2,1)} %copy-done.16) | copy-start | bytes 98308
  40.6 18.4 %copy-start.20 = (bf16[128,128]{1,0:T(8,128)(2,1)S(1)}, bf16[128,128]{1,0:T(8,128)(2,1)}, u32[]{:S(2)}) copy-start(bf16[128,128]{1,0:T(8,128)(2,1)} %copy-done.19) | copy-start | bytes 98308
  41.5 12.2 %copy-start.46 = (f32[8]{0:T(128)S(1)}, f32[8]{0:T(128)}, u32[]{:S(2)}) copy-start(f32[8]{0:T(128)} %copy-done.45) | copy-start | bytes 100
  41.5 25.6 %collective-permute-start.13 = (f32[8,256,64]{1,2,0:T(8,128)}, f32[8,256,64]{1,2,0:T(8,128)}, u32[]{:S(2)}, u32[]{:S(2)}) collective-permute-start(f32[8,256,64]{1,2,0:T(8,128)} %multiply_add_fusion.1), channel_id=1, source_target_pairs={{0,16},{4,20},{8,24},{12,28},{1,17},{5,21},{9,25},{13,29},{2,18},{... | collective-permute-start | bytes 1572872 | tf_op jit(solution)/shard_map/ppermute | solution.py:29
  48.3 10.1 %copy-start.44 = (f32[8]{0:T(128)S(1)}, f32[8]{0:T(128)}, u32[]{:S(2)}) copy-start(f32[8]{0:T(128)} %copy-done.43) | copy-start | bytes 100
  48.3 5.4 %collective-permute-start.5 = (f32[8]{0:T(128)S(1)}, f32[8]{0:T(128)S(1)}, u32[]{:S(2)}, u32[]{:S(2)}) collective-permute-start(f32[8]{0:T(128)S(1)} %get-tuple-element.20), channel_id=1, source_target_pairs={{8,0},{12,4},{16,8},{20,12},{24,16},{28,20},{9,1},{13,5},{17,9},{2... | collective-permute-start | bytes 104 | tf_op jit(solution)/shard_map/ppermute | solution.py:29
  49.7 8.7 %collective-permute-start.12 = (f32[8]{0:T(128)S(1)}, f32[8]{0:T(128)S(1)}, u32[]{:S(2)}, u32[]{:S(2)}) collective-permute-start(f32[8]{0:T(128)S(1)} %get-tuple-element.21), channel_id=1, source_target_pairs={{0,8},{4,12},{8,16},{12,20},{16,24},{20,28},{1,9},{5,13},{9,17},{1... | collective-permute-start | bytes 104 | tf_op jit(solution)/shard_map/ppermute | solution.py:29
  67.1 2.1 %copy-start.29 = (f32[128,8]{0,1:T(8,128)S(1)}, f32[128,8]{0,1:T(8,128)}, u32[]{:S(2)}) copy-start(f32[128,8]{0,1:T(8,128)} %copy-done.28) | copy-start | bytes 12292
  71.8 0.8 copy-start.3
  71.8 0.9 copy-start.5
  71.8 0.9 copy-start.23
  71.8 0.9 copy-start.24
  72.2 0.9 copy-start.1
  73.4 1.3 %copy-start.22 = (f32[128,128]{0,1:T(8,128)S(1)}, f32[128,128]{0,1:T(8,128)}, u32[]{:S(2)}) copy-start(f32[128,128]{0,1:T(8,128)} %get-tuple-element.30) | copy-start | bytes 196612
  74.9 1.3 %copy-start.27 = (f32[128,128]{1,0:T(8,128)S(1)}, f32[128,128]{1,0:T(8,128)}, u32[]{:S(2)}) copy-start(f32[128,128]{1,0:T(8,128)} %copy-done.26) | copy-start | bytes 196612
  74.9 1.3 %copy-start.33 = (f32[8,128]{1,0:T(8,128)S(1)}, f32[8,128]{1,0:T(8,128)}, u32[]{:S(2)}) copy-start(f32[8,128]{1,0:T(8,128)} %copy-done.31) | copy-start | bytes 12292
  74.9 1.3 %copy-start.42 = (f32[128,8]{0,1:T(8,128)S(1)}, f32[128,8]{0,1:T(8,128)}, u32[]{:S(2)}) copy-start(f32[128,8]{0,1:T(8,128)} %param.13) | copy-start | bytes 12292
  75.0 1.3 %copy-start.30 = (f32[128,8]{0,1:T(8,128)S(1)}, f32[128,8]{0,1:T(8,128)}, u32[]{:S(2)}) copy-start(f32[128,8]{0,1:T(8,128)} %copy-done.28) | copy-start | bytes 12292
  75.0 21.6 %collective-permute-start.14 = (bf16[128,128]{1,0:T(8,128)(2,1)S(1)}, bf16[128,128]{1,0:T(8,128)(2,1)S(1)}, u32[]{:S(2)}, u32[]{:S(2)}) collective-permute-start(bf16[128,128]{1,0:T(8,128)(2,1)S(1)} %select_convert_fusion), channel_id=1, source_target_pairs={{0,1},{1,0},{2,3},{3,2},{4,5},{5,4},{6,7},{7,6},{8,9},{9,8},{10,11... | collective-permute-start | bytes 98312 | tf_op jit(solution)/shard_map/ppermute | solution.py:16
  77.4 0.9 copy-start.8
  78.5 16.6 %collective-permute-start.7 = (f32[3,512]{1,0:T(4,128)S(1)}, f32[3,512]{1,0:T(4,128)S(1)}, u32[]{:S(2)}, u32[]{:S(2)}) collective-permute-start(f32[3,512]{1,0:T(4,128)S(1)} %slice.57), channel_id=1, source_target_pairs={{4,0},{8,4},{12,8},{16,12},{20,16},{24,20},{28,24},{5,1},{9,5},{13... | collective-permute-start | bytes 18440 | tf_op jit(solution)/shard_map/ppermute | solution.py:44
  81.5 13.6 %copy-start.38 = (f32[1,512]{1,0:T(1,128)S(1)}, f32[1,512]{1,0:T(1,128)}, u32[]{:S(2)}) copy-start(f32[1,512]{1,0:T(1,128)} %get-tuple-element.26) | copy-start | bytes 6148
  81.5 13.6 %copy-start.39 = (f32[1,512]{1,0:T(1,128)S(1)}, f32[1,512]{1,0:T(1,128)}, u32[]{:S(2)}) copy-start(f32[1,512]{1,0:T(1,128)} %get-tuple-element.27) | copy-start | bytes 6148
  81.8 15.4 %collective-permute-start.8 = (bf16[128,128]{1,0:T(8,128)(2,1)S(1)}, bf16[128,128]{1,0:T(8,128)(2,1)S(1)}, u32[]{:S(2)}, u32[]{:S(2)}) collective-permute-start(bf16[128,128]{1,0:T(8,128)(2,1)S(1)} %select_convert_fusion.1), channel_id=1, source_target_pairs={{0,1},{1,0},{2,3},{3,2},{4,5},{5,4},{6,7},{7,6},{8,9},{9,8},{10,11... | collective-permute-start | bytes 98312 | tf_op jit(solution)/shard_map/ppermute | solution.py:16
  (20 other events, 14.2 us)

commit v2 on v1

--- a/solution.py
+++ b/solution.py
@@ -36,6 +36,36 @@
                 window[k] = (win_a * far_a, win_s + win_a[:, None, None] * far_s)
         distance *= 2
     return [s for _, s in near]
+
+
+def chip_scanned_in(shards, axis):
+    peers = lax.axis_size(axis)
+    if peers % 2:
+        return scanned_in(shards, axis)
+    parity = lax.axis_index(axis) % 2
+    pairs = [(2 * k, 2 * k + 1) for k in range(peers // 2)]
+    results = []
+    for own_a, own_s, reverse in shards:
+        inward = [(b, a) for a, b in pairs] if reverse else pairs
+        heads = [b for _, b in inward]
+        mate_a, mate_s = lax.ppermute((own_a, own_s), axis, inward)
+        window = (own_a * mate_a, own_s + own_a[:, None, None] * mate_s)
+        near = (jnp.ones_like(own_a), jnp.zeros_like(own_s))
+        distance = 2
+        while distance < peers:
+            step = -distance if reverse else distance
+            route = [(i, i + step) for i in heads if 0 <= i + step < peers]
+            far_a, far_s = lax.ppermute(window, axis, route)
+            near = (near[0] * far_a, near[1] + near[0][:, None, None] * far_s)
+            if 2 * distance < peers:
+                window = (window[0] * far_a, window[1] + window[0][:, None, None] * far_s)
+            distance *= 2
+        handed = lax.ppermute(near[1], axis, [(b, a) for a, b in inward])
+        is_head = parity == (0 if reverse else 1)
+        results.append(
+            jnp.where(is_head, mate_s + mate_a[:, None, None] * near[1], handed)
+        )
+    return results
 
 
 def shifted(block, axis, distance):
@@ -82,7 +112,7 @@
     local_state = jnp.einsum("ln,lhp->hnp", keys_full, weighted, precision=precise)
     local_grad = jnp.einsum("ln,lhp->hnp", queries_full, seeded, precision=precise)
     decay_total = jnp.exp(totals)
-    entering, arriving = scanned_in(
+    entering, arriving = chip_scanned_in(
         [(decay_total, local_state, False), (decay_total, local_grad, True)], "seq"
     )
     scores = product(queries_full, keys_full.T)

time: 99.2 us -> 80.4 us (0.81)
  waiting for transfers between devices: 27.2 us -> 5.93 us
  matrix products: 7.77 us -> 9.21 us
  other arithmetic: 10 us -> 11.1 us
    ppermute x10 -> x12, waiting for transfers between devices: 14.3 us -> 3.33 us  [the longest x6 1.88 us: chip_scanned_in(): far_a, far_s = lax.ppermute(window, axis, route)]
    ppermute x1, waiting for transfers between devices: 12.9 us -> 2.59 us  [shifted(): return lax.ppermute(block, axis, route)]
    add x3 -> x5, other arithmetic: 2.05 us -> 4.36 us  [the longest x2 2.32 us: chip_scanned_in(): near = (near[0] * far_a, near[1] + near[0][:, None, None] * far_s)]
    ppermute x1, starting transfers between devices: 3.05 us -> 1.92 us  [shifted(): return lax.ppermute(block, axis, route)]
    mul x3 -> x1, other arithmetic: 1.73 us -> 0.7 us  [chip_scanned_in(): window = (own_a * mate_a, own_s + own_a[:, None, None] * mate_s)]
    ppermute x10 -> x12, starting transfers between devices: 30.2 us -> 31 us  [the longest x6 16.1 us: chip_scanned_in(): far_a, far_s = lax.ppermute(window, axis, route)]
    unnamed x111 -> x107, local copies, waits for them, and re-layouts: 10.5 us -> 9.84 us
  transfers between devices with their start and end apart: 15 -> 17, of which waited for: 6 -> 3; matrix products, arithmetic and copies ran while one was open for 18% -> 26% of each run, Pallas kernels for 0% -> 0%
where the time goes in v2:
time: 80.4 us; the launch traced here: 79.1 us
  starting transfers between devices  36.8 us (46%)
  local copies, waits for them, and re-layouts  14.8 us (18%)
  other arithmetic  11.1 us (14%)
  matrix products  9.21 us (11%)
  waiting for transfers between devices  5.93 us (7%)
  between operations  1.27 us (2%)
    ppermute x6, starting transfers between devices, chip_scanned_in(): far_a, far_s = lax.ppermute(window, axis, route)  16.1 us
    unnamed x107, local copies, waits for them, and re-layouts  9.84 us
    ppermute x4, starting transfers between devices, chip_scanned_in(): mate_a, mate_s = lax.ppermute((own_a, own_s), axis, inward)  8.7 us
    ppermute x2, starting transfers between devices, chip_scanned_in(): handed = lax.ppermute(near[1], axis, [(b, a) for a, b in inward])  6.27 us
    ppermute x4, starting transfers between devices, swapped(): return lax.ppermute(block, axis, route)  3.9 us
    ppermute x1, waiting for transfers between devices, shifted(): return lax.ppermute(block, axis, route)  2.59 us
    dot_general x1, matrix products, body(): row_sums = jnp.einsum('hts,hs->th', effect, step_heads, precision=precise)  2.51 us
    add x2, other arithmetic, chip_scanned_in(): near = (near[0] * far_a, near[1] + near[0][:, None, None] * far_s)  2.32 us
  transfers between devices with their start and end apart: 17, of which 3 were waited for; matrix products, arithmetic and copies ran while one was open for 26% of the time, Pallas kernels for 0%

profile of v2, /device:TPU:1, one launch (start us, length us, event | category | flops | bytes accessed | tf_op | source)
XLA Modules:
  0.0 79.1 jit_solution(8271290211532814015)
XLA Ops:
  0.6 2.1 %collective-permute-start.1 = (bf16[128,128]{1,0:T(8,128)(2,1)}, bf16[128,128]{1,0:T(8,128)(2,1)S(1)}, u32[]{:S(2)}, u32[]{:S(2)}) collective-permute-start(bf16[128,128]{1,0:T(8,128)(2,1)} %param.10), channel_id=1, source_target_pairs={{0,1},{1,0},{2,3},{3,2},{4,5},{5,4},{6,7},{7,6},{8,9},{9,8},{10,11... | collective-permute-start | bytes 98312 | tf_op jit(solution)/shard_map/ppermute | solution.py:16
  2.8 0.8 copy.25
  6.2 0.6 copy-done.9
  7.2 1.3 %collective-permute-start.10 = (f32[8,256,64]{1,2,0:T(8,128)S(1)}, f32[8,256,64]{1,2,0:T(8,128)S(1)}, u32[]{:S(2)}, u32[]{:S(2)}) collective-permute-start(f32[8,256,64]{1,2,0:T(8,128)S(1)} %convolution_bitcast_fusion), channel_id=1, source_target_pairs={{0,4},{8,12},{16,20},{24,28},{1,5},{9,13},{17,21},{25,29},{2,6},{1... | collective-permute-start | bytes 1572872 | tf_op jit(solution)/shard_map/ppermute | solution.py:51
  8.5 0.6 copy-done.13
  9.5 3.1 %collective-permute-start.2 = (f32[8,256,64]{1,2,0:T(8,128)S(1)}, f32[8,256,64]{1,2,0:T(8,128)S(1)}, u32[]{:S(2)}, u32[]{:S(2)}) collective-permute-start(f32[8,256,64]{1,2,0:T(8,128)S(1)} %convolution_bitcast_fusion.2), channel_id=1, source_target_pairs={{4,0},{12,8},{20,16},{28,24},{5,1},{13,9},{21,17},{29,25},{6,2},{1... | collective-permute-start | bytes 1572872 | tf_op jit(solution)/shard_map/ppermute | solution.py:51
  12.6 1.4 %collective-permute-done.2 = f32[8,256,64]{1,2,0:T(8,128)S(1)} collective-permute-done((f32[8,256,64]{1,2,0:T(8,128)S(1)}, f32[8,256,64]{1,2,0:T(8,128)S(1)}, u32[]{:S(2)}, u32[]{:S(2)}) %collective-permute-start.2) | collective-permute-done | bytes 524320 | tf_op jit(solution)/shard_map/ppermute | solution.py:51
  14.3 0.7 collective-permute-start.4
  15.0 1.3 %collective-permute-start.11 = (f32[8]{0:T(128)S(1)}, f32[8]{0:T(128)S(1)}, u32[]{:S(2)}, u32[]{:S(2)}) collective-permute-start(f32[8]{0:T(128)S(1)} %fusion.50), channel_id=1, source_target_pairs={{0,4},{8,12},{16,20},{24,28},{1,5},{9,13},{17,21},{25,29},{2,6},{1... | collective-permute-start | bytes 104 | tf_op jit(solution)/shard_map/ppermute | solution.py:51
  16.3 3.0 %collective-permute-start.3 = (f32[8]{0:T(128)S(1)}, f32[8]{0:T(128)S(1)}, u32[]{:S(2)}, u32[]{:S(2)}) collective-permute-start(f32[8]{0:T(128)S(1)} %fusion.50), channel_id=1, source_target_pairs={{4,0},{12,8},{20,16},{28,24},{5,1},{13,9},{21,17},{29,25},{6,2},{1... | collective-permute-start | bytes 104 | tf_op jit(solution)/shard_map/ppermute | solution.py:51
  19.4 4.1 %collective-permute-start.12 = (f32[8,256,64]{1,2,0:T(8,128)S(1)}, f32[8,256,64]{1,2,0:T(8,128)S(1)}, u32[]{:S(2)}, u32[]{:S(2)}) collective-permute-start(f32[8,256,64]{1,2,0:T(8,128)S(1)} %get-tuple-element.29), channel_id=1, source_target_pairs={{4,12},{12,20},{20,28},{5,13},{13,21},{21,29},{6,14},{14,22},{22,3... | collective-permute-start | bytes 1572872 | tf_op jit(solution)/shard_map/ppermute | solution.py:58
  23.5 0.6 fusion.57
  24.2 0.7 fusion.52
  25.4 0.9 %multiply_add_fusion.4 = f32[8,256,64]{1,2,0:T(8,128)} fusion(f32[8,256,64]{1,2,0:T(8,128)S(1)} %get-tuple-element.28, f32[8,256,64]{1,2,0:T(8,128)S(1)} %collective-permute-done.4, f32[8]{0:T(128)S(1)} %get-tuple-element.20), kind=kLoop, calls=%fused_computation.17 | loop fusion | flops 262144 | bytes 1572896 | tf_op jit(solution)/shard_map/add | solution.py:61
  26.3 1.4 %collective-permute-start.6 = (f32[8,256,64]{1,2,0:T(8,128)}, f32[8,256,64]{1,2,0:T(8,128)}, u32[]{:S(2)}, u32[]{:S(2)}) collective-permute-start(f32[8,256,64]{1,2,0:T(8,128)} %multiply_add_fusion.4), channel_id=1, source_target_pairs={{16,0},{24,8},{17,1},{25,9},{18,2},{26,10},{19,3},{27,11}} | collective-permute-start | bytes 1572872 | tf_op jit(solution)/shard_map/ppermute | solution.py:58
  27.7 1.9 %collective-permute-done.12 = f32[8,256,64]{1,2,0:T(8,128)S(1)} collective-permute-done((f32[8,256,64]{1,2,0:T(8,128)S(1)}, f32[8,256,64]{1,2,0:T(8,128)S(1)}, u32[]{:S(2)}, u32[]{:S(2)}) %collective-permute-start.12) | collective-permute-done | bytes 524320 | tf_op jit(solution)/shard_map/ppermute | solution.py:58
  29.6 0.9 %multiply_add_fusion.1 = f32[8,256,64]{1,2,0:T(8,128)} fusion(f32[8,256,64]{1,2,0:T(8,128)S(1)} %get-tuple-element.29, f32[8,256,64]{1,2,0:T(8,128)S(1)} %collective-permute-done.12, f32[8]{0:T(128)S(1)} %get-tuple-element.21), kind=kLoop, calls=%fused_computation.13 | loop fusion | flops 262144 | bytes 1572896 | tf_op jit(solution)/shard_map/add | solution.py:61
  30.5 5.9 %collective-permute-start.14 = (f32[8,256,64]{1,2,0:T(8,128)}, f32[8,256,64]{1,2,0:T(8,128)}, u32[]{:S(2)}, u32[]{:S(2)}) collective-permute-start(f32[8,256,64]{1,2,0:T(8,128)} %multiply_add_fusion.1), channel_id=1, source_target_pairs={{4,20},{12,28},{5,21},{13,29},{6,22},{14,30},{7,23},{15,31}} | collective-permute-start | bytes 1572872 | tf_op jit(solution)/shard_map/ppermute | solution.py:58
  36.4 0.9 %copy.26 = f32[8,128]{1,0:T(8,128)S(1)} copy(f32[8,128]{0,1:T(8,128)} %bitcast.93) | data formatting | bytes 8192 | tf_op jit(solution)/shard_map/transpose | solution.py:122
  37.4 1.9 %multiply_reduce_fusion = (f32[128,128]{0,1:T(8,128)}, f32[8,128,128]{2,1,0:T(8,128)}) fusion(f32[128,8]{0,1:T(8,128)S(1)} %copy-done.37, f32[8,128]{1,0:T(8,128)S(1)} %copy.26, pred[128,128]{1,0:T(8,128)(4,1)S(1)} %iota_compare_fusion, f32[128,8,64]{0,2,1:T(8,128)S(1)} %bitcast.87, bf16[128,8,64]{0,2,1:T(8,128)(2,1)S(1)} %bitcast.90), kind=kOutput, calls=%fused_computation.9 | convolution fusion | flops 101302272 | bytes 1007616 | tf_op jit(solution)/shard_map/thp,shp->hts/dot_general | solution.py:126
  39.3 0.7 collective-permute-start.5
  40.0 3.2 %collective-permute-start.13 = (f32[8]{0:T(128)S(1)}, f32[8]{0:T(128)S(1)}, u32[]{:S(2)}, u32[]{:S(2)}) collective-permute-start(f32[8]{0:T(128)S(1)} %copy-done.42), channel_id=1, source_target_pairs={{4,12},{12,20},{20,28},{5,13},{13,21},{21,29},{6,14},{14,22},{22,3... | collective-permute-start | bytes 104 | tf_op jit(solution)/shard_map/ppermute | solution.py:58
  43.2 1.2 %multiply_add_fusion.3 = f32[8,256,64]{1,2,0:T(8,128)S(1)} fusion(f32[8,256,64]{1,2,0:T(8,128)S(1)} %collective-permute-done.4, f32[8,256,64]{1,2,0:T(8,128)} %collective-permute-done.6, f32[8]{0:T(128)S(1)} %collective-permute-done.5), kind=kLoop, calls=%fused_computation.16 | loop fusion | flops 262144 | bytes 1572896 | tf_op jit(solution)/shard_map/add | solution.py:59
  44.4 1.3 %collective-permute-start.7 = (f32[8,256,64]{1,2,0:T(8,128)S(1)}, f32[8,256,64]{1,2,0:T(8,128)}, u32[]{:S(2)}, u32[]{:S(2)}) collective-permute-start(f32[8,256,64]{1,2,0:T(8,128)S(1)} %multiply_add_fusion.3), channel_id=1, source_target_pairs={{0,4},{8,12},{16,20},{24,28},{1,5},{9,13},{17,21},{25,29},{2,6},{1... | collective-permute-start | bytes 1572872 | tf_op jit(solution)/shard_map/ppermute | solution.py:63
  45.7 1.2 %multiply_add_fusion = f32[8,256,64]{1,2,0:T(8,128)S(1)} fusion(f32[8,256,64]{1,2,0:T(8,128)S(1)} %collective-permute-done.12, f32[8,256,64]{1,2,0:T(8,128)} %collective-permute-done.14, f32[8]{0:T(128)S(1)} %collective-permute-done.13), kind=kLoop, calls=%fused_computation.12 | loop fusion | flops 262144 | bytes 1572896 | tf_op jit(solution)/shard_map/add | solution.py:59
  46.9 5.0 %collective-permute-start.15 = (f32[8,256,64]{1,2,0:T(8,128)S(1)}, f32[8,256,64]{1,2,0:T(8,128)}, u32[]{:S(2)}, u32[]{:S(2)}) collective-permute-start(f32[8,256,64]{1,2,0:T(8,128)S(1)} %multiply_add_fusion), channel_id=1, source_target_pairs={{4,0},{12,8},{20,16},{28,24},{5,1},{13,9},{21,17},{29,25},{6,2},{1... | collective-permute-start | bytes 1572872 | tf_op jit(solution)/shard_map/ppermute | solution.py:63
  51.9 0.6 compare_convert_fusion
  52.4 1.0 %fusion.54 = f32[128,128]{1,0:T(8,128)S(1)} fusion(bf16[128,128]{1,0:T(8,128)(2,1)} %copy-done.15, bf16[128,128]{1,0:T(8,128)(2,1)} %param.10, pred[]{:T(512)S(6)} %eq.23, bf16[128,128]{1,0:T(8,128)(2,1)} %copy-done.13, bf16[128,128]{1,0:T(8,128)(2,1)} %param.11), kind=kOutput, calls=%fused_computation.95 | convolution fusion | flops 8978432 | bytes 196609 | tf_op jit(solution)/shard_map/dot_general | solution.py:78
  53.5 0.6 copy-done.21
  54.1 0.8 %fusion.5 = f32[8,128]{1,0:T(8,128)} fusion(f32[8,128,128]{2,1,0:T(8,128)S(1)} %copy-done.8, f32[128,128]{1,0:T(8,128)S(1)} %fusion.54, f32[8,128]{1,0:T(8,128)S(1)} %copy-done.29, pred[128,128]{1,0:T(8,128)(4,1)S(1)} %iota_compare_fusion), kind=kLoop, calls=%fused_computation.31 | loop fusion | flops 654336 | bytes 614400 | tf_op jit(solution)/shard_map/reduce_sum | solution.py:134
  54.9 1.4 %copy.34 = f32[8,128]{0,1:T(8,128)} copy(f32[8,128]{1,0:T(8,128)} %fusion.5) | data formatting | bytes 8192 | tf_op jit(solution)/shard_map/reduce_sum | solution.py:134
  56.3 2.5 %fusion.6 = f32[8,1,128]{2,1,0:T(1,128)} fusion(f32[8,128,1]{1,2,0:T(1,128)} %bitcast.100, f32[8,128,128]{2,1,0:T(8,128)S(1)} %copy-done.8, f32[128,128]{1,0:T(8,128)} %copy-done.21, f32[8,128]{1,0:T(8,128)} %copy-done.28, pred[128,128]{1,0:T(8,128)(4,1)S(1)} %iota_compare_fusion), kind=kOutput, calls=%fused_computation.32 | convolution fusion | flops 2097152 | bytes 618496 | tf_op jit(solution)/shard_map/hts,hs->th/dot_general | solution.py:133
  58.8 1.4 %copy.50 = f32[8,1,128]{0,2,1:T(8,128)} copy(f32[8,1,128]{2,1,0:T(1,128)} %fusion.6) | data formatting | bytes 8192 | tf_op jit(solution)/shard_map/hts,hs->th/dot_general | solution.py:133
  60.2 1.9 %multiply_reduce_fusion.1 = (f32[8]{0:T(128)}, f32[8,256,64]{1,2,0:T(8,128)S(1)}, f32[8,256,64]{1,2,0:T(8,128)S(1)}) fusion(f32[8,256,64]{1,2,0:T(8,128)S(1)} %convolution_bitcast_fusion, f32[8]{0:T(128)} %copy-done.48, f32[8,256,64]{1,2,0:T(8,128)} %collective-permute-done.15, f32[8,256,64]{1,2,0:T(8,128)S(1)} %collective-permute-done.10, ...), kind=kLoop, calls=%fused_computation.10 | loop fusion | flops 1310712 | bytes 4718722 | tf_op jit(solution)/shard_map/reduce_sum | solution.py:152
  62.2 0.6 convolution_bitcast_fusion.5
  63.6 0.6 convolution_bitcast_fusion.4
  66.0 0.7 copy.39
  66.7 0.7 copy.40
  67.6 1.6 %collective-permute-start.16 = (bf16[128,128]{1,0:T(8,128)(2,1)S(1)}, bf16[128,128]{1,0:T(8,128)(2,1)S(1)}, u32[]{:S(2)}, u32[]{:S(2)}) collective-permute-start(bf16[128,128]{1,0:T(8,128)(2,1)S(1)} %select_convert_fusion), channel_id=1, source_target_pairs={{0,1},{1,0},{2,3},{3,2},{4,5},{5,4},{6,7},{7,6},{8,9},{9,8},{10,11... | collective-permute-start | bytes 98312 | tf_op jit(solution)/shard_map/ppermute | solution.py:16
  69.2 0.6 copy-done.50
  69.8 0.5 multiply_add_fusion.6
  70.5 0.8 copy-done.7
  71.4 1.9 %collective-permute-start.8 = (f32[3,512]{1,0:T(4,128)S(1)}, f32[3,512]{1,0:T(4,128)S(1)}, u32[]{:S(2)}, u32[]{:S(2)}) collective-permute-start(f32[3,512]{1,0:T(4,128)S(1)} %slice.57), channel_id=1, source_target_pairs={{4,0},{8,4},{12,8},{16,12},{20,16},{24,20},{28,24},{5,1},{9,5},{13... | collective-permute-start | bytes 18440 | tf_op jit(solution)/shard_map/ppermute | solution.py:74
  73.8 2.6 %collective-permute-done.8 = f32[3,512]{1,0:T(4,128)S(1)} collective-permute-done((f32[3,512]{1,0:T(4,128)S(1)}, f32[3,512]{1,0:T(4,128)S(1)}, u32[]{:S(2)}, u32[]{:S(2)}) %collective-permute-start.8) | collective-permute-done | bytes 6176 | tf_op jit(solution)/shard_map/ppermute | solution.py:74
  76.4 0.7 copy-done.32
  77.0 0.8 fusion.13
  77.8 0.6 convert_add_fusion
  78.5 0.6 convert_add_fusion.1
  (141 shorter events, 7.6 us)
Async XLA Ops:
  0.6 3.8 %copy-start.6 = (bf16[128,512]{1,0:T(8,128)(2,1)S(1)}, bf16[128,512]{1,0:T(8,128)(2,1)}, u32[]{:S(2)}) copy-start(bf16[128,512]{1,0:T(8,128)(2,1)} %param.8) | copy-start | bytes 393220
  0.6 5.5 %collective-permute-start.1 = (bf16[128,128]{1,0:T(8,128)(2,1)}, bf16[128,128]{1,0:T(8,128)(2,1)S(1)}, u32[]{:S(2)}, u32[]{:S(2)}) collective-permute-start(bf16[128,128]{1,0:T(8,128)(2,1)} %param.10), channel_id=1, source_target_pairs={{0,1},{1,0},{2,3},{3,2},{4,5},{5,4},{6,7},{7,6},{8,9},{9,8},{10,11... | collective-permute-start | bytes 98312 | tf_op jit(solution)/shard_map/ppermute | solution.py:16
  2.7 5.8 %collective-permute-start = (bf16[128,128]{1,0:T(8,128)(2,1)}, bf16[128,128]{1,0:T(8,128)(2,1)S(1)}, u32[]{:S(2)}, u32[]{:S(2)}) collective-permute-start(bf16[128,128]{1,0:T(8,128)(2,1)} %param.11), channel_id=1, source_target_pairs={{0,1},{1,0},{2,3},{3,2},{4,5},{5,4},{6,7},{7,6},{8,9},{9,8},{10,11... | collective-permute-start | bytes 98312 | tf_op jit(solution)/shard_map/ppermute | solution.py:16
  3.8 8.8 %copy-start = (f32[128,8]{1,0:T(8,128)}, f32[128,8]{1,0:T(8,128)S(1)}, u32[]{:S(2)}) copy-start(f32[128,8]{1,0:T(8,128)S(1)} %reduce_window_sum.18) | copy-start | bytes 12292
  5.1 1.1 %copy-start.23 = (f32[128,8]{0,1:T(8,128)}, f32[128,8]{0,1:T(8,128)S(1)}, u32[]{:S(2)}) copy-start(f32[128,8]{0,1:T(8,128)S(1)} %copy.30) | copy-start | bytes 12292
  5.1 0.9 %copy-start.20 = (bf16[128,512]{1,0:T(8,128)(2,1)S(1)}, bf16[128,512]{1,0:T(8,128)(2,1)}, u32[]{:S(2)}) copy-start(bf16[128,512]{1,0:T(8,128)(2,1)} %param.9) | copy-start | bytes 393220
  6.1 2.5 %copy-start.26 = (f32[128,8]{0,1:T(8,128)}, f32[128,8]{0,1:T(8,128)S(1)}, u32[]{:S(2)}) copy-start(f32[128,8]{0,1:T(8,128)S(1)} %copy.31) | copy-start | bytes 12292
  6.2 1.0 %copy-start.15 = (bf16[128,128]{1,0:T(8,128)(2,1)}, bf16[128,128]{1,0:T(8,128)(2,1)S(1)}, u32[]{:S(2)}) copy-start(bf16[128,128]{1,0:T(8,128)(2,1)S(1)} %collective-permute-done.1) | copy-start | bytes 98308
  6.8 2.3 %copy-start.11 = (bf16[128,128]{1,0:T(8,128)(2,1)S(1)}, bf16[128,128]{1,0:T(8,128)(2,1)}, u32[]{:S(2)}) copy-start(bf16[128,128]{1,0:T(8,128)(2,1)} %param.11) | copy-start | bytes 98308
  7.2 5.4 %collective-permute-start.10 = (f32[8,256,64]{1,2,0:T(8,128)S(1)}, f32[8,256,64]{1,2,0:T(8,128)S(1)}, u32[]{:S(2)}, u32[]{:S(2)}) collective-permute-start(f32[8,256,64]{1,2,0:T(8,128)S(1)} %convolution_bitcast_fusion), channel_id=1, source_target_pairs={{0,4},{8,12},{16,20},{24,28},{1,5},{9,13},{17,21},{25,29},{2,6},{1... | collective-permute-start | bytes 1572872 | tf_op jit(solution)/shard_map/ppermute | solution.py:51
  9.5 4.6 %collective-permute-start.2 = (f32[8,256,64]{1,2,0:T(8,128)S(1)}, f32[8,256,64]{1,2,0:T(8,128)S(1)}, u32[]{:S(2)}, u32[]{:S(2)}) collective-permute-start(f32[8,256,64]{1,2,0:T(8,128)S(1)} %convolution_bitcast_fusion.2), channel_id=1, source_target_pairs={{4,0},{12,8},{20,16},{28,24},{5,1},{13,9},{21,17},{29,25},{6,2},{1... | collective-permute-start | bytes 1572872 | tf_op jit(solution)/shard_map/ppermute | solution.py:51
  12.6 3.7 %copy-start.48 = (f32[8]{0:T(128)}, f32[8]{0:T(128)S(1)}, u32[]{:S(2)}) copy-start(f32[8]{0:T(128)S(1)} %fusion.50) | copy-start | bytes 100
  14.1 9.4 %copy-start.35 = (f32[4,512]{1,0:T(4,128)S(1)}, f32[4,512]{1,0:T(4,128)}, u32[]{:S(2)}) copy-start(f32[4,512]{1,0:T(4,128)} %param.15) | copy-start | bytes 24580
  14.3 10.6 %collective-permute-start.4 = (f32[8,256,64]{1,2,0:T(8,128)S(1)}, f32[8,256,64]{1,2,0:T(8,128)S(1)}, u32[]{:S(2)}, u32[]{:S(2)}) collective-permute-start(f32[8,256,64]{1,2,0:T(8,128)S(1)} %get-tuple-element.28), channel_id=1, source_target_pairs={{8,0},{16,8},{24,16},{9,1},{17,9},{25,17},{10,2},{18,10},{26,18},{... | collective-permute-start | bytes 1572872 | tf_op jit(solution)/shard_map/ppermute | solution.py:58
  15.0 9.1 %collective-permute-start.11 = (f32[8]{0:T(128)S(1)}, f32[8]{0:T(128)S(1)}, u32[]{:S(2)}, u32[]{:S(2)}) collective-permute-start(f32[8]{0:T(128)S(1)} %fusion.50), channel_id=1, source_target_pairs={{0,4},{8,12},{16,20},{24,28},{1,5},{9,13},{17,21},{25,29},{2,6},{1... | collective-permute-start | bytes 104 | tf_op jit(solution)/shard_map/ppermute | solution.py:51
  16.3 7.8 %collective-permute-start.3 = (f32[8]{0:T(128)S(1)}, f32[8]{0:T(128)S(1)}, u32[]{:S(2)}, u32[]{:S(2)}) collective-permute-start(f32[8]{0:T(128)S(1)} %fusion.50), channel_id=1, source_target_pairs={{4,0},{12,8},{20,16},{28,24},{5,1},{13,9},{21,17},{29,25},{6,2},{1... | collective-permute-start | bytes 104 | tf_op jit(solution)/shard_map/ppermute | solution.py:51
  19.4 10.2 %collective-permute-start.12 = (f32[8,256,64]{1,2,0:T(8,128)S(1)}, f32[8,256,64]{1,2,0:T(8,128)S(1)}, u32[]{:S(2)}, u32[]{:S(2)}) collective-permute-start(f32[8,256,64]{1,2,0:T(8,128)S(1)} %get-tuple-element.29), channel_id=1, source_target_pairs={{4,12},{12,20},{20,28},{5,13},{13,21},{21,29},{6,14},{14,22},{22,3... | collective-permute-start | bytes 1572872 | tf_op jit(solution)/shard_map/ppermute | solution.py:58
  24.9 4.7 %copy-start.41 = (f32[8]{0:T(128)}, f32[8]{0:T(128)S(1)}, u32[]{:S(2)}) copy-start(f32[8]{0:T(128)S(1)} %get-tuple-element.21) | copy-start | bytes 100
  26.3 16.9 %collective-permute-start.6 = (f32[8,256,64]{1,2,0:T(8,128)}, f32[8,256,64]{1,2,0:T(8,128)}, u32[]{:S(2)}, u32[]{:S(2)}) collective-permute-start(f32[8,256,64]{1,2,0:T(8,128)} %multiply_add_fusion.4), channel_id=1, source_target_pairs={{16,0},{24,8},{17,1},{25,9},{18,2},{26,10},{19,3},{27,11}} | collective-permute-start | bytes 1572872 | tf_op jit(solution)/shard_map/ppermute | solution.py:58
  30.5 15.2 %collective-permute-start.14 = (f32[8,256,64]{1,2,0:T(8,128)}, f32[8,256,64]{1,2,0:T(8,128)}, u32[]{:S(2)}, u32[]{:S(2)}) collective-permute-start(f32[8,256,64]{1,2,0:T(8,128)} %multiply_add_fusion.1), channel_id=1, source_target_pairs={{4,20},{12,28},{5,21},{13,29},{6,22},{14,30},{7,23},{15,31}} | collective-permute-start | bytes 1572872 | tf_op jit(solution)/shard_map/ppermute | solution.py:58
  36.4 0.9 %copy-start.37 = (f32[128,8]{0,1:T(8,128)S(1)}, f32[128,8]{0,1:T(8,128)}, u32[]{:S(2)}) copy-start(f32[128,8]{0,1:T(8,128)} %param.13) | copy-start | bytes 12292
  37.3 2.0 %copy-start.28 = (f32[8,128]{1,0:T(8,128)}, f32[8,128]{1,0:T(8,128)S(1)}, u32[]{:S(2)}) copy-start(f32[8,128]{1,0:T(8,128)S(1)} %copy.26) | copy-start | bytes 12292
  37.3 2.0 %copy-start.44 = (f32[8]{0:T(128)S(1)}, f32[8]{0:T(128)}, u32[]{:S(2)}) copy-start(f32[8]{0:T(128)} %copy-done.43) | copy-start | bytes 100
  37.3 2.6 %copy-start.42 = (f32[8]{0:T(128)S(1)}, f32[8]{0:T(128)}, u32[]{:S(2)}) copy-start(f32[8]{0:T(128)} %copy-done.41) | copy-start | bytes 100
  39.3 3.9 %collective-permute-start.5 = (f32[8]{0:T(128)S(1)}, f32[8]{0:T(128)S(1)}, u32[]{:S(2)}, u32[]{:S(2)}) collective-permute-start(f32[8]{0:T(128)S(1)} %copy-done.44), channel_id=1, source_target_pairs={{8,0},{16,8},{24,16},{9,1},{17,9},{25,17},{10,2},{18,10},{26,18},{... | collective-permute-start | bytes 104 | tf_op jit(solution)/shard_map/ppermute | solution.py:58
  40.0 5.7 %collective-permute-start.13 = (f32[8]{0:T(128)S(1)}, f32[8]{0:T(128)S(1)}, u32[]{:S(2)}, u32[]{:S(2)}) collective-permute-start(f32[8]{0:T(128)S(1)} %copy-done.42), channel_id=1, source_target_pairs={{4,12},{12,20},{20,28},{5,13},{13,21},{21,29},{6,14},{14,22},{22,3... | collective-permute-start | bytes 104 | tf_op jit(solution)/shard_map/ppermute | solution.py:58
  44.4 15.8 %collective-permute-start.7 = (f32[8,256,64]{1,2,0:T(8,128)S(1)}, f32[8,256,64]{1,2,0:T(8,128)}, u32[]{:S(2)}, u32[]{:S(2)}) collective-permute-start(f32[8,256,64]{1,2,0:T(8,128)S(1)} %multiply_add_fusion.3), channel_id=1, source_target_pairs={{0,4},{8,12},{16,20},{24,28},{1,5},{9,13},{17,21},{25,29},{2,6},{1... | collective-permute-start | bytes 1572872 | tf_op jit(solution)/shard_map/ppermute | solution.py:63
  46.9 7.2 %copy-start.8 = (f32[8,128,128]{2,1,0:T(8,128)S(1)}, f32[8,128,128]{2,1,0:T(8,128)}, u32[]{:S(2)}) copy-start(f32[8,128,128]{2,1,0:T(8,128)} %get-tuple-element.31) | copy-start | bytes 1572868
  46.9 13.4 %collective-permute-start.15 = (f32[8,256,64]{1,2,0:T(8,128)S(1)}, f32[8,256,64]{1,2,0:T(8,128)}, u32[]{:S(2)}, u32[]{:S(2)}) collective-permute-start(f32[8,256,64]{1,2,0:T(8,128)S(1)} %multiply_add_fusion), channel_id=1, source_target_pairs={{4,0},{12,8},{20,16},{28,24},{5,1},{13,9},{21,17},{29,25},{6,2},{1... | collective-permute-start | bytes 1572872 | tf_op jit(solution)/shard_map/ppermute | solution.py:63
  52.4 1.7 %copy-start.29 = (f32[8,128]{1,0:T(8,128)S(1)}, f32[8,128]{1,0:T(8,128)}, u32[]{:S(2)}) copy-start(f32[8,128]{1,0:T(8,128)} %copy-done.28) | copy-start | bytes 12292
  60.2 1.9 %copy-start.24 = (f32[128,8]{0,1:T(8,128)S(1)}, f32[128,8]{0,1:T(8,128)}, u32[]{:S(2)}) copy-start(f32[128,8]{0,1:T(8,128)} %copy-done.23) | copy-start | bytes 12292
  62.2 0.8 copy-start.16
  64.4 0.8 %copy-start.3 = (f32[128,8]{1,0:T(8,128)S(1)}, f32[128,8]{1,0:T(8,128)}, u32[]{:S(2)}) copy-start(f32[128,8]{1,0:T(8,128)} %copy-done.2) | copy-start | bytes 12292
  64.4 0.9 %copy-start.5 = (f32[128,8]{1,0:T(8,128)S(1)}, f32[128,8]{1,0:T(8,128)}, u32[]{:S(2)}) copy-start(f32[128,8]{1,0:T(8,128)} %copy-done.4) | copy-start | bytes 12292
  64.4 0.9 %copy-start.18 = (f32[8,128]{0,1:T(8,128)S(1)}, f32[8,128]{0,1:T(8,128)}, u32[]{:S(2)}) copy-start(f32[8,128]{0,1:T(8,128)} %copy.34) | copy-start | bytes 12292
  64.4 0.9 %copy-start.19 = (f32[8,1,128]{0,2,1:T(8,128)S(1)}, f32[8,1,128]{0,2,1:T(8,128)}, u32[]{:S(2)}) copy-start(f32[8,1,128]{0,2,1:T(8,128)} %copy.50) | copy-start | bytes 12292
  64.8 0.9 %copy-start.1 = (f32[128,8]{1,0:T(8,128)S(1)}, f32[128,8]{1,0:T(8,128)}, u32[]{:S(2)}) copy-start(f32[128,8]{1,0:T(8,128)} %copy-done) | copy-start | bytes 12292
  66.0 1.3 %copy-start.17 = (f32[128,128]{0,1:T(8,128)S(1)}, f32[128,128]{0,1:T(8,128)}, u32[]{:S(2)}) copy-start(f32[128,128]{0,1:T(8,128)} %get-tuple-element.30) | copy-start | bytes 196612
  67.5 1.6 %copy-start.22 = (f32[128,128]{1,0:T(8,128)S(1)}, f32[128,128]{1,0:T(8,128)}, u32[]{:S(2)}) copy-start(f32[128,128]{1,0:T(8,128)} %copy-done.21) | copy-start | bytes 196612
  67.5 1.6 %copy-start.30 = (f32[8,128]{1,0:T(8,128)S(1)}, f32[8,128]{1,0:T(8,128)}, u32[]{:S(2)}) copy-start(f32[8,128]{1,0:T(8,128)} %copy-done.28) | copy-start | bytes 12292
  67.5 1.6 %copy-start.38 = (f32[128,8]{0,1:T(8,128)S(1)}, f32[128,8]{0,1:T(8,128)}, u32[]{:S(2)}) copy-start(f32[128,8]{0,1:T(8,128)} %param.13) | copy-start | bytes 12292
  67.6 1.6 %copy-start.25 = (f32[128,8]{0,1:T(8,128)S(1)}, f32[128,8]{0,1:T(8,128)}, u32[]{:S(2)}) copy-start(f32[128,8]{0,1:T(8,128)} %copy-done.23) | copy-start | bytes 12292
  67.6 10.2 %collective-permute-start.16 = (bf16[128,128]{1,0:T(8,128)(2,1)S(1)}, bf16[128,128]{1,0:T(8,128)(2,1)S(1)}, u32[]{:S(2)}, u32[]{:S(2)}) collective-permute-start(bf16[128,128]{1,0:T(8,128)(2,1)S(1)} %select_convert_fusion), channel_id=1, source_target_pairs={{0,1},{1,0},{2,3},{3,2},{4,5},{5,4},{6,7},{7,6},{8,9},{9,8},{10,11... | collective-permute-start | bytes 98312 | tf_op jit(solution)/shard_map/ppermute | solution.py:16
  70.4 0.9 %copy-start.7 = (bf16[128,512]{1,0:T(8,128)(2,1)S(1)}, bf16[128,512]{1,0:T(8,128)(2,1)}, u32[]{:S(2)}) copy-start(bf16[128,512]{1,0:T(8,128)(2,1)} %param.8) | copy-start | bytes 393220
  71.4 5.0 %collective-permute-start.8 = (f32[3,512]{1,0:T(4,128)S(1)}, f32[3,512]{1,0:T(4,128)S(1)}, u32[]{:S(2)}, u32[]{:S(2)}) collective-permute-start(f32[3,512]{1,0:T(4,128)S(1)} %slice.57), channel_id=1, source_target_pairs={{4,0},{8,4},{12,8},{16,12},{20,16},{24,20},{28,24},{5,1},{9,5},{13... | collective-permute-start | bytes 18440 | tf_op jit(solution)/shard_map/ppermute | solution.py:74
  73.3 3.0 %copy-start.33 = (f32[1,512]{1,0:T(1,128)S(1)}, f32[1,512]{1,0:T(1,128)}, u32[]{:S(2)}) copy-start(f32[1,512]{1,0:T(1,128)} %get-tuple-element.26) | copy-start | bytes 6148
  73.3 3.0 %copy-start.34 = (f32[1,512]{1,0:T(1,128)S(1)}, f32[1,512]{1,0:T(1,128)}, u32[]{:S(2)}) copy-start(f32[1,512]{1,0:T(1,128)} %get-tuple-element.27) | copy-start | bytes 6148
  73.6 4.8 %collective-permute-start.9 = (bf16[128,128]{1,0:T(8,128)(2,1)S(1)}, bf16[128,128]{1,0:T(8,128)(2,1)S(1)}, u32[]{:S(2)}, u32[]{:S(2)}) collective-permute-start(bf16[128,128]{1,0:T(8,128)(2,1)S(1)} %select_convert_fusion.1), channel_id=1, source_target_pairs={{0,1},{1,0},{2,3},{3,2},{4,5},{5,4},{6,7},{7,6},{8,9},{9,8},{10,11... | collective-permute-start | bytes 98312 | tf_op jit(solution)/shard_map/ppermute | solution.py:16
  (20 other events, 13.7 us)

commit v3 on v2

--- a/solution.py
+++ b/solution.py
@@ -38,6 +38,25 @@
     return [s for _, s in near]
 
 
+def packed(decay, state, kind):
+    heads, width = state.shape[0], state.shape[1]
+    if kind == jnp.float32:
+        parts = decay
+    else:
+        high = decay.astype(kind)
+        parts = jnp.concatenate([high, (decay - high.astype(decay.dtype)).astype(kind)])
+    row = jnp.pad(parts.astype(kind), (0, width - parts.shape[0]))
+    slab = jnp.broadcast_to(row[None, :, None], (1,) + state.shape[1:])
+    return jnp.concatenate([state.astype(kind), slab], 0)
+
+
+def unpacked(message):
+    heads = message.shape[0] - 1
+    row = message[heads, :, 0].astype(jnp.float32)
+    decay = row[:heads] if message.dtype == jnp.float32 else row[:heads] + row[heads : 2 * heads]
+    return decay, message[:heads].astype(jnp.float32)
+
+
 def chip_scanned_in(shards, axis):
     peers = lax.axis_size(axis)
     if peers % 2:
@@ -48,16 +67,25 @@
     for own_a, own_s, reverse in shards:
         inward = [(b, a) for a, b in pairs] if reverse else pairs
         heads = [b for _, b in inward]
-        mate_a, mate_s = lax.ppermute((own_a, own_s), axis, inward)
+        mate_a, mate_s = unpacked(
+            lax.ppermute(packed(own_a, own_s, jnp.float32), axis, inward)
+        )
         window = (own_a * mate_a, own_s + own_a[:, None, None] * mate_s)
         near = (jnp.ones_like(own_a), jnp.zeros_like(own_s))
         distance = 2
         while distance < peers:
             step = -distance if reverse else distance
             route = [(i, i + step) for i in heads if 0 <= i + step < peers]
-            far_a, far_s = lax.ppermute(window, axis, route)
-            near = (near[0] * far_a, near[1] + near[0][:, None, None] * far_s)
-            if 2 * distance < peers:
+            last = 2 * distance >= peers
+            if last:
+                far_s = lax.ppermute(window[1].astype(jnp.bfloat16), axis, route)
+                far_s = far_s.astype(jnp.float32)
+                near = (near[0], near[1] + near[0][:, None, None] * far_s)
+            else:
+                far_a, far_s = unpacked(
+                    lax.ppermute(packed(*window, jnp.bfloat16), axis, route)
+                )
+                near = (near[0] * far_a, near[1] + near[0][:, None, None] * far_s)
                 window = (window[0] * far_a, window[1] + window[0][:, None, None] * far_s)
             distance *= 2
         handed = lax.ppermute(near[1], axis, [(b, a) for a, b in inward])
@@ -86,7 +114,9 @@
     head_width = conv_output.shape[1] // head_count
     parity = lax.axis_index("head") % 2
     own_first = parity == 0
-    partner = swapped((write_keys, read_queries), "head", 0)
+    half = write_keys.shape[1]
+    both = swapped(jnp.concatenate([write_keys, read_queries], 1), "head", 0)
+    partner = (both[:, :half], both[:, half:])
     keys_full = jnp.where(
         own_first,
         jnp.concatenate([write_keys, partner[0]], 1),
@@ -167,10 +197,10 @@
     key_other = jnp.where(own_first, key_part[:, half_width:], key_part[:, :half_width])
     query_mine = jnp.where(own_first, query_part[:, :half_width], query_part[:, half_width:])
     query_other = jnp.where(own_first, query_part[:, half_width:], query_part[:, :half_width])
-    received = (
-        swapped(key_other.astype(jnp.bfloat16), "head", 0).astype(key_other.dtype),
-        swapped(query_other.astype(jnp.bfloat16), "head", 0).astype(query_other.dtype),
-    )
+    sent_back = swapped(
+        jnp.concatenate([key_other, query_other], 1).astype(jnp.bfloat16), "head", 0
+    ).astype(key_other.dtype)
+    received = (sent_back[:, :half_width], sent_back[:, half_width:])
     keys_grad = key_mine + received[0]
     queries_grad = query_mine + received[1]
     logistic = jax.nn.sigmoid(preact)

time: 80.4 us -> 67.1 us (0.83)
  starting transfers between devices: 36.8 us -> 30.3 us
  other arithmetic: 11.1 us -> 7.78 us
  local copies, waits for them, and re-layouts: 14.8 us -> 12.4 us
  matrix products: 9.21 us -> 7.47 us
  waiting for transfers between devices: 5.93 us -> 6.74 us
    ppermute x10 -> x6, starting transfers between devices: 24.8 us -> 13.8 us  [the longest x2 5.68 us: chip_scanned_in(): far_s = lax.ppermute(window[1].astype(jnp.bfloat16), axis, route)]
    ppermute x2, starting transfers between devices: 6.27 us -> 12.1 us  [chip_scanned_in(): handed = lax.ppermute(near[1], axis, [(b, a) for a, b in inward])]
    add x6 -> x4, other arithmetic: 5 us -> 0.42 us  [the longest x2 0.28 us: chip_scanned_in(): near = (near[0], near[1] + near[0][:, None, None] * far_s)]
    ppermute x1, waiting for transfers between devices: 2.59 us -> 0.37 us  [shifted(): return lax.ppermute(block, axis, route)]
    ppermute x10 -> x6, waiting for transfers between devices: 3.33 us -> 5.35 us  [the longest x2 3.25 us: chip_scanned_in(): far_s = lax.ppermute(window[1].astype(jnp.bfloat16), axis, route)]
    concatenate x0 -> x7, other arithmetic: none -> 1.94 us  [the longest x3 0.99 us: packed(): return jnp.concatenate([state.astype(kind), slab], 0)]
    ppermute x4 -> x2, starting transfers between devices: 3.9 us -> 2.4 us  [swapped(): return lax.ppermute(block, axis, route)]
    ppermute x4 -> x2, waiting for transfers between devices: 0.01 us -> 1 us  [swapped(): return lax.ppermute(block, axis, route)]
  transfers between devices with their start and end apart: 17 -> 11, of which waited for: 3 -> 4; matrix products, arithmetic and copies ran while one was open for 26% -> 16% of each run, Pallas kernels for 0% -> 0%
where the time goes in v3:
time: 67.1 us; the launch traced here: 65.9 us
  starting transfers between devices  30.3 us (45%)
  local copies, waits for them, and re-layouts  12.4 us (18%)
  other arithmetic  7.78 us (12%)
  matrix products  7.47 us (11%)
  waiting for transfers between devices  6.74 us (10%)
  between operations  1.29 us (2%)
    ppermute x2, starting transfers between devices, chip_scanned_in(): handed = lax.ppermute(near[1], axis, [(b, a) for a, b in inward])  12.1 us
    unnamed x103, local copies, waits for them, and re-layouts  9.63 us
    ppermute x2, starting transfers between devices, chip_scanned_in(): far_s = lax.ppermute(window[1].astype(jnp.bfloat16), axis, route)  5.68 us
    ppermute x2, starting transfers between devices, chip_scanned_in(): lax.ppermute(packed(own_a, own_s, jnp.float32), axis, inward)  4.17 us
    ppermute x2, starting transfers between devices, chip_scanned_in(): lax.ppermute(packed(*window, jnp.bfloat16), axis, route)  3.9 us
    ppermute x2, waiting for transfers between devices, chip_scanned_in(): far_s = lax.ppermute(window[1].astype(jnp.bfloat16), axis, route)  3.25 us
    ppermute x2, starting transfers between devices, swapped(): return lax.ppermute(block, axis, route)  2.4 us
    ppermute x2, waiting for transfers between devices, chip_scanned_in(): lax.ppermute(packed(*window, jnp.bfloat16), axis, route)  2.1 us
  transfers between devices with their start and end apart: 11, of which 4 were waited for; matrix products, arithmetic and copies ran while one was open for 16% of the time, Pallas kernels for 0%

profile of v3, /device:TPU:1, one launch (start us, length us, event | category | flops | bytes accessed | tf_op | source)
XLA Modules:
  0.0 65.9 jit_solution(103996500343230909)
XLA Ops:
  0.6 0.8 %pad_maximum_fusion.6 = bf16[128,256]{1,0:T(8,128)(2,1)S(1)} fusion(bf16[128,128]{1,0:T(8,128)(2,1)} %param.11, bf16[128,128]{1,0:T(8,128)(2,1)} %param.10), kind=kLoop, calls=%fused_computation.79 | loop fusion | flops 131072 | bytes 131072 | tf_op jit(solution)/shard_map/concatenate | solution.py:118
  1.4 2.1 %collective-permute-start = (bf16[128,256]{1,0:T(8,128)(2,1)S(1)}, bf16[128,256]{1,0:T(8,128)(2,1)S(1)}, u32[]{:S(2)}, u32[]{:S(2)}) collective-permute-start(bf16[128,256]{1,0:T(8,128)(2,1)S(1)} %pad_maximum_fusion.6), channel_id=1, source_target_pairs={{0,1},{1,0},{2,3},{3,2},{4,5},{5,4},{6,7},{7,6},{8,9},{9,8},{10,11... | collective-permute-start | bytes 196616 | tf_op jit(solution)/shard_map/ppermute | solution.py:16
  3.9 0.5 copy-done.41
  4.7 0.8 %copy-done.23 = bf16[128,512]{1,0:T(8,128)(2,1)S(1)} copy-done((bf16[128,512]{1,0:T(8,128)(2,1)S(1)}, bf16[128,512]{1,0:T(8,128)(2,1)}, u32[]{:S(2)}) %copy-start.23) | copy-done | bytes 131096
  5.7 1.9 %multiply_reduce_fusion = (f32[128,128]{0,1:T(8,128)}, f32[8,128,128]{2,1,0:T(8,128)}) fusion(f32[128,8]{0,1:T(8,128)S(1)} %copy-done.41, f32[8,128]{1,0:T(8,128)S(1)} %copy.26, pred[128,128]{1,0:T(8,128)(4,1)S(1)} %iota_compare_fusion, f32[128,8,64]{0,2,1:T(8,128)S(1)} %bitcast.102, bf16[128,8,64]{0,2,1:T(8,128)(2,1)S(1)} %bitcast.105), kind=kOutput, calls=%fused_computation.19 | convolution fusion | flops 101302272 | bytes 1007616 | tf_op jit(solution)/shard_map/thp,shp->hts/dot_general | solution.py:156
  7.9 0.5 copy-done.29
  8.6 0.4 convolution_bitcast_fusion
  9.0 0.4 copy-done.11
  9.3 0.4 convolution_bitcast_fusion.2
  9.7 0.9 %pad_maximum_fusion.1 = (f32[9,256,64]{1,2,0:T(8,128)}, f32[9,256,64]{1,2,0:T(8,128)S(1)}) fusion(f32[1,256,64]{1,2,0:T(8,128)S(1)} %broadcast_in_dim.16, f32[8,256,64]{1,2,0:T(8,128)S(1)} %convolution_bitcast_fusion.2, f32[8,256,64]{1,2,0:T(8,128)S(1)} %convolution_bitcast_fusion), kind=kLoop, calls=%fused_computation.10 | loop fusion | flops 294912 | bytes 2293760 | tf_op jit(solution)/shard_map/concatenate | solution.py:50
  10.6 2.9 %collective-permute-start.1 = (f32[9,256,64]{1,2,0:T(8,128)}, f32[9,256,64]{1,2,0:T(8,128)S(1)}, u32[]{:S(2)}, u32[]{:S(2)}) collective-permute-start(f32[9,256,64]{1,2,0:T(8,128)} %get-tuple-element.28), channel_id=1, source_target_pairs={{4,0},{12,8},{20,16},{28,24},{5,1},{13,9},{21,17},{29,25},{6,2},{1... | collective-permute-start | bytes 1769480 | tf_op jit(solution)/shard_map/ppermute | solution.py:71
  13.5 1.3 %collective-permute-start.6 = (f32[9,256,64]{1,2,0:T(8,128)S(1)}, f32[9,256,64]{1,2,0:T(8,128)S(1)}, u32[]{:S(2)}, u32[]{:S(2)}) collective-permute-start(f32[9,256,64]{1,2,0:T(8,128)S(1)} %get-tuple-element.29), channel_id=1, source_target_pairs={{0,4},{8,12},{16,20},{24,28},{1,5},{9,13},{17,21},{25,29},{2,6},{1... | collective-permute-start | bytes 1769480 | tf_op jit(solution)/shard_map/ppermute | solution.py:71
  14.8 0.6 compare_convert_fusion
  15.4 0.7 %copy-done.39 = f32[4,512]{1,0:T(4,128)S(1)} copy-done((f32[4,512]{1,0:T(4,128)S(1)}, f32[4,512]{1,0:T(4,128)}, u32[]{:S(2)}) %copy-start.39) | copy-done | bytes 8216
  16.1 0.6 fusion.88
  16.9 0.3 copy-done.19
  17.2 1.7 %fusion.10 = f32[8,1,128]{2,1,0:T(1,128)} fusion(f32[8,128,1]{1,2,0:T(1,128)S(1)} %bitcast.116, f32[8,128,128]{2,1,0:T(8,128)S(1)} %copy-done.19, f32[128,128]{1,0:T(8,128)S(1)} %fusion.73, f32[8,128]{1,0:T(8,128)S(1)} %copy.26, pred[128,128]{1,0:T(8,128)(4,1)S(1)} %iota_compare_fusion), kind=kOutput, calls=%fused_computation.38 | convolution fusion | flops 2097152 | bytes 618496 | tf_op jit(solution)/shard_map/hts,hs->th/dot_general | solution.py:163
  19.1 0.7 %collective-permute-start.2 = (bf16[9,256,64]{1,2,0:T(8,128)(2,1)S(1)}, bf16[9,256,64]{1,2,0:T(8,128)(2,1)S(1)}, u32[]{:S(2)}, u32[]{:S(2)}) collective-permute-start(bf16[9,256,64]{1,2,0:T(8,128)(2,1)S(1)} %pad_maximum_fusion.2), channel_id=1, source_target_pairs={{8,0},{16,8},{24,16},{9,1},{17,9},{25,17},{10,2},{18,10},{26,18},{... | collective-permute-start | bytes 884744 | tf_op jit(solution)/shard_map/ppermute | solution.py:86
  20.1 0.7 %collective-permute-start.3 = (bf16[8,256,64]{1,2,0:T(8,128)(2,1)S(1)}, bf16[8,256,64]{1,2,0:T(8,128)(2,1)S(1)}, u32[]{:S(2)}, u32[]{:S(2)}) collective-permute-start(bf16[8,256,64]{1,2,0:T(8,128)(2,1)S(1)} %get-tuple-element.38), channel_id=1, source_target_pairs={{16,0},{24,8},{17,1},{25,9},{18,2},{26,10},{19,3},{27,11}} | collective-permute-start | bytes 786440 | tf_op jit(solution)/shard_map/ppermute | solution.py:81
  20.9 3.2 %collective-permute-start.7 = (bf16[9,256,64]{1,2,0:T(8,128)(2,1)S(1)}, bf16[9,256,64]{1,2,0:T(8,128)(2,1)S(1)}, u32[]{:S(2)}, u32[]{:S(2)}) collective-permute-start(bf16[9,256,64]{1,2,0:T(8,128)(2,1)S(1)} %pad_maximum_fusion.3), channel_id=1, source_target_pairs={{4,12},{12,20},{20,28},{5,13},{13,21},{21,29},{6,14},{14,22},{22,3... | collective-permute-start | bytes 884744 | tf_op jit(solution)/shard_map/ppermute | solution.py:86
  24.3 1.3 %collective-permute-start.4 = (f32[8,256,64]{1,2,0:T(8,128)S(1)}, f32[8,256,64]{1,2,0:T(8,128)}, u32[]{:S(2)}, u32[]{:S(2)}) collective-permute-start(f32[8,256,64]{1,2,0:T(8,128)S(1)} %convert_add_fusion.1), channel_id=1, source_target_pairs={{0,4},{8,12},{16,20},{24,28},{1,5},{9,13},{17,21},{25,29},{2,6},{1... | collective-permute-start | bytes 1572872 | tf_op jit(solution)/shard_map/ppermute | solution.py:91
  25.6 2.1 %collective-permute-done.7 = bf16[9,256,64]{1,2,0:T(8,128)(2,1)S(1)} collective-permute-done((bf16[9,256,64]{1,2,0:T(8,128)(2,1)S(1)}, bf16[9,256,64]{1,2,0:T(8,128)(2,1)S(1)}, u32[]{:S(2)}, u32[]{:S(2)}) %collective-permute-start.7) | collective-permute-done | bytes 294944 | tf_op jit(solution)/shard_map/ppermute | solution.py:86
  27.9 5.0 %collective-permute-start.8 = (bf16[8,256,64]{1,2,0:T(8,128)(2,1)S(1)}, bf16[8,256,64]{1,2,0:T(8,128)(2,1)S(1)}, u32[]{:S(2)}, u32[]{:S(2)}) collective-permute-start(bf16[8,256,64]{1,2,0:T(8,128)(2,1)S(1)} %fusion.4), channel_id=1, source_target_pairs={{4,20},{12,28},{5,21},{13,29},{6,22},{14,30},{7,23},{15,31}} | collective-permute-start | bytes 786440 | tf_op jit(solution)/shard_map/ppermute | solution.py:81
  33.0 3.2 %collective-permute-done.8 = bf16[8,256,64]{1,2,0:T(8,128)(2,1)S(1)} collective-permute-done((bf16[8,256,64]{1,2,0:T(8,128)(2,1)S(1)}, bf16[8,256,64]{1,2,0:T(8,128)(2,1)S(1)}, u32[]{:S(2)}, u32[]{:S(2)}) %collective-permute-start.8) | collective-permute-done | bytes 262176 | tf_op jit(solution)/shard_map/ppermute | solution.py:81
  36.4 10.8 %collective-permute-start.9 = (f32[8,256,64]{1,2,0:T(8,128)S(1)}, f32[8,256,64]{1,2,0:T(8,128)}, u32[]{:S(2)}, u32[]{:S(2)}) collective-permute-start(f32[8,256,64]{1,2,0:T(8,128)S(1)} %convert_add_fusion), channel_id=1, source_target_pairs={{4,0},{12,8},{20,16},{28,24},{5,1},{13,9},{21,17},{29,25},{6,2},{1... | collective-permute-start | bytes 1572872 | tf_op jit(solution)/shard_map/ppermute | solution.py:91
  47.4 0.7 %copy.34 = f32[8,128]{0,1:T(8,128)} copy(f32[8,128]{1,0:T(8,128)S(1)} %fusion.9) | data formatting | bytes 8192 | tf_op jit(solution)/shard_map/reduce_sum | solution.py:164
  48.1 0.7 %copy.50 = f32[8,1,128]{0,2,1:T(8,128)} copy(f32[8,1,128]{2,1,0:T(1,128)S(1)} %copy-done.43) | data formatting | bytes 8192 | tf_op jit(solution)/shard_map/hts,hs->th/dot_general | solution.py:163
  48.9 0.6 copy-done.34
  49.5 1.9 %multiply_reduce_fusion.1 = (f32[8]{0:T(128)}, f32[8,256,64]{1,2,0:T(8,128)S(1)}, f32[8,256,64]{1,2,0:T(8,128)S(1)}) fusion(f32[8,256,64]{1,2,0:T(8,128)S(1)} %convolution_bitcast_fusion, f32[8]{0:T(128)S(1)} %copy-done.34, f32[8,256,64]{1,2,0:T(8,128)} %collective-permute-done.9, f32[8,256,64]{1,2,0:T(8,128)S(1)} %convert_add_fusion, ...), kind=kLoop, calls=%fused_computation.20 | loop fusion | flops 1310712 | bytes 4718722 | tf_op jit(solution)/shard_map/reduce_sum | solution.py:182
  51.4 0.6 convolution_bitcast_fusion.4
  52.1 0.4 fusion.20
  52.8 0.6 convolution_bitcast_fusion.5
  53.6 0.4 multiply_reduce_fusion.2
  54.1 0.7 %copy-done.20 = f32[128,128]{0,1:T(8,128)S(1)} copy-done((f32[128,128]{0,1:T(8,128)S(1)}, f32[128,128]{0,1:T(8,128)}, u32[]{:S(2)}) %copy-start.20) | copy-done | bytes 65560
  54.8 0.3 convolution_add_fusion.1
  55.4 0.6 copy-done.2
  56.1 0.5 multiply_add_fusion.2
  56.8 0.8 %copy-done.10 = bf16[128,512]{1,0:T(8,128)(2,1)S(1)} copy-done((bf16[128,512]{1,0:T(8,128)(2,1)S(1)}, bf16[128,512]{1,0:T(8,128)(2,1)}, u32[]{:S(2)}) %copy-start.10) | copy-done | bytes 131096
  57.7 2.1 %collective-permute-start.5 = (f32[3,512]{1,0:T(4,128)S(1)}, f32[3,512]{1,0:T(4,128)S(1)}, u32[]{:S(2)}, u32[]{:S(2)}) collective-permute-start(f32[3,512]{1,0:T(4,128)S(1)} %slice.139), channel_id=1, source_target_pairs={{4,0},{8,4},{12,8},{16,12},{20,16},{24,20},{28,24},{5,1},{9,5},{13... | collective-permute-start | bytes 18440 | tf_op jit(solution)/shard_map/ppermute | solution.py:102
  59.8 0.5 copy-done.45
  60.8 0.7 %copy.39 = f32[128,8]{0,1:T(8,128)} copy(f32[128,8]{1,0:T(8,128)S(1)} %rev.8) | data formatting | bytes 8192
  61.4 0.7 %copy.40 = f32[128,8]{0,1:T(8,128)} copy(f32[128,8]{1,0:T(8,128)S(1)} %get-tuple-element.22) | data formatting | bytes 8192
  62.1 0.3 collective-permute-start.10
  62.4 0.4 collective-permute-done.5
  62.8 0.7 %copy-done.36 = f32[1,512]{1,0:T(1,128)S(1)} copy-done((f32[1,512]{1,0:T(1,128)S(1)}, f32[1,512]{1,0:T(1,128)}, u32[]{:S(2)}) %copy-start.36) | copy-done | bytes 2072
  63.5 0.8 %fusion.17 = bf16[128,512]{1,0:T(8,128)(2,1)} fusion(f32[128,512]{1,0:T(8,128)S(1)} %fusion.25, f32[3,512]{1,0:T(4,128)S(1)} %collective-permute-done.5, f32[512]{0:T(512)S(1)} %bitcast.114, f32[512]{0:T(512)S(1)} %bitcast.115, f32[512]{0:T(512)S(1)} %bitcast.113, f32[512]{0:T(512)S(1)} %bitcast.112), kind=kLoop, calls=%fused_computation.48 | loop fusion | flops 720896 | bytes 407552 | tf_op jit(solution)/shard_map/convert_element_type | solution.py:215
  64.2 1.0 %collective-permute-done.10 = bf16[128,256]{1,0:T(8,128)(2,1)S(1)} collective-permute-done((bf16[128,256]{1,0:T(8,128)(2,1)S(1)}, bf16[128,256]{1,0:T(8,128)(2,1)S(1)}, u32[]{:S(2)}, u32[]{:S(2)}) %collective-permute-start.10) | collective-permute-done | bytes 65568 | tf_op jit(solution)/shard_map/ppermute | solution.py:16
  65.2 0.7 %slice_add_fusion = (f32[128,128]{1,0:T(8,128)}, f32[128,128]{1,0:T(8,128)}) fusion(f32[128,256]{1,0:T(8,128)S(1)} %convert_element_type.95, f32[128,256]{1,0:T(8,128)S(1)} %convolution_add_fusion, pred[]{:T(512)S(6)} %eq.23, f32[128,256]{1,0:T(8,128)S(1)} %convolution_add_fusion.1), kind=kLoop, calls=%fused_computation.83 | loop fusion | flops 65536 | bytes 524289 | tf_op jit(solution)/shard_map/add | solution.py:205
  (144 shorter events, 4.6 us)
Async XLA Ops:
  1.4 2.1 %copy-start.40 = (f32[128,8]{0,1:T(8,128)S(1)}, f32[128,8]{0,1:T(8,128)}, u32[]{:S(2)}) copy-start(f32[128,8]{0,1:T(8,128)} %param.12) | copy-start | bytes 12292
  1.4 6.4 %collective-permute-start = (bf16[128,256]{1,0:T(8,128)(2,1)S(1)}, bf16[128,256]{1,0:T(8,128)(2,1)S(1)}, u32[]{:S(2)}, u32[]{:S(2)}) collective-permute-start(bf16[128,256]{1,0:T(8,128)(2,1)S(1)} %pad_maximum_fusion.6), channel_id=1, source_target_pairs={{0,1},{1,0},{2,3},{3,2},{4,5},{5,4},{6,7},{7,6},{8,9},{9,8},{10,11... | collective-permute-start | bytes 196616 | tf_op jit(solution)/shard_map/ppermute | solution.py:16
  3.6 0.9 %copy-start.9 = (bf16[128,512]{1,0:T(8,128)(2,1)S(1)}, bf16[128,512]{1,0:T(8,128)(2,1)}, u32[]{:S(2)}) copy-start(bf16[128,512]{1,0:T(8,128)(2,1)} %param.8) | copy-start | bytes 393220
  3.9 15.0 %copy-start.3 = (f32[128,8]{1,0:T(8,128)}, f32[128,8]{1,0:T(8,128)S(1)}, u32[]{:S(2)}) copy-start(f32[128,8]{1,0:T(8,128)S(1)} %reduce_window_sum.18) | copy-start | bytes 12292
  4.4 1.3 %copy-start.44 = (f32[8]{0:T(128)}, f32[8]{0:T(128)S(1)}, u32[]{:S(2)}) copy-start(f32[8]{0:T(128)S(1)} %slice_bitcast_fusion.2) | copy-start | bytes 100
  4.5 1.2 %copy-start.5 = (f32[128,8]{1,0:T(8,128)}, f32[128,8]{1,0:T(8,128)S(1)}, u32[]{:S(2)}) copy-start(f32[128,8]{1,0:T(8,128)S(1)} %copy.29) | copy-start | bytes 12292
  4.6 0.9 %copy-start.23 = (bf16[128,512]{1,0:T(8,128)(2,1)S(1)}, bf16[128,512]{1,0:T(8,128)(2,1)}, u32[]{:S(2)}) copy-start(bf16[128,512]{1,0:T(8,128)(2,1)} %param.9) | copy-start | bytes 393220
  5.6 3.4 %copy-start = (bf16[128,512]{0,1:T(8,128)(2,1)}, bf16[128,512]{0,1:T(8,128)(2,1)S(1)}, u32[]{:S(2)}) copy-start(bf16[128,512]{0,1:T(8,128)(2,1)S(1)} %copy.28) | copy-start | bytes 393220
  5.7 11.2 %copy-start.26 = (f32[8,128]{1,0:T(8,128)}, f32[8,128]{1,0:T(8,128)S(1)}, u32[]{:S(2)}) copy-start(f32[8,128]{1,0:T(8,128)S(1)} %copy.26) | copy-start | bytes 12292
  5.7 1.9 %copy-start.7 = (f32[128,8]{1,0:T(8,128)}, f32[128,8]{1,0:T(8,128)S(1)}, u32[]{:S(2)}) copy-start(f32[128,8]{1,0:T(8,128)S(1)} %get-tuple-element.33) | copy-start | bytes 12292
  7.7 20.1 %copy-start.33 = (f32[8]{0:T(128)}, f32[8]{0:T(128)S(1)}, u32[]{:S(2)}) copy-start(f32[8]{0:T(128)S(1)} %fusion.66) | copy-start | bytes 100
  7.8 1.2 %copy-start.31 = (f32[128,8]{0,1:T(8,128)}, f32[128,8]{0,1:T(8,128)S(1)}, u32[]{:S(2)}) copy-start(f32[128,8]{0,1:T(8,128)S(1)} %copy.31) | copy-start | bytes 12292
  7.8 0.8 %copy-start.13 = (bf16[128,128]{1,0:T(8,128)(2,1)S(1)}, bf16[128,128]{1,0:T(8,128)(2,1)}, u32[]{:S(2)}) copy-start(bf16[128,128]{1,0:T(8,128)(2,1)} %param.10) | copy-start | bytes 98308
  7.8 8.9 %copy-start.15 = (bf16[128,128]{1,0:T(8,128)(2,1)}, bf16[128,128]{1,0:T(8,128)(2,1)S(1)}, u32[]{:S(2)}) copy-start(bf16[128,128]{1,0:T(8,128)(2,1)S(1)} %get-tuple-element.31) | copy-start | bytes 98308
  7.8 8.9 %copy-start.17 = (bf16[128,128]{1,0:T(8,128)(2,1)}, bf16[128,128]{1,0:T(8,128)(2,1)S(1)}, u32[]{:S(2)}) copy-start(bf16[128,128]{1,0:T(8,128)(2,1)S(1)} %get-tuple-element.30) | copy-start | bytes 98308
  8.6 0.8 %copy-start.11 = (bf16[128,128]{1,0:T(8,128)(2,1)S(1)}, bf16[128,128]{1,0:T(8,128)(2,1)}, u32[]{:S(2)}) copy-start(bf16[128,128]{1,0:T(8,128)(2,1)} %param.11) | copy-start | bytes 98308
  10.6 8.2 %collective-permute-start.1 = (f32[9,256,64]{1,2,0:T(8,128)}, f32[9,256,64]{1,2,0:T(8,128)S(1)}, u32[]{:S(2)}, u32[]{:S(2)}) collective-permute-start(f32[9,256,64]{1,2,0:T(8,128)} %get-tuple-element.28), channel_id=1, source_target_pairs={{4,0},{12,8},{20,16},{28,24},{5,1},{13,9},{21,17},{29,25},{6,2},{1... | collective-permute-start | bytes 1769480 | tf_op jit(solution)/shard_map/ppermute | solution.py:71
  13.5 5.3 %collective-permute-start.6 = (f32[9,256,64]{1,2,0:T(8,128)S(1)}, f32[9,256,64]{1,2,0:T(8,128)S(1)}, u32[]{:S(2)}, u32[]{:S(2)}) collective-permute-start(f32[9,256,64]{1,2,0:T(8,128)S(1)} %get-tuple-element.29), channel_id=1, source_target_pairs={{0,4},{8,12},{16,20},{24,28},{1,5},{9,13},{17,21},{25,29},{2,6},{1... | collective-permute-start | bytes 1769480 | tf_op jit(solution)/shard_map/ppermute | solution.py:71
  16.1 1.0 %copy-start.19 = (f32[8,128,128]{2,1,0:T(8,128)S(1)}, f32[8,128,128]{2,1,0:T(8,128)}, u32[]{:S(2)}) copy-start(f32[8,128,128]{2,1,0:T(8,128)} %get-tuple-element.41) | copy-start | bytes 1572868
  16.9 30.3 %copy-start.24 = (f32[128,128]{1,0:T(8,128)}, f32[128,128]{1,0:T(8,128)S(1)}, u32[]{:S(2)}) copy-start(f32[128,128]{1,0:T(8,128)S(1)} %fusion.73) | copy-start | bytes 196612
  19.1 0.8 %collective-permute-start.2 = (bf16[9,256,64]{1,2,0:T(8,128)(2,1)S(1)}, bf16[9,256,64]{1,2,0:T(8,128)(2,1)S(1)}, u32[]{:S(2)}, u32[]{:S(2)}) collective-permute-start(bf16[9,256,64]{1,2,0:T(8,128)(2,1)S(1)} %pad_maximum_fusion.2), channel_id=1, source_target_pairs={{8,0},{16,8},{24,16},{9,1},{17,9},{25,17},{10,2},{18,10},{26,18},{... | collective-permute-start | bytes 884744 | tf_op jit(solution)/shard_map/ppermute | solution.py:86
  20.1 4.0 %collective-permute-start.3 = (bf16[8,256,64]{1,2,0:T(8,128)(2,1)S(1)}, bf16[8,256,64]{1,2,0:T(8,128)(2,1)S(1)}, u32[]{:S(2)}, u32[]{:S(2)}) collective-permute-start(bf16[8,256,64]{1,2,0:T(8,128)(2,1)S(1)} %get-tuple-element.38), channel_id=1, source_target_pairs={{16,0},{24,8},{17,1},{25,9},{18,2},{26,10},{19,3},{27,11}} | collective-permute-start | bytes 786440 | tf_op jit(solution)/shard_map/ppermute | solution.py:81
  20.9 6.9 %collective-permute-start.7 = (bf16[9,256,64]{1,2,0:T(8,128)(2,1)S(1)}, bf16[9,256,64]{1,2,0:T(8,128)(2,1)S(1)}, u32[]{:S(2)}, u32[]{:S(2)}) collective-permute-start(bf16[9,256,64]{1,2,0:T(8,128)(2,1)S(1)} %pad_maximum_fusion.3), channel_id=1, source_target_pairs={{4,12},{12,20},{20,28},{5,13},{13,21},{21,29},{6,14},{14,22},{22,3... | collective-permute-start | bytes 884744 | tf_op jit(solution)/shard_map/ppermute | solution.py:86
  24.3 24.5 %collective-permute-start.4 = (f32[8,256,64]{1,2,0:T(8,128)S(1)}, f32[8,256,64]{1,2,0:T(8,128)}, u32[]{:S(2)}, u32[]{:S(2)}) collective-permute-start(f32[8,256,64]{1,2,0:T(8,128)S(1)} %convert_add_fusion.1), channel_id=1, source_target_pairs={{0,4},{8,12},{16,20},{24,28},{1,5},{9,13},{17,21},{25,29},{2,6},{1... | collective-permute-start | bytes 1572872 | tf_op jit(solution)/shard_map/ppermute | solution.py:91
  27.9 8.3 %collective-permute-start.8 = (bf16[8,256,64]{1,2,0:T(8,128)(2,1)S(1)}, bf16[8,256,64]{1,2,0:T(8,128)(2,1)S(1)}, u32[]{:S(2)}, u32[]{:S(2)}) collective-permute-start(bf16[8,256,64]{1,2,0:T(8,128)(2,1)S(1)} %fusion.4), channel_id=1, source_target_pairs={{4,20},{12,28},{5,21},{13,29},{6,22},{14,30},{7,23},{15,31}} | collective-permute-start | bytes 786440 | tf_op jit(solution)/shard_map/ppermute | solution.py:81
  36.2 10.9 %copy-start.27 = (f32[8,128]{1,0:T(8,128)S(1)}, f32[8,128]{1,0:T(8,128)}, u32[]{:S(2)}) copy-start(f32[8,128]{1,0:T(8,128)} %copy-done.26) | copy-start | bytes 12292
  36.4 12.5 %collective-permute-start.9 = (f32[8,256,64]{1,2,0:T(8,128)S(1)}, f32[8,256,64]{1,2,0:T(8,128)}, u32[]{:S(2)}, u32[]{:S(2)}) collective-permute-start(f32[8,256,64]{1,2,0:T(8,128)S(1)} %convert_add_fusion), channel_id=1, source_target_pairs={{4,0},{12,8},{20,16},{28,24},{5,1},{13,9},{21,17},{29,25},{6,2},{1... | collective-permute-start | bytes 1572872 | tf_op jit(solution)/shard_map/ppermute | solution.py:91
  47.4 0.7 %copy-start.43 = (f32[8,1,128]{2,1,0:T(1,128)S(1)}, f32[8,1,128]{2,1,0:T(1,128)}, u32[]{:S(2)}) copy-start(f32[8,1,128]{2,1,0:T(1,128)} %fusion.10) | copy-start | bytes 12292
  48.9 2.5 %copy-start.1 = (bf16[128,512]{0,1:T(8,128)(2,1)S(1)}, bf16[128,512]{0,1:T(8,128)(2,1)}, u32[]{:S(2)}) copy-start(bf16[128,512]{0,1:T(8,128)(2,1)} %copy-done) | copy-start | bytes 393220
  49.5 1.9 %copy-start.32 = (f32[128,8]{0,1:T(8,128)S(1)}, f32[128,8]{0,1:T(8,128)}, u32[]{:S(2)}) copy-start(f32[128,8]{0,1:T(8,128)} %copy-done.31) | copy-start | bytes 12292
  51.4 0.8 %copy-start.12 = (bf16[128,128]{1,0:T(8,128)(2,1)S(1)}, bf16[128,128]{1,0:T(8,128)(2,1)}, u32[]{:S(2)}) copy-start(bf16[128,128]{1,0:T(8,128)(2,1)} %param.11) | copy-start | bytes 98308
  51.4 0.8 %copy-start.18 = (bf16[128,128]{1,0:T(8,128)(2,1)S(1)}, bf16[128,128]{1,0:T(8,128)(2,1)}, u32[]{:S(2)}) copy-start(bf16[128,128]{1,0:T(8,128)(2,1)} %copy-done.17) | copy-start | bytes 98308
  52.8 0.8 %copy-start.14 = (bf16[128,128]{1,0:T(8,128)(2,1)S(1)}, bf16[128,128]{1,0:T(8,128)(2,1)}, u32[]{:S(2)}) copy-start(bf16[128,128]{1,0:T(8,128)(2,1)} %param.10) | copy-start | bytes 98308
  52.8 0.8 %copy-start.16 = (bf16[128,128]{1,0:T(8,128)(2,1)S(1)}, bf16[128,128]{1,0:T(8,128)(2,1)}, u32[]{:S(2)}) copy-start(bf16[128,128]{1,0:T(8,128)(2,1)} %copy-done.15) | copy-start | bytes 98308
  54.0 0.8 %copy-start.20 = (f32[128,128]{0,1:T(8,128)S(1)}, f32[128,128]{0,1:T(8,128)}, u32[]{:S(2)}) copy-start(f32[128,128]{0,1:T(8,128)} %get-tuple-element.40) | copy-start | bytes 196612
  55.1 0.9 %copy-start.2 = (bf16[128,512]{0,1:T(8,128)(2,1)S(1)}, bf16[128,512]{0,1:T(8,128)(2,1)}, u32[]{:S(2)}) copy-start(bf16[128,512]{0,1:T(8,128)(2,1)} %copy-done) | copy-start | bytes 393220
  55.1 0.9 %copy-start.25 = (f32[128,128]{1,0:T(8,128)S(1)}, f32[128,128]{1,0:T(8,128)}, u32[]{:S(2)}) copy-start(f32[128,128]{1,0:T(8,128)} %copy-done.24) | copy-start | bytes 196612
  55.1 0.9 %copy-start.42 = (f32[128,8]{0,1:T(8,128)S(1)}, f32[128,8]{0,1:T(8,128)}, u32[]{:S(2)}) copy-start(f32[128,8]{0,1:T(8,128)} %param.13) | copy-start | bytes 12292
  56.6 0.9 %copy-start.10 = (bf16[128,512]{1,0:T(8,128)(2,1)S(1)}, bf16[128,512]{1,0:T(8,128)(2,1)}, u32[]{:S(2)}) copy-start(bf16[128,512]{1,0:T(8,128)(2,1)} %param.8) | copy-start | bytes 393220
  57.5 2.3 %copy-start.21 = (f32[8,128]{0,1:T(8,128)S(1)}, f32[8,128]{0,1:T(8,128)}, u32[]{:S(2)}) copy-start(f32[8,128]{0,1:T(8,128)} %copy.34) | copy-start | bytes 12292
  57.5 2.3 %copy-start.22 = (f32[8,1,128]{0,2,1:T(8,128)S(1)}, f32[8,1,128]{0,2,1:T(8,128)}, u32[]{:S(2)}) copy-start(f32[8,1,128]{0,2,1:T(8,128)} %copy.50) | copy-start | bytes 12292
  57.6 2.2 %copy-start.4 = (f32[128,8]{1,0:T(8,128)S(1)}, f32[128,8]{1,0:T(8,128)}, u32[]{:S(2)}) copy-start(f32[128,8]{1,0:T(8,128)} %copy-done.3) | copy-start | bytes 12292
  57.7 2.2 %copy-start.6 = (f32[128,8]{1,0:T(8,128)S(1)}, f32[128,8]{1,0:T(8,128)}, u32[]{:S(2)}) copy-start(f32[128,8]{1,0:T(8,128)} %copy-done.5) | copy-start | bytes 12292
  57.7 2.2 %copy-start.8 = (f32[128,8]{1,0:T(8,128)S(1)}, f32[128,8]{1,0:T(8,128)}, u32[]{:S(2)}) copy-start(f32[128,8]{1,0:T(8,128)} %copy-done.7) | copy-start | bytes 12292
  57.7 5.1 %collective-permute-start.5 = (f32[3,512]{1,0:T(4,128)S(1)}, f32[3,512]{1,0:T(4,128)S(1)}, u32[]{:S(2)}, u32[]{:S(2)}) collective-permute-start(f32[3,512]{1,0:T(4,128)S(1)} %slice.139), channel_id=1, source_target_pairs={{4,0},{8,4},{12,8},{16,12},{20,16},{24,20},{28,24},{5,1},{9,5},{13... | collective-permute-start | bytes 18440 | tf_op jit(solution)/shard_map/ppermute | solution.py:102
  60.8 2.0 %copy-start.37 = (f32[1,512]{1,0:T(1,128)S(1)}, f32[1,512]{1,0:T(1,128)}, u32[]{:S(2)}) copy-start(f32[1,512]{1,0:T(1,128)} %get-tuple-element.36) | copy-start | bytes 6148
  60.8 2.0 %copy-start.38 = (f32[1,512]{1,0:T(1,128)S(1)}, f32[1,512]{1,0:T(1,128)}, u32[]{:S(2)}) copy-start(f32[1,512]{1,0:T(1,128)} %get-tuple-element.37) | copy-start | bytes 6148
  62.1 3.1 %collective-permute-start.10 = (bf16[128,256]{1,0:T(8,128)(2,1)S(1)}, bf16[128,256]{1,0:T(8,128)(2,1)S(1)}, u32[]{:S(2)}, u32[]{:S(2)}) collective-permute-start(bf16[128,256]{1,0:T(8,128)(2,1)S(1)} %pad_maximum_fusion.8), channel_id=1, source_target_pairs={{0,1},{1,0},{2,3},{3,2},{4,5},{5,4},{6,7},{7,6},{8,9},{9,8},{10,11... | collective-permute-start | bytes 196616 | tf_op jit(solution)/shard_map/ppermute | solution.py:16
  (12 other events, 8.0 us)

commit v4 on v1

--- a/solution.py
+++ b/solution.py
@@ -38,6 +38,53 @@
     return [s for _, s in near]
 
 
+def packed(decay, state, kind):
+    heads, width = state.shape[0], state.shape[1]
+    if kind == jnp.float32:
+        parts = decay
+    else:
+        high = decay.astype(kind)
+        parts = jnp.concatenate([high, (decay - high.astype(decay.dtype)).astype(kind)])
+    row = jnp.pad(parts.astype(kind), (0, width - parts.shape[0]))
+    slab = jnp.broadcast_to(row[None, :, None], (1,) + state.shape[1:])
+    return jnp.concatenate([state.astype(kind), slab], 0)
+
+
+def unpacked(message):
+    heads = message.shape[0] - 1
+    row = message[heads, :, 0].astype(jnp.float32)
+    decay = row[:heads] if message.dtype == jnp.float32 else row[:heads] + row[heads : 2 * heads]
+    return decay, message[:heads].astype(jnp.float32)
+
+
+def paired_scan(decay, state, state_grad, axis):
+    peers = lax.axis_size(axis)
+    if peers % 2:
+        return scanned_in([(decay, state, False), (decay, state_grad, True)], axis)
+    is_odd = lax.axis_index(axis) % 2 == 1
+    swap = [(i, i ^ 1) for i in range(peers)]
+    sent = jnp.where(is_odd, state_grad, state)
+    mate_a, mate_s = unpacked(lax.ppermute(packed(decay, sent, jnp.float32), axis, swap))
+    own = jnp.where(is_odd, state, state_grad)
+    window = (decay * mate_a, own + decay[:, None, None] * mate_s)
+    near = (jnp.ones_like(decay), jnp.zeros_like(own))
+    distance = 2
+    while distance < peers:
+        route = [(i, i + distance) for i in range(1, peers, 2) if i + distance < peers]
+        route += [(i, i - distance) for i in range(0, peers, 2) if i - distance >= 0]
+        if 2 * distance >= peers:
+            far_s = lax.ppermute(window[1].astype(jnp.bfloat16), axis, route)
+            near = (near[0], near[1] + near[0][:, None, None] * far_s.astype(jnp.float32))
+        else:
+            far_a, far_s = unpacked(lax.ppermute(packed(*window, jnp.bfloat16), axis, route))
+            near = (near[0] * far_a, near[1] + near[0][:, None, None] * far_s)
+            window = (window[0] * far_a, window[1] + window[0][:, None, None] * far_s)
+        distance *= 2
+    handed = lax.ppermute(near[1], axis, swap)
+    mine = mate_s + mate_a[:, None, None] * near[1]
+    return jnp.where(is_odd, mine, handed), jnp.where(is_odd, handed, mine)
+
+
 def shifted(block, axis, distance):
     devices = range(lax.axis_size(axis))
     route = [(i - distance, i) for i in devices if i - distance in devices]
@@ -56,7 +103,9 @@
     head_width = conv_output.shape[1] // head_count
     parity = lax.axis_index("head") % 2
     own_first = parity == 0
-    partner = swapped((write_keys, read_queries), "head", 0)
+    half = write_keys.shape[1]
+    both = swapped(jnp.concatenate([write_keys, read_queries], 1), "head", 0)
+    partner = (both[:, :half], both[:, half:])
     keys_full = jnp.where(
         own_first,
         jnp.concatenate([write_keys, partner[0]], 1),
@@ -82,9 +131,7 @@
     local_state = jnp.einsum("ln,lhp->hnp", keys_full, weighted, precision=precise)
     local_grad = jnp.einsum("ln,lhp->hnp", queries_full, seeded, precision=precise)
     decay_total = jnp.exp(totals)
-    entering, arriving = scanned_in(
-        [(decay_total, local_state, False), (decay_total, local_grad, True)], "seq"
-    )
+    entering, arriving = paired_scan(decay_total, local_state, local_grad, "seq")
     scores = product(queries_full, keys_full.T)
     row_ids = lax.broadcasted_iota(jnp.int32, (length, length), 0)
     col_ids = lax.broadcasted_iota(jnp.int32, (length, length), 1)
@@ -137,10 +184,10 @@
     key_other = jnp.where(own_first, key_part[:, half_width:], key_part[:, :half_width])
     query_mine = jnp.where(own_first, query_part[:, :half_width], query_part[:, half_width:])
     query_other = jnp.where(own_first, query_part[:, half_width:], query_part[:, :half_width])
-    received = (
-        swapped(key_other.astype(jnp.bfloat16), "head", 0).astype(key_other.dtype),
-        swapped(query_other.astype(jnp.bfloat16), "head", 0).astype(query_other.dtype),
-    )
+    sent_back = swapped(
+        jnp.concatenate([key_other, query_other], 1).astype(jnp.bfloat16), "head", 0
+    ).astype(key_other.dtype)
+    received = (sent_back[:, :half_width], sent_back[:, half_width:])
     keys_grad = key_mine + received[0]
     queries_grad = query_mine + received[1]
     logistic = jax.nn.sigmoid(preact)

time: 99.2 us -> 50.7 us (0.51)
  waiting for transfers between devices: 27.2 us -> 6.1 us
  starting transfers between devices: 37 us -> 20 us
  other arithmetic: 10 us -> 5.27 us
  local copies, waits for them, and re-layouts: 14.6 us -> 10.3 us
    ppermute x10 -> x4, starting transfers between devices: 30.2 us -> 14.9 us  [the longest x1 5.53 us: paired_scan(): handed = lax.ppermute(near[1], axis, swap)]
    ppermute x1, waiting for transfers between devices: 12.9 us -> 0.01 us  [shifted(): return lax.ppermute(block, axis, route)]
    ppermute x10 -> x4, waiting for transfers between devices: 14.3 us -> 6.1 us  [the longest x1 3.25 us: paired_scan(): far_s = lax.ppermute(window[1].astype(jnp.bfloat16), axis, route)]
    unnamed x111 -> x79, local copies, waits for them, and re-layouts: 10.5 us -> 7.55 us
    add x4 -> x2, other arithmetic: 2.69 us -> 0.21 us  [the longest x1 0.14 us: paired_scan(): near[1] + near[0][:, None, None] * far_s.astype(jnp.float32)]
    mul x3 -> x0, other arithmetic: 1.73 us -> none  [the longest x2 1.04 us: scanned_in(): near[k] = (near_a * far_a, near_s + near_a[:, None, None] * far_s)]
    reduce_sum x1, other arithmetic: 2.1 us -> 0.83 us  [body(): jnp.sum(arriving * leaving, (1, 2))[None, :]]
    ppermute x4 -> x2, starting transfers between devices: 3.78 us -> 2.74 us  [swapped(): return lax.ppermute(block, axis, route)]
  transfers between devices with their start and end apart: 15 -> 7, of which waited for: 6 -> 2; matrix products, arithmetic and copies ran while one was open for 18% -> 23% of each run, Pallas kernels for 0% -> 0%
where the time goes in v4:
time: 50.7 us; the launch traced here: 50 us
  starting transfers between devices  20 us (39%)
  local copies, waits for them, and re-layouts  10.3 us (20%)
  matrix products  7.12 us (14%)
  waiting for transfers between devices  6.1 us (12%)
  other arithmetic  5.27 us (10%)
  between operations  1.14 us (2%)
    unnamed x79, local copies, waits for them, and re-layouts  7.55 us
    ppermute x1, starting transfers between devices, paired_scan(): handed = lax.ppermute(near[1], axis, swap)  5.53 us
    ppermute x1, starting transfers between devices, paired_scan(): far_s = lax.ppermute(window[1].astype(jnp.bfloat16), axis, route)  5.13 us
    ppermute x1, waiting for transfers between devices, paired_scan(): far_s = lax.ppermute(window[1].astype(jnp.bfloat16), axis, route)  3.25 us
    ppermute x1, starting transfers between devices, paired_scan(): lax.ppermute(packed(*window, jnp.bfloat16), axis, route)  3.22 us
    ppermute x1, waiting for transfers between devices, paired_scan(): lax.ppermute(packed(*window, jnp.bfloat16), axis, route)  2.84 us
    ppermute x2, starting transfers between devices, swapped(): return lax.ppermute(block, axis, route)  2.74 us
    ppermute x1, starting transfers between devices, shifted(): return lax.ppermute(block, axis, route)  2.38 us
  transfers between devices with their start and end apart: 7, of which 2 were waited for; matrix products, arithmetic and copies ran while one was open for 23% of the time, Pallas kernels for 0%

profile of v4, /device:TPU:1, one launch (start us, length us, event | category | flops | bytes accessed | tf_op | source)
XLA Modules:
  0.0 50.0 jit_solution(15750761265689636698)
XLA Ops:
  0.6 0.8 %pad_maximum_fusion.4 = bf16[128,256]{1,0:T(8,128)(2,1)S(1)} fusion(bf16[128,128]{1,0:T(8,128)(2,1)} %param.11, bf16[128,128]{1,0:T(8,128)(2,1)} %param.10), kind=kLoop, calls=%fused_computation.74 | loop fusion | flops 131072 | bytes 131072 | tf_op jit(solution)/shard_map/concatenate | solution.py:107
  1.5 2.1 %collective-permute-start = (bf16[128,256]{1,0:T(8,128)(2,1)S(1)}, bf16[128,256]{1,0:T(8,128)(2,1)S(1)}, u32[]{:S(2)}, u32[]{:S(2)}) collective-permute-start(bf16[128,256]{1,0:T(8,128)(2,1)S(1)} %pad_maximum_fusion.4), channel_id=1, source_target_pairs={{0,1},{1,0},{2,3},{3,2},{4,5},{5,4},{6,7},{7,6},{8,9},{9,8},{10,11... | collective-permute-start | bytes 196616 | tf_op jit(solution)/shard_map/ppermute | solution.py:16
  3.8 0.6 %copy-done.29 = f32[128,8]{0,1:T(8,128)S(1)} copy-done((f32[128,8]{0,1:T(8,128)S(1)}, f32[128,8]{0,1:T(8,128)}, u32[]{:S(2)}) %copy-start.29) | copy-done | bytes 4120
  4.5 0.2 reduce_window_sum.18
  4.7 0.5 copy-done.32
  5.4 0.7 %copy-done.11 = bf16[128,512]{1,0:T(8,128)(2,1)S(1)} copy-done((bf16[128,512]{1,0:T(8,128)(2,1)S(1)}, bf16[128,512]{1,0:T(8,128)(2,1)}, u32[]{:S(2)}) %copy-start.11) | copy-done | bytes 131096
  6.3 0.7 %copy-done.1 = bf16[128,128]{1,0:T(8,128)(2,1)S(1)} copy-done((bf16[128,128]{1,0:T(8,128)(2,1)S(1)}, bf16[128,128]{1,0:T(8,128)(2,1)}, u32[]{:S(2)}) %copy-start.1) | copy-done | bytes 32792
  7.0 0.4 convolution_bitcast_fusion.2
  7.5 0.4 copy-done.2
  7.8 0.4 broadcast_select_fusion.2
  8.2 1.0 %collective-permute-start.1 = (f32[9,256,64]{1,2,0:T(8,128)S(1)}, f32[9,256,64]{1,2,0:T(8,128)S(1)}, u32[]{:S(2)}, u32[]{:S(2)}) collective-permute-start(f32[9,256,64]{1,2,0:T(8,128)S(1)} %pad_maximum_fusion), channel_id=1, source_target_pairs={{0,4},{4,0},{8,12},{12,8},{16,20},{20,16},{24,28},{28,24},{1,5},{5... | collective-permute-start | bytes 1769480 | tf_op jit(solution)/shard_map/ppermute | solution.py:67
  9.3 0.6 %compare_convert_fusion = f32[128]{0:T(128)} fusion(), kind=kLoop, calls=%fused_computation.94 | loop fusion | flops 256 | bytes 512 | tf_op jit(solution)/shard_map/convert_element_type | solution.py:168
  9.9 1.1 %multiply_reduce_fusion = (f32[128,128]{0,1:T(8,128)}, f32[8,128,128]{2,1,0:T(8,128)S(1)}) fusion(f32[128,8]{0,1:T(8,128)S(1)} %copy-done.29, f32[8,128]{1,0:T(8,128)S(1)} %copy.26, pred[128,128]{1,0:T(8,128)(4,1)S(1)} %iota_compare_fusion, f32[128,8,64]{0,2,1:T(8,128)S(1)} %bitcast.95, bf16[128,8,64]{0,2,1:T(8,128)(2,1)S(1)} %bitcast.98), kind=kOutput, calls=%fused_computation.14 | convolution fusion | flops 101302272 | bytes 1007616 | tf_op jit(solution)/shard_map/thp,shp->hts/dot_general | solution.py:143
  11.2 0.2 fusion.73
  11.4 3.2 %collective-permute-start.2 = (bf16[9,256,64]{1,2,0:T(8,128)(2,1)S(1)}, bf16[9,256,64]{1,2,0:T(8,128)(2,1)S(1)}, u32[]{:S(2)}, u32[]{:S(2)}) collective-permute-start(bf16[9,256,64]{1,2,0:T(8,128)(2,1)S(1)} %pad_maximum_fusion.1), channel_id=1, source_target_pairs={{4,12},{12,20},{20,28},{8,0},{16,8},{24,16},{5,13},{13,21},{21,29}... | collective-permute-start | bytes 884744 | tf_op jit(solution)/shard_map/ppermute | solution.py:79
  14.7 0.6 %fusion.78 = (f32[1,512]{1,0:T(1,128)}, f32[1,512]{1,0:T(1,128)}, f32[1,512]{1,0:T(1,128)}, f32[1,512]{1,0:T(1,128)}) fusion(f32[4,512]{1,0:T(4,128)S(1)} %copy-done.25), kind=kLoop, calls=%fused_computation.116 | loop fusion | bytes 16384 | tf_op jit(solution)/shard_map/slice | solution.py:200
  15.3 0.1 fusion.64
  15.5 2.8 %collective-permute-done.2 = bf16[9,256,64]{1,2,0:T(8,128)(2,1)S(1)} collective-permute-done((bf16[9,256,64]{1,2,0:T(8,128)(2,1)S(1)}, bf16[9,256,64]{1,2,0:T(8,128)(2,1)S(1)}, u32[]{:S(2)}, u32[]{:S(2)}) %collective-permute-start.2) | collective-permute-done | bytes 294944 | tf_op jit(solution)/shard_map/ppermute | solution.py:79
  18.4 5.1 %collective-permute-start.3 = (bf16[8,256,64]{1,2,0:T(8,128)(2,1)S(1)}, bf16[8,256,64]{1,2,0:T(8,128)(2,1)S(1)}, u32[]{:S(2)}, u32[]{:S(2)}) collective-permute-start(bf16[8,256,64]{1,2,0:T(8,128)(2,1)S(1)} %fusion.2), channel_id=1, source_target_pairs={{4,20},{12,28},{16,0},{24,8},{5,21},{13,29},{17,1},{25,9},{6,22},{... | collective-permute-start | bytes 786440 | tf_op jit(solution)/shard_map/ppermute | solution.py:76
  23.7 3.2 %collective-permute-done.3 = bf16[8,256,64]{1,2,0:T(8,128)(2,1)S(1)} collective-permute-done((bf16[8,256,64]{1,2,0:T(8,128)(2,1)S(1)}, bf16[8,256,64]{1,2,0:T(8,128)(2,1)S(1)}, u32[]{:S(2)}, u32[]{:S(2)}) %collective-permute-start.3) | collective-permute-done | bytes 262176 | tf_op jit(solution)/shard_map/ppermute | solution.py:76
  26.9 0.1 convert_add_fusion
  27.0 5.5 %collective-permute-start.4 = (f32[8,256,64]{1,2,0:T(8,128)S(1)}, f32[8,256,64]{1,2,0:T(8,128)S(1)}, u32[]{:S(2)}, u32[]{:S(2)}) collective-permute-start(f32[8,256,64]{1,2,0:T(8,128)S(1)} %convert_add_fusion), channel_id=1, source_target_pairs={{0,4},{4,0},{8,12},{12,8},{16,20},{20,16},{24,28},{28,24},{1,5},{5... | collective-permute-start | bytes 1572872 | tf_op jit(solution)/shard_map/ppermute | solution.py:83
  32.6 0.2 fusion.7
  32.8 0.7 %copy.34 = f32[8,128]{0,1:T(8,128)} copy(f32[8,128]{1,0:T(8,128)S(1)} %fusion.7) | data formatting | bytes 8192 | tf_op jit(solution)/shard_map/reduce_sum | solution.py:151
  33.6 2.1 %fusion.8 = f32[8,1,128]{2,1,0:T(1,128)S(1)} fusion(f32[8,128,1]{1,2,0:T(1,128)S(1)} %bitcast.108, f32[8,128,128]{2,1,0:T(8,128)} %copy-done.7, f32[128,128]{1,0:T(8,128)S(1)} %fusion.64, f32[8,128]{1,0:T(8,128)S(1)} %copy-done.19, pred[128,128]{1,0:T(8,128)(4,1)S(1)} %iota_compare_fusion), kind=kOutput, calls=%fused_computation.31 | convolution fusion | flops 2097152 | bytes 618496 | tf_op jit(solution)/shard_map/hts,hs->th/dot_general | solution.py:150
  35.7 0.7 %copy.50 = f32[8,1,128]{0,2,1:T(8,128)} copy(f32[8,1,128]{2,1,0:T(1,128)S(1)} %fusion.8) | data formatting | bytes 8192 | tf_op jit(solution)/shard_map/hts,hs->th/dot_general | solution.py:150
  36.4 0.6 %copy-done.27 = f32[8]{0:T(128)S(1)} copy-done((f32[8]{0:T(128)S(1)}, f32[8]{0:T(128)}, u32[]{:S(2)}) %copy-start.27) | copy-done | bytes 56
  37.0 0.8 %multiply_reduce_fusion.1 = (f32[8]{0:T(128)}, f32[8,256,64]{1,2,0:T(8,128)S(1)}, f32[8,256,64]{1,2,0:T(8,128)S(1)}) fusion(f32[8,256,64]{1,2,0:T(8,128)S(1)} %convolution_bitcast_fusion.2, f32[8]{0:T(128)S(1)} %copy-done.27, f32[8,256,64]{1,2,0:T(8,128)S(1)} %collective-permute-done.4, f32[8,256,64]{1,2,0:T(8,128)S(1)} %convert_add_fusion, ...), kind=kLoop, calls=%fused_computation.15 | loop fusion | flops 1048568 | bytes 3145825 | tf_op jit(solution)/shard_map/reduce_sum | solution.py:169
  37.9 0.6 %convolution_bitcast_fusion.5 = f32[128,256]{1,0:T(8,128)S(1)} fusion(f32[8,256,64]{1,2,0:T(8,128)S(1)} %get-tuple-element.17, f32[128,8,64]{0,2,1:T(8,128)S(1)} %bitcast.96, f32[128,8]{0,1:T(8,128)S(1)} %copy-done.15), kind=kOutput, calls=%fused_computation.6 | convolution fusion | flops 201392128 | bytes 921600 | tf_op jit(solution)/shard_map/lhp,hnp->ln/dot_general | solution.py:181
  38.5 0.4 multiply_reduce_fusion.2
  38.9 0.4 copy-done.13
  39.3 0.3 copy-done.20
  39.6 0.5 %multiply_add_fusion.2 = f32[128,8,64]{0,2,1:T(8,128)S(1)} fusion(f32[128,8,64]{0,2,1:T(8,128)S(1)} %bitcast.103, bf16[128,8,64]{0,2,1:T(8,128)(2,1)S(1)} %bitcast.99, f32[8,128]{1,0:T(8,128)S(1)} %bitcast.109, f32[128,128]{1,0:T(8,128)S(1)} %copy-done.13, f32[8,128]{1,0:T(8,128)S(1)} %copy-done.20, pred[128,128]{1,0:T(8,128)(4,1)S(1)} %iota_compare_fusion, ...), kind=kOutput, calls=%fused_computation.52 | convolution fusion | flops 101515264 | bytes 749600 | tf_op jit(solution)/shard_map/hts,thp->shp/dot_general | solution.py:146
  40.4 2.4 %collective-permute-start.5 = (f32[3,512]{1,0:T(4,128)S(1)}, f32[3,512]{1,0:T(4,128)S(1)}, u32[]{:S(2)}, u32[]{:S(2)}) collective-permute-start(f32[3,512]{1,0:T(4,128)S(1)} %slice.113), channel_id=1, source_target_pairs={{4,0},{8,4},{12,8},{16,12},{20,16},{24,20},{28,24},{5,1},{9,5},{13... | collective-permute-start | bytes 18440 | tf_op jit(solution)/shard_map/ppermute | solution.py:91
  42.8 0.6 %convolution_bitcast_fusion.4 = f32[128,256]{1,0:T(8,128)S(1)} fusion(f32[8,256,64]{1,2,0:T(8,128)S(1)} %get-tuple-element.16, bf16[128,8,64]{0,2,1:T(8,128)(2,1)S(1)} %bitcast.100, f32[128,8]{0,1:T(8,128)S(1)} %copy-done.17), kind=kOutput, calls=%fused_computation.5 | convolution fusion | flops 201457664 | bytes 790528 | tf_op jit(solution)/shard_map/lhp,hnp->ln/dot_general | solution.py:171
  43.4 0.2 copy-done.8
  43.7 0.2 convolution_add_fusion
  43.9 0.3 convolution_add_fusion.1
  44.2 0.6 %collective-permute-start.6 = (bf16[128,256]{1,0:T(8,128)(2,1)S(1)}, bf16[128,256]{1,0:T(8,128)(2,1)S(1)}, u32[]{:S(2)}, u32[]{:S(2)}) collective-permute-start(bf16[128,256]{1,0:T(8,128)(2,1)S(1)} %pad_maximum_fusion.6), channel_id=1, source_target_pairs={{0,1},{1,0},{2,3},{3,2},{4,5},{5,4},{6,7},{7,6},{8,9},{9,8},{10,11... | collective-permute-start | bytes 196616 | tf_op jit(solution)/shard_map/ppermute | solution.py:16
  44.9 0.4 fusion.18
  45.4 0.3 copy-done.10
  45.8 0.4 copy-done.9
  46.3 0.2 reduce_window_sum.19
  46.5 0.7 %copy.39 = f32[128,8]{0,1:T(8,128)} copy(f32[128,8]{1,0:T(8,128)S(1)} %rev.8) | data formatting | bytes 8192
  47.1 0.7 %copy.40 = f32[128,8]{0,1:T(8,128)} copy(f32[128,8]{1,0:T(8,128)S(1)} %get-tuple-element.22) | data formatting | bytes 8192
  47.8 0.6 %copy-done.22 = f32[1,512]{1,0:T(1,128)S(1)} copy-done((f32[1,512]{1,0:T(1,128)S(1)}, f32[1,512]{1,0:T(1,128)}, u32[]{:S(2)}) %copy-start.22) | copy-done | bytes 2072
  48.5 0.8 %fusion.15 = bf16[128,512]{1,0:T(8,128)(2,1)} fusion(f32[128,512]{1,0:T(8,128)S(1)} %fusion.23, f32[3,512]{1,0:T(4,128)S(1)} %collective-permute-done.5, f32[512]{0:T(512)S(1)} %bitcast.106, f32[512]{0:T(512)S(1)} %bitcast.107, f32[512]{0:T(512)S(1)} %bitcast.105, f32[512]{0:T(512)S(1)} %bitcast.104), kind=kLoop, calls=%fused_computation.40 | loop fusion | flops 720896 | bytes 407552 | tf_op jit(solution)/shard_map/convert_element_type | solution.py:202
  49.3 0.7 %slice_add_fusion = (f32[128,128]{1,0:T(8,128)}, f32[128,128]{1,0:T(8,128)}) fusion(f32[128,256]{1,0:T(8,128)S(1)} %convert_element_type.60, f32[128,256]{1,0:T(8,128)S(1)} %convolution_add_fusion, pred[]{:T(512)S(6)} %eq.20, f32[128,256]{1,0:T(8,128)S(1)} %convolution_add_fusion.1), kind=kLoop, calls=%fused_computation.78 | loop fusion | flops 65536 | bytes 524289 | tf_op jit(solution)/shard_map/add | solution.py:192
  (103 shorter events, 2.0 us)
Async XLA Ops:
  0.6 2.9 %copy-start = (bf16[128,512]{1,0:T(8,128)(2,1)S(1)}, bf16[128,512]{1,0:T(8,128)(2,1)}, u32[]{:S(2)}) copy-start(bf16[128,512]{1,0:T(8,128)(2,1)} %param.8) | copy-start | bytes 393220
  1.5 2.2 %copy-start.28 = (f32[128,8]{0,1:T(8,128)S(1)}, f32[128,8]{0,1:T(8,128)}, u32[]{:S(2)}) copy-start(f32[128,8]{0,1:T(8,128)} %param.12) | copy-start | bytes 12292
  1.5 4.8 %collective-permute-start = (bf16[128,256]{1,0:T(8,128)(2,1)S(1)}, bf16[128,256]{1,0:T(8,128)(2,1)S(1)}, u32[]{:S(2)}, u32[]{:S(2)}) collective-permute-start(bf16[128,256]{1,0:T(8,128)(2,1)S(1)} %pad_maximum_fusion.4), channel_id=1, source_target_pairs={{0,1},{1,0},{2,3},{3,2},{4,5},{5,4},{6,7},{7,6},{8,9},{9,8},{10,11... | collective-permute-start | bytes 196616 | tf_op jit(solution)/shard_map/ppermute | solution.py:16
  3.7 0.7 %copy-start.29 = (f32[128,8]{0,1:T(8,128)S(1)}, f32[128,8]{0,1:T(8,128)}, u32[]{:S(2)}) copy-start(f32[128,8]{0,1:T(8,128)} %param.13) | copy-start | bytes 12292
  4.6 0.5 %copy-start.32 = (f32[8]{0:T(128)}, f32[8]{0:T(128)S(1)}, u32[]{:S(2)}) copy-start(f32[8]{0:T(128)S(1)} %slice_bitcast_fusion.1) | copy-start | bytes 100
  5.2 6.0 %copy-start.26 = (f32[8]{0:T(128)}, f32[8]{0:T(128)S(1)}, u32[]{:S(2)}) copy-start(f32[8]{0:T(128)S(1)} %fusion.58) | copy-start | bytes 100
  5.2 0.9 %copy-start.11 = (bf16[128,512]{1,0:T(8,128)(2,1)S(1)}, bf16[128,512]{1,0:T(8,128)(2,1)}, u32[]{:S(2)}) copy-start(bf16[128,512]{1,0:T(8,128)(2,1)} %param.9) | copy-start | bytes 393220
  5.4 1.0 %copy-start.14 = (f32[128,8]{0,1:T(8,128)}, f32[128,8]{0,1:T(8,128)S(1)}, u32[]{:S(2)}) copy-start(f32[128,8]{0,1:T(8,128)S(1)} %copy.30) | copy-start | bytes 12292
  6.3 1.2 %copy-start.16 = (f32[128,8]{0,1:T(8,128)}, f32[128,8]{0,1:T(8,128)S(1)}, u32[]{:S(2)}) copy-start(f32[128,8]{0,1:T(8,128)S(1)} %copy.32) | copy-start | bytes 12292
  6.3 0.8 %copy-start.1 = (bf16[128,128]{1,0:T(8,128)(2,1)S(1)}, bf16[128,128]{1,0:T(8,128)(2,1)}, u32[]{:S(2)}) copy-start(bf16[128,128]{1,0:T(8,128)(2,1)} %param.10) | copy-start | bytes 98308
  6.3 1.1 %copy-start.5 = (bf16[128,128]{1,0:T(8,128)(2,1)}, bf16[128,128]{1,0:T(8,128)(2,1)S(1)}, u32[]{:S(2)}) copy-start(bf16[128,128]{1,0:T(8,128)(2,1)S(1)} %get-tuple-element.27) | copy-start | bytes 98308
  6.3 1.1 %copy-start.3 = (bf16[128,128]{1,0:T(8,128)(2,1)}, bf16[128,128]{1,0:T(8,128)(2,1)S(1)}, u32[]{:S(2)}) copy-start(bf16[128,128]{1,0:T(8,128)(2,1)S(1)} %get-tuple-element.26) | copy-start | bytes 98308
  7.0 0.8 %copy-start.2 = (bf16[128,128]{1,0:T(8,128)(2,1)S(1)}, bf16[128,128]{1,0:T(8,128)(2,1)}, u32[]{:S(2)}) copy-start(bf16[128,128]{1,0:T(8,128)(2,1)} %param.11) | copy-start | bytes 98308
  8.2 2.8 %collective-permute-start.1 = (f32[9,256,64]{1,2,0:T(8,128)S(1)}, f32[9,256,64]{1,2,0:T(8,128)S(1)}, u32[]{:S(2)}, u32[]{:S(2)}) collective-permute-start(f32[9,256,64]{1,2,0:T(8,128)S(1)} %pad_maximum_fusion), channel_id=1, source_target_pairs={{0,4},{4,0},{8,12},{12,8},{16,20},{20,16},{24,28},{28,24},{1,5},{5... | collective-permute-start | bytes 1769480 | tf_op jit(solution)/shard_map/ppermute | solution.py:67
  9.3 0.6 %copy-start.18 = (f32[8,128]{1,0:T(8,128)}, f32[8,128]{1,0:T(8,128)S(1)}, u32[]{:S(2)}) copy-start(f32[8,128]{1,0:T(8,128)S(1)} %copy.26) | copy-start | bytes 12292
  11.1 21.5 %copy-start.7 = (f32[8,128,128]{2,1,0:T(8,128)}, f32[8,128,128]{2,1,0:T(8,128)S(1)}, u32[]{:S(2)}) copy-start(f32[8,128,128]{2,1,0:T(8,128)S(1)} %get-tuple-element.37) | copy-start | bytes 1572868
  11.4 3.3 %copy-start.25 = (f32[4,512]{1,0:T(4,128)S(1)}, f32[4,512]{1,0:T(4,128)}, u32[]{:S(2)}) copy-start(f32[4,512]{1,0:T(4,128)} %param.15) | copy-start | bytes 24580
  11.4 3.9 %copy-start.4 = (bf16[128,128]{1,0:T(8,128)(2,1)S(1)}, bf16[128,128]{1,0:T(8,128)(2,1)}, u32[]{:S(2)}) copy-start(bf16[128,128]{1,0:T(8,128)(2,1)} %copy-done.3) | copy-start | bytes 98308
  11.4 3.9 %copy-start.6 = (bf16[128,128]{1,0:T(8,128)(2,1)S(1)}, bf16[128,128]{1,0:T(8,128)(2,1)}, u32[]{:S(2)}) copy-start(bf16[128,128]{1,0:T(8,128)(2,1)} %copy-done.5) | copy-start | bytes 98308
  11.4 6.9 %collective-permute-start.2 = (bf16[9,256,64]{1,2,0:T(8,128)(2,1)S(1)}, bf16[9,256,64]{1,2,0:T(8,128)(2,1)S(1)}, u32[]{:S(2)}, u32[]{:S(2)}) collective-permute-start(bf16[9,256,64]{1,2,0:T(8,128)(2,1)S(1)} %pad_maximum_fusion.1), channel_id=1, source_target_pairs={{4,12},{12,20},{20,28},{8,0},{16,8},{24,16},{5,13},{13,21},{21,29}... | collective-permute-start | bytes 884744 | tf_op jit(solution)/shard_map/ppermute | solution.py:79
  15.4 18.1 %copy-start.12 = (f32[128,128]{1,0:T(8,128)}, f32[128,128]{1,0:T(8,128)S(1)}, u32[]{:S(2)}) copy-start(f32[128,128]{1,0:T(8,128)S(1)} %fusion.64) | copy-start | bytes 196612
  18.4 8.5 %collective-permute-start.3 = (bf16[8,256,64]{1,2,0:T(8,128)(2,1)S(1)}, bf16[8,256,64]{1,2,0:T(8,128)(2,1)S(1)}, u32[]{:S(2)}, u32[]{:S(2)}) collective-permute-start(bf16[8,256,64]{1,2,0:T(8,128)(2,1)S(1)} %fusion.2), channel_id=1, source_target_pairs={{4,20},{12,28},{16,0},{24,8},{5,21},{13,29},{17,1},{25,9},{6,22},{... | collective-permute-start | bytes 786440 | tf_op jit(solution)/shard_map/ppermute | solution.py:76
  26.9 5.7 %copy-start.19 = (f32[8,128]{1,0:T(8,128)S(1)}, f32[8,128]{1,0:T(8,128)}, u32[]{:S(2)}) copy-start(f32[8,128]{1,0:T(8,128)} %copy-done.18) | copy-start | bytes 12292
  27.0 9.4 %collective-permute-start.4 = (f32[8,256,64]{1,2,0:T(8,128)S(1)}, f32[8,256,64]{1,2,0:T(8,128)S(1)}, u32[]{:S(2)}, u32[]{:S(2)}) collective-permute-start(f32[8,256,64]{1,2,0:T(8,128)S(1)} %convert_add_fusion), channel_id=1, source_target_pairs={{0,4},{4,0},{8,12},{12,8},{16,20},{20,16},{24,28},{28,24},{1,5},{5... | collective-permute-start | bytes 1572872 | tf_op jit(solution)/shard_map/ppermute | solution.py:83
  32.8 0.7 %copy-start.30 = (f32[128,8]{0,1:T(8,128)S(1)}, f32[128,8]{0,1:T(8,128)}, u32[]{:S(2)}) copy-start(f32[128,8]{0,1:T(8,128)} %param.13) | copy-start | bytes 12292
  36.4 0.6 %copy-start.27 = (f32[8]{0:T(128)S(1)}, f32[8]{0:T(128)}, u32[]{:S(2)}) copy-start(f32[8]{0:T(128)} %copy-done.26) | copy-start | bytes 100
  37.0 0.8 %copy-start.15 = (f32[128,8]{0,1:T(8,128)S(1)}, f32[128,8]{0,1:T(8,128)}, u32[]{:S(2)}) copy-start(f32[128,8]{0,1:T(8,128)} %copy-done.14) | copy-start | bytes 12292
  38.5 0.8 %copy-start.13 = (f32[128,128]{1,0:T(8,128)S(1)}, f32[128,128]{1,0:T(8,128)}, u32[]{:S(2)}) copy-start(f32[128,128]{1,0:T(8,128)} %copy-done.12) | copy-start | bytes 196612
  38.5 0.8 %copy-start.31 = (f32[128,8]{0,1:T(8,128)S(1)}, f32[128,8]{0,1:T(8,128)}, u32[]{:S(2)}) copy-start(f32[128,8]{0,1:T(8,128)} %param.13) | copy-start | bytes 12292
  38.9 0.7 %copy-start.20 = (f32[8,128]{1,0:T(8,128)S(1)}, f32[8,128]{1,0:T(8,128)}, u32[]{:S(2)}) copy-start(f32[8,128]{1,0:T(8,128)} %copy-done.18) | copy-start | bytes 12292
  38.9 0.7 %copy-start.36 = (f32[8]{0:T(128)S(1)}, f32[8]{0:T(128)}, u32[]{:S(2)}) copy-start(f32[8]{0:T(128)} %param.14) | copy-start | bytes 100
  40.4 2.4 %copy-start.17 = (f32[128,8]{0,1:T(8,128)S(1)}, f32[128,8]{0,1:T(8,128)}, u32[]{:S(2)}) copy-start(f32[128,8]{0,1:T(8,128)} %copy-done.16) | copy-start | bytes 12292
  40.4 7.4 %collective-permute-start.5 = (f32[3,512]{1,0:T(4,128)S(1)}, f32[3,512]{1,0:T(4,128)S(1)}, u32[]{:S(2)}, u32[]{:S(2)}) collective-permute-start(f32[3,512]{1,0:T(4,128)S(1)} %slice.113), channel_id=1, source_target_pairs={{4,0},{8,4},{12,8},{16,12},{20,16},{24,20},{28,24},{5,1},{9,5},{13... | collective-permute-start | bytes 18440 | tf_op jit(solution)/shard_map/ppermute | solution.py:91
  42.8 0.8 %copy-start.8 = (f32[128,128]{0,1:T(8,128)S(1)}, f32[128,128]{0,1:T(8,128)}, u32[]{:S(2)}) copy-start(f32[128,128]{0,1:T(8,128)} %get-tuple-element.36) | copy-start | bytes 196612
  44.2 5.1 %collective-permute-start.6 = (bf16[128,256]{1,0:T(8,128)(2,1)S(1)}, bf16[128,256]{1,0:T(8,128)(2,1)S(1)}, u32[]{:S(2)}, u32[]{:S(2)}) collective-permute-start(bf16[128,256]{1,0:T(8,128)(2,1)S(1)} %pad_maximum_fusion.6), channel_id=1, source_target_pairs={{0,1},{1,0},{2,3},{3,2},{4,5},{5,4},{6,7},{7,6},{8,9},{9,8},{10,11... | collective-permute-start | bytes 196616 | tf_op jit(solution)/shard_map/ppermute | solution.py:16
  44.9 0.8 %copy-start.10 = (f32[8,1,128]{0,2,1:T(8,128)S(1)}, f32[8,1,128]{0,2,1:T(8,128)}, u32[]{:S(2)}) copy-start(f32[8,1,128]{0,2,1:T(8,128)} %copy.50) | copy-start | bytes 12292
  45.3 0.9 %copy-start.9 = (f32[8,128]{0,1:T(8,128)S(1)}, f32[8,128]{0,1:T(8,128)}, u32[]{:S(2)}) copy-start(f32[8,128]{0,1:T(8,128)} %copy.34) | copy-start | bytes 12292
  45.4 0.7 %copy-start.33 = (f32[8]{0:T(128)S(1)}, f32[8]{0:T(128)}, u32[]{:S(2)}) copy-start(f32[8]{0:T(128)} %copy-done.32) | copy-start | bytes 100
  45.4 0.7 %copy-start.34 = (f32[8]{0:T(128)S(1)}, f32[8]{0:T(128)}, u32[]{:S(2)}) copy-start(f32[8]{0:T(128)} %get-tuple-element.15) | copy-start | bytes 100
  45.4 0.7 %copy-start.35 = (f32[128]{0:T(128)S(1)}, f32[128]{0:T(128)}, u32[]{:S(2)}) copy-start(f32[128]{0:T(128)} %compare_convert_fusion) | copy-start | bytes 1540
  46.4 1.4 %copy-start.23 = (f32[1,512]{1,0:T(1,128)S(1)}, f32[1,512]{1,0:T(1,128)}, u32[]{:S(2)}) copy-start(f32[1,512]{1,0:T(1,128)} %get-tuple-element.32) | copy-start | bytes 6148
  46.4 1.4 %copy-start.24 = (f32[1,512]{1,0:T(1,128)S(1)}, f32[1,512]{1,0:T(1,128)}, u32[]{:S(2)}) copy-start(f32[1,512]{1,0:T(1,128)} %get-tuple-element.33) | copy-start | bytes 6148
  47.8 0.7 %copy-start.22 = (f32[1,512]{1,0:T(1,128)S(1)}, f32[1,512]{1,0:T(1,128)}, u32[]{:S(2)}) copy-start(f32[1,512]{1,0:T(1,128)} %get-tuple-element.31) | copy-start | bytes 6148
  47.8 0.7 %copy-start.21 = (f32[1,512]{1,0:T(1,128)S(1)}, f32[1,512]{1,0:T(1,128)}, u32[]{:S(2)}) copy-start(f32[1,512]{1,0:T(1,128)} %get-tuple-element.30) | copy-start | bytes 6148

commit v5 on v4

--- a/solution.py
+++ b/solution.py
@@ -57,14 +57,22 @@
     return decay, message[:heads].astype(jnp.float32)
 
 
-def paired_scan(decay, state, state_grad, axis):
+def paired_scan(decay, state, state_grad, axis, rider_fn, rider_inputs):
     peers = lax.axis_size(axis)
     if peers % 2:
-        return scanned_in([(decay, state, False), (decay, state_grad, True)], axis)
+        found = scanned_in([(decay, state, False), (decay, state_grad, True)], axis)
+        return found[0], found[1], rider_fn(*rider_inputs)
     is_odd = lax.axis_index(axis) % 2 == 1
     swap = [(i, i ^ 1) for i in range(peers)]
     sent = jnp.where(is_odd, state_grad, state)
-    mate_a, mate_s = unpacked(lax.ppermute(packed(decay, sent, jnp.float32), axis, swap))
+    message = packed(decay, sent, jnp.float32)
+    if peers == 2:
+        message, rider_inputs = lax.optimization_barrier((message, rider_inputs))
+        riders = rider_fn(*rider_inputs)
+    mate = lax.ppermute(message, axis, swap)
+    if peers == 2:
+        mate, riders = lax.optimization_barrier((mate, riders))
+    mate_a, mate_s = unpacked(mate)
     own = jnp.where(is_odd, state, state_grad)
     window = (decay * mate_a, own + decay[:, None, None] * mate_s)
     near = (jnp.ones_like(decay), jnp.zeros_like(own))
@@ -74,15 +82,23 @@
         route += [(i, i - distance) for i in range(0, peers, 2) if i - distance >= 0]
         if 2 * distance >= peers:
             far_s = lax.ppermute(window[1].astype(jnp.bfloat16), axis, route)
+            if distance == 2:
+                far_s, rider_inputs = lax.optimization_barrier((far_s, rider_inputs))
+                riders = rider_fn(*rider_inputs)
             near = (near[0], near[1] + near[0][:, None, None] * far_s.astype(jnp.float32))
         else:
-            far_a, far_s = unpacked(lax.ppermute(packed(*window, jnp.bfloat16), axis, route))
+            far = lax.ppermute(packed(*window, jnp.bfloat16), axis, route)
+            if distance == 2:
+                far, rider_inputs = lax.optimization_barrier((far, rider_inputs))
+                riders = rider_fn(*rider_inputs)
+            far_a, far_s = unpacked(far)
             near = (near[0] * far_a, near[1] + near[0][:, None, None] * far_s)
             window = (window[0] * far_a, window[1] + window[0][:, None, None] * far_s)
         distance *= 2
-    handed = lax.ppermute(near[1], axis, swap)
+    passing, riders = lax.optimization_barrier((near[1], riders))
+    handed = lax.ppermute(passing, axis, swap)
     mine = mate_s + mate_a[:, None, None] * near[1]
-    return jnp.where(is_odd, mine, handed), jnp.where(is_odd, handed, mine)
+    return jnp.where(is_odd, mine, handed), jnp.where(is_odd, handed, mine), riders
 
 
 def shifted(block, axis, distance):
@@ -131,54 +147,75 @@
     local_state = jnp.einsum("ln,lhp->hnp", keys_full, weighted, precision=precise)
     local_grad = jnp.einsum("ln,lhp->hnp", queries_full, seeded, precision=precise)
     decay_total = jnp.exp(totals)
-    entering, arriving = paired_scan(decay_total, local_state, local_grad, "seq")
-    scores = product(queries_full, keys_full.T)
-    row_ids = lax.broadcasted_iota(jnp.int32, (length, length), 0)
-    col_ids = lax.broadcasted_iota(jnp.int32, (length, length), 1)
-    causal = row_ids >= col_ids
-    cum_heads = cumulative.T
-    step_heads = step_size.T
-    log_gap = jnp.where(causal[None], cum_heads[:, :, None] - cum_heads[:, None, :], -1e30)
-    decay_mask = jnp.exp(log_gap)
-    pair_dots = jnp.einsum("thp,shp->hts", upstream3, values3, precision=precise)
-    masked_scores = decay_mask * scores[None]
-    weight_sum = jnp.einsum("hts,hs->ts", decay_mask * pair_dots, step_heads, precision=precise)
-    within = jnp.einsum(
-        "hts,thp->shp", masked_scores * step_heads[:, None, :], upstream3, precision=precise
-    )
-    effect = masked_scores * pair_dots
-    row_sums = jnp.einsum("hts,hs->th", effect, step_heads, precision=precise)
-    col_sums = jnp.sum(effect, 1).T
+    def local_terms(keys_full, queries_full, values3, upstream3, cumulative, step_size, preact):
+        scores = product(queries_full, keys_full.T)
+        row_ids = lax.broadcasted_iota(jnp.int32, (length, length), 0)
+        col_ids = lax.broadcasted_iota(jnp.int32, (length, length), 1)
+        causal = row_ids >= col_ids
+        cum_heads = cumulative.T
+        step_heads = step_size.T
+        log_gap = jnp.where(causal[None], cum_heads[:, :, None] - cum_heads[:, None, :], -1e30)
+        decay_mask = jnp.exp(log_gap)
+        pair_dots = jnp.einsum("thp,shp->hts", upstream3, values3, precision=precise)
+        masked_scores = decay_mask * scores[None]
+        weight_sum = jnp.einsum("hts,hs->ts", decay_mask * pair_dots, step_heads, precision=precise)
+        within = jnp.einsum(
+            "hts,thp->shp", masked_scores * step_heads[:, None, :], upstream3, precision=precise
+        )
+        effect = masked_scores * pair_dots
+        row_sums = jnp.einsum("hts,hs->th", effect, step_heads, precision=precise)
+        col_sums = jnp.sum(effect, 1).T
+        logistic = jax.nn.sigmoid(preact)
+        return (
+            within + skip_gain[None, :, None] * upstream3,
+            row_sums - col_sums * step_size,
+            col_sums,
+            product(weight_sum, keys_full),
+            lax.dot_general(
+                weight_sum,
+                queries_full,
+                (((0,), (0,)), ((), ())),
+                preferred_element_type=jnp.float32,
+                precision=precise,
+            ),
+            logistic * (1.0 + preact * (1.0 - logistic)),
+        )
+    def local_block(*inputs):
+        always = lax.axis_index("seq") >= 0
+        return lax.cond(
+            always,
+            local_terms,
+            lambda *a: jax.tree.map(jnp.zeros_like, local_terms(*a)),
+            *inputs,
+        )
+
+    entering, arriving, riders = paired_scan(
+        decay_total,
+        local_state,
+        local_grad,
+        "seq",
+        local_block,
+        (keys_full, queries_full, values3, upstream3, cumulative, step_size, preact),
+    )
+    within_part, local_decay, col_sums, query_local, key_local, silu_slope = riders
     from_state = jnp.einsum("ln,hnp->lhp", queries_full, entering, precision=precise)
     into_state = jnp.einsum("ln,hnp->lhp", keys_full, arriving, precision=precise)
     carried = jnp.sum(values3 * into_state, 2)
     step_grad = col_sums + to_end * carried
-    value_grad = (
-        within
-        + skip_gain[None, :, None] * upstream3
-        + (to_end * step_size)[:, :, None] * into_state
-    )
+    value_grad = within_part + (to_end * step_size)[:, :, None] * into_state
     leaving = decay_total[:, None, None] * entering + local_state
     decay_terms = (
-        row_sums
-        - col_sums * step_size
+        local_decay
         + from_start * jnp.sum(upstream3 * from_state, 2)
         - to_end * step_size * carried
     )
     last_row = (lax.broadcasted_iota(jnp.int32, (length, 1), 0) == length - 1).astype(jnp.float32)
     decay_terms = decay_terms + last_row * jnp.sum(arriving * leaving, (1, 2))[None, :]
     decay_grad = jnp.flip(jnp.cumsum(jnp.flip(decay_terms, 0), 0), 0)
-    query_part = product(weight_sum, keys_full) + jnp.einsum(
+    query_part = query_local + jnp.einsum(
         "lhp,hnp->ln", seeded, entering, precision=precise
     )
-    key_part = lax.dot_general(
-        weight_sum,
-        queries_full,
-        (((0,), (0,)), ((), ())),
-        preferred_element_type=jnp.float32,
-        precision=precise,
-    )
-    key_part = key_part + jnp.einsum("lhp,hnp->ln", weighted, arriving, precision=precise)
+    key_part = key_local + jnp.einsum("lhp,hnp->ln", weighted, arriving, precision=precise)
     half_width = state_count // 2
     key_mine = jnp.where(own_first, key_part[:, :half_width], key_part[:, half_width:])
     key_other = jnp.where(own_first, key_part[:, half_width:], key_part[:, :half_width])
@@ -190,8 +227,7 @@
     received = (sent_back[:, :half_width], sent_back[:, half_width:])
     keys_grad = key_mine + received[0]
     queries_grad = query_mine + received[1]
-    logistic = jax.nn.sigmoid(preact)
-    conv_grad = value_grad.reshape(length, -1) * logistic * (1.0 + preact * (1.0 - logistic))
+    conv_grad = value_grad.reshape(length, -1) * silu_slope
     following = shifted(conv_grad[:3], "seq", -1)
     extended = jnp.concatenate([conv_grad, following], 0)
     input_grad = jnp.zeros_like(conv_grad)

time: 50.7 us -> 47.3 us (0.933)
  local copies, waits for them, and re-layouts: 10.3 us -> 6.65 us
  other arithmetic: 5.27 us -> 6.37 us
  starting transfers between devices: 20 us -> 19.1 us
  waiting for transfers between devices: 6.1 us -> 6.98 us
  matrix products: 7.12 us -> 6.5 us
    ppermute x3, waiting for transfers between devices: 2.85 us -> 6.97 us  [the longest x1 3.85 us: paired_scan(): far = lax.ppermute(packed(*window, jnp.bfloat16), axis, route)]
    ppermute x1, waiting for transfers between devices: 3.25 us -> 0.01 us  [paired_scan(): far_s = lax.ppermute(window[1].astype(jnp.bfloat16), axis, route)]
    unnamed x79 -> x48, local copies, waits for them, and re-layouts: 7.55 us -> 5.97 us
    reduce_sum x3 -> x0, local copies, waits for them, and re-layouts: 0.93 us -> none  [the longest x1 0.73 us: body(): col_sums = jnp.sum(effect, 1).T]
    ppermute x3, starting transfers between devices: 9.77 us -> 8.86 us  [the longest x1 4.51 us: paired_scan(): handed = lax.ppermute(passing, axis, swap)]
    dot_general x4, matrix products: 4.03 us -> 3.21 us  [the longest x1 1.09 us: local_terms(): jnp.einsum('thp,shp->hts', upstream3, values3, precision=precise)]
    dot_general x1 -> x0, local copies, waits for them, and re-layouts: 0.74 us -> none  [body(): row_sums = jnp.einsum('hts,hs->th', effect, step_heads, precision=precise)]
    concatenate x2, other arithmetic: 0.07 us -> 0.78 us  [packed(): return jnp.concatenate([state.astype(kind), slab], 0)]
  transfers between devices with their start and end apart: 7 -> 7, of which waited for: 2 -> 3; matrix products, arithmetic and copies ran while one was open for 23% -> 20% of each run, Pallas kernels for 0% -> 0%
where the time goes in v5:
time: 47.3 us; the launch traced here: 46.7 us
  starting transfers between devices  19.1 us (40%)
  waiting for transfers between devices  6.98 us (15%)
  local copies, waits for them, and re-layouts  6.65 us (14%)
  matrix products  6.5 us (14%)
  other arithmetic  6.37 us (13%)
  between operations  1.06 us (2%)
    unnamed x48, local copies, waits for them, and re-layouts  5.97 us
    ppermute x1, starting transfers between devices, paired_scan(): far_s = lax.ppermute(window[1].astype(jnp.bfloat16), axis, route)  5.14 us
    ppermute x1, starting transfers between devices, paired_scan(): handed = lax.ppermute(passing, axis, swap)  4.51 us
    ppermute x1, waiting for transfers between devices, paired_scan(): far = lax.ppermute(packed(*window, jnp.bfloat16), axis, route)  3.85 us
    ppermute x1, starting transfers between devices, paired_scan(): far = lax.ppermute(packed(*window, jnp.bfloat16), axis, route)  3.34 us
    ppermute x2, starting transfers between devices, swapped(): return lax.ppermute(block, axis, route)  2.76 us
    ppermute x1, starting transfers between devices, shifted(): return lax.ppermute(block, axis, route)  2.28 us
    ppermute x1, waiting for transfers between devices, paired_scan(): mate = lax.ppermute(message, axis, swap)  1.63 us
  transfers between devices with their start and end apart: 7, of which 3 were waited for; matrix products, arithmetic and copies ran while one was open for 20% of the time, Pallas kernels for 0%

profile of v5, /device:TPU:1, one launch (start us, length us, event | category | flops | bytes accessed | tf_op | source)
XLA Modules:
  0.0 46.7 jit_solution(9684763417881609937)
XLA Ops:
  0.6 0.8 %pad_maximum_fusion.4 = bf16[128,256]{1,0:T(8,128)(2,1)S(1)} fusion(bf16[128,128]{1,0:T(8,128)(2,1)} %param.13, bf16[128,128]{1,0:T(8,128)(2,1)} %param.12), kind=kLoop, calls=%fused_computation.70 | loop fusion | flops 131072 | bytes 131072 | tf_op jit(solution)/shard_map/concatenate | solution.py:123
  1.4 2.1 %collective-permute-start = (bf16[128,256]{1,0:T(8,128)(2,1)S(1)}, bf16[128,256]{1,0:T(8,128)(2,1)S(1)}, u32[]{:S(2)}, u32[]{:S(2)}) collective-permute-start(bf16[128,256]{1,0:T(8,128)(2,1)S(1)} %pad_maximum_fusion.4), channel_id=1, source_target_pairs={{0,1},{1,0},{2,3},{3,2},{4,5},{5,4},{6,7},{7,6},{8,9},{9,8},{10,11... | collective-permute-start | bytes 196616 | tf_op jit(solution)/shard_map/ppermute | solution.py:16
  3.6 0.2 reduce_window_sum.18
  4.0 0.4 copy-done.19
  4.4 0.2 copy-done.9
  4.7 0.5 %copy-done.15 = f32[8]{0:T(128)} copy-done((f32[8]{0:T(128)}, f32[8]{0:T(128)S(1)}, u32[]{:S(2)}) %copy-start.15) | copy-done | bytes 56
  5.3 0.8 %copy-done.8 = bf16[128,512]{1,0:T(8,128)(2,1)S(1)} copy-done((bf16[128,512]{1,0:T(8,128)(2,1)S(1)}, bf16[128,512]{1,0:T(8,128)(2,1)}, u32[]{:S(2)}) %copy-start.8) | copy-done | bytes 131096
  6.2 0.7 %copy-done.2 = bf16[128,128]{1,0:T(8,128)(2,1)S(1)} copy-done((bf16[128,128]{1,0:T(8,128)(2,1)S(1)}, bf16[128,128]{1,0:T(8,128)(2,1)}, u32[]{:S(2)}) %copy-start.2) | copy-done | bytes 32792
  7.0 0.4 convolution_bitcast_fusion.2
  7.3 0.4 copy-done
  7.7 0.4 broadcast_select_fusion.2
  8.2 1.0 %collective-permute-start.1 = (f32[9,256,64]{1,2,0:T(8,128)S(1)}, f32[9,256,64]{1,2,0:T(8,128)S(1)}, u32[]{:S(2)}, u32[]{:S(2)}) collective-permute-start(f32[9,256,64]{1,2,0:T(8,128)S(1)} %pad_maximum_fusion), channel_id=1, source_target_pairs={{0,4},{4,0},{8,12},{12,8},{16,20},{20,16},{24,28},{28,24},{1,5},{5... | collective-permute-start | bytes 1769480 | tf_op jit(solution)/shard_map/ppermute | solution.py:72
  9.2 1.6 %collective-permute-done.1 = f32[9,256,64]{1,2,0:T(8,128)S(1)} collective-permute-done((f32[9,256,64]{1,2,0:T(8,128)S(1)}, f32[9,256,64]{1,2,0:T(8,128)S(1)}, u32[]{:S(2)}, u32[]{:S(2)}) %collective-permute-start.1) | collective-permute-done | bytes 589856 | tf_op jit(solution)/shard_map/ppermute | solution.py:72
  10.8 0.5 %copy-done.21 = f32[8]{0:T(128)} copy-done((f32[8]{0:T(128)}, f32[8]{0:T(128)S(1)}, u32[]{:S(2)}) %copy-start.21) | copy-done | bytes 56
  11.4 0.7 %copy-done.16 = f32[8]{0:T(128)S(1)} copy-done((f32[8]{0:T(128)S(1)}, f32[8]{0:T(128)}, u32[]{:S(2)}) %copy-start.16) | copy-done | bytes 56
  12.1 0.2 fusion.63
  12.3 0.7 %pad_maximum_fusion.1 = bf16[9,256,64]{1,2,0:T(8,128)(2,1)} fusion(bf16[1,256,64]{1,2,0:T(8,128)(2,1)S(1)} %broadcast_in_dim.13, bf16[8,256,64]{1,2,0:T(8,128)(2,1)S(1)} %get-tuple-element.115), kind=kLoop, calls=%fused_computation.41 | loop fusion | flops 147456 | bytes 589824 | tf_op jit(solution)/shard_map/concatenate | solution.py:50
  13.0 3.3 %collective-permute-start.2 = (bf16[9,256,64]{1,2,0:T(8,128)(2,1)}, bf16[9,256,64]{1,2,0:T(8,128)(2,1)S(1)}, u32[]{:S(2)}, u32[]{:S(2)}) collective-permute-start(bf16[9,256,64]{1,2,0:T(8,128)(2,1)} %pad_maximum_fusion.1), channel_id=1, source_target_pairs={{4,12},{12,20},{20,28},{8,0},{16,8},{24,16},{5,13},{13,21},{21,29}... | collective-permute-start | bytes 884744 | tf_op jit(solution)/shard_map/ppermute | solution.py:90
  16.5 3.9 %collective-permute-done.2 = bf16[9,256,64]{1,2,0:T(8,128)(2,1)S(1)} collective-permute-done((bf16[9,256,64]{1,2,0:T(8,128)(2,1)}, bf16[9,256,64]{1,2,0:T(8,128)(2,1)S(1)}, u32[]{:S(2)}, u32[]{:S(2)}) %collective-permute-start.2) | collective-permute-done | bytes 294944 | tf_op jit(solution)/shard_map/ppermute | solution.py:90
  20.3 0.8 %fusion.24 = bf16[8,256,64]{1,2,0:T(8,128)(2,1)} fusion(f32[8,256,64]{1,2,0:T(8,128)S(1)} %get-tuple-element.116, f32[8]{0:T(128)S(1)} %copy-done.22, bf16[9,256,64]{1,2,0:T(8,128)(2,1)S(1)} %collective-permute-done.2), kind=kLoop, calls=%fused_computation.35 | loop fusion | flops 524288 | bytes 1048608 | tf_op jit(solution)/shard_map/convert_element_type | solution.py:84
  21.2 5.1 %collective-permute-start.3 = (bf16[8,256,64]{1,2,0:T(8,128)(2,1)}, bf16[8,256,64]{1,2,0:T(8,128)(2,1)S(1)}, u32[]{:S(2)}, u32[]{:S(2)}) collective-permute-start(bf16[8,256,64]{1,2,0:T(8,128)(2,1)} %fusion.24), channel_id=1, source_target_pairs={{4,20},{12,28},{16,0},{24,8},{5,21},{13,29},{17,1},{25,9},{6,22},{... | collective-permute-start | bytes 786440 | tf_op jit(solution)/shard_map/ppermute | solution.py:84
  26.3 4.2 %conditional.1 = (f32[128,8,64]{0,2,1:T(8,128)S(1)}, f32[128,8]{0,1:T(8,128)S(1)}, f32[128,8]{0,1:T(8,128)}, f32[128,256]{1,0:T(8,128)S(1)}, f32[128,256]{1,0:T(8,128)S(1)}, /*index=5*/f32[128,512]{1,0:T(8,128)S(1)}) conditional(s32[]{:T(128)} %convert_element_type.68, () %tuple.19, (f32[128,8]{1,0:T(8,128)S(1)}, f32[128,256]{1,0:T(8,128)S(1)}, ...), branch_computations={%region_1.2_spmd, %region_2.4_spmd} | conditional | flops 356844544 | bytes 4550764 | solution.py:185
  26.3 0.3 fusion.68
  26.7 0.8 %fusion = f32[128,8,64]{0,2,1:T(8,128)S(1)} fusion(f32[128,8,64]{0,2,1:T(8,128)S(1)} %get-tuple-element.20, f32[8,128]{1,0:T(8,128)S(1)} %bitcast.101, f32[128,128]{1,0:T(8,128)S(1)} %fusion.68, f32[8,128]{1,0:T(8,128)S(1)} %bitcast.97, pred[128,128]{1,0:T(8,128)(4,1)S(1)} %iota_compare_fusion, f32[8]{0:T(128)S(1)} %get-tuple-element.72), kind=kOutput, calls=%fused_computation.1 | convolution fusion | flops 101318656 | bytes 614432 | tf_op jit(solution)/shard_map/cond/branch_1_fun/hts,thp->shp/dot_general | solution.py:162
  27.5 1.1 %fusion.5 = (f32[8,128]{1,0:T(8,128)S(1)}, f32[8,128,128]{2,1,0:T(8,128)S(1)}) fusion(f32[128,128]{1,0:T(8,128)S(1)} %fusion.68, f32[8,128]{1,0:T(8,128)S(1)} %bitcast.98, pred[128,128]{1,0:T(8,128)(4,1)S(1)} %iota_compare_fusion, f32[128,8,64]{0,2,1:T(8,128)S(1)} %get-tuple-element.20, f32[128,8,64]{0,2,1:T(8,128)S(1)} %get-tuple-element.22), kind=kOutput, calls=%fused_computation.7 | convolution fusion | flops 101317632 | bytes 1138688 | tf_op jit(solution)/shard_map/cond/branch_1_fun/thp,shp->hts/dot_general | solution.py:159
  28.6 1.1 %fusion.6 = f32[8,1,128]{2,1,0:T(1,128)S(1)} fusion(f32[8,128,1]{1,2,0:T(1,128)S(1)} %bitcast.102, f32[8,128,128]{2,1,0:T(8,128)S(1)} %get-tuple-element.120, f32[128,128]{1,0:T(8,128)S(1)} %fusion.68, f32[8,128]{1,0:T(8,128)S(1)} %bitcast.99, pred[128,128]{1,0:T(8,128)(4,1)S(1)} %iota_compare_fusion), kind=kOutput, calls=%fused_computation.8 | convolution fusion | flops 2097152 | bytes 618496 | tf_op jit(solution)/shard_map/cond/branch_1_fun/hts,hs->th/dot_general | solution.py:166
  29.6 0.2 multiply_reduce_fusion
  29.9 0.3 fusion.69
  30.1 0.3 fusion.70
  30.7 0.1 convert_add_fusion
  30.8 0.4 copy-done.6
  31.2 4.5 %collective-permute-start.4 = (f32[8,256,64]{1,2,0:T(8,128)S(1)}, f32[8,256,64]{1,2,0:T(8,128)S(1)}, u32[]{:S(2)}, u32[]{:S(2)}) collective-permute-start(f32[8,256,64]{1,2,0:T(8,128)S(1)} %convert_add_fusion), channel_id=1, source_target_pairs={{0,4},{4,0},{8,12},{12,8},{16,20},{20,16},{24,28},{28,24},{1,5},{5... | collective-permute-start | bytes 1572872 | tf_op jit(solution)/shard_map/ppermute | solution.py:99
  35.8 1.5 %collective-permute-done.4 = f32[8,256,64]{1,2,0:T(8,128)S(1)} collective-permute-done((f32[8,256,64]{1,2,0:T(8,128)S(1)}, f32[8,256,64]{1,2,0:T(8,128)S(1)}, u32[]{:S(2)}, u32[]{:S(2)}) %collective-permute-start.4) | collective-permute-done | bytes 524320 | tf_op jit(solution)/shard_map/ppermute | solution.py:99
  37.3 0.3 multiply_reduce_fusion.1
  37.6 0.4 multiply_reduce_fusion.2
  38.0 0.1 copy.56
  38.2 2.3 %collective-permute-start.5 = (f32[3,512]{1,0:T(4,128)S(1)}, f32[3,512]{1,0:T(4,128)S(1)}, u32[]{:S(2)}, u32[]{:S(2)}) collective-permute-start(f32[3,512]{1,0:T(4,128)S(1)} %slice.111), channel_id=1, source_target_pairs={{4,0},{8,4},{12,8},{16,12},{20,16},{24,20},{28,24},{5,1},{9,5},{13... | collective-permute-start | bytes 18440 | tf_op jit(solution)/shard_map/ppermute | solution.py:107
  40.5 0.6 %fusion.21 = f32[128,256]{1,0:T(8,128)S(1)} fusion(f32[128,256]{1,0:T(8,128)S(1)} %copy-done.7, f32[8,256,64]{1,2,0:T(8,128)S(1)} %get-tuple-element.114, f32[128,8,64]{0,2,1:T(8,128)S(1)} %bitcast.92, f32[128,8]{0,1:T(8,128)S(1)} %get-tuple-element.131), kind=kOutput, calls=%fused_computation.29 | convolution fusion | flops 201424896 | bytes 1052672 | tf_op jit(solution)/shard_map/lhp,hnp->ln/dot_general | solution.py:218
  41.2 0.6 %fusion.22 = f32[128,256]{1,0:T(8,128)S(1)} fusion(f32[128,256]{1,0:T(8,128)S(1)} %get-tuple-element.68, f32[8,256,64]{1,2,0:T(8,128)S(1)} %get-tuple-element.113, f32[128,8,64]{0,2,1:T(8,128)S(1)} %bitcast.89, f32[128,8]{0,1:T(8,128)S(1)} %get-tuple-element.132), kind=kOutput, calls=%fused_computation.30 | convolution fusion | flops 201424896 | bytes 1052672 | tf_op jit(solution)/shard_map/lhp,hnp->ln/dot_general | solution.py:215
  41.8 0.7 %collective-permute-start.6 = (bf16[128,256]{1,0:T(8,128)(2,1)S(1)}, bf16[128,256]{1,0:T(8,128)(2,1)S(1)}, u32[]{:S(2)}, u32[]{:S(2)}) collective-permute-start(bf16[128,256]{1,0:T(8,128)(2,1)S(1)} %pad_maximum_fusion.6), channel_id=1, source_target_pairs={{0,1},{1,0},{2,3},{3,2},{4,5},{5,4},{6,7},{7,6},{8,9},{9,8},{10,11... | collective-permute-start | bytes 196616 | tf_op jit(solution)/shard_map/ppermute | solution.py:16
  42.5 0.4 multiply_reduce_fusion.3
  42.9 0.3 copy-done.11
  43.2 0.3 copy-done.20
  43.5 0.7 %multiply_add_fusion.3 = (f32[128,8]{0,1:T(8,128)}, f32[128,8]{0,1:T(8,128)S(1)}) fusion(f32[128,8]{0,1:T(8,128)S(1)} %copy-done.11, f32[128,8]{0,1:T(8,128)S(1)} %get-tuple-element.135, f32[128,8]{0,1:T(8,128)S(1)} %copy.52, f32[8]{0:T(128)S(1)} %copy-done.20, f32[8]{0:T(128)S(1)} %get-tuple-element.112, f32[128]{0:T(128)S(1)} %compare_convert_fusion, ...), kind=kLoop, calls=%fused_computation.81 | loop fusion | flops 9216 | bytes 33344 | tf_op jit(solution)/shard_map/add | solution.py:204
  44.3 0.2 reduce_window_sum.19
  44.5 0.7 %copy.58 = f32[128,8]{0,1:T(8,128)} copy(f32[128,8]{1,0:T(8,128)S(1)} %rev.8) | data formatting | bytes 8192
  45.2 0.8 %fusion.30 = bf16[128,512]{1,0:T(8,128)(2,1)} fusion(f32[128,512]{1,0:T(8,128)S(1)} %mul.207, f32[3,512]{1,0:T(4,128)S(1)} %collective-permute-done.5, f32[512]{0:T(512)S(1)} %bitcast.106, f32[512]{0:T(512)S(1)} %bitcast.107, f32[512]{0:T(512)S(1)} %bitcast.105, f32[512]{0:T(512)S(1)} %bitcast.104), kind=kLoop, calls=%fused_computation.49 | loop fusion | flops 720896 | bytes 407552 | tf_op jit(solution)/shard_map/convert_element_type | solution.py:238
  46.0 0.7 %slice_add_fusion = (f32[128,128]{1,0:T(8,128)}, f32[128,128]{1,0:T(8,128)}) fusion(f32[128,256]{1,0:T(8,128)S(1)} %convert_element_type.70, f32[128,256]{1,0:T(8,128)S(1)} %fusion.22, pred[]{:T(512)S(6)} %eq.21, f32[128,256]{1,0:T(8,128)S(1)} %fusion.21), kind=kLoop, calls=%fused_computation.74 | loop fusion | flops 65536 | bytes 524289 | tf_op jit(solution)/shard_map/add | solution.py:229
  (78 shorter events, 1.4 us)
Async XLA Ops:
  0.6 2.9 %copy-start.18 = (f32[128,8]{0,1:T(8,128)S(1)}, f32[128,8]{0,1:T(8,128)}, u32[]{:S(2)}) copy-start(f32[128,8]{0,1:T(8,128)} %param.14) | copy-start | bytes 12292
  1.4 2.4 %copy-start.1 = (bf16[128,512]{1,0:T(8,128)(2,1)S(1)}, bf16[128,512]{1,0:T(8,128)(2,1)}, u32[]{:S(2)}) copy-start(bf16[128,512]{1,0:T(8,128)(2,1)} %param.10) | copy-start | bytes 393220
  1.4 4.8 %collective-permute-start = (bf16[128,256]{1,0:T(8,128)(2,1)S(1)}, bf16[128,256]{1,0:T(8,128)(2,1)S(1)}, u32[]{:S(2)}, u32[]{:S(2)}) collective-permute-start(bf16[128,256]{1,0:T(8,128)(2,1)S(1)} %pad_maximum_fusion.4), channel_id=1, source_target_pairs={{0,1},{1,0},{2,3},{3,2},{4,5},{5,4},{6,7},{7,6},{8,9},{9,8},{10,11... | collective-permute-start | bytes 196616 | tf_op jit(solution)/shard_map/ppermute | solution.py:16
  3.9 0.5 %copy-start.19 = (f32[8]{0:T(128)}, f32[8]{0:T(128)S(1)}, u32[]{:S(2)}) copy-start(f32[8]{0:T(128)S(1)} %slice_bitcast_fusion.1) | copy-start | bytes 100
  3.9 0.7 %copy-start.9 = (f32[128,8]{0,1:T(8,128)S(1)}, f32[128,8]{0,1:T(8,128)}, u32[]{:S(2)}) copy-start(f32[128,8]{0,1:T(8,128)} %param.15) | copy-start | bytes 12292
  4.7 0.5 %copy-start.15 = (f32[8]{0:T(128)}, f32[8]{0:T(128)S(1)}, u32[]{:S(2)}) copy-start(f32[8]{0:T(128)S(1)} %fusion.51) | copy-start | bytes 100
  5.2 0.9 %copy-start.8 = (bf16[128,512]{1,0:T(8,128)(2,1)S(1)}, bf16[128,512]{1,0:T(8,128)(2,1)}, u32[]{:S(2)}) copy-start(bf16[128,512]{1,0:T(8,128)(2,1)} %param.11) | copy-start | bytes 393220
  6.2 0.8 %copy-start.2 = (bf16[128,128]{1,0:T(8,128)(2,1)S(1)}, bf16[128,128]{1,0:T(8,128)(2,1)}, u32[]{:S(2)}) copy-start(bf16[128,128]{1,0:T(8,128)(2,1)} %param.12) | copy-start | bytes 98308
  6.2 1.1 %copy-start.3 = (bf16[128,128]{1,0:T(8,128)(2,1)}, bf16[128,128]{1,0:T(8,128)(2,1)S(1)}, u32[]{:S(2)}) copy-start(bf16[128,128]{1,0:T(8,128)(2,1)S(1)} %get-tuple-element.123) | copy-start | bytes 98308
  7.0 0.8 %copy-start = (bf16[128,128]{1,0:T(8,128)(2,1)S(1)}, bf16[128,128]{1,0:T(8,128)(2,1)}, u32[]{:S(2)}) copy-start(bf16[128,128]{1,0:T(8,128)(2,1)} %param.13) | copy-start | bytes 98308
  8.2 2.7 %collective-permute-start.1 = (f32[9,256,64]{1,2,0:T(8,128)S(1)}, f32[9,256,64]{1,2,0:T(8,128)S(1)}, u32[]{:S(2)}, u32[]{:S(2)}) collective-permute-start(f32[9,256,64]{1,2,0:T(8,128)S(1)} %pad_maximum_fusion), channel_id=1, source_target_pairs={{0,4},{4,0},{8,12},{12,8},{16,20},{20,16},{24,28},{28,24},{1,5},{5... | collective-permute-start | bytes 1769480 | tf_op jit(solution)/shard_map/ppermute | solution.py:72
  10.8 0.5 %copy-start.21 = (f32[8]{0:T(128)}, f32[8]{0:T(128)S(1)}, u32[]{:S(2)}) copy-start(f32[8]{0:T(128)S(1)} %get-tuple-element.118) | copy-start | bytes 100
  11.4 0.7 %copy-start.16 = (f32[8]{0:T(128)S(1)}, f32[8]{0:T(128)}, u32[]{:S(2)}) copy-start(f32[8]{0:T(128)} %copy-done.15) | copy-start | bytes 100
  13.0 3.4 %copy-start.4 = (bf16[128,128]{1,0:T(8,128)(2,1)S(1)}, bf16[128,128]{1,0:T(8,128)(2,1)}, u32[]{:S(2)}) copy-start(bf16[128,128]{1,0:T(8,128)(2,1)} %copy-done.3) | copy-start | bytes 98308
  13.0 7.3 %collective-permute-start.2 = (bf16[9,256,64]{1,2,0:T(8,128)(2,1)}, bf16[9,256,64]{1,2,0:T(8,128)(2,1)S(1)}, u32[]{:S(2)}, u32[]{:S(2)}) collective-permute-start(bf16[9,256,64]{1,2,0:T(8,128)(2,1)} %pad_maximum_fusion.1), channel_id=1, source_target_pairs={{4,12},{12,20},{20,28},{8,0},{16,8},{24,16},{5,13},{13,21},{21,29}... | collective-permute-start | bytes 884744 | tf_op jit(solution)/shard_map/ppermute | solution.py:90
  16.4 3.9 %copy-start.22 = (f32[8]{0:T(128)S(1)}, f32[8]{0:T(128)}, u32[]{:S(2)}) copy-start(f32[8]{0:T(128)} %copy-done.21) | copy-start | bytes 100
  21.2 5.2 %copy-start.23 = (f32[8]{0:T(128)S(1)}, f32[8]{0:T(128)}, u32[]{:S(2)}) copy-start(f32[8]{0:T(128)} %param.16) | copy-start | bytes 100
  21.2 9.5 %collective-permute-start.3 = (bf16[8,256,64]{1,2,0:T(8,128)(2,1)}, bf16[8,256,64]{1,2,0:T(8,128)(2,1)S(1)}, u32[]{:S(2)}, u32[]{:S(2)}) collective-permute-start(bf16[8,256,64]{1,2,0:T(8,128)(2,1)} %fusion.24), channel_id=1, source_target_pairs={{4,20},{12,28},{16,0},{24,8},{5,21},{13,29},{17,1},{25,9},{6,22},{... | collective-permute-start | bytes 786440 | tf_op jit(solution)/shard_map/ppermute | solution.py:84
  28.6 1.1 %copy-start.10 = (f32[8,128]{1,0:T(8,128)}, f32[8,128]{1,0:T(8,128)S(1)}, u32[]{:S(2)}) copy-start(f32[8,128]{1,0:T(8,128)S(1)} %get-tuple-element.119) | copy-start | bytes 12292 | tf_op jit(solution)/shard_map/cond
  30.6 0.7 %copy-start.6 = (f32[128,256]{1,0:T(8,128)}, f32[128,256]{1,0:T(8,128)S(1)}, u32[]{:S(2)}) copy-start(f32[128,256]{1,0:T(8,128)S(1)} %get-tuple-element.67) | copy-start | bytes 393220
  30.6 0.6 %copy-start.12 = (f32[128,8]{0,1:T(8,128)}, f32[128,8]{0,1:T(8,128)S(1)}, u32[]{:S(2)}) copy-start(f32[128,8]{0,1:T(8,128)S(1)} %get-tuple-element.69) | copy-start | bytes 12292
  31.2 4.5 %copy-start.14 = (f32[4,512]{1,0:T(4,128)S(1)}, f32[4,512]{1,0:T(4,128)}, u32[]{:S(2)}) copy-start(f32[4,512]{1,0:T(4,128)} %param.17) | copy-start | bytes 24580
  31.2 6.0 %collective-permute-start.4 = (f32[8,256,64]{1,2,0:T(8,128)S(1)}, f32[8,256,64]{1,2,0:T(8,128)S(1)}, u32[]{:S(2)}, u32[]{:S(2)}) collective-permute-start(f32[8,256,64]{1,2,0:T(8,128)S(1)} %convert_add_fusion), channel_id=1, source_target_pairs={{0,4},{4,0},{8,12},{12,8},{16,20},{20,16},{24,28},{28,24},{1,5},{5... | collective-permute-start | bytes 1572872 | tf_op jit(solution)/shard_map/ppermute | solution.py:99
  35.7 1.5 %copy-start.17 = (f32[8]{0:T(128)S(1)}, f32[8]{0:T(128)}, u32[]{:S(2)}) copy-start(f32[8]{0:T(128)} %copy-done.15) | copy-start | bytes 100
  35.8 1.8 %copy-start.5 = (bf16[128,128]{1,0:T(8,128)(2,1)S(1)}, bf16[128,128]{1,0:T(8,128)(2,1)}, u32[]{:S(2)}) copy-start(bf16[128,128]{1,0:T(8,128)(2,1)} %copy-done.3) | copy-start | bytes 98308
  38.2 2.4 %copy-start.7 = (f32[128,256]{1,0:T(8,128)S(1)}, f32[128,256]{1,0:T(8,128)}, u32[]{:S(2)}) copy-start(f32[128,256]{1,0:T(8,128)} %copy-done.6) | copy-start | bytes 393220
  38.2 7.0 %collective-permute-start.5 = (f32[3,512]{1,0:T(4,128)S(1)}, f32[3,512]{1,0:T(4,128)S(1)}, u32[]{:S(2)}, u32[]{:S(2)}) collective-permute-start(f32[3,512]{1,0:T(4,128)S(1)} %slice.111), channel_id=1, source_target_pairs={{4,0},{8,4},{12,8},{16,12},{20,16},{24,20},{28,24},{5,1},{9,5},{13... | collective-permute-start | bytes 18440 | tf_op jit(solution)/shard_map/ppermute | solution.py:107
  41.8 4.1 %collective-permute-start.6 = (bf16[128,256]{1,0:T(8,128)(2,1)S(1)}, bf16[128,256]{1,0:T(8,128)(2,1)S(1)}, u32[]{:S(2)}, u32[]{:S(2)}) collective-permute-start(bf16[128,256]{1,0:T(8,128)(2,1)S(1)} %pad_maximum_fusion.6), channel_id=1, source_target_pairs={{0,1},{1,0},{2,3},{3,2},{4,5},{5,4},{6,7},{7,6},{8,9},{9,8},{10,11... | collective-permute-start | bytes 196616 | tf_op jit(solution)/shard_map/ppermute | solution.py:16
  42.5 0.7 %copy-start.11 = (f32[128,8]{0,1:T(8,128)S(1)}, f32[128,8]{0,1:T(8,128)}, u32[]{:S(2)}) copy-start(f32[128,8]{0,1:T(8,128)} %get-tuple-element.70) | copy-start | bytes 12292
  42.5 0.7 %copy-start.13 = (f32[128,8]{0,1:T(8,128)S(1)}, f32[128,8]{0,1:T(8,128)}, u32[]{:S(2)}) copy-start(f32[128,8]{0,1:T(8,128)} %copy-done.12) | copy-start | bytes 12292
  42.9 0.6 %copy-start.20 = (f32[8]{0:T(128)S(1)}, f32[8]{0:T(128)}, u32[]{:S(2)}) copy-start(f32[8]{0:T(128)} %copy-done.19) | copy-start | bytes 100

commit v6 on v5

--- a/solution.py
+++ b/solution.py
@@ -4,6 +4,7 @@
 from jax.sharding import PartitionSpec as P
 
 precise = lax.Precision.HIGHEST
+split_bf16 = lax.Precision.HIGH
 
 
 def swapped(block, axis, bit):
@@ -144,8 +145,8 @@
     from_start = jnp.exp(cumulative)
     weighted = values3 * (to_end * step_size)[:, :, None]
     seeded = upstream3 * from_start[:, :, None]
-    local_state = jnp.einsum("ln,lhp->hnp", keys_full, weighted, precision=precise)
-    local_grad = jnp.einsum("ln,lhp->hnp", queries_full, seeded, precision=precise)
+    local_state = jnp.einsum("ln,lhp->hnp", keys_full, weighted, precision=split_bf16)
+    local_grad = jnp.einsum("ln,lhp->hnp", queries_full, seeded, precision=split_bf16)
     decay_total = jnp.exp(totals)
     def local_terms(keys_full, queries_full, values3, upstream3, cumulative, step_size, preact):
         scores = product(queries_full, keys_full.T)
@@ -198,8 +199,8 @@
         (keys_full, queries_full, values3, upstream3, cumulative, step_size, preact),
     )
     within_part, local_decay, col_sums, query_local, key_local, silu_slope = riders
-    from_state = jnp.einsum("ln,hnp->lhp", queries_full, entering, precision=precise)
-    into_state = jnp.einsum("ln,hnp->lhp", keys_full, arriving, precision=precise)
+    from_state = jnp.einsum("ln,hnp->lhp", queries_full, entering, precision=split_bf16)
+    into_state = jnp.einsum("ln,hnp->lhp", keys_full, arriving, precision=split_bf16)
     carried = jnp.sum(values3 * into_state, 2)
     step_grad = col_sums + to_end * carried
     value_grad = within_part + (to_end * step_size)[:, :, None] * into_state
@@ -212,23 +213,31 @@
     last_row = (lax.broadcasted_iota(jnp.int32, (length, 1), 0) == length - 1).astype(jnp.float32)
     decay_terms = decay_terms + last_row * jnp.sum(arriving * leaving, (1, 2))[None, :]
     decay_grad = jnp.flip(jnp.cumsum(jnp.flip(decay_terms, 0), 0), 0)
-    query_part = query_local + jnp.einsum(
-        "lhp,hnp->ln", seeded, entering, precision=precise
-    )
-    key_part = key_local + jnp.einsum("lhp,hnp->ln", weighted, arriving, precision=precise)
     half_width = state_count // 2
-    key_mine = jnp.where(own_first, key_part[:, :half_width], key_part[:, half_width:])
-    key_other = jnp.where(own_first, key_part[:, half_width:], key_part[:, :half_width])
-    query_mine = jnp.where(own_first, query_part[:, :half_width], query_part[:, half_width:])
-    query_other = jnp.where(own_first, query_part[:, half_width:], query_part[:, :half_width])
+    other_at = jnp.where(own_first, half_width, 0)
+    mine_at = half_width - other_at
+
+    def key_query_half(at):
+        pick = lambda part: lax.dynamic_slice_in_dim(part, at, half_width, 1)
+        return (
+            pick(key_local)
+            + jnp.einsum("lhp,hnp->ln", weighted, pick(arriving), precision=precise),
+            pick(query_local)
+            + jnp.einsum("lhp,hnp->ln", seeded, pick(entering), precision=precise),
+        )
+
+    key_other, query_other = key_query_half(other_at)
     sent_back = swapped(
         jnp.concatenate([key_other, query_other], 1).astype(jnp.bfloat16), "head", 0
     ).astype(key_other.dtype)
-    received = (sent_back[:, :half_width], sent_back[:, half_width:])
-    keys_grad = key_mine + received[0]
-    queries_grad = query_mine + received[1]
+    key_mine, query_mine = key_query_half(mine_at)
+    keys_grad = key_mine + sent_back[:, :half_width]
+    queries_grad = query_mine + sent_back[:, half_width:]
+    head_rows = within_part[:3] + (to_end * step_size)[:3, :, None] * jnp.einsum(
+        "ln,hnp->lhp", keys_full[:3], arriving, precision=split_bf16
+    )
+    following = shifted(head_rows.reshape(3, -1) * silu_slope[:3], "seq", -1)
     conv_grad = value_grad.reshape(length, -1) * silu_slope
-    following = shifted(conv_grad[:3], "seq", -1)
     extended = jnp.concatenate([conv_grad, following], 0)
     input_grad = jnp.zeros_like(conv_grad)
     for offset in range(4):

time: 47.3 us -> 55.1 us (1.16)
  matrix products: 6.5 us -> 12.1 us
  other arithmetic: 6.37 us -> 8.87 us
  local copies, waits for them, and re-layouts: 6.65 us -> 8.21 us
  waiting for transfers between devices: 6.98 us -> 5.53 us
  starting transfers between devices: 19.1 us -> 18.5 us
    dot_general x4 -> x7, matrix products: 1.97 us -> 7.04 us  [the longest x2 3.52 us: key_query_half(): jnp.einsum('lhp,hnp->ln', weighted, pick(arriving), precision=precise)]
    reduce_sum x1, other arithmetic: 0.33 us -> 1.9 us  [body(): jnp.sum(arriving * leaving, (1, 2))[None, :]]
    ppermute x1, waiting for transfers between devices: 1.49 us -> 0.01 us  [paired_scan(): handed = lax.ppermute(passing, axis, swap)]
    ppermute x1, starting transfers between devices: 4.51 us -> 3.12 us  [paired_scan(): handed = lax.ppermute(passing, axis, swap)]
    add x1, other arithmetic: 0.14 us -> 1.17 us  [paired_scan(): near[1] + near[0][:, None, None] * far_s.astype(jnp.float32)]
    optimization_barrier x0 -> x1, local copies, waits for them, and re-layouts: none -> 1.02 us  [paired_scan(): passing, riders = lax.optimization_barrier((near[1], riders))]
    unnamed x48 -> x60, local copies, waits for them, and re-layouts: 5.97 us -> 5.25 us
    ppermute x1, starting transfers between devices: 5.14 us -> 5.85 us  [paired_scan(): far_s = lax.ppermute(window[1].astype(jnp.bfloat16), axis, route)]
  transfers between devices with their start and end apart: 7 -> 7, of which waited for: 3 -> 2; matrix products, arithmetic and copies ran while one was open for 20% -> 24% of each run, Pallas kernels for 0% -> 0%
where the time goes in v6:
time: 55.1 us; the launch traced here: 54.4 us
  starting transfers between devices  18.5 us (34%)
  matrix products  12.1 us (22%)
  other arithmetic  8.87 us (16%)
  local copies, waits for them, and re-layouts  8.21 us (15%)
  waiting for transfers between devices  5.53 us (10%)
  between operations  1.11 us (2%)
    ppermute x1, starting transfers between devices, paired_scan(): far_s = lax.ppermute(window[1].astype(jnp.bfloat16), axis, route)  5.85 us
    unnamed x60, local copies, waits for them, and re-layouts  5.25 us
    ppermute x1, waiting for transfers between devices, paired_scan(): far = lax.ppermute(packed(*window, jnp.bfloat16), axis, route)  3.88 us
    dot_general x2, matrix products, key_query_half(): jnp.einsum('lhp,hnp->ln', weighted, pick(arriving), precision=precise)  3.52 us
    ppermute x2, starting transfers between devices, swapped(): return lax.ppermute(block, axis, route)  3.25 us
    ppermute x1, starting transfers between devices, paired_scan(): far = lax.ppermute(packed(*window, jnp.bfloat16), axis, route)  3.21 us
    ppermute x1, starting transfers between devices, paired_scan(): handed = lax.ppermute(passing, axis, swap)  3.12 us
    ppermute x1, starting transfers between devices, shifted(): return lax.ppermute(block, axis, route)  2.08 us
  transfers between devices with their start and end apart: 7, of which 2 were waited for; matrix products, arithmetic and copies ran while one was open for 24% of the time, Pallas kernels for 0%

profile of v6, /device:TPU:1, one launch (start us, length us, event | category | flops | bytes accessed | tf_op | source)
XLA Modules:
  0.0 54.4 jit_solution(3893617415859124420)
XLA Ops:
  0.6 0.8 %pad_maximum_fusion.4 = bf16[128,256]{1,0:T(8,128)(2,1)S(1)} fusion(bf16[128,128]{1,0:T(8,128)(2,1)} %param.13, bf16[128,128]{1,0:T(8,128)(2,1)} %param.12), kind=kLoop, calls=%fused_computation.88 | loop fusion | flops 131072 | bytes 131072 | tf_op jit(solution)/shard_map/concatenate | solution.py:124
  1.4 2.1 %collective-permute-start = (bf16[128,256]{1,0:T(8,128)(2,1)S(1)}, bf16[128,256]{1,0:T(8,128)(2,1)S(1)}, u32[]{:S(2)}, u32[]{:S(2)}) collective-permute-start(bf16[128,256]{1,0:T(8,128)(2,1)S(1)} %pad_maximum_fusion.4), channel_id=1, source_target_pairs={{0,1},{1,0},{2,3},{3,2},{4,5},{5,4},{6,7},{7,6},{8,9},{9,8},{10,11... | collective-permute-start | bytes 196616 | tf_op jit(solution)/shard_map/ppermute | solution.py:17
  3.6 0.2 reduce_window_sum.18
  4.0 0.5 copy-done.25
  4.9 0.7 %copy-done.10 = bf16[128,512]{1,0:T(8,128)(2,1)S(1)} copy-done((bf16[128,512]{1,0:T(8,128)(2,1)S(1)}, bf16[128,512]{1,0:T(8,128)(2,1)}, u32[]{:S(2)}) %copy-start.10) | copy-done | bytes 131096
  5.8 0.7 %copy-done.11 = bf16[128,128]{1,0:T(8,128)(2,1)S(1)} copy-done((bf16[128,128]{1,0:T(8,128)(2,1)S(1)}, bf16[128,128]{1,0:T(8,128)(2,1)}, u32[]{:S(2)}) %copy-start.11) | copy-done | bytes 32792
  6.5 0.3 convolution_bitcast_fusion.2
  6.8 0.4 copy-done.3
  7.3 0.3 broadcast_select_fusion.2
  7.6 1.0 %collective-permute-start.1 = (f32[9,256,64]{1,2,0:T(8,128)S(1)}, f32[9,256,64]{1,2,0:T(8,128)S(1)}, u32[]{:S(2)}, u32[]{:S(2)}) collective-permute-start(f32[9,256,64]{1,2,0:T(8,128)S(1)} %pad_maximum_fusion), channel_id=1, source_target_pairs={{0,4},{4,0},{8,12},{12,8},{16,20},{20,16},{24,28},{28,24},{1,5},{5... | collective-permute-start | bytes 1769480 | tf_op jit(solution)/shard_map/ppermute | solution.py:73
  8.6 1.6 %collective-permute-done.1 = f32[9,256,64]{1,2,0:T(8,128)S(1)} collective-permute-done((f32[9,256,64]{1,2,0:T(8,128)S(1)}, f32[9,256,64]{1,2,0:T(8,128)S(1)}, u32[]{:S(2)}, u32[]{:S(2)}) %collective-permute-start.1) | collective-permute-done | bytes 589856 | tf_op jit(solution)/shard_map/ppermute | solution.py:73
  10.4 0.2 fusion.80
  10.6 0.7 %pad_maximum_fusion.1 = bf16[9,256,64]{1,2,0:T(8,128)(2,1)} fusion(bf16[1,256,64]{1,2,0:T(8,128)(2,1)S(1)} %broadcast_in_dim.13, bf16[8,256,64]{1,2,0:T(8,128)(2,1)S(1)} %get-tuple-element.130), kind=kLoop, calls=%fused_computation.51 | loop fusion | flops 147456 | bytes 589824 | tf_op jit(solution)/shard_map/concatenate | solution.py:51
  11.3 3.2 %collective-permute-start.2 = (bf16[9,256,64]{1,2,0:T(8,128)(2,1)}, bf16[9,256,64]{1,2,0:T(8,128)(2,1)S(1)}, u32[]{:S(2)}, u32[]{:S(2)}) collective-permute-start(bf16[9,256,64]{1,2,0:T(8,128)(2,1)} %pad_maximum_fusion.1), channel_id=1, source_target_pairs={{4,12},{12,20},{20,28},{8,0},{16,8},{24,16},{5,13},{13,21},{21,29}... | collective-permute-start | bytes 884744 | tf_op jit(solution)/shard_map/ppermute | solution.py:91
  14.6 3.9 %collective-permute-done.2 = bf16[9,256,64]{1,2,0:T(8,128)(2,1)S(1)} collective-permute-done((bf16[9,256,64]{1,2,0:T(8,128)(2,1)}, bf16[9,256,64]{1,2,0:T(8,128)(2,1)S(1)}, u32[]{:S(2)}, u32[]{:S(2)}) %collective-permute-start.2) | collective-permute-done | bytes 294944 | tf_op jit(solution)/shard_map/ppermute | solution.py:91
  18.5 0.8 %fusion.31 = bf16[8,256,64]{1,2,0:T(8,128)(2,1)} fusion(f32[8,256,64]{1,2,0:T(8,128)S(1)} %get-tuple-element.131, f32[8]{0:T(128)S(1)} %get-tuple-element.133, bf16[9,256,64]{1,2,0:T(8,128)(2,1)S(1)} %collective-permute-done.2), kind=kLoop, calls=%fused_computation.45 | loop fusion | flops 524288 | bytes 1048608 | tf_op jit(solution)/shard_map/convert_element_type | solution.py:85
  19.3 5.9 %collective-permute-start.3 = (bf16[8,256,64]{1,2,0:T(8,128)(2,1)}, bf16[8,256,64]{1,2,0:T(8,128)(2,1)}, u32[]{:S(2)}, u32[]{:S(2)}) collective-permute-start(bf16[8,256,64]{1,2,0:T(8,128)(2,1)} %fusion.31), channel_id=1, source_target_pairs={{4,20},{12,28},{16,0},{24,8},{5,21},{13,29},{17,1},{25,9},{6,22},{... | collective-permute-start | bytes 786440 | tf_op jit(solution)/shard_map/ppermute | solution.py:85
  25.2 4.9 %conditional.1 = (f32[128,8,64]{0,2,1:T(8,128)S(1)}, f32[128,8]{0,1:T(8,128)S(1)}, f32[128,8]{0,1:T(8,128)}, f32[128,256]{1,0:T(8,128)S(1)}, f32[128,256]{1,0:T(8,128)}, /*index=5*/f32[128,512]{1,0:T(8,128)S(1)}) conditional(s32[]{:T(128)} %convert_element_type.68, () %tuple.19, (f32[128,8]{1,0:T(8,128)S(1)}, f32[128,256]{1,0:T(8,128)S(1)}, ...), branch_computations={%region_1.2_spmd, %region_2.4_spmd} | conditional | flops 356844544 | bytes 4550764 | solution.py:186
  25.2 0.3 fusion.85
  25.6 0.8 %fusion = f32[128,8,64]{0,2,1:T(8,128)S(1)} fusion(f32[128,8,64]{0,2,1:T(8,128)S(1)} %get-tuple-element.20, f32[8,128]{1,0:T(8,128)S(1)} %bitcast.124, f32[128,128]{1,0:T(8,128)S(1)} %fusion.85, f32[8,128]{1,0:T(8,128)S(1)} %bitcast.120, pred[128,128]{1,0:T(8,128)(4,1)S(1)} %iota_compare_fusion, f32[8]{0:T(128)S(1)} %get-tuple-element.72), kind=kOutput, calls=%fused_computation.1 | convolution fusion | flops 101318656 | bytes 614432 | tf_op jit(solution)/shard_map/cond/branch_1_fun/hts,thp->shp/dot_general | solution.py:163
  26.3 1.1 %fusion.5 = (f32[8,128]{1,0:T(8,128)S(1)}, f32[8,128,128]{2,1,0:T(8,128)S(1)}) fusion(f32[128,128]{1,0:T(8,128)S(1)} %fusion.85, f32[8,128]{1,0:T(8,128)S(1)} %bitcast.121, pred[128,128]{1,0:T(8,128)(4,1)S(1)} %iota_compare_fusion, f32[128,8,64]{0,2,1:T(8,128)S(1)} %get-tuple-element.20, f32[128,8,64]{0,2,1:T(8,128)S(1)} %get-tuple-element.22), kind=kOutput, calls=%fused_computation.7 | convolution fusion | flops 101317632 | bytes 1138688 | tf_op jit(solution)/shard_map/cond/branch_1_fun/thp,shp->hts/dot_general | solution.py:160
  27.4 1.1 %fusion.6 = f32[8,1,128]{2,1,0:T(1,128)S(1)} fusion(f32[8,128,1]{1,2,0:T(1,128)S(1)} %bitcast.125, f32[8,128,128]{2,1,0:T(8,128)S(1)} %get-tuple-element.135, f32[128,128]{1,0:T(8,128)S(1)} %fusion.85, f32[8,128]{1,0:T(8,128)S(1)} %bitcast.122, pred[128,128]{1,0:T(8,128)(4,1)S(1)} %iota_compare_fusion), kind=kOutput, calls=%fused_computation.8 | convolution fusion | flops 2097152 | bytes 618496 | tf_op jit(solution)/shard_map/cond/branch_1_fun/hts,hs->th/dot_general | solution.py:167
  28.5 0.2 multiply_reduce_fusion
  28.7 0.3 fusion.86
  29.0 1.0 %fusion.87 = f32[128,256]{1,0:T(8,128)} fusion(f32[128,128]{0,1:T(8,128)S(1)} %multiply_reduce_fusion, f32[128,256]{1,0:T(8,128)S(1)} %get-tuple-element.17), kind=kOutput, calls=%fused_computation.127 | convolution fusion | flops 50331648 | bytes 327680 | tf_op jit(solution)/shard_map/cond/branch_1_fun/dot_general | solution.py:175
  30.2 0.6 %copy-done.8 = f32[128,256]{1,0:T(8,128)} copy-done((f32[128,256]{1,0:T(8,128)}, f32[128,256]{1,0:T(8,128)S(1)}, u32[]{:S(2)}) %copy-start.8) | copy-done | bytes 131096
  30.7 1.2 %convert_add_fusion = f32[8,256,64]{1,2,0:T(8,128)S(1)} fusion(bf16[8,256,64]{1,2,0:T(8,128)(2,1)} %collective-permute-done.3, f32[8]{0:T(128)S(1)} %fusion.69, bf16[9,256,64]{1,2,0:T(8,128)(2,1)} %copy-done.2), kind=kLoop, calls=%fused_computation.41 | loop fusion | flops 524288 | bytes 1048608 | tf_op jit(solution)/shard_map/add | solution.py:89
  31.9 3.1 %collective-permute-start.4 = (f32[8,256,64]{1,2,0:T(8,128)S(1)}, f32[8,256,64]{1,2,0:T(8,128)}, u32[]{:S(2)}, u32[]{:S(2)}) collective-permute-start(f32[8,256,64]{1,2,0:T(8,128)S(1)} %convert_add_fusion), channel_id=1, source_target_pairs={{0,4},{4,0},{8,12},{12,8},{16,20},{20,16},{24,28},{28,24},{1,5},{5... | collective-permute-start | bytes 1572872 | tf_op jit(solution)/shard_map/ppermute | solution.py:100
  35.0 0.6 %compare_convert_fusion = f32[128]{0:T(128)} fusion(), kind=kLoop, calls=%fused_computation.105 | loop fusion | flops 256 | bytes 512 | tf_op jit(solution)/shard_map/convert_element_type | solution.py:213
  35.6 0.6 %fusion.84 = (f32[1,512]{1,0:T(1,128)}, f32[1,512]{1,0:T(1,128)}, f32[1,512]{1,0:T(1,128)}, f32[1,512]{1,0:T(1,128)}) fusion(f32[4,512]{1,0:T(4,128)S(1)} %copy-done.21), kind=kLoop, calls=%fused_computation.124 | loop fusion | bytes 16384 | tf_op jit(solution)/shard_map/slice | solution.py:245
  36.2 0.6 %slice_bitcast_fusion.2 = f32[8]{0:T(128)} fusion(f32[9,256,64]{1,2,0:T(8,128)S(1)} %collective-permute-done.1), kind=kLoop, calls=%fused_computation.113 | loop fusion | bytes 64 | tf_op jit(solution)/shard_map/slice | solution.py:57
  36.8 1.0 %copy.88 = f32[128,8,64]{2,0,1:T(8,128)} copy(f32[128,8,64]{0,2,1:T(8,128)S(1)} %get-tuple-element.64) | data formatting | bytes 524288 | tf_op jit(solution)/shard_map/optimization_barrier | solution.py:99
  37.8 1.9 %multiply_reduce_fusion.1 = (f32[8]{0:T(128)}, f32[8,256,64]{1,2,0:T(8,128)S(1)}, f32[8,256,64]{1,2,0:T(8,128)S(1)}) fusion(f32[8,256,64]{1,2,0:T(8,128)S(1)} %convolution_bitcast_fusion.2, f32[8]{0:T(128)S(1)} %copy-done.23, f32[8,256,64]{1,2,0:T(8,128)} %collective-permute-done.4, f32[8,256,64]{1,2,0:T(8,128)S(1)} %convert_add_fusion, ...), kind=kLoop, calls=%fused_computation.46 | loop fusion | flops 1048568 | bytes 3145825 | tf_op jit(solution)/shard_map/reduce_sum | solution.py:214
  39.7 0.3 multiply_reduce_fusion.2
  40.2 1.1 %fusion.29 = f32[3,8,64]{2,0,1:T(4,128)S(1)} fusion(f32[8,256,64]{1,2,0:T(8,128)S(1)} %get-tuple-element.127, f32[128,8,64]{2,0,1:T(8,128)} %copy.88, f32[3,8]{0,1:T(8,128)S(1)} %bitcast.119, bf16[128,256]{1,0:T(8,128)(2,1)S(1)} %get-tuple-element.129), kind=kOutput, calls=%fused_computation.40 | convolution fusion | flops 2362368 | bytes 542720 | tf_op jit(solution)/shard_map/ln,hnp->lhp/dot_general | solution.py:236
  41.5 2.1 %collective-permute-start.5 = (f32[3,512]{1,0:T(4,128)S(1)}, f32[3,512]{1,0:T(4,128)S(1)}, u32[]{:S(2)}, u32[]{:S(2)}) collective-permute-start(f32[3,512]{1,0:T(4,128)S(1)} %slice_multiply_fusion), channel_id=1, source_target_pairs={{4,0},{8,4},{12,8},{16,12},{20,16},{24,20},{28,24},{5,1},{9,5},{13... | collective-permute-start | bytes 18440 | tf_op jit(solution)/shard_map/ppermute | solution.py:108
  43.6 1.4 %fusion.28 = bf16[128,128]{1,0:T(8,128)(2,1)S(1)} fusion(f32[8,256,64]{1,2,0:T(8,128)S(1)} %get-tuple-element.127, s32[]{:T(128)S(6)} %select_n.70, f32[128,8,64]{0,2,1:T(8,128)S(1)} %bitcast.109, f32[128,8]{0,1:T(8,128)S(1)} %get-tuple-element.144, f32[128,256]{1,0:T(8,128)} %get-tuple-element.67), kind=kOutput, calls=%fused_computation.38 | convolution fusion | flops 100761600 | bytes 627712 | tf_op jit(solution)/shard_map/lhp,hnp->ln/dot_general | solution.py:224
  45.0 0.6 %fusion.27 = bf16[128,128]{1,0:T(8,128)(2,1)S(1)} fusion(f32[8,256,64]{1,2,0:T(8,128)S(1)} %get-tuple-element.126, s32[]{:T(128)S(6)} %select_n.70, f32[128,8,64]{0,2,1:T(8,128)S(1)} %bitcast.113, f32[128,8]{0,1:T(8,128)S(1)} %get-tuple-element.145, f32[128,256]{1,0:T(8,128)S(1)} %copy-done.9), kind=kOutput, calls=%fused_computation.37 | convolution fusion | flops 100761600 | bytes 627712 | tf_op jit(solution)/shard_map/lhp,hnp->ln/dot_general | solution.py:226
  45.7 1.1 %collective-permute-start.6 = (bf16[128,256]{1,0:T(8,128)(2,1)S(1)}, bf16[128,256]{1,0:T(8,128)(2,1)S(1)}, u32[]{:S(2)}, u32[]{:S(2)}) collective-permute-start(bf16[128,256]{1,0:T(8,128)(2,1)S(1)} %pad_maximum_fusion.6), channel_id=1, source_target_pairs={{0,1},{1,0},{2,3},{3,2},{4,5},{5,4},{6,7},{7,6},{8,9},{9,8},{10,11... | collective-permute-start | bytes 196616 | tf_op jit(solution)/shard_map/ppermute | solution.py:17
  46.9 0.3 multiply_reduce_fusion.3
  47.2 0.3 copy-done.14
  47.5 0.3 copy-done.26
  47.9 0.7 %multiply_add_fusion.3 = (f32[128,8]{0,1:T(8,128)}, f32[128,8]{0,1:T(8,128)S(1)}) fusion(f32[128,8]{0,1:T(8,128)S(1)} %copy-done.14, f32[128,8]{0,1:T(8,128)S(1)} %get-tuple-element.148, f32[128,8]{0,1:T(8,128)S(1)} %copy.83, f32[8]{0:T(128)S(1)} %copy-done.26, f32[8]{0:T(128)S(1)} %copy-done.27, f32[128]{0:T(128)S(1)} %copy-done.28, ...), kind=kLoop, calls=%fused_computation.96 | loop fusion | flops 9216 | bytes 33344 | tf_op jit(solution)/shard_map/add | solution.py:205
  48.9 0.7 %copy.93 = f32[128,8]{0,1:T(8,128)} copy(f32[128,8]{1,0:T(8,128)S(1)} %rev.8) | data formatting | bytes 8192
  49.6 0.6 %copy-done.18 = f32[1,512]{1,0:T(1,128)S(1)} copy-done((f32[1,512]{1,0:T(1,128)S(1)}, f32[1,512]{1,0:T(1,128)}, u32[]{:S(2)}) %copy-start.18) | copy-done | bytes 2072
  50.3 0.8 %fusion.37 = bf16[128,512]{1,0:T(8,128)(2,1)} fusion(f32[128,512]{1,0:T(8,128)S(1)} %mul.219, f32[3,512]{1,0:T(4,128)S(1)} %collective-permute-done.5, f32[512]{0:T(512)S(1)} %bitcast.129, f32[512]{0:T(512)S(1)} %bitcast.130, f32[512]{0:T(512)S(1)} %bitcast.128, f32[512]{0:T(512)S(1)} %bitcast.127), kind=kLoop, calls=%fused_computation.59 | loop fusion | flops 720896 | bytes 407552 | tf_op jit(solution)/shard_map/convert_element_type | solution.py:247
  51.1 2.1 %fusion.22 = f32[128,128]{1,0:T(8,128)} fusion(f32[8,256,64]{1,2,0:T(8,128)S(1)} %get-tuple-element.127, s32[]{:T(128)S(6)} %select_n.71, f32[128,8,64]{0,2,1:T(8,128)S(1)} %bitcast.110, f32[128,8]{0,1:T(8,128)S(1)} %get-tuple-element.144, f32[128,256]{1,0:T(8,128)S(1)} %convert_element_type.70, f32[128,256]{1,0:T(8,128)} %get-tuple-element.67), kind=kOutput, calls=%fused_computation.32 | convolution fusion | flops 100761600 | bytes 726016 | tf_op jit(solution)/shard_map/lhp,hnp->ln/dot_general | solution.py:224
  53.1 1.2 %fusion.26 = f32[128,128]{1,0:T(8,128)} fusion(f32[8,256,64]{1,2,0:T(8,128)S(1)} %get-tuple-element.126, s32[]{:T(128)S(6)} %select_n.71, f32[128,8,64]{0,2,1:T(8,128)S(1)} %bitcast.114, f32[128,8]{0,1:T(8,128)S(1)} %get-tuple-element.145, f32[128,256]{1,0:T(8,128)S(1)} %convert_element_type.70, f32[128,256]{1,0:T(8,128)S(1)} %copy-done.9), kind=kOutput, calls=%fused_computation.36 | convolution fusion | flops 100761600 | bytes 726016 | tf_op jit(solution)/shard_map/lhp,hnp->ln/dot_general | solution.py:226
  (94 shorter events, 2.0 us)
Async XLA Ops:
  0.6 2.9 %copy-start.24 = (f32[128,8]{0,1:T(8,128)S(1)}, f32[128,8]{0,1:T(8,128)}, u32[]{:S(2)}) copy-start(f32[128,8]{0,1:T(8,128)} %param.14) | copy-start | bytes 12292
  1.4 2.4 %copy-start.7 = (bf16[128,512]{1,0:T(8,128)(2,1)S(1)}, bf16[128,512]{1,0:T(8,128)(2,1)}, u32[]{:S(2)}) copy-start(bf16[128,512]{1,0:T(8,128)(2,1)} %param.10) | copy-start | bytes 393220
  1.4 4.3 %collective-permute-start = (bf16[128,256]{1,0:T(8,128)(2,1)S(1)}, bf16[128,256]{1,0:T(8,128)(2,1)S(1)}, u32[]{:S(2)}, u32[]{:S(2)}) collective-permute-start(bf16[128,256]{1,0:T(8,128)(2,1)S(1)} %pad_maximum_fusion.4), channel_id=1, source_target_pairs={{0,1},{1,0},{2,3},{3,2},{4,5},{5,4},{6,7},{7,6},{8,9},{9,8},{10,11... | collective-permute-start | bytes 196616 | tf_op jit(solution)/shard_map/ppermute | solution.py:17
  3.9 0.6 %copy-start.25 = (f32[8]{0:T(128)}, f32[8]{0:T(128)S(1)}, u32[]{:S(2)}) copy-start(f32[8]{0:T(128)S(1)} %slice_bitcast_fusion.3) | copy-start | bytes 100
  3.9 0.7 %copy-start.12 = (f32[128,8]{0,1:T(8,128)S(1)}, f32[128,8]{0,1:T(8,128)}, u32[]{:S(2)}) copy-start(f32[128,8]{0,1:T(8,128)} %param.15) | copy-start | bytes 12292
  4.7 5.7 %copy-start.22 = (f32[8]{0:T(128)}, f32[8]{0:T(128)S(1)}, u32[]{:S(2)}) copy-start(f32[8]{0:T(128)S(1)} %fusion.70) | copy-start | bytes 100
  4.7 0.9 %copy-start.10 = (bf16[128,512]{1,0:T(8,128)(2,1)S(1)}, bf16[128,512]{1,0:T(8,128)(2,1)}, u32[]{:S(2)}) copy-start(bf16[128,512]{1,0:T(8,128)(2,1)} %param.11) | copy-start | bytes 393220
  5.7 0.8 %copy-start.11 = (bf16[128,128]{1,0:T(8,128)(2,1)S(1)}, bf16[128,128]{1,0:T(8,128)(2,1)}, u32[]{:S(2)}) copy-start(bf16[128,128]{1,0:T(8,128)(2,1)} %param.12) | copy-start | bytes 98308
  5.7 8.8 %copy-start.5 = (bf16[128,128]{1,0:T(8,128)(2,1)}, bf16[128,128]{1,0:T(8,128)(2,1)S(1)}, u32[]{:S(2)}) copy-start(bf16[128,128]{1,0:T(8,128)(2,1)S(1)} %get-tuple-element.137) | copy-start | bytes 98308
  6.5 0.8 %copy-start.3 = (bf16[128,128]{1,0:T(8,128)(2,1)S(1)}, bf16[128,128]{1,0:T(8,128)(2,1)}, u32[]{:S(2)}) copy-start(bf16[128,128]{1,0:T(8,128)(2,1)} %param.13) | copy-start | bytes 98308
  7.6 2.7 %collective-permute-start.1 = (f32[9,256,64]{1,2,0:T(8,128)S(1)}, f32[9,256,64]{1,2,0:T(8,128)S(1)}, u32[]{:S(2)}, u32[]{:S(2)}) collective-permute-start(f32[9,256,64]{1,2,0:T(8,128)S(1)} %pad_maximum_fusion), channel_id=1, source_target_pairs={{0,4},{4,0},{8,12},{12,8},{16,20},{20,16},{24,28},{28,24},{1,5},{5... | collective-permute-start | bytes 1769480 | tf_op jit(solution)/shard_map/ppermute | solution.py:73
  11.3 7.2 %collective-permute-start.2 = (bf16[9,256,64]{1,2,0:T(8,128)(2,1)}, bf16[9,256,64]{1,2,0:T(8,128)(2,1)S(1)}, u32[]{:S(2)}, u32[]{:S(2)}) collective-permute-start(bf16[9,256,64]{1,2,0:T(8,128)(2,1)} %pad_maximum_fusion.1), channel_id=1, source_target_pairs={{4,12},{12,20},{20,28},{8,0},{16,8},{24,16},{5,13},{13,21},{21,29}... | collective-permute-start | bytes 884744 | tf_op jit(solution)/shard_map/ppermute | solution.py:91
  18.5 6.7 %copy-start.2 = (bf16[9,256,64]{1,2,0:T(8,128)(2,1)}, bf16[9,256,64]{1,2,0:T(8,128)(2,1)S(1)}, u32[]{:S(2)}) copy-start(bf16[9,256,64]{1,2,0:T(8,128)(2,1)S(1)} %collective-permute-done.2) | copy-start | bytes 884740
  19.3 5.9 %copy-start.29 = (f32[8]{0:T(128)S(1)}, f32[8]{0:T(128)}, u32[]{:S(2)}) copy-start(f32[8]{0:T(128)} %param.16) | copy-start | bytes 100
  19.3 11.4 %collective-permute-start.3 = (bf16[8,256,64]{1,2,0:T(8,128)(2,1)}, bf16[8,256,64]{1,2,0:T(8,128)(2,1)}, u32[]{:S(2)}, u32[]{:S(2)}) collective-permute-start(bf16[8,256,64]{1,2,0:T(8,128)(2,1)} %fusion.31), channel_id=1, source_target_pairs={{4,20},{12,28},{16,0},{24,8},{5,21},{13,29},{17,1},{25,9},{6,22},{... | collective-permute-start | bytes 786440 | tf_op jit(solution)/shard_map/ppermute | solution.py:85
  27.4 1.1 %copy-start.13 = (f32[8,128]{1,0:T(8,128)}, f32[8,128]{1,0:T(8,128)S(1)}, u32[]{:S(2)}) copy-start(f32[8,128]{1,0:T(8,128)S(1)} %get-tuple-element.134) | copy-start | bytes 12292 | tf_op jit(solution)/shard_map/cond
  30.1 0.7 %copy-start.8 = (f32[128,256]{1,0:T(8,128)}, f32[128,256]{1,0:T(8,128)S(1)}, u32[]{:S(2)}) copy-start(f32[128,256]{1,0:T(8,128)S(1)} %get-tuple-element.68) | copy-start | bytes 393220
  30.1 0.6 %copy-start.15 = (f32[128,8]{0,1:T(8,128)}, f32[128,8]{0,1:T(8,128)S(1)}, u32[]{:S(2)}) copy-start(f32[128,8]{0,1:T(8,128)S(1)} %get-tuple-element.69) | copy-start | bytes 12292
  30.1 1.8 %copy-start = (f32[128,512]{1,0:T(8,128)}, f32[128,512]{1,0:T(8,128)S(1)}, u32[]{:S(2)}) copy-start(f32[128,512]{1,0:T(8,128)S(1)} %get-tuple-element.66) | copy-start | bytes 786436
  31.9 3.7 %copy-start.21 = (f32[4,512]{1,0:T(4,128)S(1)}, f32[4,512]{1,0:T(4,128)}, u32[]{:S(2)}) copy-start(f32[4,512]{1,0:T(4,128)} %param.17) | copy-start | bytes 24580
  31.9 5.9 %collective-permute-start.4 = (f32[8,256,64]{1,2,0:T(8,128)S(1)}, f32[8,256,64]{1,2,0:T(8,128)}, u32[]{:S(2)}, u32[]{:S(2)}) collective-permute-start(f32[8,256,64]{1,2,0:T(8,128)S(1)} %convert_add_fusion), channel_id=1, source_target_pairs={{0,4},{4,0},{8,12},{12,8},{16,20},{20,16},{24,28},{28,24},{1,5},{5... | collective-permute-start | bytes 1572872 | tf_op jit(solution)/shard_map/ppermute | solution.py:100
  36.8 1.0 %copy-start.23 = (f32[8]{0:T(128)S(1)}, f32[8]{0:T(128)}, u32[]{:S(2)}) copy-start(f32[8]{0:T(128)} %copy-done.22) | copy-start | bytes 100
  40.2 1.2 %copy-start.1 = (f32[128,512]{1,0:T(8,128)S(1)}, f32[128,512]{1,0:T(8,128)}, u32[]{:S(2)}) copy-start(f32[128,512]{1,0:T(8,128)} %copy-done) | copy-start | bytes 786436
  41.5 3.5 %copy-start.9 = (f32[128,256]{1,0:T(8,128)S(1)}, f32[128,256]{1,0:T(8,128)}, u32[]{:S(2)}) copy-start(f32[128,256]{1,0:T(8,128)} %copy-done.8) | copy-start | bytes 393220
  41.5 8.1 %collective-permute-start.5 = (f32[3,512]{1,0:T(4,128)S(1)}, f32[3,512]{1,0:T(4,128)S(1)}, u32[]{:S(2)}, u32[]{:S(2)}) collective-permute-start(f32[3,512]{1,0:T(4,128)S(1)} %slice_multiply_fusion), channel_id=1, source_target_pairs={{4,0},{8,4},{12,8},{16,12},{20,16},{24,20},{28,24},{5,1},{9,5},{13... | collective-permute-start | bytes 18440 | tf_op jit(solution)/shard_map/ppermute | solution.py:108
  45.7 1.2 %copy-start.4 = (bf16[128,128]{1,0:T(8,128)(2,1)S(1)}, bf16[128,128]{1,0:T(8,128)(2,1)}, u32[]{:S(2)}) copy-start(bf16[128,128]{1,0:T(8,128)(2,1)} %param.13) | copy-start | bytes 98308
  45.7 1.2 %copy-start.6 = (bf16[128,128]{1,0:T(8,128)(2,1)S(1)}, bf16[128,128]{1,0:T(8,128)(2,1)}, u32[]{:S(2)}) copy-start(bf16[128,128]{1,0:T(8,128)(2,1)} %copy-done.5) | copy-start | bytes 98308
  45.7 5.4 %collective-permute-start.6 = (bf16[128,256]{1,0:T(8,128)(2,1)S(1)}, bf16[128,256]{1,0:T(8,128)(2,1)S(1)}, u32[]{:S(2)}, u32[]{:S(2)}) collective-permute-start(bf16[128,256]{1,0:T(8,128)(2,1)S(1)} %pad_maximum_fusion.6), channel_id=1, source_target_pairs={{0,1},{1,0},{2,3},{3,2},{4,5},{5,4},{6,7},{7,6},{8,9},{9,8},{10,11... | collective-permute-start | bytes 196616 | tf_op jit(solution)/shard_map/ppermute | solution.py:17
  46.8 0.7 %copy-start.14 = (f32[128,8]{0,1:T(8,128)S(1)}, f32[128,8]{0,1:T(8,128)}, u32[]{:S(2)}) copy-start(f32[128,8]{0,1:T(8,128)} %get-tuple-element.70) | copy-start | bytes 12292
  46.8 0.7 %copy-start.16 = (f32[128,8]{0,1:T(8,128)S(1)}, f32[128,8]{0,1:T(8,128)}, u32[]{:S(2)}) copy-start(f32[128,8]{0,1:T(8,128)} %copy-done.15) | copy-start | bytes 12292
  47.2 0.7 %copy-start.26 = (f32[8]{0:T(128)S(1)}, f32[8]{0:T(128)}, u32[]{:S(2)}) copy-start(f32[8]{0:T(128)} %copy-done.25) | copy-start | bytes 100
  47.2 0.7 %copy-start.27 = (f32[8]{0:T(128)S(1)}, f32[8]{0:T(128)}, u32[]{:S(2)}) copy-start(f32[8]{0:T(128)} %get-tuple-element.125) | copy-start | bytes 100
  47.2 0.7 %copy-start.28 = (f32[128]{0:T(128)S(1)}, f32[128]{0:T(128)}, u32[]{:S(2)}) copy-start(f32[128]{0:T(128)} %compare_convert_fusion) | copy-start | bytes 1540
  48.9 0.7 %copy-start.19 = (f32[1,512]{1,0:T(1,128)S(1)}, f32[1,512]{1,0:T(1,128)}, u32[]{:S(2)}) copy-start(f32[1,512]{1,0:T(1,128)} %get-tuple-element.142) | copy-start | bytes 6148
  48.9 0.7 %copy-start.20 = (f32[1,512]{1,0:T(1,128)S(1)}, f32[1,512]{1,0:T(1,128)}, u32[]{:S(2)}) copy-start(f32[1,512]{1,0:T(1,128)} %get-tuple-element.143) | copy-start | bytes 6148
  49.6 0.7 %copy-start.18 = (f32[1,512]{1,0:T(1,128)S(1)}, f32[1,512]{1,0:T(1,128)}, u32[]{:S(2)}) copy-start(f32[1,512]{1,0:T(1,128)} %get-tuple-element.141) | copy-start | bytes 6148
  49.6 0.7 %copy-start.17 = (f32[1,512]{1,0:T(1,128)S(1)}, f32[1,512]{1,0:T(1,128)}, u32[]{:S(2)}) copy-start(f32[1,512]{1,0:T(1,128)} %get-tuple-element.140) | copy-start | bytes 6148

commit v7 on v5

--- a/solution.py
+++ b/solution.py
@@ -4,6 +4,7 @@
 from jax.sharding import PartitionSpec as P
 
 precise = lax.Precision.HIGHEST
+split_bf16 = lax.Precision.HIGH
 
 
 def swapped(block, axis, bit):
@@ -120,8 +121,7 @@
     parity = lax.axis_index("head") % 2
     own_first = parity == 0
     half = write_keys.shape[1]
-    both = swapped(jnp.concatenate([write_keys, read_queries], 1), "head", 0)
-    partner = (both[:, :half], both[:, half:])
+    partner = swapped((write_keys, read_queries), "head", 0)
     keys_full = jnp.where(
         own_first,
         jnp.concatenate([write_keys, partner[0]], 1),
@@ -144,8 +144,8 @@
     from_start = jnp.exp(cumulative)
     weighted = values3 * (to_end * step_size)[:, :, None]
     seeded = upstream3 * from_start[:, :, None]
-    local_state = jnp.einsum("ln,lhp->hnp", keys_full, weighted, precision=precise)
-    local_grad = jnp.einsum("ln,lhp->hnp", queries_full, seeded, precision=precise)
+    local_state = jnp.einsum("ln,lhp->hnp", keys_full, weighted, precision=split_bf16)
+    local_grad = jnp.einsum("ln,lhp->hnp", queries_full, seeded, precision=split_bf16)
     decay_total = jnp.exp(totals)
     def local_terms(keys_full, queries_full, values3, upstream3, cumulative, step_size, preact):
         scores = product(queries_full, keys_full.T)

time: 47.3 us -> 48.1 us (1.017)
  starting transfers between devices: 19.1 us -> 20.2 us
  other arithmetic: 6.37 us -> 5.56 us
  local copies, waits for them, and re-layouts: 6.65 us -> 7.31 us
    ppermute x2 -> x3, starting transfers between devices: 2.76 us -> 3.91 us  [swapped(): return lax.ppermute(block, axis, route)]
    concatenate x1 -> x0, other arithmetic: 0.79 us -> none  [body(): both = swapped(jnp.concatenate([write_keys, read_queries], 1), 'head', 0)]
    unnamed x48 -> x46, local copies, waits for them, and re-layouts: 5.97 us -> 6.64 us
  transfers between devices with their start and end apart: 7 -> 8, of which waited for: 3 -> 3; matrix products, arithmetic and copies ran while one was open for 20% -> 21% of each run, Pallas kernels for 0% -> 0%
where the time goes in v7:
time: 48.1 us; the launch traced here: 47.5 us
  starting transfers between devices  20.2 us (42%)
  local copies, waits for them, and re-layouts  7.31 us (15%)
  waiting for transfers between devices  6.98 us (15%)
  matrix products  6.36 us (13%)
  other arithmetic  5.56 us (12%)
  between operations  1.05 us (2%)
    unnamed x46, local copies, waits for them, and re-layouts  6.64 us
    ppermute x1, starting transfers between devices, paired_scan(): far_s = lax.ppermute(window[1].astype(jnp.bfloat16), axis, route)  5.15 us
    ppermute x1, starting transfers between devices, paired_scan(): handed = lax.ppermute(passing, axis, swap)  4.06 us
    ppermute x3, starting transfers between devices, swapped(): return lax.ppermute(block, axis, route)  3.91 us
    ppermute x1, waiting for transfers between devices, paired_scan(): far = lax.ppermute(packed(*window, jnp.bfloat16), axis, route)  3.85 us
    ppermute x1, starting transfers between devices, paired_scan(): far = lax.ppermute(packed(*window, jnp.bfloat16), axis, route)  3.79 us
    ppermute x1, starting transfers between devices, shifted(): return lax.ppermute(block, axis, route)  2.28 us
    ppermute x1, waiting for transfers between devices, paired_scan(): mate = lax.ppermute(message, axis, swap)  1.63 us
  transfers between devices with their start and end apart: 8, of which 3 were waited for; matrix products, arithmetic and copies ran while one was open for 21% of the time, Pallas kernels for 0%

profile of v7, /device:TPU:1, one launch (start us, length us, event | category | flops | bytes accessed | tf_op | source)
XLA Modules:
  0.0 47.5 jit_solution(5646040512709719491)
XLA Ops:
  0.6 2.1 %collective-permute-start = (bf16[128,128]{1,0:T(8,128)(2,1)}, bf16[128,128]{1,0:T(8,128)(2,1)S(1)}, u32[]{:S(2)}, u32[]{:S(2)}) collective-permute-start(bf16[128,128]{1,0:T(8,128)(2,1)} %param.12), channel_id=1, source_target_pairs={{0,1},{1,0},{2,3},{3,2},{4,5},{5,4},{6,7},{7,6},{8,9},{9,8},{10,11... | collective-permute-start | bytes 98312 | tf_op jit(solution)/shard_map/ppermute | solution.py:17
  2.8 0.8 %copy.51 = f32[128,8]{1,0:T(8,128)S(1)} copy(f32[128,8]{0,1:T(8,128)} %param.14) | data formatting | bytes 8192 | tf_op args[4]
  3.6 0.2 reduce_window_sum.18
  4.0 0.4 copy-done.18
  4.4 0.2 copy-done.9
  4.7 0.5 %copy-done.15 = f32[8]{0:T(128)} copy-done((f32[8]{0:T(128)}, f32[8]{0:T(128)S(1)}, u32[]{:S(2)}) %copy-start.15) | copy-done | bytes 56
  5.3 0.8 %copy-done.8 = bf16[128,512]{1,0:T(8,128)(2,1)S(1)} copy-done((bf16[128,512]{1,0:T(8,128)(2,1)S(1)}, bf16[128,512]{1,0:T(8,128)(2,1)}, u32[]{:S(2)}) %copy-start.8) | copy-done | bytes 131096
  6.2 0.6 %copy-done.4 = bf16[128,128]{1,0:T(8,128)(2,1)S(1)} copy-done((bf16[128,128]{1,0:T(8,128)(2,1)S(1)}, bf16[128,128]{1,0:T(8,128)(2,1)}, u32[]{:S(2)}) %copy-start.4) | copy-done | bytes 32792
  6.8 0.3 convolution_bitcast_fusion.2
  7.2 0.4 copy-done.3
  7.6 0.3 broadcast_select_fusion.2
  7.9 1.0 %collective-permute-start.2 = (f32[9,256,64]{1,2,0:T(8,128)S(1)}, f32[9,256,64]{1,2,0:T(8,128)S(1)}, u32[]{:S(2)}, u32[]{:S(2)}) collective-permute-start(f32[9,256,64]{1,2,0:T(8,128)S(1)} %pad_maximum_fusion), channel_id=1, source_target_pairs={{0,4},{4,0},{8,12},{12,8},{16,20},{20,16},{24,28},{28,24},{1,5},{5... | collective-permute-start | bytes 1769480 | tf_op jit(solution)/shard_map/ppermute | solution.py:73
  9.0 1.6 %collective-permute-done.2 = f32[9,256,64]{1,2,0:T(8,128)S(1)} collective-permute-done((f32[9,256,64]{1,2,0:T(8,128)S(1)}, f32[9,256,64]{1,2,0:T(8,128)S(1)}, u32[]{:S(2)}, u32[]{:S(2)}) %collective-permute-start.2) | collective-permute-done | bytes 589856 | tf_op jit(solution)/shard_map/ppermute | solution.py:73
  10.6 0.5 %copy-done.20 = f32[8]{0:T(128)} copy-done((f32[8]{0:T(128)}, f32[8]{0:T(128)S(1)}, u32[]{:S(2)}) %copy-start.20) | copy-done | bytes 56
  11.2 0.7 %copy-done.16 = f32[8]{0:T(128)S(1)} copy-done((f32[8]{0:T(128)S(1)}, f32[8]{0:T(128)}, u32[]{:S(2)}) %copy-start.16) | copy-done | bytes 56
  11.9 0.2 fusion.55
  12.1 0.7 %pad_maximum_fusion.1 = bf16[9,256,64]{1,2,0:T(8,128)(2,1)} fusion(bf16[1,256,64]{1,2,0:T(8,128)(2,1)S(1)} %broadcast_in_dim.13, bf16[8,256,64]{1,2,0:T(8,128)(2,1)S(1)} %get-tuple-element.115), kind=kLoop, calls=%fused_computation.41 | loop fusion | flops 147456 | bytes 589824 | tf_op jit(solution)/shard_map/concatenate | solution.py:51
  12.8 3.8 %collective-permute-start.3 = (bf16[9,256,64]{1,2,0:T(8,128)(2,1)}, bf16[9,256,64]{1,2,0:T(8,128)(2,1)S(1)}, u32[]{:S(2)}, u32[]{:S(2)}) collective-permute-start(bf16[9,256,64]{1,2,0:T(8,128)(2,1)} %pad_maximum_fusion.1), channel_id=1, source_target_pairs={{4,12},{12,20},{20,28},{8,0},{16,8},{24,16},{5,13},{13,21},{21,29}... | collective-permute-start | bytes 884744 | tf_op jit(solution)/shard_map/ppermute | solution.py:91
  16.7 3.9 %collective-permute-done.3 = bf16[9,256,64]{1,2,0:T(8,128)(2,1)S(1)} collective-permute-done((bf16[9,256,64]{1,2,0:T(8,128)(2,1)}, bf16[9,256,64]{1,2,0:T(8,128)(2,1)S(1)}, u32[]{:S(2)}, u32[]{:S(2)}) %collective-permute-start.3) | collective-permute-done | bytes 294944 | tf_op jit(solution)/shard_map/ppermute | solution.py:91
  20.6 0.8 %fusion.24 = bf16[8,256,64]{1,2,0:T(8,128)(2,1)} fusion(f32[8,256,64]{1,2,0:T(8,128)S(1)} %get-tuple-element.116, f32[8]{0:T(128)S(1)} %copy-done.21, bf16[9,256,64]{1,2,0:T(8,128)(2,1)S(1)} %collective-permute-done.3), kind=kLoop, calls=%fused_computation.35 | loop fusion | flops 524288 | bytes 1048608 | tf_op jit(solution)/shard_map/convert_element_type | solution.py:85
  21.4 5.1 %collective-permute-start.4 = (bf16[8,256,64]{1,2,0:T(8,128)(2,1)}, bf16[8,256,64]{1,2,0:T(8,128)(2,1)S(1)}, u32[]{:S(2)}, u32[]{:S(2)}) collective-permute-start(bf16[8,256,64]{1,2,0:T(8,128)(2,1)} %fusion.24), channel_id=1, source_target_pairs={{4,20},{12,28},{16,0},{24,8},{5,21},{13,29},{17,1},{25,9},{6,22},{... | collective-permute-start | bytes 786440 | tf_op jit(solution)/shard_map/ppermute | solution.py:85
  26.6 4.2 %conditional.1 = (f32[128,8,64]{0,2,1:T(8,128)S(1)}, f32[128,8]{0,1:T(8,128)S(1)}, f32[128,8]{0,1:T(8,128)}, f32[128,256]{1,0:T(8,128)S(1)}, f32[128,256]{1,0:T(8,128)S(1)}, /*index=5*/f32[128,512]{1,0:T(8,128)S(1)}) conditional(s32[]{:T(128)} %convert_element_type.68, () %tuple.19, (f32[128,8]{1,0:T(8,128)S(1)}, f32[128,256]{1,0:T(8,128)S(1)}, ...), branch_computations={%region_1.2_spmd, %region_2.4_spmd} | conditional | flops 356844544 | bytes 4550764 | solution.py:185
  26.6 0.3 fusion.59
  26.9 0.8 %fusion = f32[128,8,64]{0,2,1:T(8,128)S(1)} fusion(f32[128,8,64]{0,2,1:T(8,128)S(1)} %get-tuple-element.20, f32[8,128]{1,0:T(8,128)S(1)} %bitcast.101, f32[128,128]{1,0:T(8,128)S(1)} %fusion.59, f32[8,128]{1,0:T(8,128)S(1)} %bitcast.97, pred[128,128]{1,0:T(8,128)(4,1)S(1)} %iota_compare_fusion, f32[8]{0:T(128)S(1)} %get-tuple-element.72), kind=kOutput, calls=%fused_computation.1 | convolution fusion | flops 101318656 | bytes 614432 | tf_op jit(solution)/shard_map/cond/branch_1_fun/hts,thp->shp/dot_general | solution.py:162
  27.7 1.1 %fusion.5 = (f32[8,128]{1,0:T(8,128)S(1)}, f32[8,128,128]{2,1,0:T(8,128)S(1)}) fusion(f32[128,128]{1,0:T(8,128)S(1)} %fusion.59, f32[8,128]{1,0:T(8,128)S(1)} %bitcast.98, pred[128,128]{1,0:T(8,128)(4,1)S(1)} %iota_compare_fusion, f32[128,8,64]{0,2,1:T(8,128)S(1)} %get-tuple-element.20, f32[128,8,64]{0,2,1:T(8,128)S(1)} %get-tuple-element.22), kind=kOutput, calls=%fused_computation.7 | convolution fusion | flops 101317632 | bytes 1138688 | tf_op jit(solution)/shard_map/cond/branch_1_fun/thp,shp->hts/dot_general | solution.py:159
  28.8 1.1 %fusion.6 = f32[8,1,128]{2,1,0:T(1,128)S(1)} fusion(f32[8,128,1]{1,2,0:T(1,128)S(1)} %bitcast.102, f32[8,128,128]{2,1,0:T(8,128)S(1)} %get-tuple-element.120, f32[128,128]{1,0:T(8,128)S(1)} %fusion.59, f32[8,128]{1,0:T(8,128)S(1)} %bitcast.99, pred[128,128]{1,0:T(8,128)(4,1)S(1)} %iota_compare_fusion), kind=kOutput, calls=%fused_computation.8 | convolution fusion | flops 2097152 | bytes 618496 | tf_op jit(solution)/shard_map/cond/branch_1_fun/hts,hs->th/dot_general | solution.py:166
  29.9 0.2 multiply_reduce_fusion
  30.1 0.3 fusion.60
  30.4 0.3 fusion.61
  30.9 0.1 convert_add_fusion
  31.0 0.4 copy-done.1
  31.5 4.1 %collective-permute-start.5 = (f32[8,256,64]{1,2,0:T(8,128)S(1)}, f32[8,256,64]{1,2,0:T(8,128)S(1)}, u32[]{:S(2)}, u32[]{:S(2)}) collective-permute-start(f32[8,256,64]{1,2,0:T(8,128)S(1)} %convert_add_fusion), channel_id=1, source_target_pairs={{0,4},{4,0},{8,12},{12,8},{16,20},{20,16},{24,28},{28,24},{1,5},{5... | collective-permute-start | bytes 1572872 | tf_op jit(solution)/shard_map/ppermute | solution.py:100
  35.6 1.5 %collective-permute-done.5 = f32[8,256,64]{1,2,0:T(8,128)S(1)} collective-permute-done((f32[8,256,64]{1,2,0:T(8,128)S(1)}, f32[8,256,64]{1,2,0:T(8,128)S(1)}, u32[]{:S(2)}, u32[]{:S(2)}) %collective-permute-start.5) | collective-permute-done | bytes 524320 | tf_op jit(solution)/shard_map/ppermute | solution.py:100
  37.1 0.3 multiply_reduce_fusion.1
  37.4 0.4 multiply_reduce_fusion.2
  37.8 0.1 copy.56
  38.0 2.3 %collective-permute-start.6 = (f32[3,512]{1,0:T(4,128)S(1)}, f32[3,512]{1,0:T(4,128)S(1)}, u32[]{:S(2)}, u32[]{:S(2)}) collective-permute-start(f32[3,512]{1,0:T(4,128)S(1)} %slice.101), channel_id=1, source_target_pairs={{4,0},{8,4},{12,8},{16,12},{20,16},{24,20},{28,24},{5,1},{9,5},{13... | collective-permute-start | bytes 18440 | tf_op jit(solution)/shard_map/ppermute | solution.py:108
  40.3 0.6 %fusion.21 = f32[128,256]{1,0:T(8,128)S(1)} fusion(f32[128,256]{1,0:T(8,128)S(1)} %copy-done.2, f32[8,256,64]{1,2,0:T(8,128)S(1)} %get-tuple-element.114, f32[128,8,64]{0,2,1:T(8,128)S(1)} %bitcast.92, f32[128,8]{0,1:T(8,128)S(1)} %get-tuple-element.129), kind=kOutput, calls=%fused_computation.29 | convolution fusion | flops 201424896 | bytes 1052672 | tf_op jit(solution)/shard_map/lhp,hnp->ln/dot_general | solution.py:218
  41.0 0.6 %fusion.22 = f32[128,256]{1,0:T(8,128)S(1)} fusion(f32[128,256]{1,0:T(8,128)S(1)} %get-tuple-element.68, f32[8,256,64]{1,2,0:T(8,128)S(1)} %get-tuple-element.113, f32[128,8,64]{0,2,1:T(8,128)S(1)} %bitcast.89, f32[128,8]{0,1:T(8,128)S(1)} %get-tuple-element.130), kind=kOutput, calls=%fused_computation.30 | convolution fusion | flops 201424896 | bytes 1052672 | tf_op jit(solution)/shard_map/lhp,hnp->ln/dot_general | solution.py:215
  41.6 1.7 %collective-permute-start.7 = (bf16[128,256]{1,0:T(8,128)(2,1)S(1)}, bf16[128,256]{1,0:T(8,128)(2,1)S(1)}, u32[]{:S(2)}, u32[]{:S(2)}) collective-permute-start(bf16[128,256]{1,0:T(8,128)(2,1)S(1)} %pad_maximum_fusion.3), channel_id=1, source_target_pairs={{0,1},{1,0},{2,3},{3,2},{4,5},{5,4},{6,7},{7,6},{8,9},{9,8},{10,11... | collective-permute-start | bytes 196616 | tf_op jit(solution)/shard_map/ppermute | solution.py:17
  43.3 0.4 multiply_reduce_fusion.3
  43.7 0.3 copy-done.11
  44.0 0.3 copy-done.19
  44.4 0.7 %multiply_add_fusion.3 = (f32[128,8]{0,1:T(8,128)}, f32[128,8]{0,1:T(8,128)S(1)}) fusion(f32[128,8]{0,1:T(8,128)S(1)} %copy-done.11, f32[128,8]{0,1:T(8,128)S(1)} %get-tuple-element.133, f32[128,8]{0,1:T(8,128)S(1)} %copy.52, f32[8]{0:T(128)S(1)} %copy-done.19, f32[8]{0:T(128)S(1)} %get-tuple-element.112, f32[128]{0:T(128)S(1)} %compare_convert_fusion, ...), kind=kLoop, calls=%fused_computation.78 | loop fusion | flops 9216 | bytes 33344 | tf_op jit(solution)/shard_map/add | solution.py:204
  45.2 0.2 reduce_window_sum.19
  45.4 0.7 %copy.58 = f32[128,8]{0,1:T(8,128)} copy(f32[128,8]{1,0:T(8,128)S(1)} %rev.8) | data formatting | bytes 8192
  46.1 0.8 %fusion.30 = bf16[128,512]{1,0:T(8,128)(2,1)} fusion(f32[128,512]{1,0:T(8,128)S(1)} %mul.207, f32[3,512]{1,0:T(4,128)S(1)} %collective-permute-done.6, f32[512]{0:T(512)S(1)} %bitcast.106, f32[512]{0:T(512)S(1)} %bitcast.107, f32[512]{0:T(512)S(1)} %bitcast.105, f32[512]{0:T(512)S(1)} %bitcast.104), kind=kLoop, calls=%fused_computation.49 | loop fusion | flops 720896 | bytes 407552 | tf_op jit(solution)/shard_map/convert_element_type | solution.py:238
  46.9 0.7 %slice_add_fusion = (f32[128,128]{1,0:T(8,128)}, f32[128,128]{1,0:T(8,128)}) fusion(f32[128,256]{1,0:T(8,128)S(1)} %convert_element_type.70, f32[128,256]{1,0:T(8,128)S(1)} %fusion.22, pred[]{:T(512)S(6)} %eq.21, f32[128,256]{1,0:T(8,128)S(1)} %fusion.21), kind=kLoop, calls=%fused_computation.69 | loop fusion | flops 65536 | bytes 524289 | tf_op jit(solution)/shard_map/add | solution.py:229
  (76 shorter events, 1.4 us)
Async XLA Ops:
  0.6 3.2 %copy-start = (bf16[128,512]{1,0:T(8,128)(2,1)S(1)}, bf16[128,512]{1,0:T(8,128)(2,1)}, u32[]{:S(2)}) copy-start(bf16[128,512]{1,0:T(8,128)(2,1)} %param.10) | copy-start | bytes 393220
  0.6 5.5 %collective-permute-start = (bf16[128,128]{1,0:T(8,128)(2,1)}, bf16[128,128]{1,0:T(8,128)(2,1)S(1)}, u32[]{:S(2)}, u32[]{:S(2)}) collective-permute-start(bf16[128,128]{1,0:T(8,128)(2,1)} %param.12), channel_id=1, source_target_pairs={{0,1},{1,0},{2,3},{3,2},{4,5},{5,4},{6,7},{7,6},{8,9},{9,8},{10,11... | collective-permute-start | bytes 98312 | tf_op jit(solution)/shard_map/ppermute | solution.py:17
  2.7 4.4 %collective-permute-start.1 = (bf16[128,128]{1,0:T(8,128)(2,1)}, bf16[128,128]{1,0:T(8,128)(2,1)S(1)}, u32[]{:S(2)}, u32[]{:S(2)}) collective-permute-start(bf16[128,128]{1,0:T(8,128)(2,1)} %param.13), channel_id=1, source_target_pairs={{0,1},{1,0},{2,3},{3,2},{4,5},{5,4},{6,7},{7,6},{8,9},{9,8},{10,11... | collective-permute-start | bytes 98312 | tf_op jit(solution)/shard_map/ppermute | solution.py:17
  3.8 0.6 %copy-start.18 = (f32[8]{0:T(128)}, f32[8]{0:T(128)S(1)}, u32[]{:S(2)}) copy-start(f32[8]{0:T(128)S(1)} %slice_bitcast_fusion.1) | copy-start | bytes 100
  3.9 0.7 %copy-start.9 = (f32[128,8]{0,1:T(8,128)S(1)}, f32[128,8]{0,1:T(8,128)}, u32[]{:S(2)}) copy-start(f32[128,8]{0,1:T(8,128)} %param.15) | copy-start | bytes 12292
  4.6 0.5 %copy-start.15 = (f32[8]{0:T(128)}, f32[8]{0:T(128)S(1)}, u32[]{:S(2)}) copy-start(f32[8]{0:T(128)S(1)} %fusion.49) | copy-start | bytes 100
  5.2 0.9 %copy-start.8 = (bf16[128,512]{1,0:T(8,128)(2,1)S(1)}, bf16[128,512]{1,0:T(8,128)(2,1)}, u32[]{:S(2)}) copy-start(bf16[128,512]{1,0:T(8,128)(2,1)} %param.11) | copy-start | bytes 393220
  6.1 0.8 %copy-start.4 = (bf16[128,128]{1,0:T(8,128)(2,1)S(1)}, bf16[128,128]{1,0:T(8,128)(2,1)}, u32[]{:S(2)}) copy-start(bf16[128,128]{1,0:T(8,128)(2,1)} %param.12) | copy-start | bytes 98308
  6.2 1.0 %copy-start.5 = (bf16[128,128]{1,0:T(8,128)(2,1)}, bf16[128,128]{1,0:T(8,128)(2,1)S(1)}, u32[]{:S(2)}) copy-start(bf16[128,128]{1,0:T(8,128)(2,1)S(1)} %collective-permute-done) | copy-start | bytes 98308
  6.8 0.8 %copy-start.3 = (bf16[128,128]{1,0:T(8,128)(2,1)S(1)}, bf16[128,128]{1,0:T(8,128)(2,1)}, u32[]{:S(2)}) copy-start(bf16[128,128]{1,0:T(8,128)(2,1)} %param.13) | copy-start | bytes 98308
  7.9 2.7 %collective-permute-start.2 = (f32[9,256,64]{1,2,0:T(8,128)S(1)}, f32[9,256,64]{1,2,0:T(8,128)S(1)}, u32[]{:S(2)}, u32[]{:S(2)}) collective-permute-start(f32[9,256,64]{1,2,0:T(8,128)S(1)} %pad_maximum_fusion), channel_id=1, source_target_pairs={{0,4},{4,0},{8,12},{12,8},{16,20},{20,16},{24,28},{28,24},{1,5},{5... | collective-permute-start | bytes 1769480 | tf_op jit(solution)/shard_map/ppermute | solution.py:73
  10.6 0.5 %copy-start.20 = (f32[8]{0:T(128)}, f32[8]{0:T(128)S(1)}, u32[]{:S(2)}) copy-start(f32[8]{0:T(128)S(1)} %get-tuple-element.118) | copy-start | bytes 100
  11.2 0.7 %copy-start.16 = (f32[8]{0:T(128)S(1)}, f32[8]{0:T(128)}, u32[]{:S(2)}) copy-start(f32[8]{0:T(128)} %copy-done.15) | copy-start | bytes 100
  12.8 3.8 %copy-start.6 = (bf16[128,128]{1,0:T(8,128)(2,1)S(1)}, bf16[128,128]{1,0:T(8,128)(2,1)}, u32[]{:S(2)}) copy-start(bf16[128,128]{1,0:T(8,128)(2,1)} %copy-done.5) | copy-start | bytes 98308
  12.8 7.7 %collective-permute-start.3 = (bf16[9,256,64]{1,2,0:T(8,128)(2,1)}, bf16[9,256,64]{1,2,0:T(8,128)(2,1)S(1)}, u32[]{:S(2)}, u32[]{:S(2)}) collective-permute-start(bf16[9,256,64]{1,2,0:T(8,128)(2,1)} %pad_maximum_fusion.1), channel_id=1, source_target_pairs={{4,12},{12,20},{20,28},{8,0},{16,8},{24,16},{5,13},{13,21},{21,29}... | collective-permute-start | bytes 884744 | tf_op jit(solution)/shard_map/ppermute | solution.py:91
  16.7 3.9 %copy-start.21 = (f32[8]{0:T(128)S(1)}, f32[8]{0:T(128)}, u32[]{:S(2)}) copy-start(f32[8]{0:T(128)} %copy-done.20) | copy-start | bytes 100
  21.4 5.2 %copy-start.22 = (f32[8]{0:T(128)S(1)}, f32[8]{0:T(128)}, u32[]{:S(2)}) copy-start(f32[8]{0:T(128)} %param.16) | copy-start | bytes 100
  21.4 9.5 %collective-permute-start.4 = (bf16[8,256,64]{1,2,0:T(8,128)(2,1)}, bf16[8,256,64]{1,2,0:T(8,128)(2,1)S(1)}, u32[]{:S(2)}, u32[]{:S(2)}) collective-permute-start(bf16[8,256,64]{1,2,0:T(8,128)(2,1)} %fusion.24), channel_id=1, source_target_pairs={{4,20},{12,28},{16,0},{24,8},{5,21},{13,29},{17,1},{25,9},{6,22},{... | collective-permute-start | bytes 786440 | tf_op jit(solution)/shard_map/ppermute | solution.py:85
  28.8 1.1 %copy-start.10 = (f32[8,128]{1,0:T(8,128)}, f32[8,128]{1,0:T(8,128)S(1)}, u32[]{:S(2)}) copy-start(f32[8,128]{1,0:T(8,128)S(1)} %get-tuple-element.119) | copy-start | bytes 12292 | tf_op jit(solution)/shard_map/cond
  30.8 0.7 %copy-start.1 = (f32[128,256]{1,0:T(8,128)}, f32[128,256]{1,0:T(8,128)S(1)}, u32[]{:S(2)}) copy-start(f32[128,256]{1,0:T(8,128)S(1)} %get-tuple-element.67) | copy-start | bytes 393220
  30.8 0.6 %copy-start.12 = (f32[128,8]{0,1:T(8,128)}, f32[128,8]{0,1:T(8,128)S(1)}, u32[]{:S(2)}) copy-start(f32[128,8]{0,1:T(8,128)S(1)} %get-tuple-element.69) | copy-start | bytes 12292
  31.5 4.1 %copy-start.14 = (f32[4,512]{1,0:T(4,128)S(1)}, f32[4,512]{1,0:T(4,128)}, u32[]{:S(2)}) copy-start(f32[4,512]{1,0:T(4,128)} %param.17) | copy-start | bytes 24580
  31.5 5.6 %collective-permute-start.5 = (f32[8,256,64]{1,2,0:T(8,128)S(1)}, f32[8,256,64]{1,2,0:T(8,128)S(1)}, u32[]{:S(2)}, u32[]{:S(2)}) collective-permute-start(f32[8,256,64]{1,2,0:T(8,128)S(1)} %convert_add_fusion), channel_id=1, source_target_pairs={{0,4},{4,0},{8,12},{12,8},{16,20},{20,16},{24,28},{28,24},{1,5},{5... | collective-permute-start | bytes 1572872 | tf_op jit(solution)/shard_map/ppermute | solution.py:100
  35.5 1.5 %copy-start.17 = (f32[8]{0:T(128)S(1)}, f32[8]{0:T(128)}, u32[]{:S(2)}) copy-start(f32[8]{0:T(128)} %copy-done.15) | copy-start | bytes 100
  35.6 1.8 %copy-start.7 = (bf16[128,128]{1,0:T(8,128)(2,1)S(1)}, bf16[128,128]{1,0:T(8,128)(2,1)}, u32[]{:S(2)}) copy-start(bf16[128,128]{1,0:T(8,128)(2,1)} %copy-done.5) | copy-start | bytes 98308
  38.0 2.4 %copy-start.2 = (f32[128,256]{1,0:T(8,128)S(1)}, f32[128,256]{1,0:T(8,128)}, u32[]{:S(2)}) copy-start(f32[128,256]{1,0:T(8,128)} %copy-done.1) | copy-start | bytes 393220
  38.0 8.0 %collective-permute-start.6 = (f32[3,512]{1,0:T(4,128)S(1)}, f32[3,512]{1,0:T(4,128)S(1)}, u32[]{:S(2)}, u32[]{:S(2)}) collective-permute-start(f32[3,512]{1,0:T(4,128)S(1)} %slice.101), channel_id=1, source_target_pairs={{4,0},{8,4},{12,8},{16,12},{20,16},{24,20},{28,24},{5,1},{9,5},{13... | collective-permute-start | bytes 18440 | tf_op jit(solution)/shard_map/ppermute | solution.py:108
  41.6 5.2 %collective-permute-start.7 = (bf16[128,256]{1,0:T(8,128)(2,1)S(1)}, bf16[128,256]{1,0:T(8,128)(2,1)S(1)}, u32[]{:S(2)}, u32[]{:S(2)}) collective-permute-start(bf16[128,256]{1,0:T(8,128)(2,1)S(1)} %pad_maximum_fusion.3), channel_id=1, source_target_pairs={{0,1},{1,0},{2,3},{3,2},{4,5},{5,4},{6,7},{7,6},{8,9},{9,8},{10,11... | collective-permute-start | bytes 196616 | tf_op jit(solution)/shard_map/ppermute | solution.py:17
  43.3 0.7 %copy-start.11 = (f32[128,8]{0,1:T(8,128)S(1)}, f32[128,8]{0,1:T(8,128)}, u32[]{:S(2)}) copy-start(f32[128,8]{0,1:T(8,128)} %get-tuple-element.70) | copy-start | bytes 12292
  43.3 0.7 %copy-start.13 = (f32[128,8]{0,1:T(8,128)S(1)}, f32[128,8]{0,1:T(8,128)}, u32[]{:S(2)}) copy-start(f32[128,8]{0,1:T(8,128)} %copy-done.12) | copy-start | bytes 12292
  43.7 0.6 %copy-start.19 = (f32[8]{0:T(128)S(1)}, f32[8]{0:T(128)}, u32[]{:S(2)}) copy-start(f32[8]{0:T(128)} %copy-done.18) | copy-start | bytes 100

commit v8 on v6

--- a/solution.py
+++ b/solution.py
@@ -4,7 +4,6 @@
 from jax.sharding import PartitionSpec as P
 
 precise = lax.Precision.HIGHEST
-split_bf16 = lax.Precision.HIGH
 
 
 def swapped(block, axis, bit):
@@ -145,8 +144,8 @@
     from_start = jnp.exp(cumulative)
     weighted = values3 * (to_end * step_size)[:, :, None]
     seeded = upstream3 * from_start[:, :, None]
-    local_state = jnp.einsum("ln,lhp->hnp", keys_full, weighted, precision=split_bf16)
-    local_grad = jnp.einsum("ln,lhp->hnp", queries_full, seeded, precision=split_bf16)
+    local_state = jnp.einsum("ln,lhp->hnp", keys_full, weighted, precision=precise)
+    local_grad = jnp.einsum("ln,lhp->hnp", queries_full, seeded, precision=precise)
     decay_total = jnp.exp(totals)
     def local_terms(keys_full, queries_full, values3, upstream3, cumulative, step_size, preact):
         scores = product(queries_full, keys_full.T)
@@ -199,25 +198,11 @@
         (keys_full, queries_full, values3, upstream3, cumulative, step_size, preact),
     )
     within_part, local_decay, col_sums, query_local, key_local, silu_slope = riders
-    from_state = jnp.einsum("ln,hnp->lhp", queries_full, entering, precision=split_bf16)
-    into_state = jnp.einsum("ln,hnp->lhp", keys_full, arriving, precision=split_bf16)
-    carried = jnp.sum(values3 * into_state, 2)
-    step_grad = col_sums + to_end * carried
-    value_grad = within_part + (to_end * step_size)[:, :, None] * into_state
-    leaving = decay_total[:, None, None] * entering + local_state
-    decay_terms = (
-        local_decay
-        + from_start * jnp.sum(upstream3 * from_state, 2)
-        - to_end * step_size * carried
-    )
-    last_row = (lax.broadcasted_iota(jnp.int32, (length, 1), 0) == length - 1).astype(jnp.float32)
-    decay_terms = decay_terms + last_row * jnp.sum(arriving * leaving, (1, 2))[None, :]
-    decay_grad = jnp.flip(jnp.cumsum(jnp.flip(decay_terms, 0), 0), 0)
     half_width = state_count // 2
     other_at = jnp.where(own_first, half_width, 0)
     mine_at = half_width - other_at
 
-    def key_query_half(at):
+    def key_query_half(at, arriving, entering):
         pick = lambda part: lax.dynamic_slice_in_dim(part, at, half_width, 1)
         return (
             pick(key_local)
@@ -226,18 +211,51 @@
             + jnp.einsum("lhp,hnp->ln", seeded, pick(entering), precision=precise),
         )
 
-    key_other, query_other = key_query_half(other_at)
-    sent_back = swapped(
-        jnp.concatenate([key_other, query_other], 1).astype(jnp.bfloat16), "head", 0
-    ).astype(key_other.dtype)
-    key_mine, query_mine = key_query_half(mine_at)
+    key_other, query_other = key_query_half(other_at, arriving, entering)
+    outgoing = jnp.concatenate([key_other, query_other], 1).astype(jnp.bfloat16)
+    head_rows = within_part[:3] + (to_end * step_size)[:3, :, None] * jnp.einsum(
+        "ln,hnp->lhp", keys_full[:3], arriving, precision=precise
+    )
+    head_rows = head_rows.reshape(3, -1) * silu_slope[:3]
+    outgoing, head_rows, entering, arriving = lax.optimization_barrier(
+        (outgoing, head_rows, entering, arriving)
+    )
+    sent_back = swapped(outgoing, "head", 0).astype(jnp.float32)
+    following = shifted(head_rows, "seq", -1)
+
+    def remaining(entering, arriving):
+        from_state = jnp.einsum("ln,hnp->lhp", queries_full, entering, precision=precise)
+        into_state = jnp.einsum("ln,hnp->lhp", keys_full, arriving, precision=precise)
+        carried = jnp.sum(values3 * into_state, 2)
+        step_grad = col_sums + to_end * carried
+        value_grad = within_part + (to_end * step_size)[:, :, None] * into_state
+        leaving = decay_total[:, None, None] * entering + local_state
+        decay_terms = (
+            local_decay
+            + from_start * jnp.sum(upstream3 * from_state, 2)
+            - to_end * step_size * carried
+        )
+        last_row = lax.broadcasted_iota(jnp.int32, (length, 1), 0) == length - 1
+        decay_terms = decay_terms + last_row.astype(jnp.float32) * jnp.sum(
+            arriving * leaving, (1, 2)
+        )[None, :]
+        decay_grad = jnp.flip(jnp.cumsum(jnp.flip(decay_terms, 0), 0), 0)
+        key_mine, query_mine = key_query_half(mine_at, arriving, entering)
+        conv_grad = value_grad.reshape(length, -1) * silu_slope
+        return decay_grad, step_grad, key_mine, query_mine, conv_grad
+
+    always = lax.axis_index("seq") >= 0
+    rest = lax.cond(
+        always,
+        remaining,
+        lambda *a: jax.tree.map(jnp.zeros_like, remaining(*a)),
+        entering,
+        arriving,
+    )
+    sent_back, following, rest = lax.optimization_barrier((sent_back, following, rest))
+    decay_grad, step_grad, key_mine, query_mine, conv_grad = rest
     keys_grad = key_mine + sent_back[:, :half_width]
     queries_grad = query_mine + sent_back[:, half_width:]
-    head_rows = within_part[:3] + (to_end * step_size)[:3, :, None] * jnp.einsum(
-        "ln,hnp->lhp", keys_full[:3], arriving, precision=split_bf16
-    )
-    following = shifted(head_rows.reshape(3, -1) * silu_slope[:3], "seq", -1)
-    conv_grad = value_grad.reshape(length, -1) * silu_slope
     extended = jnp.concatenate([conv_grad, following], 0)
     input_grad = jnp.zeros_like(conv_grad)
     for offset in range(4):

time: 55.1 us -> 67.8 us (1.23)
  local copies, waits for them, and re-layouts: 8.21 us -> 17 us
  other arithmetic: 8.87 us -> 13.1 us
  matrix products: 12.1 us -> 11.4 us
    cond x2 -> x12, local copies, waits for them, and re-layouts: 0.01 us -> 2.84 us
    cond x0 -> x2, matrix products: none -> 1.87 us
    reduce_sum x1, other arithmetic: 1.9 us -> 0.24 us  [remaining(): jnp.sum(arriving * leaving, (1, 2))[None, :]]
    dot_general x2, matrix products: 3.52 us -> 1.94 us  [key_query_half(): jnp.einsum('lhp,hnp->ln', weighted, pick(arriving), precision=precise)]
    unnamed x60 -> x67, local copies, waits for them, and re-layouts: 5.25 us -> 6.81 us
    optimization_barrier x1 -> x3, local copies, waits for them, and re-layouts: 1.02 us -> 2.5 us  [paired_scan(): passing, riders = lax.optimization_barrier((near[1], riders))]
    select_n x0 -> x1, other arithmetic: none -> 1.38 us  [paired_scan(): jnp.where(is_odd, handed, mine)]
    mul x2 -> x3, other arithmetic: 0.05 us -> 1.36 us  [the longest x1 0.73 us: remaining(): conv_grad = value_grad.reshape(length, -1) * silu_slope]
  transfers between devices with their start and end apart: 7 -> 7, of which waited for: 2 -> 2; matrix products, arithmetic and copies ran while one was open for 24% -> 28% of each run, Pallas kernels for 0% -> 0%
where the time goes in v8:
time: 67.8 us; the launch traced here: 66.9 us
  starting transfers between devices  18.6 us (27%)
  local copies, waits for them, and re-layouts  17 us (25%)
  other arithmetic  13.1 us (19%)
  matrix products  11.4 us (17%)
  waiting for transfers between devices  5.53 us (8%)
  between operations  1.05 us (2%)
    unnamed x67, local copies, waits for them, and re-layouts  6.81 us
    ppermute x1, starting transfers between devices, paired_scan(): far_s = lax.ppermute(window[1].astype(jnp.bfloat16), axis, route)  5.84 us
    ppermute x1, waiting for transfers between devices, paired_scan(): far = lax.ppermute(packed(*window, jnp.bfloat16), axis, route)  3.89 us
    ppermute x1, starting transfers between devices, paired_scan(): handed = lax.ppermute(passing, axis, swap)  3.6 us
    ppermute x1, starting transfers between devices, paired_scan(): far = lax.ppermute(packed(*window, jnp.bfloat16), axis, route)  3.21 us
    cond x12, local copies, waits for them, and re-layouts  2.84 us
    ppermute x2, starting transfers between devices, swapped(): return lax.ppermute(block, axis, route)  2.78 us
    optimization_barrier x3, local copies, waits for them, and re-layouts, paired_scan(): passing, riders = lax.optimization_barrier((near[1], riders))  2.5 us
  transfers between devices with their start and end apart: 7, of which 2 were waited for; matrix products, arithmetic and copies ran while one was open for 28% of the time, Pallas kernels for 0%

profile of v8, /device:TPU:1, one launch (start us, length us, event | category | flops | bytes accessed | tf_op | source)
XLA Modules:
  0.0 66.9 jit_solution(13979083080748882942)
XLA Ops:
  0.6 0.8 %pad_maximum_fusion.4 = bf16[128,256]{1,0:T(8,128)(2,1)S(1)} fusion(bf16[128,128]{1,0:T(8,128)(2,1)} %param.15, bf16[128,128]{1,0:T(8,128)(2,1)} %param.14), kind=kLoop, calls=%fused_computation.82 | loop fusion | flops 131072 | bytes 131072 | tf_op jit(solution)/shard_map/concatenate | solution.py:123
  1.5 2.1 %collective-permute-start = (bf16[128,256]{1,0:T(8,128)(2,1)S(1)}, bf16[128,256]{1,0:T(8,128)(2,1)S(1)}, u32[]{:S(2)}, u32[]{:S(2)}) collective-permute-start(bf16[128,256]{1,0:T(8,128)(2,1)S(1)} %pad_maximum_fusion.4), channel_id=1, source_target_pairs={{0,1},{1,0},{2,3},{3,2},{4,5},{5,4},{6,7},{7,6},{8,9},{9,8},{10,11... | collective-permute-start | bytes 196616 | tf_op jit(solution)/shard_map/ppermute | solution.py:16
  4.7 0.7 fusion.65
  6.2 0.7 %copy-done.22 = bf16[128,128]{1,0:T(8,128)(2,1)S(1)} copy-done((bf16[128,128]{1,0:T(8,128)(2,1)S(1)}, bf16[128,128]{1,0:T(8,128)(2,1)}, u32[]{:S(2)}) %copy-start.22) | copy-done | bytes 32792
  8.2 1.0 %collective-permute-start.1 = (f32[9,256,64]{1,2,0:T(8,128)S(1)}, f32[9,256,64]{1,2,0:T(8,128)S(1)}, u32[]{:S(2)}, u32[]{:S(2)}) collective-permute-start(f32[9,256,64]{1,2,0:T(8,128)S(1)} %pad_maximum_fusion), channel_id=1, source_target_pairs={{0,4},{4,0},{8,12},{12,8},{16,20},{20,16},{24,28},{28,24},{1,5},{5... | collective-permute-start | bytes 1769480 | tf_op jit(solution)/shard_map/ppermute | solution.py:72
  9.2 1.6 %collective-permute-done.1 = f32[9,256,64]{1,2,0:T(8,128)S(1)} collective-permute-done((f32[9,256,64]{1,2,0:T(8,128)S(1)}, f32[9,256,64]{1,2,0:T(8,128)S(1)}, u32[]{:S(2)}, u32[]{:S(2)}) %collective-permute-start.1) | collective-permute-done | bytes 589856 | tf_op jit(solution)/shard_map/ppermute | solution.py:72
  11.6 0.8 %pad_maximum_fusion.1 = bf16[9,256,64]{1,2,0:T(8,128)(2,1)} fusion(bf16[1,256,64]{1,2,0:T(8,128)(2,1)S(1)} %broadcast_in_dim.13, bf16[8,256,64]{1,2,0:T(8,128)(2,1)S(1)} %get-tuple-element.276), kind=kLoop, calls=%fused_computation.60 | loop fusion | flops 147456 | bytes 589824 | tf_op jit(solution)/shard_map/concatenate | solution.py:50
  12.4 3.2 %collective-permute-start.2 = (bf16[9,256,64]{1,2,0:T(8,128)(2,1)}, bf16[9,256,64]{1,2,0:T(8,128)(2,1)S(1)}, u32[]{:S(2)}, u32[]{:S(2)}) collective-permute-start(bf16[9,256,64]{1,2,0:T(8,128)(2,1)} %pad_maximum_fusion.1), channel_id=1, source_target_pairs={{4,12},{12,20},{20,28},{8,0},{16,8},{24,16},{5,13},{13,21},{21,29}... | collective-permute-start | bytes 884744 | tf_op jit(solution)/shard_map/ppermute | solution.py:90
  15.7 3.9 %collective-permute-done.2 = bf16[9,256,64]{1,2,0:T(8,128)(2,1)S(1)} collective-permute-done((bf16[9,256,64]{1,2,0:T(8,128)(2,1)}, bf16[9,256,64]{1,2,0:T(8,128)(2,1)S(1)}, u32[]{:S(2)}, u32[]{:S(2)}) %collective-permute-start.2) | collective-permute-done | bytes 294944 | tf_op jit(solution)/shard_map/ppermute | solution.py:90
  19.6 0.8 %fusion.33 = bf16[8,256,64]{1,2,0:T(8,128)(2,1)} fusion(f32[8,256,64]{1,2,0:T(8,128)S(1)} %get-tuple-element.277, f32[8]{0:T(128)S(1)} %get-tuple-element.279, bf16[9,256,64]{1,2,0:T(8,128)(2,1)S(1)} %collective-permute-done.2), kind=kLoop, calls=%fused_computation.55 | loop fusion | flops 524288 | bytes 1048608 | tf_op jit(solution)/shard_map/convert_element_type | solution.py:84
  20.4 5.8 %collective-permute-start.3 = (bf16[8,256,64]{1,2,0:T(8,128)(2,1)}, bf16[8,256,64]{1,2,0:T(8,128)(2,1)}, u32[]{:S(2)}, u32[]{:S(2)}) collective-permute-start(bf16[8,256,64]{1,2,0:T(8,128)(2,1)} %fusion.33), channel_id=1, source_target_pairs={{4,20},{12,28},{16,0},{24,8},{5,21},{13,29},{17,1},{25,9},{6,22},{... | collective-permute-start | bytes 786440 | tf_op jit(solution)/shard_map/ppermute | solution.py:84
  26.3 4.8 %conditional.2 = (f32[128,8,64]{0,2,1:T(8,128)S(1)}, f32[128,8]{0,1:T(8,128)S(1)}, f32[128,8]{0,1:T(8,128)S(1)}, f32[128,256]{1,0:T(8,128)S(1)}, f32[128,256]{1,0:T(8,128)S(1)}, /*index=5*/f32[128,512]{1,0:T(8,128)S(1)}) conditional(s32[]{:T(128)} %convert_element_type.69, () %tuple.29, (f32[128,8]{1,0:T(8,128)S(1)}, f32[128,256]{1,0:T(8,128)S(1)}, ...), branch_computations={%region_1.2_spmd, %region_2.4_spmd} | conditional | flops 356844544 | bytes 4567176 | solution.py:185
  26.6 0.8 %fusion.6 = f32[128,8,64]{0,2,1:T(8,128)S(1)} fusion(f32[128,8,64]{0,2,1:T(8,128)S(1)} %get-tuple-element.63, f32[8,128]{1,0:T(8,128)S(1)} %bitcast.125, f32[128,128]{1,0:T(8,128)S(1)} %fusion.68, f32[8,128]{1,0:T(8,128)S(1)} %bitcast.121, pred[128,128]{1,0:T(8,128)(4,1)S(1)} %iota_compare_fusion, f32[8]{0:T(128)S(1)} %get-tuple-element.167), kind=kOutput, calls=%fused_computation.17 | convolution fusion | flops 101318656 | bytes 614432 | tf_op jit(solution)/shard_map/cond/branch_1_fun/hts,thp->shp/dot_general | solution.py:162
  27.4 1.1 %fusion.11 = (f32[8,128]{1,0:T(8,128)S(1)}, f32[8,128,128]{2,1,0:T(8,128)S(1)}) fusion(f32[128,128]{1,0:T(8,128)S(1)} %fusion.68, f32[8,128]{1,0:T(8,128)S(1)} %bitcast.122, pred[128,128]{1,0:T(8,128)(4,1)S(1)} %iota_compare_fusion, f32[128,8,64]{0,2,1:T(8,128)S(1)} %get-tuple-element.63, f32[128,8,64]{0,2,1:T(8,128)S(1)} %get-tuple-element.65), kind=kOutput, calls=%fused_computation.23 | convolution fusion | flops 101317632 | bytes 1138688 | tf_op jit(solution)/shard_map/cond/branch_1_fun/thp,shp->hts/dot_general | solution.py:159
  28.5 1.1 %fusion.12 = f32[8,1,128]{2,1,0:T(1,128)S(1)} fusion(f32[8,128,1]{1,2,0:T(1,128)S(1)} %bitcast.126, f32[8,128,128]{2,1,0:T(8,128)S(1)} %get-tuple-element.286, f32[128,128]{1,0:T(8,128)S(1)} %fusion.68, f32[8,128]{1,0:T(8,128)S(1)} %bitcast.123, pred[128,128]{1,0:T(8,128)(4,1)S(1)} %iota_compare_fusion), kind=kOutput, calls=%fused_computation.24 | convolution fusion | flops 2097152 | bytes 618496 | tf_op jit(solution)/shard_map/cond/branch_1_fun/hts,hs->th/dot_general | solution.py:166
  31.2 1.2 %convert_add_fusion = f32[8,256,64]{1,2,0:T(8,128)S(1)} fusion(bf16[8,256,64]{1,2,0:T(8,128)(2,1)} %collective-permute-done.3, f32[8]{0:T(128)S(1)} %fusion.56, bf16[9,256,64]{1,2,0:T(8,128)(2,1)S(1)} %copy-done.13), kind=kLoop, calls=%fused_computation.51 | loop fusion | flops 524288 | bytes 1048608 | tf_op jit(solution)/shard_map/add | solution.py:88
  32.4 3.6 %collective-permute-start.4 = (f32[8,256,64]{1,2,0:T(8,128)S(1)}, f32[8,256,64]{1,2,0:T(8,128)}, u32[]{:S(2)}, u32[]{:S(2)}) collective-permute-start(f32[8,256,64]{1,2,0:T(8,128)S(1)} %convert_add_fusion), channel_id=1, source_target_pairs={{0,4},{4,0},{8,12},{12,8},{16,20},{20,16},{24,28},{28,24},{1,5},{5... | collective-permute-start | bytes 1572872 | tf_op jit(solution)/shard_map/ppermute | solution.py:99
  36.0 0.7 %slice.104 = f32[3,8]{1,0:T(4,128)S(1)} slice(f32[128,8]{1,0:T(8,128)} %copy-done.19), slice={[0:3], [0:8]} | slice | bytes 192 | tf_op jit(solution)/shard_map/slice | solution.py:216
  36.8 0.7 %slice_bitcast_fusion.2 = f32[8]{0:T(128)S(1)} fusion(f32[9,256,64]{1,2,0:T(8,128)} %copy-done.2), kind=kLoop, calls=%fused_computation.104 | loop fusion | bytes 64 | tf_op jit(solution)/shard_map/slice | solution.py:56
  37.5 0.8 %copy.73 = f32[128,256]{0,1:T(8,128)} copy(f32[128,256]{1,0:T(8,128)S(1)} %get-tuple-element.145) | data formatting | bytes 262144 | tf_op jit(solution)/shard_map/optimization_barrier | solution.py:98
  38.2 0.8 %copy.72 = f32[128,256]{0,1:T(8,128)} copy(f32[128,256]{1,0:T(8,128)S(1)} %get-tuple-element.143) | data formatting | bytes 262144 | tf_op jit(solution)/shard_map/optimization_barrier | solution.py:98
  39.0 1.0 %copy.74 = f32[128,8,64]{2,0,1:T(8,128)} copy(f32[128,8,64]{0,2,1:T(8,128)S(1)} %get-tuple-element.146) | data formatting | bytes 524288 | tf_op jit(solution)/shard_map/optimization_barrier | solution.py:98
  40.0 1.4 %broadcast_select_fusion.1 = (f32[8,256,64]{1,2,0:T(8,128)S(1)}, f32[8,256,64]{1,2,0:T(8,128)S(1)}) fusion(f32[8,256,64]{1,2,0:T(8,128)} %collective-permute-done.4, pred[]{:T(512)S(6)} %eq.17, f32[8,256,64]{1,2,0:T(8,128)S(1)} %convert_add_fusion, f32[8]{0:T(128)S(1)} %slice_bitcast_fusion.2, f32[9,256,64]{1,2,0:T(8,128)} %copy-done.2), kind=kLoop, calls=%fused_computation.77 | loop fusion | flops 524288 | bytes 2621473 | tf_op jit(solution)/shard_map/jit(_where)/select_n | solution.py:101
  41.4 1.2 %fusion.31 = f32[3,8,64]{2,0,1:T(4,128)S(1)} fusion(f32[8,256,64]{1,2,0:T(8,128)S(1)} %get-tuple-element.152, f32[128,8,64]{2,0,1:T(8,128)} %copy.74, f32[3,8]{0,1:T(8,128)S(1)} %copy.75, bf16[128,256]{1,0:T(8,128)(2,1)} %copy-done.18), kind=kOutput, calls=%fused_computation.50 | convolution fusion | flops 4721664 | bytes 548960 | tf_op jit(solution)/shard_map/ln,hnp->lhp/dot_general | solution.py:216
  42.7 0.6 fusion.29
  43.6 0.6 fusion.30
  44.2 0.6 pad_maximum_fusion.6
  44.9 0.6 slice_multiply_fusion
  45.5 0.7 %collective-permute-start.5 = (bf16[128,256]{0,1:T(8,128)(2,1)}, bf16[128,256]{0,1:T(8,128)(2,1)}, u32[]{:S(2)}, u32[]{:S(2)}) collective-permute-start(bf16[128,256]{0,1:T(8,128)(2,1)} %pad_maximum_fusion.6), channel_id=1, source_target_pairs={{0,1},{1,0},{2,3},{3,2},{4,5},{5,4},{6,7},{7,6},{8,9},{9,8},{10,11... | collective-permute-start | bytes 196616 | tf_op jit(solution)/shard_map/ppermute | solution.py:16
  46.1 2.2 %collective-permute-start.6 = (f32[3,512]{1,0:T(4,128)}, f32[3,512]{1,0:T(4,128)}, u32[]{:S(2)}, u32[]{:S(2)}) collective-permute-start(f32[3,512]{1,0:T(4,128)} %slice_multiply_fusion), channel_id=1, source_target_pairs={{4,0},{8,4},{12,8},{16,12},{20,16},{24,20},{28,24},{5,1},{9,5},{13... | collective-permute-start | bytes 18440 | tf_op jit(solution)/shard_map/ppermute | solution.py:107
  48.3 0.6 fusion.67
  49.0 9.8 %conditional.3 = (f32[128,8]{1,0:T(8,128)}, f32[128,8]{0,1:T(8,128)}, f32[128,128]{0,1:T(8,128)}, f32[128,128]{0,1:T(8,128)}, f32[128,512]{0,1:T(8,128)}) conditional(s32[]{:T(128)} %convert_element_type.69, () %tuple.33, (f32[128,8]{1,0:T(8,128)}, f32[128,256]{1,0:T(8,128)S(1)}, f32[8,256,64]{1,2,0:T(8,128)S(1)}, f32[128,8,64]{0,2,1:T(8,128)S(1)}, ...), branch_computations={%region_4.5_spmd, %region_5.10_spmd} | conditional | flops 605133056 | bytes 8789418 | solution.py:248
  49.0 1.3 %multiply_reduce_fusion.1 = (f32[128,8]{0,1:T(8,128)S(1)}, f32[128,512]{0,1}) fusion(f32[128,8,64]{0,2,1:T(8,128)S(1)} %get-tuple-element.74, f32[128,256]{1,0:T(8,128)S(1)} %get-tuple-element.75, f32[256,512]{0,1:T(8,128)S(1)} %bitcast.113), kind=kOutput, calls=%fused_computation.9 | convolution fusion | flops 201456640 | bytes 1183744 | tf_op jit(solution)/shard_map/cond
  52.0 0.6 copy-done.20
  52.6 0.6 multiply_add_fusion.2
  53.6 0.6 rev.6
  54.3 1.3 %fusion = f32[128,128]{0,1:T(8,128)} fusion(f32[128,8,64]{0,2,1:T(8,128)S(1)} %get-tuple-element.82, f32[8,256,64]{1,2,0:T(8,128)S(1)} %get-tuple-element.76, s32[]{:T(128)S(6)} %select_n.49, f32[128,256]{0,1:T(8,128)S(1)} %copy.79), kind=kOutput, calls=%fused_computation.2 | convolution fusion | flops 100679680 | bytes 656384 | tf_op jit(solution)/shard_map/cond/branch_1_fun/lhp,hnp->ln/dot_general | solution.py:209
  55.8 1.3 %fusion.1 = f32[128,128]{0,1:T(8,128)} fusion(f32[128,8,64]{0,2,1:T(8,128)S(1)} %get-tuple-element.84, f32[8,256,64]{1,2,0:T(8,128)S(1)} %get-tuple-element.71, s32[]{:T(128)S(6)} %select_n.49, f32[128,256]{0,1:T(8,128)S(1)} %copy.80), kind=kOutput, calls=%fused_computation.3 | convolution fusion | flops 100679680 | bytes 656384 | tf_op jit(solution)/shard_map/cond/branch_1_fun/lhp,hnp->ln/dot_general | solution.py:211
  57.2 0.8 %copy-done.11 = f32[128,512]{0,1:S(1)} copy-done((f32[128,512]{0,1:S(1)}, f32[128,512]{0,1}, u32[]{:S(2)}) %copy-start.11) | copy-done | bytes 262168 | tf_op jit(solution)/shard_map/cond
  58.1 0.7 %bitcast_multiply_fusion = f32[128,512]{0,1:T(8,128)} fusion(f32[128,512]{0,1:T(8,128)S(1)} %copy.81, f32[128,8,64]{0,2,1:T(8,128)S(1)} %multiply_add_fusion), kind=kLoop, calls=%fused_computation.5 | loop fusion | flops 65536 | bytes 786432 | tf_op jit(solution)/shard_map/cond/branch_1_fun/mul | solution.py:244
  58.8 0.8 %convert_element_type.70 = f32[128,256]{0,1:T(8,128)S(1)} convert(bf16[128,256]{0,1:T(8,128)(2,1)} %collective-permute-done.5) | non-fusion elementwise | flops 32768 | bytes 196608 | tf_op jit(solution)/shard_map/convert_element_type | solution.py:223
  59.7 1.1 %copy.82 = f32[128,512]{1,0:T(8,128)S(1)} copy(f32[128,512]{0,1:T(8,128)} %get-tuple-element.159) | data formatting | bytes 524288 | tf_op jit(solution)/shard_map/optimization_barrier | solution.py:255
  60.7 0.9 %slice_add_fusion = (f32[128,128]{0,1:T(8,128)S(1)}, f32[128,128]{0,1:T(8,128)S(1)}) fusion(f32[128,128]{0,1:T(8,128)} %get-tuple-element.163, f32[128,256]{0,1:T(8,128)S(1)} %convert_element_type.70, f32[128,128]{0,1:T(8,128)} %get-tuple-element.161), kind=kLoop, calls=%fused_computation.89 | loop fusion | flops 32768 | bytes 393216 | tf_op jit(solution)/shard_map/add | solution.py:258
  61.6 0.7 %copy.84 = f32[128,128]{1,0:T(8,128)} copy(f32[128,128]{0,1:T(8,128)S(1)} %get-tuple-element.290) | data formatting | bytes 131072
  62.4 0.7 %copy.85 = f32[128,128]{1,0:T(8,128)} copy(f32[128,128]{0,1:T(8,128)S(1)} %get-tuple-element.289) | data formatting | bytes 131072
  63.1 1.5 %copy.86 = f32[128,8]{0,1:T(8,128)} copy(f32[128,8]{1,0:T(8,128)} %get-tuple-element.270) | data formatting | bytes 8192
  64.6 0.7 copy-done.29
  65.3 1.6 %fusion.39 = bf16[128,512]{1,0:T(8,128)(2,1)} fusion(f32[128,512]{1,0:T(8,128)S(1)} %copy.82, f32[3,512]{1,0:T(4,128)} %collective-permute-done.6, f32[512]{0:T(512)S(1)} %bitcast.130, f32[512]{0:T(512)S(1)} %bitcast.131, f32[512]{0:T(512)S(1)} %bitcast.129, f32[512]{0:T(512)S(1)} %bitcast.128), kind=kLoop, calls=%fused_computation.68 | loop fusion | flops 720896 | bytes 407552 | tf_op jit(solution)/shard_map/convert_element_type | solution.py:265
  (126 shorter events, 8.8 us)
Async XLA Ops:
  0.6 2.9 %copy-start.21 = (bf16[128,512]{1,0:T(8,128)(2,1)S(1)}, bf16[128,512]{1,0:T(8,128)(2,1)}, u32[]{:S(2)}) copy-start(bf16[128,512]{1,0:T(8,128)(2,1)} %param.13) | copy-start | bytes 393220
  1.5 2.2 %copy-start.23 = (f32[128,8]{0,1:T(8,128)S(1)}, f32[128,8]{0,1:T(8,128)}, u32[]{:S(2)}) copy-start(f32[128,8]{0,1:T(8,128)} %param.17) | copy-start | bytes 12292
  1.5 4.7 %collective-permute-start = (bf16[128,256]{1,0:T(8,128)(2,1)S(1)}, bf16[128,256]{1,0:T(8,128)(2,1)S(1)}, u32[]{:S(2)}, u32[]{:S(2)}) collective-permute-start(bf16[128,256]{1,0:T(8,128)(2,1)S(1)} %pad_maximum_fusion.4), channel_id=1, source_target_pairs={{0,1},{1,0},{2,3},{3,2},{4,5},{5,4},{6,7},{7,6},{8,9},{9,8},{10,11... | collective-permute-start | bytes 196616 | tf_op jit(solution)/shard_map/ppermute | solution.py:16
  3.7 0.7 %copy-start.35 = (f32[128,8]{0,1:T(8,128)S(1)}, f32[128,8]{0,1:T(8,128)}, u32[]{:S(2)}) copy-start(f32[128,8]{0,1:T(8,128)} %param.16) | copy-start | bytes 12292
  4.7 21.6 %copy-start.9 = (f32[128,8]{1,0:T(8,128)}, f32[128,8]{1,0:T(8,128)S(1)}, u32[]{:S(2)}) copy-start(f32[128,8]{1,0:T(8,128)S(1)} %reduce_window_sum.18) | copy-start | bytes 12292
  4.7 1.0 %copy-start.14 = (bf16[128,512]{1,0:T(8,128)(2,1)S(1)}, bf16[128,512]{1,0:T(8,128)(2,1)}, u32[]{:S(2)}) copy-start(bf16[128,512]{1,0:T(8,128)(2,1)} %param.12) | copy-start | bytes 393220
  5.3 0.6 copy-start.19
  6.1 4.8 %copy-start.33 = (f32[8]{0:T(128)}, f32[8]{0:T(128)S(1)}, u32[]{:S(2)}) copy-start(f32[8]{0:T(128)S(1)} %fusion.58) | copy-start | bytes 100
  6.1 0.8 %copy-start.22 = (bf16[128,128]{1,0:T(8,128)(2,1)S(1)}, bf16[128,128]{1,0:T(8,128)(2,1)}, u32[]{:S(2)}) copy-start(bf16[128,128]{1,0:T(8,128)(2,1)} %param.14) | copy-start | bytes 98308
  6.9 0.6 copy-start.18
  6.9 0.8 %copy-start.15 = (bf16[128,128]{1,0:T(8,128)(2,1)S(1)}, bf16[128,128]{1,0:T(8,128)(2,1)}, u32[]{:S(2)}) copy-start(bf16[128,128]{1,0:T(8,128)(2,1)} %param.15) | copy-start | bytes 98308
  8.2 2.6 %collective-permute-start.1 = (f32[9,256,64]{1,2,0:T(8,128)S(1)}, f32[9,256,64]{1,2,0:T(8,128)S(1)}, u32[]{:S(2)}, u32[]{:S(2)}) collective-permute-start(f32[9,256,64]{1,2,0:T(8,128)S(1)} %pad_maximum_fusion), channel_id=1, source_target_pairs={{0,4},{4,0},{8,12},{12,8},{16,20},{20,16},{24,28},{28,24},{1,5},{5... | collective-permute-start | bytes 1769480 | tf_op jit(solution)/shard_map/ppermute | solution.py:72
  10.8 0.8 %copy-start.2 = (f32[9,256,64]{1,2,0:T(8,128)}, f32[9,256,64]{1,2,0:T(8,128)S(1)}, u32[]{:S(2)}) copy-start(f32[9,256,64]{1,2,0:T(8,128)S(1)} %collective-permute-done.1) | copy-start | bytes 1769476
  12.4 7.2 %collective-permute-start.2 = (bf16[9,256,64]{1,2,0:T(8,128)(2,1)}, bf16[9,256,64]{1,2,0:T(8,128)(2,1)S(1)}, u32[]{:S(2)}, u32[]{:S(2)}) collective-permute-start(bf16[9,256,64]{1,2,0:T(8,128)(2,1)} %pad_maximum_fusion.1), channel_id=1, source_target_pairs={{4,12},{12,20},{20,28},{8,0},{16,8},{24,16},{5,13},{13,21},{21,29}... | collective-permute-start | bytes 884744 | tf_op jit(solution)/shard_map/ppermute | solution.py:90
  15.7 10.6 %copy-start = (f32[128,256]{1,0:T(8,128)}, f32[128,256]{1,0:T(8,128)S(1)}, u32[]{:S(2)}) copy-start(f32[128,256]{1,0:T(8,128)S(1)} %fusion.49) | copy-start | bytes 393220
  19.6 6.7 %copy-start.12 = (bf16[9,256,64]{1,2,0:T(8,128)(2,1)}, bf16[9,256,64]{1,2,0:T(8,128)(2,1)S(1)}, u32[]{:S(2)}) copy-start(bf16[9,256,64]{1,2,0:T(8,128)(2,1)S(1)} %collective-permute-done.2) | copy-start | bytes 884740
  20.4 5.8 %copy-start.36 = (f32[8]{0:T(128)S(1)}, f32[8]{0:T(128)}, u32[]{:S(2)}) copy-start(f32[8]{0:T(128)} %param.18) | copy-start | bytes 100
  20.4 10.8 %collective-permute-start.3 = (bf16[8,256,64]{1,2,0:T(8,128)(2,1)}, bf16[8,256,64]{1,2,0:T(8,128)(2,1)}, u32[]{:S(2)}, u32[]{:S(2)}) collective-permute-start(bf16[8,256,64]{1,2,0:T(8,128)(2,1)} %fusion.33), channel_id=1, source_target_pairs={{4,20},{12,28},{16,0},{24,8},{5,21},{13,29},{17,1},{25,9},{6,22},{... | collective-permute-start | bytes 786440 | tf_op jit(solution)/shard_map/ppermute | solution.py:84
  26.2 4.9 %copy-start.13 = (bf16[9,256,64]{1,2,0:T(8,128)(2,1)S(1)}, bf16[9,256,64]{1,2,0:T(8,128)(2,1)}, u32[]{:S(2)}) copy-start(bf16[9,256,64]{1,2,0:T(8,128)(2,1)} %copy-done.12) | copy-start | bytes 884740
  28.5 1.1 %copy-start.24 = (f32[8,128]{1,0:T(8,128)}, f32[8,128]{1,0:T(8,128)S(1)}, u32[]{:S(2)}) copy-start(f32[8,128]{1,0:T(8,128)S(1)} %get-tuple-element.285) | copy-start | bytes 12292 | tf_op jit(solution)/shard_map/cond
  30.4 0.7 %copy-start.25 = (f32[8,128]{1,0:T(8,128)S(1)}, f32[8,128]{1,0:T(8,128)}, u32[]{:S(2)}) copy-start(f32[8,128]{1,0:T(8,128)} %copy-done.24) | copy-start | bytes 12292 | tf_op jit(solution)/shard_map/cond
  31.1 1.3 %copy-start.7 = (f32[128,512]{1,0:T(8,128)}, f32[128,512]{1,0:T(8,128)S(1)}, u32[]{:S(2)}) copy-start(f32[128,512]{1,0:T(8,128)S(1)} %get-tuple-element.147) | copy-start | bytes 786436
  31.1 1.3 %copy-start.26 = (f32[128,8]{0,1:T(8,128)}, f32[128,8]{0,1:T(8,128)S(1)}, u32[]{:S(2)}) copy-start(f32[128,8]{0,1:T(8,128)S(1)} %get-tuple-element.151) | copy-start | bytes 12292
  31.1 6.4 %copy-start.3 = (f32[128,256]{1,0:T(8,128)}, f32[128,256]{1,0:T(8,128)S(1)}, u32[]{:S(2)}) copy-start(f32[128,256]{1,0:T(8,128)S(1)} %get-tuple-element.145) | copy-start | bytes 393220
  31.1 7.1 %copy-start.5 = (f32[128,256]{1,0:T(8,128)}, f32[128,256]{1,0:T(8,128)S(1)}, u32[]{:S(2)}) copy-start(f32[128,256]{1,0:T(8,128)S(1)} %get-tuple-element.143) | copy-start | bytes 393220
  32.4 7.6 %collective-permute-start.4 = (f32[8,256,64]{1,2,0:T(8,128)S(1)}, f32[8,256,64]{1,2,0:T(8,128)}, u32[]{:S(2)}, u32[]{:S(2)}) collective-permute-start(f32[8,256,64]{1,2,0:T(8,128)S(1)} %convert_add_fusion), channel_id=1, source_target_pairs={{0,4},{4,0},{8,12},{12,8},{16,20},{20,16},{24,28},{28,24},{1,5},{5... | collective-permute-start | bytes 1572872 | tf_op jit(solution)/shard_map/ppermute | solution.py:99
  41.4 1.3 %copy-start.17 = (f32[128,256]{0,1:T(8,128)S(1)}, f32[128,256]{0,1:T(8,128)}, u32[]{:S(2)}) copy-start(f32[128,256]{0,1:T(8,128)} %copy.72) | copy-start | bytes 393220
  42.7 0.9 %copy-start.16 = (f32[128,256]{0,1:T(8,128)S(1)}, f32[128,256]{0,1:T(8,128)}, u32[]{:S(2)}) copy-start(f32[128,256]{0,1:T(8,128)} %copy.73) | copy-start | bytes 393220
  43.6 1.3 %copy-start.8 = (f32[128,512]{1,0:T(8,128)S(1)}, f32[128,512]{1,0:T(8,128)}, u32[]{:S(2)}) copy-start(f32[128,512]{1,0:T(8,128)} %copy-done.7) | copy-start | bytes 786436
  43.6 5.4 %copy-start.4 = (f32[128,256]{1,0:T(8,128)S(1)}, f32[128,256]{1,0:T(8,128)}, u32[]{:S(2)}) copy-start(f32[128,256]{1,0:T(8,128)} %copy-done.3) | copy-start | bytes 393220
  43.6 5.4 %copy-start.6 = (f32[128,256]{1,0:T(8,128)S(1)}, f32[128,256]{1,0:T(8,128)}, u32[]{:S(2)}) copy-start(f32[128,256]{1,0:T(8,128)} %copy-done.5) | copy-start | bytes 393220
  44.2 4.7 %copy-start.1 = (f32[128,256]{1,0:T(8,128)S(1)}, f32[128,256]{1,0:T(8,128)}, u32[]{:S(2)}) copy-start(f32[128,256]{1,0:T(8,128)} %copy-done) | copy-start | bytes 393220
  44.9 3.5 %copy-start.32 = (f32[4,512]{1,0:T(4,128)S(1)}, f32[4,512]{1,0:T(4,128)}, u32[]{:S(2)}) copy-start(f32[4,512]{1,0:T(4,128)} %param.19) | copy-start | bytes 24580
  45.5 3.5 %copy-start.27 = (f32[128,8]{0,1:T(8,128)S(1)}, f32[128,8]{0,1:T(8,128)}, u32[]{:S(2)}) copy-start(f32[128,8]{0,1:T(8,128)} %copy-done.26) | copy-start | bytes 12292
  45.5 13.3 %collective-permute-start.5 = (bf16[128,256]{0,1:T(8,128)(2,1)}, bf16[128,256]{0,1:T(8,128)(2,1)}, u32[]{:S(2)}, u32[]{:S(2)}) collective-permute-start(bf16[128,256]{0,1:T(8,128)(2,1)} %pad_maximum_fusion.6), channel_id=1, source_target_pairs={{0,1},{1,0},{2,3},{3,2},{4,5},{5,4},{6,7},{7,6},{8,9},{9,8},{10,11... | collective-permute-start | bytes 196616 | tf_op jit(solution)/shard_map/ppermute | solution.py:16
  46.1 13.5 %collective-permute-start.6 = (f32[3,512]{1,0:T(4,128)}, f32[3,512]{1,0:T(4,128)}, u32[]{:S(2)}, u32[]{:S(2)}) collective-permute-start(f32[3,512]{1,0:T(4,128)} %slice_multiply_fusion), channel_id=1, source_target_pairs={{4,0},{8,4},{12,8},{16,12},{20,16},{24,20},{28,24},{5,1},{9,5},{13... | collective-permute-start | bytes 18440 | tf_op jit(solution)/shard_map/ppermute | solution.py:107
  50.3 0.8 %copy-start.10 = (f32[128,8]{1,0:T(8,128)S(1)}, f32[128,8]{1,0:T(8,128)}, u32[]{:S(2)}) copy-start(f32[128,8]{1,0:T(8,128)} %get-tuple-element.247) | copy-start | bytes 12292 | tf_op jit(solution)/shard_map/cond
  51.1 0.6 copy-start.34
  51.7 0.8 %copy-start.20 = (f32[128,8]{1,0:T(8,128)S(1)}, f32[128,8]{1,0:T(8,128)}, u32[]{:S(2)}) copy-start(f32[128,8]{1,0:T(8,128)} %get-tuple-element.252) | copy-start | bytes 12292 | tf_op jit(solution)/shard_map/cond
  57.1 0.9 %copy-start.11 = (f32[128,512]{0,1:S(1)}, f32[128,512]{0,1}, u32[]{:S(2)}) copy-start(f32[128,512]{0,1} %get-tuple-element.284) | copy-start | bytes 786436 | tf_op jit(solution)/shard_map/cond
  62.4 2.2 %copy-start.30 = (f32[1,512]{1,0:T(1,128)S(1)}, f32[1,512]{1,0:T(1,128)}, u32[]{:S(2)}) copy-start(f32[1,512]{1,0:T(1,128)} %get-tuple-element.296) | copy-start | bytes 6148
  62.4 2.2 %copy-start.31 = (f32[1,512]{1,0:T(1,128)S(1)}, f32[1,512]{1,0:T(1,128)}, u32[]{:S(2)}) copy-start(f32[1,512]{1,0:T(1,128)} %get-tuple-element.297) | copy-start | bytes 6148
  64.6 0.7 %copy-start.29 = (f32[1,512]{1,0:T(1,128)S(1)}, f32[1,512]{1,0:T(1,128)}, u32[]{:S(2)}) copy-start(f32[1,512]{1,0:T(1,128)} %get-tuple-element.295) | copy-start | bytes 6148
  64.6 0.7 %copy-start.28 = (f32[1,512]{1,0:T(1,128)S(1)}, f32[1,512]{1,0:T(1,128)}, u32[]{:S(2)}) copy-start(f32[1,512]{1,0:T(1,128)} %get-tuple-element.294) | copy-start | bytes 6148

commit v9 on v5

--- a/solution.py
+++ b/solution.py
@@ -65,7 +65,7 @@
     is_odd = lax.axis_index(axis) % 2 == 1
     swap = [(i, i ^ 1) for i in range(peers)]
     sent = jnp.where(is_odd, state_grad, state)
-    message = packed(decay, sent, jnp.float32)
+    message = packed(decay, sent, jnp.bfloat16)
     if peers == 2:
         message, rider_inputs = lax.optimization_barrier((message, rider_inputs))
         riders = rider_fn(*rider_inputs)
@@ -96,7 +96,7 @@
             window = (window[0] * far_a, window[1] + window[0][:, None, None] * far_s)
         distance *= 2
     passing, riders = lax.optimization_barrier((near[1], riders))
-    handed = lax.ppermute(passing, axis, swap)
+    handed = lax.ppermute(passing.astype(jnp.bfloat16), axis, swap).astype(jnp.float32)
     mine = mate_s + mate_a[:, None, None] * near[1]
     return jnp.where(is_odd, mine, handed), jnp.where(is_odd, handed, mine), riders
 

time: 47.3 us -> 46.3 us (0.979)
  other arithmetic: 6.37 us -> 9.31 us
  starting transfers between devices: 19.1 us -> 16.9 us
  waiting for transfers between devices: 6.98 us -> 5.9 us
  local copies, waits for them, and re-layouts: 6.65 us -> 5.84 us
    ppermute x1, starting transfers between devices: 4.51 us -> 1.88 us  [paired_scan(): lax.ppermute(passing.astype(jnp.bfloat16), axis, swap).astype(jnp.float32)]
    unnamed x48 -> x32, local copies, waits for them, and re-layouts: 5.97 us -> 4.58 us
    add x1, other arithmetic: 0.14 us -> 1.09 us  [paired_scan(): near[1] + near[0][:, None, None] * far_s.astype(jnp.float32)]
    ppermute x1, starting transfers between devices: 5.14 us -> 5.93 us  [paired_scan(): far_s = lax.ppermute(window[1].astype(jnp.bfloat16), axis, route)]
    add x1, other arithmetic: 0.07 us -> 0.8 us  [unpacked(): row[:heads] + row[heads:2 * heads]]
    concatenate x2, other arithmetic: 0.78 us -> 0.06 us  [packed(): return jnp.concatenate([state.astype(kind), slab], 0)]
    convert_element_type x1, other arithmetic: 0.01 us -> 0.64 us  [packed(): high = decay.astype(kind)]
    sub x1, other arithmetic: 0.01 us -> 0.61 us  [local_terms(): row_sums - col_sums * step_size]
  transfers between devices with their start and end apart: 7 -> 7, of which waited for: 3 -> 3; matrix products, arithmetic and copies ran while one was open for 20% -> 24% of each run, Pallas kernels for 0% -> 0%
where the time goes in v9:
time: 46.3 us; the launch traced here: 45.5 us
  starting transfers between devices  16.9 us (37%)
  other arithmetic  9.31 us (20%)
  matrix products  6.49 us (14%)
  waiting for transfers between devices  5.9 us (13%)
  local copies, waits for them, and re-layouts  5.84 us (13%)
  between operations  0.95 us (2%)
    ppermute x1, starting transfers between devices, paired_scan(): far_s = lax.ppermute(window[1].astype(jnp.bfloat16), axis, route)  5.93 us
    unnamed x32, local copies, waits for them, and re-layouts  4.58 us
    ppermute x1, waiting for transfers between devices, paired_scan(): far = lax.ppermute(packed(*window, jnp.bfloat16), axis, route)  3.56 us
    ppermute x1, starting transfers between devices, paired_scan(): far = lax.ppermute(packed(*window, jnp.bfloat16), axis, route)  3.22 us
    ppermute x2, starting transfers between devices, swapped(): return lax.ppermute(block, axis, route)  2.57 us
    ppermute x1, starting transfers between devices, shifted(): return lax.ppermute(block, axis, route)  2.29 us
    ppermute x1, starting transfers between devices, paired_scan(): lax.ppermute(passing.astype(jnp.bfloat16), axis, swap).astype(jnp.float32)  1.88 us
    ppermute x1, waiting for transfers between devices, paired_scan(): mate = lax.ppermute(message, axis, swap)  1.21 us
  transfers between devices with their start and end apart: 7, of which 3 were waited for; matrix products, arithmetic and copies ran while one was open for 24% of the time, Pallas kernels for 0%

profile of v9, /device:TPU:1, one launch (start us, length us, event | category | flops | bytes accessed | tf_op | source)
XLA Modules:
  0.0 45.5 jit_solution(18317300861044314178)
XLA Ops:
  0.6 0.8 %pad_maximum_fusion.4 = bf16[128,256]{1,0:T(8,128)(2,1)S(1)} fusion(bf16[128,128]{1,0:T(8,128)(2,1)} %param.13, bf16[128,128]{1,0:T(8,128)(2,1)} %param.12), kind=kLoop, calls=%fused_computation.71 | loop fusion | flops 131072 | bytes 131072 | tf_op jit(solution)/shard_map/concatenate | solution.py:123
  1.4 2.1 %collective-permute-start = (bf16[128,256]{1,0:T(8,128)(2,1)S(1)}, bf16[128,256]{1,0:T(8,128)(2,1)S(1)}, u32[]{:S(2)}, u32[]{:S(2)}) collective-permute-start(bf16[128,256]{1,0:T(8,128)(2,1)S(1)} %pad_maximum_fusion.4), channel_id=1, source_target_pairs={{0,1},{1,0},{2,3},{3,2},{4,5},{5,4},{6,7},{7,6},{8,9},{9,8},{10,11... | collective-permute-start | bytes 196616 | tf_op jit(solution)/shard_map/ppermute | solution.py:16
  3.6 0.2 reduce_window_sum.18
  3.9 0.7 %copy-done = bf16[128,512]{1,0:T(8,128)(2,1)S(1)} copy-done((bf16[128,512]{1,0:T(8,128)(2,1)S(1)}, bf16[128,512]{1,0:T(8,128)(2,1)}, u32[]{:S(2)}) %copy-start) | copy-done | bytes 131096
  4.6 0.1 copy.50
  4.8 0.7 %copy-done.5 = bf16[128,512]{1,0:T(8,128)(2,1)S(1)} copy-done((bf16[128,512]{1,0:T(8,128)(2,1)S(1)}, bf16[128,512]{1,0:T(8,128)(2,1)}, u32[]{:S(2)}) %copy-start.5) | copy-done | bytes 131096
  5.6 0.6 %copy-done.6 = f32[128,8]{0,1:T(8,128)S(1)} copy-done((f32[128,8]{0,1:T(8,128)S(1)}, f32[128,8]{0,1:T(8,128)}, u32[]{:S(2)}) %copy-start.6) | copy-done | bytes 4120
  6.4 0.7 %copy-done.1 = bf16[128,128]{1,0:T(8,128)(2,1)S(1)} copy-done((bf16[128,128]{1,0:T(8,128)(2,1)S(1)}, bf16[128,128]{1,0:T(8,128)(2,1)}, u32[]{:S(2)}) %copy-start.1) | copy-done | bytes 32792
  7.1 0.4 convolution_bitcast_fusion.2
  7.5 0.4 copy-done.2
  7.9 0.4 select_convert_fusion
  8.3 1.0 %collective-permute-start.1 = (bf16[9,256,64]{1,2,0:T(8,128)(2,1)S(1)}, bf16[9,256,64]{1,2,0:T(8,128)(2,1)S(1)}, u32[]{:S(2)}, u32[]{:S(2)}) collective-permute-start(bf16[9,256,64]{1,2,0:T(8,128)(2,1)S(1)} %pad_maximum_fusion), channel_id=1, source_target_pairs={{0,4},{4,0},{8,12},{12,8},{16,20},{20,16},{24,28},{28,24},{1,5},{5... | collective-permute-start | bytes 884744 | tf_op jit(solution)/shard_map/ppermute | solution.py:72
  9.3 1.2 %collective-permute-done.1 = bf16[9,256,64]{1,2,0:T(8,128)(2,1)S(1)} collective-permute-done((bf16[9,256,64]{1,2,0:T(8,128)(2,1)S(1)}, bf16[9,256,64]{1,2,0:T(8,128)(2,1)S(1)}, u32[]{:S(2)}, u32[]{:S(2)}) %collective-permute-start.1) | collective-permute-done | bytes 294944 | tf_op jit(solution)/shard_map/ppermute | solution.py:72
  10.5 0.6 %fusion.70 = (bf16[8]{0:T(256)(128)(2,1)S(1)}, f32[8]{0:T(128)S(1)}, f32[8]{0:T(128)}) fusion(f32[128,8]{1,0:T(8,128)S(1)} %reduce_window_sum.18, f32[1,256,1]{1,2,0:T(1,128)S(1)} %slice_convert_fusion), kind=kLoop, calls=%fused_computation.111 | loop fusion | flops 24 | bytes 176 | tf_op jit(solution)/shard_map/convert_element_type | solution.py:46
  11.3 0.2 fusion.69
  11.5 3.2 %collective-permute-start.2 = (bf16[9,256,64]{1,2,0:T(8,128)(2,1)S(1)}, bf16[9,256,64]{1,2,0:T(8,128)(2,1)S(1)}, u32[]{:S(2)}, u32[]{:S(2)}) collective-permute-start(bf16[9,256,64]{1,2,0:T(8,128)(2,1)S(1)} %pad_maximum_fusion.1), channel_id=1, source_target_pairs={{4,12},{12,20},{20,28},{8,0},{16,8},{24,16},{5,13},{13,21},{21,29}... | collective-permute-start | bytes 884744 | tf_op jit(solution)/shard_map/ppermute | solution.py:90
  14.8 3.6 %collective-permute-done.2 = bf16[9,256,64]{1,2,0:T(8,128)(2,1)S(1)} collective-permute-done((bf16[9,256,64]{1,2,0:T(8,128)(2,1)S(1)}, bf16[9,256,64]{1,2,0:T(8,128)(2,1)S(1)}, u32[]{:S(2)}, u32[]{:S(2)}) %collective-permute-start.2) | collective-permute-done | bytes 294944 | tf_op jit(solution)/shard_map/ppermute | solution.py:90
  18.4 0.9 %fusion.25 = bf16[8,256,64]{1,2,0:T(8,128)(2,1)} fusion(f32[8]{0:T(128)S(1)} %get-tuple-element.116, bf16[9,256,64]{1,2,0:T(8,128)(2,1)S(1)} %collective-permute-done.2, bf16[9,256,64]{1,2,0:T(8,128)(2,1)S(1)} %collective-permute-done.1, f32[8]{0:T(128)S(1)} %get-tuple-element.122, f32[8,256,64]{1,2,0:T(8,128)S(1)} %convolution_bitcast_fusion.2, ...), kind=kLoop, calls=%fused_computation.39 | loop fusion | flops 1048576 | bytes 1835073 | tf_op jit(solution)/shard_map/convert_element_type | solution.py:84
  19.3 5.9 %collective-permute-start.3 = (bf16[8,256,64]{1,2,0:T(8,128)(2,1)}, bf16[8,256,64]{1,2,0:T(8,128)(2,1)}, u32[]{:S(2)}, u32[]{:S(2)}) collective-permute-start(bf16[8,256,64]{1,2,0:T(8,128)(2,1)} %fusion.25), channel_id=1, source_target_pairs={{4,20},{12,28},{16,0},{24,8},{5,21},{13,29},{17,1},{25,9},{6,22},{... | collective-permute-start | bytes 786440 | tf_op jit(solution)/shard_map/ppermute | solution.py:84
  25.2 0.6 %slice_convert_fusion.1 = f32[1,256,1]{1,2,0:T(1,128)} fusion(bf16[9,256,64]{1,2,0:T(8,128)(2,1)S(1)} %collective-permute-done.2), kind=kLoop, calls=%fused_computation.93 | loop fusion | flops 256 | bytes 1536 | tf_op jit(solution)/shard_map/convert_element_type | solution.py:55
  25.8 5.4 %conditional.1 = (f32[128,8,64]{0,2,1:T(8,128)S(1)}, f32[128,8]{0,1:T(8,128)S(1)}, f32[128,8]{0,1:T(8,128)S(1)}, f32[128,256]{1,0:T(8,128)S(1)}, f32[128,256]{1,0:T(8,128)S(1)}, /*index=5*/f32[128,512]{1,0:T(8,128)S(1)}) conditional(s32[]{:T(128)} %convert_element_type.98, () %tuple.19, (f32[128,8]{1,0:T(8,128)S(1)}, f32[128,256]{1,0:T(8,128)S(1)}, ...), branch_computations={%region_1.2_spmd, %region_2.4_spmd} | conditional | flops 356844544 | bytes 4583588 | solution.py:185
  25.8 0.3 fusion.75
  26.1 0.8 %fusion = f32[128,8,64]{0,2,1:T(8,128)S(1)} fusion(f32[128,8,64]{0,2,1:T(8,128)S(1)} %get-tuple-element.20, f32[8,128]{1,0:T(8,128)S(1)} %bitcast.103, f32[128,128]{1,0:T(8,128)S(1)} %fusion.75, f32[8,128]{1,0:T(8,128)S(1)} %bitcast.99, pred[128,128]{1,0:T(8,128)(4,1)S(1)} %iota_compare_fusion, f32[8]{0:T(128)S(1)} %get-tuple-element.72), kind=kOutput, calls=%fused_computation.1 | convolution fusion | flops 101318656 | bytes 614432 | tf_op jit(solution)/shard_map/cond/branch_1_fun/hts,thp->shp/dot_general | solution.py:162
  26.9 1.1 %fusion.5 = (f32[8,128]{1,0:T(8,128)S(1)}, f32[8,128,128]{2,1,0:T(8,128)S(1)}) fusion(f32[128,128]{1,0:T(8,128)S(1)} %fusion.75, f32[8,128]{1,0:T(8,128)S(1)} %bitcast.100, pred[128,128]{1,0:T(8,128)(4,1)S(1)} %iota_compare_fusion, f32[128,8,64]{0,2,1:T(8,128)S(1)} %get-tuple-element.20, f32[128,8,64]{0,2,1:T(8,128)S(1)} %get-tuple-element.22), kind=kOutput, calls=%fused_computation.7 | convolution fusion | flops 101317632 | bytes 1138688 | tf_op jit(solution)/shard_map/cond/branch_1_fun/thp,shp->hts/dot_general | solution.py:159
  28.0 1.1 %fusion.6 = f32[8,1,128]{2,1,0:T(1,128)S(1)} fusion(f32[8,128,1]{1,2,0:T(1,128)S(1)} %bitcast.104, f32[8,128,128]{2,1,0:T(8,128)S(1)} %get-tuple-element.119, f32[128,128]{1,0:T(8,128)S(1)} %fusion.75, f32[8,128]{1,0:T(8,128)S(1)} %bitcast.101, pred[128,128]{1,0:T(8,128)(4,1)S(1)} %iota_compare_fusion), kind=kOutput, calls=%fused_computation.8 | convolution fusion | flops 2097152 | bytes 618496 | tf_op jit(solution)/shard_map/cond/branch_1_fun/hts,hs->th/dot_general | solution.py:166
  29.1 0.6 %multiply_subtract_fusion = f32[128,8]{0,1:T(8,128)} fusion(f32[128,8]{0,1:T(8,128)S(1)} %bitcast.110, f32[128,8]{0,1:T(8,128)S(1)} %get-tuple-element.19, f32[8,128]{1,0:T(8,128)S(1)} %get-tuple-element.118), kind=kLoop, calls=%fused_computation.22 | loop fusion | flops 2048 | bytes 16384 | tf_op jit(solution)/shard_map/cond/branch_1_fun/sub | solution.py:171
  29.7 0.2 multiply_reduce_fusion
  29.9 0.3 fusion.76
  30.2 0.3 fusion.77
  30.6 0.6 %copy-done.8 = f32[8,128]{1,0:T(8,128)S(1)} copy-done((f32[8,128]{1,0:T(8,128)S(1)}, f32[8,128]{1,0:T(8,128)}, u32[]{:S(2)}) %copy-start.8) | copy-done | bytes 4120 | tf_op jit(solution)/shard_map/cond
  31.2 0.8 %fusion.54 = f32[8]{0:T(128)S(1)} fusion(f32[1,256,1]{1,2,0:T(1,128)} %slice_convert_fusion.1), kind=kLoop, calls=%fused_computation.97 | loop fusion | flops 8 | bytes 96 | tf_op jit(solution)/shard_map/add | solution.py:56
  32.0 1.1 %convert_add_fusion = f32[8,256,64]{1,2,0:T(8,128)S(1)} fusion(bf16[8,256,64]{1,2,0:T(8,128)(2,1)} %collective-permute-done.3, f32[8]{0:T(128)S(1)} %fusion.54, bf16[9,256,64]{1,2,0:T(8,128)(2,1)S(1)} %collective-permute-done.2), kind=kLoop, calls=%fused_computation.33 | loop fusion | flops 524288 | bytes 1048608 | tf_op jit(solution)/shard_map/add | solution.py:88
  33.1 1.9 %collective-permute-start.4 = (bf16[8,256,64]{1,2,0:T(8,128)(2,1)S(1)}, bf16[8,256,64]{1,2,0:T(8,128)(2,1)S(1)}, u32[]{:S(2)}, u32[]{:S(2)}) collective-permute-start(bf16[8,256,64]{1,2,0:T(8,128)(2,1)S(1)} %convert_element_type.99), channel_id=1, source_target_pairs={{0,4},{4,0},{8,12},{12,8},{16,20},{20,16},{24,28},{28,24},{1,5},{5... | collective-permute-start | bytes 786440 | tf_op jit(solution)/shard_map/ppermute | solution.py:99
  35.1 1.1 %collective-permute-done.4 = bf16[8,256,64]{1,2,0:T(8,128)(2,1)S(1)} collective-permute-done((bf16[8,256,64]{1,2,0:T(8,128)(2,1)S(1)}, bf16[8,256,64]{1,2,0:T(8,128)(2,1)S(1)}, u32[]{:S(2)}, u32[]{:S(2)}) %collective-permute-start.4) | collective-permute-done | bytes 262176 | tf_op jit(solution)/shard_map/ppermute | solution.py:99
  36.2 0.3 multiply_reduce_fusion.1
  36.5 0.4 multiply_reduce_fusion.2
  37.0 0.1 copy.56
  37.2 2.3 %collective-permute-start.5 = (f32[3,512]{1,0:T(4,128)S(1)}, f32[3,512]{1,0:T(4,128)S(1)}, u32[]{:S(2)}, u32[]{:S(2)}) collective-permute-start(f32[3,512]{1,0:T(4,128)S(1)} %slice.117), channel_id=1, source_target_pairs={{4,0},{8,4},{12,8},{16,12},{20,16},{24,20},{28,24},{5,1},{9,5},{13... | collective-permute-start | bytes 18440 | tf_op jit(solution)/shard_map/ppermute | solution.py:107
  39.5 0.6 %fusion.21 = f32[128,256]{1,0:T(8,128)S(1)} fusion(f32[128,256]{1,0:T(8,128)S(1)} %copy-done.4, f32[8,256,64]{1,2,0:T(8,128)S(1)} %get-tuple-element.114, f32[128,8,64]{0,2,1:T(8,128)S(1)} %bitcast.91, f32[128,8]{0,1:T(8,128)S(1)} %get-tuple-element.133), kind=kOutput, calls=%fused_computation.29 | convolution fusion | flops 201424896 | bytes 1052672 | tf_op jit(solution)/shard_map/lhp,hnp->ln/dot_general | solution.py:218
  40.1 0.6 %fusion.22 = f32[128,256]{1,0:T(8,128)S(1)} fusion(f32[128,256]{1,0:T(8,128)S(1)} %get-tuple-element.68, f32[8,256,64]{1,2,0:T(8,128)S(1)} %get-tuple-element.113, f32[128,8,64]{0,2,1:T(8,128)S(1)} %bitcast.94, f32[128,8]{0,1:T(8,128)S(1)} %get-tuple-element.134), kind=kOutput, calls=%fused_computation.30 | convolution fusion | flops 201424896 | bytes 1052672 | tf_op jit(solution)/shard_map/lhp,hnp->ln/dot_general | solution.py:215
  40.8 0.5 %collective-permute-start.6 = (bf16[128,256]{1,0:T(8,128)(2,1)S(1)}, bf16[128,256]{1,0:T(8,128)(2,1)S(1)}, u32[]{:S(2)}, u32[]{:S(2)}) collective-permute-start(bf16[128,256]{1,0:T(8,128)(2,1)S(1)} %pad_maximum_fusion.6), channel_id=1, source_target_pairs={{0,1},{1,0},{2,3},{3,2},{4,5},{5,4},{6,7},{7,6},{8,9},{9,8},{10,11... | collective-permute-start | bytes 196616 | tf_op jit(solution)/shard_map/ppermute | solution.py:16
  41.2 0.4 multiply_reduce_fusion.3
  41.6 0.7 %copy-done.15 = f32[8]{0:T(128)S(1)} copy-done((f32[8]{0:T(128)S(1)}, f32[8]{0:T(128)}, u32[]{:S(2)}) %copy-start.15) | copy-done | bytes 56
  42.3 0.7 %multiply_add_fusion.1 = (f32[128,8]{0,1:T(8,128)}, f32[128,8]{0,1:T(8,128)S(1)}) fusion(f32[128,8]{0,1:T(8,128)S(1)} %get-tuple-element.70, f32[128,8]{0,1:T(8,128)S(1)} %get-tuple-element.137, f32[128,8]{0,1:T(8,128)S(1)} %copy.52, f32[8]{0:T(128)S(1)} %copy-done.15, f32[8]{0:T(128)S(1)} %get-tuple-element.112, f32[128]{0:T(128)S(1)} %compare_convert_fusion, ...), kind=kLoop, calls=%fused_computation.82 | loop fusion | flops 9216 | bytes 33344 | tf_op jit(solution)/shard_map/add | solution.py:204
  43.1 0.2 reduce_window_sum.19
  43.3 0.7 %copy.58 = f32[128,8]{0,1:T(8,128)} copy(f32[128,8]{1,0:T(8,128)S(1)} %rev.8) | data formatting | bytes 8192
  44.0 0.8 %fusion.31 = bf16[128,512]{1,0:T(8,128)(2,1)} fusion(f32[128,512]{1,0:T(8,128)S(1)} %mul.203, f32[3,512]{1,0:T(4,128)S(1)} %collective-permute-done.5, f32[512]{0:T(512)S(1)} %bitcast.108, f32[512]{0:T(512)S(1)} %bitcast.109, f32[512]{0:T(512)S(1)} %bitcast.107, f32[512]{0:T(512)S(1)} %bitcast.106), kind=kLoop, calls=%fused_computation.53 | loop fusion | flops 720896 | bytes 407552 | tf_op jit(solution)/shard_map/convert_element_type | solution.py:238
  44.8 0.7 %slice_add_fusion = (f32[128,128]{1,0:T(8,128)}, f32[128,128]{1,0:T(8,128)}) fusion(f32[128,256]{1,0:T(8,128)S(1)} %convert_element_type.102, f32[128,256]{1,0:T(8,128)S(1)} %fusion.22, pred[]{:T(512)S(6)} %eq.21, f32[128,256]{1,0:T(8,128)S(1)} %fusion.21), kind=kLoop, calls=%fused_computation.75 | loop fusion | flops 65536 | bytes 524289 | tf_op jit(solution)/shard_map/add | solution.py:229
  (67 shorter events, 1.3 us)
Async XLA Ops:
  0.6 2.9 %copy-start.13 = (f32[128,8]{0,1:T(8,128)S(1)}, f32[128,8]{0,1:T(8,128)}, u32[]{:S(2)}) copy-start(f32[128,8]{0,1:T(8,128)} %param.14) | copy-start | bytes 12292
  1.4 4.9 %collective-permute-start = (bf16[128,256]{1,0:T(8,128)(2,1)S(1)}, bf16[128,256]{1,0:T(8,128)(2,1)S(1)}, u32[]{:S(2)}, u32[]{:S(2)}) collective-permute-start(bf16[128,256]{1,0:T(8,128)(2,1)S(1)} %pad_maximum_fusion.4), channel_id=1, source_target_pairs={{0,1},{1,0},{2,3},{3,2},{4,5},{5,4},{6,7},{7,6},{8,9},{9,8},{10,11... | collective-permute-start | bytes 196616 | tf_op jit(solution)/shard_map/ppermute | solution.py:16
  3.6 0.9 %copy-start = (bf16[128,512]{1,0:T(8,128)(2,1)S(1)}, bf16[128,512]{1,0:T(8,128)(2,1)}, u32[]{:S(2)}) copy-start(bf16[128,512]{1,0:T(8,128)(2,1)} %param.10) | copy-start | bytes 393220
  3.8 14.5 %copy-start.11 = (f32[8]{0:T(128)}, f32[8]{0:T(128)S(1)}, u32[]{:S(2)}) copy-start(f32[8]{0:T(128)S(1)} %get-tuple-element.122) | copy-start | bytes 100
  3.9 1.8 %copy-start.14 = (f32[8]{0:T(128)}, f32[8]{0:T(128)S(1)}, u32[]{:S(2)}) copy-start(f32[8]{0:T(128)S(1)} %slice_bitcast_fusion) | copy-start | bytes 100
  4.6 0.9 %copy-start.5 = (bf16[128,512]{1,0:T(8,128)(2,1)S(1)}, bf16[128,512]{1,0:T(8,128)(2,1)}, u32[]{:S(2)}) copy-start(bf16[128,512]{1,0:T(8,128)(2,1)} %param.11) | copy-start | bytes 393220
  5.5 0.7 %copy-start.6 = (f32[128,8]{0,1:T(8,128)S(1)}, f32[128,8]{0,1:T(8,128)}, u32[]{:S(2)}) copy-start(f32[128,8]{0,1:T(8,128)} %param.15) | copy-start | bytes 12292
  6.4 0.8 %copy-start.1 = (bf16[128,128]{1,0:T(8,128)(2,1)S(1)}, bf16[128,128]{1,0:T(8,128)(2,1)}, u32[]{:S(2)}) copy-start(bf16[128,128]{1,0:T(8,128)(2,1)} %param.12) | copy-start | bytes 98308
  7.1 0.8 %copy-start.2 = (bf16[128,128]{1,0:T(8,128)(2,1)S(1)}, bf16[128,128]{1,0:T(8,128)(2,1)}, u32[]{:S(2)}) copy-start(bf16[128,128]{1,0:T(8,128)(2,1)} %param.13) | copy-start | bytes 98308
  8.3 2.2 %collective-permute-start.1 = (bf16[9,256,64]{1,2,0:T(8,128)(2,1)S(1)}, bf16[9,256,64]{1,2,0:T(8,128)(2,1)S(1)}, u32[]{:S(2)}, u32[]{:S(2)}) collective-permute-start(bf16[9,256,64]{1,2,0:T(8,128)(2,1)S(1)} %pad_maximum_fusion), channel_id=1, source_target_pairs={{0,4},{4,0},{8,12},{12,8},{16,20},{20,16},{24,28},{28,24},{1,5},{5... | collective-permute-start | bytes 884744 | tf_op jit(solution)/shard_map/ppermute | solution.py:72
  11.5 6.9 %collective-permute-start.2 = (bf16[9,256,64]{1,2,0:T(8,128)(2,1)S(1)}, bf16[9,256,64]{1,2,0:T(8,128)(2,1)S(1)}, u32[]{:S(2)}, u32[]{:S(2)}) collective-permute-start(bf16[9,256,64]{1,2,0:T(8,128)(2,1)S(1)} %pad_maximum_fusion.1), channel_id=1, source_target_pairs={{4,12},{12,20},{20,28},{8,0},{16,8},{24,16},{5,13},{13,21},{21,29}... | collective-permute-start | bytes 884744 | tf_op jit(solution)/shard_map/ppermute | solution.py:90
  19.3 6.5 %copy-start.17 = (f32[8]{0:T(128)S(1)}, f32[8]{0:T(128)}, u32[]{:S(2)}) copy-start(f32[8]{0:T(128)} %param.16) | copy-start | bytes 100
  19.3 12.7 %collective-permute-start.3 = (bf16[8,256,64]{1,2,0:T(8,128)(2,1)}, bf16[8,256,64]{1,2,0:T(8,128)(2,1)}, u32[]{:S(2)}, u32[]{:S(2)}) collective-permute-start(bf16[8,256,64]{1,2,0:T(8,128)(2,1)} %fusion.25), channel_id=1, source_target_pairs={{4,20},{12,28},{16,0},{24,8},{5,21},{13,29},{17,1},{25,9},{6,22},{... | collective-permute-start | bytes 786440 | tf_op jit(solution)/shard_map/ppermute | solution.py:84
  28.0 1.1 %copy-start.7 = (f32[8,128]{1,0:T(8,128)}, f32[8,128]{1,0:T(8,128)S(1)}, u32[]{:S(2)}) copy-start(f32[8,128]{1,0:T(8,128)S(1)} %get-tuple-element.118) | copy-start | bytes 12292 | tf_op jit(solution)/shard_map/cond
  30.5 0.7 %copy-start.8 = (f32[8,128]{1,0:T(8,128)S(1)}, f32[8,128]{1,0:T(8,128)}, u32[]{:S(2)}) copy-start(f32[8,128]{1,0:T(8,128)} %copy-done.7) | copy-start | bytes 12292 | tf_op jit(solution)/shard_map/cond
  30.5 0.7 %copy-start.9 = (f32[128,8]{0,1:T(8,128)S(1)}, f32[128,8]{0,1:T(8,128)}, u32[]{:S(2)}) copy-start(f32[128,8]{0,1:T(8,128)} %multiply_subtract_fusion) | copy-start | bytes 12292 | tf_op jit(solution)/shard_map/cond
  31.2 1.9 %copy-start.3 = (f32[128,256]{1,0:T(8,128)}, f32[128,256]{1,0:T(8,128)S(1)}, u32[]{:S(2)}) copy-start(f32[128,256]{1,0:T(8,128)S(1)} %get-tuple-element.67) | copy-start | bytes 393220
  33.1 1.9 %copy-start.10 = (f32[4,512]{1,0:T(4,128)S(1)}, f32[4,512]{1,0:T(4,128)}, u32[]{:S(2)}) copy-start(f32[4,512]{1,0:T(4,128)} %param.17) | copy-start | bytes 24580
  33.1 3.0 %collective-permute-start.4 = (bf16[8,256,64]{1,2,0:T(8,128)(2,1)S(1)}, bf16[8,256,64]{1,2,0:T(8,128)(2,1)S(1)}, u32[]{:S(2)}, u32[]{:S(2)}) collective-permute-start(bf16[8,256,64]{1,2,0:T(8,128)(2,1)S(1)} %convert_element_type.99), channel_id=1, source_target_pairs={{0,4},{4,0},{8,12},{12,8},{16,20},{20,16},{24,28},{28,24},{1,5},{5... | collective-permute-start | bytes 786440 | tf_op jit(solution)/shard_map/ppermute | solution.py:99
  35.0 1.1 %copy-start.12 = (f32[8]{0:T(128)S(1)}, f32[8]{0:T(128)}, u32[]{:S(2)}) copy-start(f32[8]{0:T(128)} %copy-done.11) | copy-start | bytes 100
  35.1 1.1 %copy-start.16 = (f32[8]{0:T(128)S(1)}, f32[8]{0:T(128)}, u32[]{:S(2)}) copy-start(f32[8]{0:T(128)} %get-tuple-element.117) | copy-start | bytes 100
  37.1 2.4 %copy-start.4 = (f32[128,256]{1,0:T(8,128)S(1)}, f32[128,256]{1,0:T(8,128)}, u32[]{:S(2)}) copy-start(f32[128,256]{1,0:T(8,128)} %copy-done.3) | copy-start | bytes 393220
  37.2 6.8 %collective-permute-start.5 = (f32[3,512]{1,0:T(4,128)S(1)}, f32[3,512]{1,0:T(4,128)S(1)}, u32[]{:S(2)}, u32[]{:S(2)}) collective-permute-start(f32[3,512]{1,0:T(4,128)S(1)} %slice.117), channel_id=1, source_target_pairs={{4,0},{8,4},{12,8},{16,12},{20,16},{24,20},{28,24},{5,1},{9,5},{13... | collective-permute-start | bytes 18440 | tf_op jit(solution)/shard_map/ppermute | solution.py:107
  40.8 4.0 %collective-permute-start.6 = (bf16[128,256]{1,0:T(8,128)(2,1)S(1)}, bf16[128,256]{1,0:T(8,128)(2,1)S(1)}, u32[]{:S(2)}, u32[]{:S(2)}) collective-permute-start(bf16[128,256]{1,0:T(8,128)(2,1)S(1)} %pad_maximum_fusion.6), channel_id=1, source_target_pairs={{0,1},{1,0},{2,3},{3,2},{4,5},{5,4},{6,7},{7,6},{8,9},{9,8},{10,11... | collective-permute-start | bytes 196616 | tf_op jit(solution)/shard_map/ppermute | solution.py:16
  41.6 0.7 %copy-start.15 = (f32[8]{0:T(128)S(1)}, f32[8]{0:T(128)}, u32[]{:S(2)}) copy-start(f32[8]{0:T(128)} %copy-done.14) | copy-start | bytes 100

commit v10 on v9

--- a/solution.py
+++ b/solution.py
@@ -50,6 +50,20 @@
     return jnp.concatenate([state.astype(kind), slab], 0)
 
 
+def split_packed(decay, state):
+    high = state.astype(jnp.bfloat16)
+    low = (state - high.astype(state.dtype)).astype(jnp.bfloat16)
+    return jnp.concatenate([high, low, packed(decay, state, jnp.bfloat16)[-1:]], 0)
+
+
+def split_unpacked(message):
+    heads = (message.shape[0] - 1) // 2
+    row = message[2 * heads, :, 0].astype(jnp.float32)
+    decay = row[:heads] + row[heads : 2 * heads]
+    both = message[: 2 * heads].astype(jnp.float32)
+    return decay, both[:heads] + both[heads:]
+
+
 def unpacked(message):
     heads = message.shape[0] - 1
     row = message[heads, :, 0].astype(jnp.float32)
@@ -65,14 +79,14 @@
     is_odd = lax.axis_index(axis) % 2 == 1
     swap = [(i, i ^ 1) for i in range(peers)]
     sent = jnp.where(is_odd, state_grad, state)
-    message = packed(decay, sent, jnp.bfloat16)
+    message = split_packed(decay, sent)
     if peers == 2:
         message, rider_inputs = lax.optimization_barrier((message, rider_inputs))
         riders = rider_fn(*rider_inputs)
     mate = lax.ppermute(message, axis, swap)
     if peers == 2:
         mate, riders = lax.optimization_barrier((mate, riders))
-    mate_a, mate_s = unpacked(mate)
+    mate_a, mate_s = split_unpacked(mate)
     own = jnp.where(is_odd, state, state_grad)
     window = (decay * mate_a, own + decay[:, None, None] * mate_s)
     near = (jnp.ones_like(decay), jnp.zeros_like(own))
@@ -96,7 +110,10 @@
             window = (window[0] * far_a, window[1] + window[0][:, None, None] * far_s)
         distance *= 2
     passing, riders = lax.optimization_barrier((near[1], riders))
-    handed = lax.ppermute(passing.astype(jnp.bfloat16), axis, swap).astype(jnp.float32)
+    high = passing.astype(jnp.bfloat16)
+    low = (passing - high.astype(passing.dtype)).astype(jnp.bfloat16)
+    handed = lax.ppermute(jnp.concatenate([high, low], 0), axis, swap).astype(jnp.float32)
+    handed = handed[: passing.shape[0]] + handed[passing.shape[0] :]
     mine = mate_s + mate_a[:, None, None] * near[1]
     return jnp.where(is_odd, mine, handed), jnp.where(is_odd, handed, mine), riders
 

time: 46.3 us -> 52 us (1.12)
  local copies, waits for them, and re-layouts: 5.84 us -> 10.4 us
  starting transfers between devices: 16.9 us -> 14.7 us
  other arithmetic: 9.31 us -> 11.3 us
  matrix products: 6.49 us -> 7.81 us
    unnamed x32 -> x44, local copies, waits for them, and re-layouts: 4.58 us -> 8.5 us
    ppermute x1, starting transfers between devices: 1.88 us -> 0.07 us  [paired_scan(): lax.ppermute(jnp.concatenate([high, low], 0), axis, swap)]
    convert_element_type x1, other arithmetic: 0.01 us -> 0.87 us  [body(): queries_full = jnp.where(own_first, jnp.concatenate([read_queries, partne...]
    concatenate x2 -> x1, other arithmetic: 0.06 us -> 0.75 us  [packed(): return jnp.concatenate([state.astype(kind), slab], 0)]
    cond x6 -> x8, local copies, waits for them, and re-layouts: 0.59 us -> 1.26 us
    dot_general x1, matrix products: 0.31 us -> 0.97 us  [local_terms(): lax.dot_general(weight_sum, queries_full, (((0,), (0,)), ((), ())), prefe...]
    dot_general x2, matrix products: 0.54 us -> 1.2 us  [product(): jnp.dot(left, right, preferred_element_type=jnp.float32, precision=precise)]
  transfers between devices with their start and end apart: 7 -> 7, of which waited for: 3 -> 3; matrix products, arithmetic and copies ran while one was open for 24% -> 26% of each run, Pallas kernels for 0% -> 0%
where the time goes in v10:
time: 52 us; the launch traced here: 51.2 us
  starting transfers between devices  14.7 us (28%)
  other arithmetic  11.3 us (22%)
  local copies, waits for them, and re-layouts  10.4 us (20%)
  matrix products  7.81 us (15%)
  waiting for transfers between devices  5.97 us (11%)
  between operations  1.03 us (2%)
    unnamed x44, local copies, waits for them, and re-layouts  8.5 us
    ppermute x1, starting transfers between devices, paired_scan(): far_s = lax.ppermute(window[1].astype(jnp.bfloat16), axis, route)  5.72 us
    ppermute x1, starting transfers between devices, paired_scan(): far = lax.ppermute(packed(*window, jnp.bfloat16), axis, route)  3.2 us
    ppermute x1, waiting for transfers between devices, paired_scan(): far = lax.ppermute(packed(*window, jnp.bfloat16), axis, route)  3.04 us
    ppermute x2, starting transfers between devices, swapped(): return lax.ppermute(block, axis, route)  2.6 us
    ppermute x1, starting transfers between devices, shifted(): return lax.ppermute(block, axis, route)  2.05 us
    ppermute x1, waiting for transfers between devices, paired_scan(): mate = lax.ppermute(message, axis, swap)  1.58 us
    ppermute x1, waiting for transfers between devices, paired_scan(): lax.ppermute(jnp.concatenate([high, low], 0), axis, swap)  1.34 us
  transfers between devices with their start and end apart: 7, of which 3 were waited for; matrix products, arithmetic and copies ran while one was open for 26% of the time, Pallas kernels for 0%

profile of v10, /device:TPU:1, one launch (start us, length us, event | category | flops | bytes accessed | tf_op | source)
XLA Modules:
  0.0 51.2 jit_solution(6141868078086761677)
XLA Ops:
  0.6 0.8 %pad_maximum_fusion.5 = bf16[128,256]{1,0:T(8,128)(2,1)S(1)} fusion(bf16[128,128]{1,0:T(8,128)(2,1)} %param.13, bf16[128,128]{1,0:T(8,128)(2,1)} %param.12), kind=kLoop, calls=%fused_computation.77 | loop fusion | flops 131072 | bytes 131072 | tf_op jit(solution)/shard_map/concatenate | solution.py:140
  1.4 2.1 %collective-permute-start = (bf16[128,256]{1,0:T(8,128)(2,1)S(1)}, bf16[128,256]{1,0:T(8,128)(2,1)S(1)}, u32[]{:S(2)}, u32[]{:S(2)}) collective-permute-start(bf16[128,256]{1,0:T(8,128)(2,1)S(1)} %pad_maximum_fusion.5), channel_id=1, source_target_pairs={{0,1},{1,0},{2,3},{3,2},{4,5},{5,4},{6,7},{7,6},{8,9},{9,8},{10,11... | collective-permute-start | bytes 196616 | tf_op jit(solution)/shard_map/ppermute | solution.py:16
  3.9 0.7 %copy-done = bf16[128,512]{1,0:T(8,128)(2,1)S(1)} copy-done((bf16[128,512]{1,0:T(8,128)(2,1)S(1)}, bf16[128,512]{1,0:T(8,128)(2,1)}, u32[]{:S(2)}) %copy-start) | copy-done | bytes 131096
  4.8 0.7 %copy-done.10 = bf16[128,512]{1,0:T(8,128)(2,1)S(1)} copy-done((bf16[128,512]{1,0:T(8,128)(2,1)S(1)}, bf16[128,512]{1,0:T(8,128)(2,1)}, u32[]{:S(2)}) %copy-start.10) | copy-done | bytes 131096
  5.6 0.6 %copy-done.11 = f32[128,8]{0,1:T(8,128)S(1)} copy-done((f32[128,8]{0,1:T(8,128)S(1)}, f32[128,8]{0,1:T(8,128)}, u32[]{:S(2)}) %copy-start.11) | copy-done | bytes 4120
  6.4 0.7 %copy-done.1 = bf16[128,128]{1,0:T(8,128)(2,1)S(1)} copy-done((bf16[128,128]{1,0:T(8,128)(2,1)S(1)}, bf16[128,128]{1,0:T(8,128)(2,1)}, u32[]{:S(2)}) %copy-start.1) | copy-done | bytes 32792
  7.1 0.4 convolution_bitcast_fusion.2
  7.5 0.4 copy-done.2
  7.9 0.4 subtract_convert_fusion.1
  8.4 1.0 %collective-permute-start.1 = (bf16[17,256,64]{1,2,0:T(8,128)(2,1)S(1)}, bf16[17,256,64]{1,2,0:T(8,128)(2,1)S(1)}, u32[]{:S(2)}, u32[]{:S(2)}) collective-permute-start(bf16[17,256,64]{1,2,0:T(8,128)(2,1)S(1)} %pad_maximum_fusion), channel_id=1, source_target_pairs={{0,4},{4,0},{8,12},{12,8},{16,20},{20,16},{24,28},{28,24},{1,5},{5... | collective-permute-start | bytes 1671176 | tf_op jit(solution)/shard_map/ppermute | solution.py:86
  9.5 1.6 %collective-permute-done.1 = bf16[17,256,64]{1,2,0:T(8,128)(2,1)S(1)} collective-permute-done((bf16[17,256,64]{1,2,0:T(8,128)(2,1)S(1)}, bf16[17,256,64]{1,2,0:T(8,128)(2,1)S(1)}, u32[]{:S(2)}, u32[]{:S(2)}) %collective-permute-start.1) | collective-permute-done | bytes 557088 | tf_op jit(solution)/shard_map/ppermute | solution.py:86
  11.1 0.6 %fusion.70 = (bf16[8]{0:T(256)(128)(2,1)S(1)}, f32[8]{0:T(128)S(1)}, f32[8]{0:T(128)}) fusion(f32[128,8]{1,0:T(8,128)S(1)} %reduce_window_sum.18, f32[1,256,1]{1,2,0:T(1,128)S(1)} %slice_convert_fusion.1), kind=kLoop, calls=%fused_computation.117 | loop fusion | flops 24 | bytes 176 | tf_op jit(solution)/shard_map/convert_element_type | solution.py:46
  11.7 0.5 copy-done.22
  12.6 0.8 %pad_maximum_fusion.2 = bf16[9,256,64]{1,2,0:T(8,128)(2,1)} fusion(bf16[1,256,64]{1,2,0:T(8,128)(2,1)S(1)} %broadcast_in_dim.13, bf16[8,256,64]{1,2,0:T(8,128)(2,1)S(1)} %get-tuple-element.119), kind=kLoop, calls=%fused_computation.47 | loop fusion | flops 147456 | bytes 589824 | tf_op jit(solution)/shard_map/concatenate | solution.py:50
  13.4 3.2 %collective-permute-start.2 = (bf16[9,256,64]{1,2,0:T(8,128)(2,1)}, bf16[9,256,64]{1,2,0:T(8,128)(2,1)S(1)}, u32[]{:S(2)}, u32[]{:S(2)}) collective-permute-start(bf16[9,256,64]{1,2,0:T(8,128)(2,1)} %pad_maximum_fusion.2), channel_id=1, source_target_pairs={{4,12},{12,20},{20,28},{8,0},{16,8},{24,16},{5,13},{13,21},{21,29}... | collective-permute-start | bytes 884744 | tf_op jit(solution)/shard_map/ppermute | solution.py:104
  16.6 0.9 %fusion.61 = (f32[128,256]{1,0:T(8,128)S(1)}, f32[128,256]{1,0:T(8,128)S(1)}) fusion(bf16[128,128]{1,0:T(8,128)(2,1)} %param.13, bf16[128,128]{1,0:T(8,128)(2,1)} %copy-done.4, pred[]{:T(512)S(6)} %eq.21, bf16[128,128]{1,0:T(8,128)(2,1)S(1)} %copy-done.1, bf16[128,128]{1,0:T(8,128)(2,1)} %copy-done.6), kind=kLoop, calls=%fused_computation.113 | loop fusion | flops 655360 | bytes 393217 | tf_op jit(solution)/shard_map/convert_element_type | solution.py:151
  17.5 3.0 %collective-permute-done.2 = bf16[9,256,64]{1,2,0:T(8,128)(2,1)S(1)} collective-permute-done((bf16[9,256,64]{1,2,0:T(8,128)(2,1)}, bf16[9,256,64]{1,2,0:T(8,128)(2,1)S(1)}, u32[]{:S(2)}, u32[]{:S(2)}) %collective-permute-start.2) | collective-permute-done | bytes 294944 | tf_op jit(solution)/shard_map/ppermute | solution.py:104
  20.5 0.7 %copy-done.23 = f32[8]{0:T(128)S(1)} copy-done((f32[8]{0:T(128)S(1)}, f32[8]{0:T(128)}, u32[]{:S(2)}) %copy-start.23) | copy-done | bytes 56
  21.2 0.8 %fusion.24 = bf16[8,256,64]{1,2,0:T(8,128)(2,1)} fusion(f32[8,256,64]{1,2,0:T(8,128)S(1)} %get-tuple-element.120, f32[8]{0:T(128)S(1)} %copy-done.23, bf16[9,256,64]{1,2,0:T(8,128)(2,1)S(1)} %collective-permute-done.2), kind=kLoop, calls=%fused_computation.35 | loop fusion | flops 524288 | bytes 1048608 | tf_op jit(solution)/shard_map/convert_element_type | solution.py:98
  22.0 5.7 %collective-permute-start.3 = (bf16[8,256,64]{1,2,0:T(8,128)(2,1)}, bf16[8,256,64]{1,2,0:T(8,128)(2,1)}, u32[]{:S(2)}, u32[]{:S(2)}) collective-permute-start(bf16[8,256,64]{1,2,0:T(8,128)(2,1)} %fusion.24), channel_id=1, source_target_pairs={{4,20},{12,28},{16,0},{24,8},{5,21},{13,29},{17,1},{25,9},{6,22},{... | collective-permute-start | bytes 786440 | tf_op jit(solution)/shard_map/ppermute | solution.py:98
  27.7 0.6 %slice_convert_fusion.2 = f32[1,256,1]{1,2,0:T(1,128)} fusion(bf16[9,256,64]{1,2,0:T(8,128)(2,1)S(1)} %collective-permute-done.2), kind=kLoop, calls=%fused_computation.99 | loop fusion | flops 256 | bytes 1536 | tf_op jit(solution)/shard_map/convert_element_type | solution.py:69
  28.3 7.4 %conditional.1 = (f32[128,8,64]{0,2,1:T(8,128)S(1)}, f32[128,8]{0,1:T(8,128)S(1)}, f32[128,8]{0,1:T(8,128)S(1)}, f32[128,256]{1,0:T(8,128)}, f32[128,256]{1,0:T(8,128)}, /*index=5*/f32[128,512]{1,0:T(8,128)S(1)}) conditional(s32[]{:T(128)} %convert_element_type.112, () %tuple.19, (f32[128,8]{1,0:T(8,128)S(1)}, f32[128,256]{1,0:T(8,128)S(1)}, ...), branch_computations={%region_1.2_spmd, %region_2.4_spmd} | conditional | flops 356844544 | bytes 4583744 | solution.py:202
  28.7 0.6 %copy-done.24 = f32[8]{0:T(128)S(1)} copy-done((f32[8]{0:T(128)S(1)}, f32[8]{0:T(128)}, u32[]{:S(2)}) %copy-start.24) | copy-done | bytes 56 | tf_op jit(solution)/shard_map/cond
  29.4 0.8 %fusion = f32[128,8,64]{0,2,1:T(8,128)S(1)} fusion(f32[128,8,64]{0,2,1:T(8,128)S(1)} %get-tuple-element.20, f32[8,128]{1,0:T(8,128)S(1)} %bitcast.103, f32[128,128]{1,0:T(8,128)S(1)} %fusion.75, f32[8,128]{1,0:T(8,128)S(1)} %bitcast.99, pred[128,128]{1,0:T(8,128)(4,1)S(1)} %iota_compare_fusion, f32[8]{0:T(128)S(1)} %copy-done.24), kind=kOutput, calls=%fused_computation.1 | convolution fusion | flops 101318656 | bytes 614432 | tf_op jit(solution)/shard_map/cond/branch_1_fun/hts,thp->shp/dot_general | solution.py:179
  30.1 1.1 %fusion.5 = (f32[8,128]{1,0:T(8,128)S(1)}, f32[8,128,128]{2,1,0:T(8,128)S(1)}) fusion(f32[128,128]{1,0:T(8,128)S(1)} %fusion.75, f32[8,128]{1,0:T(8,128)S(1)} %bitcast.100, pred[128,128]{1,0:T(8,128)(4,1)S(1)} %iota_compare_fusion, f32[128,8,64]{0,2,1:T(8,128)S(1)} %get-tuple-element.20, f32[128,8,64]{0,2,1:T(8,128)S(1)} %get-tuple-element.22), kind=kOutput, calls=%fused_computation.7 | convolution fusion | flops 101317632 | bytes 1138688 | tf_op jit(solution)/shard_map/cond/branch_1_fun/thp,shp->hts/dot_general | solution.py:176
  31.2 1.1 %fusion.6 = f32[8,1,128]{2,1,0:T(1,128)S(1)} fusion(f32[8,128,1]{1,2,0:T(1,128)S(1)} %bitcast.104, f32[8,128,128]{2,1,0:T(8,128)S(1)} %get-tuple-element.125, f32[128,128]{1,0:T(8,128)S(1)} %fusion.75, f32[8,128]{1,0:T(8,128)S(1)} %bitcast.101, pred[128,128]{1,0:T(8,128)(4,1)S(1)} %iota_compare_fusion), kind=kOutput, calls=%fused_computation.8 | convolution fusion | flops 2097152 | bytes 618496 | tf_op jit(solution)/shard_map/cond/branch_1_fun/hts,hs->th/dot_general | solution.py:183
  32.3 0.6 %multiply_subtract_fusion = f32[128,8]{0,1:T(8,128)} fusion(f32[128,8]{0,1:T(8,128)S(1)} %bitcast.110, f32[128,8]{0,1:T(8,128)S(1)} %get-tuple-element.19, f32[8,128]{1,0:T(8,128)S(1)} %get-tuple-element.124), kind=kLoop, calls=%fused_computation.22 | loop fusion | flops 2048 | bytes 16384 | tf_op jit(solution)/shard_map/cond/branch_1_fun/sub | solution.py:188
  33.1 0.9 %fusion.76 = f32[128,256]{1,0:T(8,128)} fusion(f32[128,128]{0,1:T(8,128)S(1)} %multiply_reduce_fusion, f32[128,256]{1,0:T(8,128)S(1)} %get-tuple-element.18), kind=kOutput, calls=%fused_computation.121 | convolution fusion | flops 50331648 | bytes 327680 | tf_op jit(solution)/shard_map/cond/branch_1_fun/dot_general | solution.py:128
  34.0 1.0 %fusion.77 = f32[128,256]{1,0:T(8,128)} fusion(f32[128,128]{0,1:T(8,128)S(1)} %multiply_reduce_fusion, f32[128,256]{1,0:T(8,128)S(1)} %get-tuple-element.17), kind=kOutput, calls=%fused_computation.122 | convolution fusion | flops 50331648 | bytes 327680 | tf_op jit(solution)/shard_map/cond/branch_1_fun/dot_general | solution.py:191
  35.1 0.6 %copy-done.13 = f32[8,128]{1,0:T(8,128)S(1)} copy-done((f32[8,128]{1,0:T(8,128)S(1)}, f32[8,128]{1,0:T(8,128)}, u32[]{:S(2)}) %copy-start.13) | copy-done | bytes 4120 | tf_op jit(solution)/shard_map/cond
  35.7 0.8 %fusion.54 = f32[8]{0:T(128)S(1)} fusion(f32[1,256,1]{1,2,0:T(1,128)} %slice_convert_fusion.2), kind=kLoop, calls=%fused_computation.103 | loop fusion | flops 8 | bytes 96 | tf_op jit(solution)/shard_map/add | solution.py:70
  36.5 0.7 %copy-done.21 = f32[8]{0:T(128)S(1)} copy-done((f32[8]{0:T(128)S(1)}, f32[8]{0:T(128)}, u32[]{:S(2)}) %copy-start.21) | copy-done | bytes 56
  37.2 1.2 %multiply_add_fusion = (f32[8,256,64]{1,2,0:T(8,128)S(1)}, f32[8,256,64]{1,2,0:T(8,128)S(1)}) fusion(f32[8]{0:T(128)S(1)} %copy-done.21, f32[16,256,64]{1,2,0:T(8,128)S(1)} %slice_convert_fusion, bf16[8,256,64]{1,2,0:T(8,128)(2,1)} %collective-permute-done.3, f32[8]{0:T(128)S(1)} %fusion.54, bf16[9,256,64]{1,2,0:T(8,128)(2,1)S(1)} %collective-permute-done.2), kind=kLoop, calls=%fused_computation.41 | loop fusion | flops 917504 | bytes 2621504 | tf_op jit(solution)/shard_map/add | solution.py:117
  38.6 0.5 %copy-done.15 = f32[4,512]{1,0:T(4,128)S(1)} copy-done((f32[4,512]{1,0:T(4,128)S(1)}, f32[4,512]{1,0:T(4,128)}, u32[]{:S(2)}) %copy-start.15) | copy-done | bytes 8216
  39.1 1.3 %collective-permute-done.4 = bf16[16,256,64]{1,2,0:T(8,128)(2,1)S(1)} collective-permute-done((bf16[16,256,64]{1,2,0:T(8,128)(2,1)S(1)}, bf16[16,256,64]{1,2,0:T(8,128)(2,1)S(1)}, u32[]{:S(2)}, u32[]{:S(2)}) %collective-permute-start.4) | collective-permute-done | bytes 524320 | tf_op jit(solution)/shard_map/ppermute | solution.py:115
  40.6 0.6 %copy-done.17 = f32[8]{0:T(128)S(1)} copy-done((f32[8]{0:T(128)S(1)}, f32[8]{0:T(128)}, u32[]{:S(2)}) %copy-start.17) | copy-done | bytes 56
  41.5 0.5 copy-done.7
  42.0 0.4 multiply_reduce_fusion.2
  42.6 2.0 %collective-permute-start.5 = (f32[3,512]{1,0:T(4,128)S(1)}, f32[3,512]{1,0:T(4,128)S(1)}, u32[]{:S(2)}, u32[]{:S(2)}) collective-permute-start(f32[3,512]{1,0:T(4,128)S(1)} %slice.137), channel_id=1, source_target_pairs={{4,0},{8,4},{12,8},{16,12},{20,16},{24,20},{28,24},{5,1},{9,5},{13... | collective-permute-start | bytes 18440 | tf_op jit(solution)/shard_map/ppermute | solution.py:124
  44.7 0.6 %fusion.22 = f32[128,256]{1,0:T(8,128)S(1)} fusion(f32[128,256]{1,0:T(8,128)S(1)} %copy-done.8, f32[8,256,64]{1,2,0:T(8,128)S(1)} %get-tuple-element.113, f32[128,8,64]{0,2,1:T(8,128)S(1)} %bitcast.94, f32[128,8]{0,1:T(8,128)S(1)} %get-tuple-element.140), kind=kOutput, calls=%fused_computation.30 | convolution fusion | flops 201424896 | bytes 1052672 | tf_op jit(solution)/shard_map/lhp,hnp->ln/dot_general | solution.py:232
  45.6 0.6 %fusion.21 = f32[128,256]{1,0:T(8,128)S(1)} fusion(f32[128,256]{1,0:T(8,128)S(1)} %copy-done.9, f32[8,256,64]{1,2,0:T(8,128)S(1)} %get-tuple-element.114, f32[128,8,64]{0,2,1:T(8,128)S(1)} %bitcast.91, f32[128,8]{0,1:T(8,128)S(1)} %get-tuple-element.139), kind=kOutput, calls=%fused_computation.29 | convolution fusion | flops 201424896 | bytes 1052672 | tf_op jit(solution)/shard_map/lhp,hnp->ln/dot_general | solution.py:235
  46.2 0.5 collective-permute-start.6
  47.0 0.4 multiply_reduce_fusion.3
  47.4 0.7 %copy-done.20 = f32[8]{0:T(128)S(1)} copy-done((f32[8]{0:T(128)S(1)}, f32[8]{0:T(128)}, u32[]{:S(2)}) %copy-start.20) | copy-done | bytes 56
  48.0 0.7 %multiply_add_fusion.3 = (f32[128,8]{0,1:T(8,128)}, f32[128,8]{0,1:T(8,128)S(1)}) fusion(f32[128,8]{0,1:T(8,128)S(1)} %get-tuple-element.70, f32[128,8]{0,1:T(8,128)S(1)} %get-tuple-element.143, f32[128,8]{0,1:T(8,128)S(1)} %copy.52, f32[8]{0:T(128)S(1)} %copy-done.20, f32[8]{0:T(128)S(1)} %get-tuple-element.112, f32[128]{0:T(128)S(1)} %compare_convert_fusion, ...), kind=kLoop, calls=%fused_computation.88 | loop fusion | flops 9216 | bytes 33344 | tf_op jit(solution)/shard_map/add | solution.py:221
  49.1 0.7 %copy.58 = f32[128,8]{0,1:T(8,128)} copy(f32[128,8]{1,0:T(8,128)S(1)} %rev.8) | data formatting | bytes 8192
  49.7 0.8 %fusion.30 = bf16[128,512]{1,0:T(8,128)(2,1)} fusion(f32[128,512]{1,0:T(8,128)S(1)} %mul.203, f32[3,512]{1,0:T(4,128)S(1)} %collective-permute-done.5, f32[512]{0:T(512)S(1)} %bitcast.108, f32[512]{0:T(512)S(1)} %bitcast.109, f32[512]{0:T(512)S(1)} %bitcast.107, f32[512]{0:T(512)S(1)} %bitcast.106), kind=kLoop, calls=%fused_computation.55 | loop fusion | flops 720896 | bytes 407552 | tf_op jit(solution)/shard_map/convert_element_type | solution.py:255
  50.5 0.7 %slice_add_fusion.2 = (f32[128,128]{1,0:T(8,128)}, f32[128,128]{1,0:T(8,128)}) fusion(f32[128,256]{1,0:T(8,128)S(1)} %convert_element_type.118, f32[128,256]{1,0:T(8,128)S(1)} %fusion.22, pred[]{:T(512)S(6)} %eq.21, f32[128,256]{1,0:T(8,128)S(1)} %fusion.21), kind=kLoop, calls=%fused_computation.81 | loop fusion | flops 65536 | bytes 524289 | tf_op jit(solution)/shard_map/add | solution.py:246
  (85 shorter events, 3.8 us)
Async XLA Ops:
  0.6 2.9 %copy-start.18 = (f32[128,8]{0,1:T(8,128)S(1)}, f32[128,8]{0,1:T(8,128)}, u32[]{:S(2)}) copy-start(f32[128,8]{0,1:T(8,128)} %param.14) | copy-start | bytes 12292
  1.4 4.9 %collective-permute-start = (bf16[128,256]{1,0:T(8,128)(2,1)S(1)}, bf16[128,256]{1,0:T(8,128)(2,1)S(1)}, u32[]{:S(2)}, u32[]{:S(2)}) collective-permute-start(bf16[128,256]{1,0:T(8,128)(2,1)S(1)} %pad_maximum_fusion.5), channel_id=1, source_target_pairs={{0,1},{1,0},{2,3},{3,2},{4,5},{5,4},{6,7},{7,6},{8,9},{9,8},{10,11... | collective-permute-start | bytes 196616 | tf_op jit(solution)/shard_map/ppermute | solution.py:16
  3.6 0.9 %copy-start = (bf16[128,512]{1,0:T(8,128)(2,1)S(1)}, bf16[128,512]{1,0:T(8,128)(2,1)}, u32[]{:S(2)}) copy-start(bf16[128,512]{1,0:T(8,128)(2,1)} %param.10) | copy-start | bytes 393220
  3.8 8.5 %copy-start.16 = (f32[8]{0:T(128)}, f32[8]{0:T(128)S(1)}, u32[]{:S(2)}) copy-start(f32[8]{0:T(128)S(1)} %get-tuple-element.128) | copy-start | bytes 100
  3.9 1.8 %copy-start.19 = (f32[8]{0:T(128)}, f32[8]{0:T(128)S(1)}, u32[]{:S(2)}) copy-start(f32[8]{0:T(128)S(1)} %slice_bitcast_fusion) | copy-start | bytes 100
  4.6 0.9 %copy-start.10 = (bf16[128,512]{1,0:T(8,128)(2,1)S(1)}, bf16[128,512]{1,0:T(8,128)(2,1)}, u32[]{:S(2)}) copy-start(bf16[128,512]{1,0:T(8,128)(2,1)} %param.11) | copy-start | bytes 393220
  5.5 0.7 %copy-start.11 = (f32[128,8]{0,1:T(8,128)S(1)}, f32[128,8]{0,1:T(8,128)}, u32[]{:S(2)}) copy-start(f32[128,8]{0,1:T(8,128)} %param.15) | copy-start | bytes 12292
  6.4 0.8 %copy-start.1 = (bf16[128,128]{1,0:T(8,128)(2,1)S(1)}, bf16[128,128]{1,0:T(8,128)(2,1)}, u32[]{:S(2)}) copy-start(bf16[128,128]{1,0:T(8,128)(2,1)} %param.12) | copy-start | bytes 98308
  6.4 1.1 %copy-start.6 = (bf16[128,128]{1,0:T(8,128)(2,1)}, bf16[128,128]{1,0:T(8,128)(2,1)S(1)}, u32[]{:S(2)}) copy-start(bf16[128,128]{1,0:T(8,128)(2,1)S(1)} %get-tuple-element.131) | copy-start | bytes 98308
  6.4 1.1 %copy-start.4 = (bf16[128,128]{1,0:T(8,128)(2,1)}, bf16[128,128]{1,0:T(8,128)(2,1)S(1)}, u32[]{:S(2)}) copy-start(bf16[128,128]{1,0:T(8,128)(2,1)S(1)} %get-tuple-element.132) | copy-start | bytes 98308
  7.1 0.8 %copy-start.2 = (bf16[128,128]{1,0:T(8,128)(2,1)S(1)}, bf16[128,128]{1,0:T(8,128)(2,1)}, u32[]{:S(2)}) copy-start(bf16[128,128]{1,0:T(8,128)(2,1)} %param.13) | copy-start | bytes 98308
  8.4 2.6 %collective-permute-start.1 = (bf16[17,256,64]{1,2,0:T(8,128)(2,1)S(1)}, bf16[17,256,64]{1,2,0:T(8,128)(2,1)S(1)}, u32[]{:S(2)}, u32[]{:S(2)}) collective-permute-start(bf16[17,256,64]{1,2,0:T(8,128)(2,1)S(1)} %pad_maximum_fusion), channel_id=1, source_target_pairs={{0,4},{4,0},{8,12},{12,8},{16,20},{20,16},{24,28},{28,24},{1,5},{5... | collective-permute-start | bytes 1671176 | tf_op jit(solution)/shard_map/ppermute | solution.py:86
  11.7 0.5 copy-start.22
  13.4 7.2 %collective-permute-start.2 = (bf16[9,256,64]{1,2,0:T(8,128)(2,1)}, bf16[9,256,64]{1,2,0:T(8,128)(2,1)S(1)}, u32[]{:S(2)}, u32[]{:S(2)}) collective-permute-start(bf16[9,256,64]{1,2,0:T(8,128)(2,1)} %pad_maximum_fusion.2), channel_id=1, source_target_pairs={{4,12},{12,20},{20,28},{8,0},{16,8},{24,16},{5,13},{13,21},{21,29}... | collective-permute-start | bytes 884744 | tf_op jit(solution)/shard_map/ppermute | solution.py:104
  20.5 0.7 %copy-start.23 = (f32[8]{0:T(128)S(1)}, f32[8]{0:T(128)}, u32[]{:S(2)}) copy-start(f32[8]{0:T(128)} %copy-done.22) | copy-start | bytes 100
  22.0 14.5 %collective-permute-start.3 = (bf16[8,256,64]{1,2,0:T(8,128)(2,1)}, bf16[8,256,64]{1,2,0:T(8,128)(2,1)}, u32[]{:S(2)}, u32[]{:S(2)}) collective-permute-start(bf16[8,256,64]{1,2,0:T(8,128)(2,1)} %fusion.24), channel_id=1, source_target_pairs={{4,20},{12,28},{16,0},{24,8},{5,21},{13,29},{17,1},{25,9},{6,22},{... | collective-permute-start | bytes 786440 | tf_op jit(solution)/shard_map/ppermute | solution.py:98
  28.7 0.7 %copy-start.24 = (f32[8]{0:T(128)S(1)}, f32[8]{0:T(128)}, u32[]{:S(2)}) copy-start(f32[8]{0:T(128)} %get-tuple-element.72) | copy-start | bytes 100 | tf_op jit(solution)/shard_map/cond
  31.2 1.1 %copy-start.12 = (f32[8,128]{1,0:T(8,128)}, f32[8,128]{1,0:T(8,128)S(1)}, u32[]{:S(2)}) copy-start(f32[8,128]{1,0:T(8,128)S(1)} %get-tuple-element.124) | copy-start | bytes 12292 | tf_op jit(solution)/shard_map/cond
  35.0 0.7 %copy-start.13 = (f32[8,128]{1,0:T(8,128)S(1)}, f32[8,128]{1,0:T(8,128)}, u32[]{:S(2)}) copy-start(f32[8,128]{1,0:T(8,128)} %copy-done.12) | copy-start | bytes 12292 | tf_op jit(solution)/shard_map/cond
  35.0 0.7 %copy-start.14 = (f32[128,8]{0,1:T(8,128)S(1)}, f32[128,8]{0,1:T(8,128)}, u32[]{:S(2)}) copy-start(f32[128,8]{0,1:T(8,128)} %multiply_subtract_fusion) | copy-start | bytes 12292 | tf_op jit(solution)/shard_map/cond
  36.5 0.7 %copy-start.21 = (f32[8]{0:T(128)S(1)}, f32[8]{0:T(128)}, u32[]{:S(2)}) copy-start(f32[8]{0:T(128)} %get-tuple-element.123) | copy-start | bytes 100
  38.4 0.7 %copy-start.15 = (f32[4,512]{1,0:T(4,128)S(1)}, f32[4,512]{1,0:T(4,128)}, u32[]{:S(2)}) copy-start(f32[4,512]{1,0:T(4,128)} %param.17) | copy-start | bytes 24580
  38.5 2.0 %collective-permute-start.4 = (bf16[16,256,64]{1,2,0:T(8,128)(2,1)S(1)}, bf16[16,256,64]{1,2,0:T(8,128)(2,1)S(1)}, u32[]{:S(2)}, u32[]{:S(2)}) collective-permute-start(bf16[16,256,64]{1,2,0:T(8,128)(2,1)S(1)} %pad_maximum_fusion.1), channel_id=1, source_target_pairs={{0,4},{4,0},{8,12},{12,8},{16,20},{20,16},{24,28},{28,24},{1,5},{5... | collective-permute-start | bytes 1572872 | tf_op jit(solution)/shard_map/ppermute | solution.py:115
  40.6 0.6 %copy-start.17 = (f32[8]{0:T(128)S(1)}, f32[8]{0:T(128)}, u32[]{:S(2)}) copy-start(f32[8]{0:T(128)} %copy-done.16) | copy-start | bytes 100
  41.2 0.8 %copy-start.7 = (bf16[128,128]{1,0:T(8,128)(2,1)S(1)}, bf16[128,128]{1,0:T(8,128)(2,1)}, u32[]{:S(2)}) copy-start(bf16[128,128]{1,0:T(8,128)(2,1)} %copy-done.6) | copy-start | bytes 98308
  42.5 2.1 %copy-start.8 = (f32[128,256]{1,0:T(8,128)S(1)}, f32[128,256]{1,0:T(8,128)}, u32[]{:S(2)}) copy-start(f32[128,256]{1,0:T(8,128)} %get-tuple-element.68) | copy-start | bytes 393220
  42.6 7.1 %collective-permute-start.5 = (f32[3,512]{1,0:T(4,128)S(1)}, f32[3,512]{1,0:T(4,128)S(1)}, u32[]{:S(2)}, u32[]{:S(2)}) collective-permute-start(f32[3,512]{1,0:T(4,128)S(1)} %slice.137), channel_id=1, source_target_pairs={{4,0},{8,4},{12,8},{16,12},{20,16},{24,20},{28,24},{5,1},{9,5},{13... | collective-permute-start | bytes 18440 | tf_op jit(solution)/shard_map/ppermute | solution.py:124
  44.7 0.9 %copy-start.9 = (f32[128,256]{1,0:T(8,128)S(1)}, f32[128,256]{1,0:T(8,128)}, u32[]{:S(2)}) copy-start(f32[128,256]{1,0:T(8,128)} %get-tuple-element.67) | copy-start | bytes 393220
  46.2 0.8 %copy-start.3 = (bf16[128,128]{1,0:T(8,128)(2,1)S(1)}, bf16[128,128]{1,0:T(8,128)(2,1)}, u32[]{:S(2)}) copy-start(bf16[128,128]{1,0:T(8,128)(2,1)} %param.13) | copy-start | bytes 98308
  46.2 0.8 %copy-start.5 = (bf16[128,128]{1,0:T(8,128)(2,1)S(1)}, bf16[128,128]{1,0:T(8,128)(2,1)}, u32[]{:S(2)}) copy-start(bf16[128,128]{1,0:T(8,128)(2,1)} %copy-done.4) | copy-start | bytes 98308
  46.2 4.3 %collective-permute-start.6 = (bf16[128,256]{1,0:T(8,128)(2,1)S(1)}, bf16[128,256]{1,0:T(8,128)(2,1)S(1)}, u32[]{:S(2)}, u32[]{:S(2)}) collective-permute-start(bf16[128,256]{1,0:T(8,128)(2,1)S(1)} %pad_maximum_fusion.7), channel_id=1, source_target_pairs={{0,1},{1,0},{2,3},{3,2},{4,5},{5,4},{6,7},{7,6},{8,9},{9,8},{10,11... | collective-permute-start | bytes 196616 | tf_op jit(solution)/shard_map/ppermute | solution.py:16
  47.4 0.7 %copy-start.20 = (f32[8]{0:T(128)S(1)}, f32[8]{0:T(128)}, u32[]{:S(2)}) copy-start(f32[8]{0:T(128)} %copy-done.19) | copy-start | bytes 100

commit v11 on v5

--- a/solution.py
+++ b/solution.py
@@ -138,7 +138,9 @@
     upstream = output_grad.astype(jnp.float32)
     values3 = values.reshape(length, head_count, head_width)
     upstream3 = upstream.reshape(length, head_count, head_width)
-    cumulative = jnp.cumsum(log_decay, axis=0)
+    token_row = lax.broadcasted_iota(jnp.int32, (length, length), 0)
+    token_col = lax.broadcasted_iota(jnp.int32, (length, length), 1)
+    cumulative = product((token_row >= token_col).astype(jnp.float32), log_decay)
     totals = cumulative[-1]
     to_end = jnp.exp(totals[None, :] - cumulative)
     from_start = jnp.exp(cumulative)
@@ -211,7 +213,7 @@
     )
     last_row = (lax.broadcasted_iota(jnp.int32, (length, 1), 0) == length - 1).astype(jnp.float32)
     decay_terms = decay_terms + last_row * jnp.sum(arriving * leaving, (1, 2))[None, :]
-    decay_grad = jnp.flip(jnp.cumsum(jnp.flip(decay_terms, 0), 0), 0)
+    decay_grad = product((token_row <= token_col).astype(jnp.float32), decay_terms)
     query_part = query_local + jnp.einsum(
         "lhp,hnp->ln", seeded, entering, precision=precise
     )

time: 47.3 us -> 45.3 us (0.958)
  local copies, waits for them, and re-layouts: 6.65 us -> 4 us
  matrix products: 6.5 us -> 7.45 us
    unnamed x48 -> x54, local copies, waits for them, and re-layouts: 5.97 us -> 3.36 us
    dot_general x2 -> x4, matrix products: 0.53 us -> 1.48 us  [product(): jnp.dot(left, right, preferred_element_type=jnp.float32, precision=precise)]
    ppermute x1, starting transfers between devices: 4.51 us -> 3.64 us  [paired_scan(): handed = lax.ppermute(passing, axis, swap)]
    add x1, other arithmetic: 0.07 us -> 0.81 us  [unpacked(): row[:heads] + row[heads:2 * heads]]
    concatenate x2, other arithmetic: 0.78 us -> 0.07 us  [packed(): return jnp.concatenate([state.astype(kind), slab], 0)]
    convert_element_type x1, other arithmetic: 0.01 us -> 0.58 us  [unpacked(): row = message[heads, :, 0].astype(jnp.float32)]
    ppermute x2, starting transfers between devices: 2.76 us -> 3.25 us  [swapped(): return lax.ppermute(block, axis, route)]
  transfers between devices with their start and end apart: 7 -> 7, of which waited for: 3 -> 3; matrix products, arithmetic and copies ran while one was open for 20% -> 23% of each run, Pallas kernels for 0% -> 0%
where the time goes in v11:
time: 45.3 us; the launch traced here: 44.7 us
  starting transfers between devices  18.8 us (42%)
  matrix products  7.45 us (16%)
  other arithmetic  6.65 us (15%)
  waiting for transfers between devices  6.64 us (15%)
  local copies, waits for them, and re-layouts  4 us (9%)
  between operations  1.13 us (2%)
    ppermute x1, starting transfers between devices, paired_scan(): far_s = lax.ppermute(window[1].astype(jnp.bfloat16), axis, route)  5.25 us
    ppermute x1, starting transfers between devices, paired_scan(): handed = lax.ppermute(passing, axis, swap)  3.64 us
    ppermute x1, waiting for transfers between devices, paired_scan(): far = lax.ppermute(packed(*window, jnp.bfloat16), axis, route)  3.53 us
    unnamed x54, local copies, waits for them, and re-layouts  3.36 us
    ppermute x2, starting transfers between devices, swapped(): return lax.ppermute(block, axis, route)  3.25 us
    ppermute x1, starting transfers between devices, paired_scan(): far = lax.ppermute(packed(*window, jnp.bfloat16), axis, route)  3.22 us
    ppermute x1, starting transfers between devices, shifted(): return lax.ppermute(block, axis, route)  2.41 us
    ppermute x1, waiting for transfers between devices, paired_scan(): mate = lax.ppermute(message, axis, swap)  1.63 us
  transfers between devices with their start and end apart: 7, of which 3 were waited for; matrix products, arithmetic and copies ran while one was open for 23% of the time, Pallas kernels for 0%

profile of v11, /device:TPU:1, one launch (start us, length us, event | category | flops | bytes accessed | tf_op | source)
XLA Modules:
  0.0 44.7 jit_solution(41342487346743239)
XLA Ops:
  0.7 0.8 %pad_maximum_fusion.4 = bf16[128,256]{1,0:T(8,128)(2,1)S(1)} fusion(bf16[128,128]{1,0:T(8,128)(2,1)} %param.13, bf16[128,128]{1,0:T(8,128)(2,1)} %param.12), kind=kLoop, calls=%fused_computation.70 | loop fusion | flops 131072 | bytes 131072 | tf_op jit(solution)/shard_map/concatenate | solution.py:123
  1.5 2.1 %collective-permute-start = (bf16[128,256]{1,0:T(8,128)(2,1)S(1)}, bf16[128,256]{1,0:T(8,128)(2,1)S(1)}, u32[]{:S(2)}, u32[]{:S(2)}) collective-permute-start(bf16[128,256]{1,0:T(8,128)(2,1)S(1)} %pad_maximum_fusion.4), channel_id=1, source_target_pairs={{0,1},{1,0},{2,3},{3,2},{4,5},{5,4},{6,7},{7,6},{8,9},{9,8},{10,11... | collective-permute-start | bytes 196616 | tf_op jit(solution)/shard_map/ppermute | solution.py:16
  3.6 0.1 fusion.46
  3.7 0.2 slice_reduce_fusion
  4.1 0.6 %copy-done.14 = f32[128,8]{0,1:T(8,128)S(1)} copy-done((f32[128,8]{0,1:T(8,128)S(1)}, f32[128,8]{0,1:T(8,128)}, u32[]{:S(2)}) %copy-start.14) | copy-done | bytes 4120
  4.7 0.1 copy.17
  4.9 0.8 %copy-done.13 = bf16[128,512]{1,0:T(8,128)(2,1)S(1)} copy-done((bf16[128,512]{1,0:T(8,128)(2,1)S(1)}, bf16[128,512]{1,0:T(8,128)(2,1)}, u32[]{:S(2)}) %copy-start.13) | copy-done | bytes 131096
  5.7 0.1 copy.18
  5.8 0.7 %copy-done.5 = bf16[128,128]{1,0:T(8,128)(2,1)S(1)} copy-done((bf16[128,128]{1,0:T(8,128)(2,1)S(1)}, bf16[128,128]{1,0:T(8,128)(2,1)}, u32[]{:S(2)}) %copy-start.5) | copy-done | bytes 32792
  6.5 0.4 convolution_bitcast_fusion.2
  6.9 0.4 copy-done.1
  7.3 0.4 broadcast_select_fusion.2
  7.7 1.0 %collective-permute-start.1 = (f32[9,256,64]{1,2,0:T(8,128)S(1)}, f32[9,256,64]{1,2,0:T(8,128)S(1)}, u32[]{:S(2)}, u32[]{:S(2)}) collective-permute-start(f32[9,256,64]{1,2,0:T(8,128)S(1)} %pad_maximum_fusion), channel_id=1, source_target_pairs={{0,4},{4,0},{8,12},{12,8},{16,20},{20,16},{24,28},{28,24},{1,5},{5... | collective-permute-start | bytes 1769480 | tf_op jit(solution)/shard_map/ppermute | solution.py:72
  8.8 1.6 %collective-permute-done.1 = f32[9,256,64]{1,2,0:T(8,128)S(1)} collective-permute-done((f32[9,256,64]{1,2,0:T(8,128)S(1)}, f32[9,256,64]{1,2,0:T(8,128)S(1)}, u32[]{:S(2)}, u32[]{:S(2)}) %collective-permute-start.1) | collective-permute-done | bytes 589856 | tf_op jit(solution)/shard_map/ppermute | solution.py:72
  10.4 0.5 %copy-done.25 = f32[8]{0:T(128)} copy-done((f32[8]{0:T(128)}, f32[8]{0:T(128)S(1)}, u32[]{:S(2)}) %copy-start.25) | copy-done | bytes 56
  10.9 0.1 fusion.59
  11.0 0.2 fusion.73
  11.2 3.2 %collective-permute-start.2 = (bf16[9,256,64]{1,2,0:T(8,128)(2,1)S(1)}, bf16[9,256,64]{1,2,0:T(8,128)(2,1)S(1)}, u32[]{:S(2)}, u32[]{:S(2)}) collective-permute-start(bf16[9,256,64]{1,2,0:T(8,128)(2,1)S(1)} %pad_maximum_fusion.1), channel_id=1, source_target_pairs={{4,12},{12,20},{20,28},{8,0},{16,8},{24,16},{5,13},{13,21},{21,29}... | collective-permute-start | bytes 884744 | tf_op jit(solution)/shard_map/ppermute | solution.py:90
  14.6 3.5 %collective-permute-done.2 = bf16[9,256,64]{1,2,0:T(8,128)(2,1)S(1)} collective-permute-done((bf16[9,256,64]{1,2,0:T(8,128)(2,1)S(1)}, bf16[9,256,64]{1,2,0:T(8,128)(2,1)S(1)}, u32[]{:S(2)}, u32[]{:S(2)}) %collective-permute-start.2) | collective-permute-done | bytes 294944 | tf_op jit(solution)/shard_map/ppermute | solution.py:90
  18.1 0.8 %fusion.24 = bf16[8,256,64]{1,2,0:T(8,128)(2,1)} fusion(f32[8,256,64]{1,2,0:T(8,128)S(1)} %get-tuple-element.77, f32[8]{0:T(128)S(1)} %copy-done.26, bf16[9,256,64]{1,2,0:T(8,128)(2,1)S(1)} %collective-permute-done.2), kind=kLoop, calls=%fused_computation.35 | loop fusion | flops 524288 | bytes 1048608 | tf_op jit(solution)/shard_map/convert_element_type | solution.py:84
  18.9 5.3 %collective-permute-start.3 = (bf16[8,256,64]{1,2,0:T(8,128)(2,1)}, bf16[8,256,64]{1,2,0:T(8,128)(2,1)S(1)}, u32[]{:S(2)}, u32[]{:S(2)}) collective-permute-start(bf16[8,256,64]{1,2,0:T(8,128)(2,1)} %fusion.24), channel_id=1, source_target_pairs={{4,20},{12,28},{16,0},{24,8},{5,21},{13,29},{17,1},{25,9},{6,22},{... | collective-permute-start | bytes 786440 | tf_op jit(solution)/shard_map/ppermute | solution.py:84
  24.2 0.6 %slice_convert_fusion = f32[1,256,1]{1,2,0:T(1,128)} fusion(bf16[9,256,64]{1,2,0:T(8,128)(2,1)S(1)} %collective-permute-done.2), kind=kLoop, calls=%fused_computation.101 | loop fusion | flops 256 | bytes 1536 | tf_op jit(solution)/shard_map/convert_element_type | solution.py:55
  24.8 4.2 %conditional.1 = (f32[128,8,64]{0,2,1:T(8,128)S(1)}, f32[128,8]{0,1:T(8,128)S(1)}, f32[128,8]{0,1:T(8,128)}, f32[128,256]{1,0:T(8,128)S(1)}, f32[128,256]{1,0:T(8,128)S(1)}, /*index=5*/f32[128,512]{1,0:T(8,128)S(1)}) conditional(s32[]{:T(128)} %convert_element_type.70, () %tuple.19, (f32[128,8]{0,1:T(8,128)S(1)}, f32[128,256]{1,0:T(8,128)S(1)}, ...), branch_computations={%region_0.1_spmd, %region_1.3_spmd} | conditional | flops 356844544 | bytes 4542572 | solution.py:187
  24.8 0.3 fusion.78
  25.1 0.8 %fusion = f32[128,8,64]{0,2,1:T(8,128)S(1)} fusion(f32[128,8,64]{0,2,1:T(8,128)S(1)} %get-tuple-element.20, f32[8,128]{1,0:T(8,128)S(1)} %bitcast.95, f32[128,128]{1,0:T(8,128)S(1)} %fusion.78, f32[8,128]{1,0:T(8,128)S(1)} %bitcast.91, pred[128,128]{1,0:T(8,128)(4,1)S(1)} %iota_compare_fusion, f32[8]{0:T(128)S(1)} %get-tuple-element.72), kind=kOutput, calls=%fused_computation.1 | convolution fusion | flops 101318656 | bytes 614432 | tf_op jit(solution)/shard_map/cond/branch_1_fun/hts,thp->shp/dot_general | solution.py:164
  25.8 1.1 %fusion.5 = (f32[8,128]{1,0:T(8,128)S(1)}, f32[8,128,128]{2,1,0:T(8,128)S(1)}) fusion(f32[128,128]{1,0:T(8,128)S(1)} %fusion.78, f32[8,128]{1,0:T(8,128)S(1)} %bitcast.92, pred[128,128]{1,0:T(8,128)(4,1)S(1)} %iota_compare_fusion, f32[128,8,64]{0,2,1:T(8,128)S(1)} %get-tuple-element.20, f32[128,8,64]{0,2,1:T(8,128)S(1)} %get-tuple-element.22), kind=kOutput, calls=%fused_computation.7 | convolution fusion | flops 101317632 | bytes 1138688 | tf_op jit(solution)/shard_map/cond/branch_1_fun/thp,shp->hts/dot_general | solution.py:161
  27.0 1.1 %fusion.6 = f32[8,1,128]{2,1,0:T(1,128)S(1)} fusion(f32[8,128,1]{1,2,0:T(1,128)S(1)} %bitcast.96, f32[8,128,128]{2,1,0:T(8,128)S(1)} %get-tuple-element.81, f32[128,128]{1,0:T(8,128)S(1)} %fusion.78, f32[8,128]{1,0:T(8,128)S(1)} %bitcast.93, pred[128,128]{1,0:T(8,128)(4,1)S(1)} %iota_compare_fusion), kind=kOutput, calls=%fused_computation.8 | convolution fusion | flops 2097152 | bytes 618496 | tf_op jit(solution)/shard_map/cond/branch_1_fun/hts,hs->th/dot_general | solution.py:168
  28.0 0.2 multiply_reduce_fusion
  28.3 0.3 fusion.79
  28.5 0.3 fusion.80
  28.8 0.1 add_multiply_fusion
  29.0 0.8 %fusion.60 = f32[8]{0:T(128)S(1)} fusion(f32[1,256,1]{1,2,0:T(1,128)} %slice_convert_fusion), kind=kLoop, calls=%fused_computation.104 | loop fusion | flops 8 | bytes 96 | tf_op jit(solution)/shard_map/add | solution.py:56
  29.8 0.1 convert_add_fusion
  30.0 3.6 %collective-permute-start.4 = (f32[8,256,64]{1,2,0:T(8,128)S(1)}, f32[8,256,64]{1,2,0:T(8,128)S(1)}, u32[]{:S(2)}, u32[]{:S(2)}) collective-permute-start(f32[8,256,64]{1,2,0:T(8,128)S(1)} %convert_add_fusion), channel_id=1, source_target_pairs={{0,4},{4,0},{8,12},{12,8},{16,20},{20,16},{24,28},{28,24},{1,5},{5... | collective-permute-start | bytes 1572872 | tf_op jit(solution)/shard_map/ppermute | solution.py:99
  33.7 1.5 %collective-permute-done.4 = f32[8,256,64]{1,2,0:T(8,128)S(1)} collective-permute-done((f32[8,256,64]{1,2,0:T(8,128)S(1)}, f32[8,256,64]{1,2,0:T(8,128)S(1)}, u32[]{:S(2)}, u32[]{:S(2)}) %collective-permute-start.4) | collective-permute-done | bytes 524320 | tf_op jit(solution)/shard_map/ppermute | solution.py:99
  35.2 0.4 multiply_reduce_fusion.1
  35.5 0.4 multiply_reduce_fusion.2
  36.0 0.1 copy.19
  36.2 2.4 %collective-permute-start.5 = (f32[3,512]{1,0:T(4,128)S(1)}, f32[3,512]{1,0:T(4,128)S(1)}, u32[]{:S(2)}, u32[]{:S(2)}) collective-permute-start(f32[3,512]{1,0:T(4,128)S(1)} %slice.110), channel_id=1, source_target_pairs={{4,0},{8,4},{12,8},{16,12},{20,16},{24,20},{28,24},{5,1},{9,5},{13... | collective-permute-start | bytes 18440 | tf_op jit(solution)/shard_map/ppermute | solution.py:107
  38.6 0.6 %fusion.21 = f32[128,256]{1,0:T(8,128)S(1)} fusion(f32[128,256]{1,0:T(8,128)S(1)} %copy-done.12, f32[8,256,64]{1,2,0:T(8,128)S(1)} %get-tuple-element.75, f32[128,8,64]{0,2,1:T(8,128)S(1)} %bitcast.86, f32[128,8]{0,1:T(8,128)S(1)} %get-tuple-element.90), kind=kOutput, calls=%fused_computation.29 | convolution fusion | flops 201424896 | bytes 1052672 | tf_op jit(solution)/shard_map/lhp,hnp->ln/dot_general | solution.py:220
  39.2 0.6 %fusion.22 = f32[128,256]{1,0:T(8,128)S(1)} fusion(f32[128,256]{1,0:T(8,128)S(1)} %copy-done.10, f32[8,256,64]{1,2,0:T(8,128)S(1)} %get-tuple-element.74, f32[128,8,64]{0,2,1:T(8,128)S(1)} %bitcast.83, f32[128,8]{0,1:T(8,128)S(1)} %get-tuple-element.91), kind=kOutput, calls=%fused_computation.30 | convolution fusion | flops 201424896 | bytes 1052672 | tf_op jit(solution)/shard_map/lhp,hnp->ln/dot_general | solution.py:217
  39.9 1.1 %collective-permute-start.6 = (bf16[128,256]{1,0:T(8,128)(2,1)S(1)}, bf16[128,256]{1,0:T(8,128)(2,1)S(1)}, u32[]{:S(2)}, u32[]{:S(2)}) collective-permute-start(bf16[128,256]{1,0:T(8,128)(2,1)S(1)} %pad_maximum_fusion.6), channel_id=1, source_target_pairs={{0,1},{1,0},{2,3},{3,2},{4,5},{5,4},{6,7},{7,6},{8,9},{9,8},{10,11... | collective-permute-start | bytes 196616 | tf_op jit(solution)/shard_map/ppermute | solution.py:16
  41.1 0.4 multiply_reduce_fusion.3
  41.5 0.3 copy-done.24
  41.8 0.8 %fusion.47 = f32[128,8]{0,1:T(8,128)} fusion(f32[128,8]{0,1:T(8,128)S(1)} %get-tuple-element.90, f32[128,8]{0,1:T(8,128)S(1)} %get-tuple-element.94, f32[128,8]{0,1:T(8,128)S(1)} %copy-done.24, f32[128,8]{0,1:T(8,128)S(1)} %multiply_reduce_fusion.3, f32[8]{0:T(128)S(1)} %get-tuple-element.73, f32[128]{0:T(128)S(1)} %compare_convert_fusion, ...), kind=kOutput, calls=%fused_computation.84 | convolution fusion | flops 1595392 | bytes 25120 | tf_op jit(solution)/shard_map/dot_general | solution.py:111
  42.6 0.7 %multiply_add_fusion.3 = f32[128,8]{0,1:T(8,128)} fusion(f32[128,8]{0,1:T(8,128)S(1)} %copy-done.17, f32[128,8]{0,1:T(8,128)S(1)} %get-tuple-element.94, f32[128,8]{0,1:T(8,128)S(1)} %fusion.46, f32[8]{0:T(128)S(1)} %copy-done.19), kind=kLoop, calls=%fused_computation.85 | loop fusion | flops 3072 | bytes 16416 | tf_op jit(solution)/shard_map/add | solution.py:206
  43.3 0.8 %fusion.30 = bf16[128,512]{1,0:T(8,128)(2,1)} fusion(f32[128,512]{1,0:T(8,128)S(1)} %mul.207, f32[3,512]{1,0:T(4,128)S(1)} %collective-permute-done.5, f32[512]{0:T(512)S(1)} %bitcast.100, f32[512]{0:T(512)S(1)} %bitcast.101, f32[512]{0:T(512)S(1)} %bitcast.99, f32[512]{0:T(512)S(1)} %bitcast.98), kind=kLoop, calls=%fused_computation.49 | loop fusion | flops 720896 | bytes 407552 | tf_op jit(solution)/shard_map/convert_element_type | solution.py:240
  44.1 0.7 %slice_add_fusion = (f32[128,128]{1,0:T(8,128)}, f32[128,128]{1,0:T(8,128)}) fusion(f32[128,256]{1,0:T(8,128)S(1)} %convert_element_type.72, f32[128,256]{1,0:T(8,128)S(1)} %fusion.22, pred[]{:T(512)S(6)} %eq.21, f32[128,256]{1,0:T(8,128)S(1)} %fusion.21), kind=kLoop, calls=%fused_computation.74 | loop fusion | flops 65536 | bytes 524289 | tf_op jit(solution)/shard_map/add | solution.py:231
  (79 shorter events, 0.6 us)
Async XLA Ops:
  0.6 3.0 %copy-start = (f32[128,8]{0,1:T(8,128)S(1)}, f32[128,8]{0,1:T(8,128)}, u32[]{:S(2)}) copy-start(f32[128,8]{0,1:T(8,128)} %param.14) | copy-start | bytes 12292
  0.6 3.3 %copy-start.4 = (bf16[128,512]{1,0:T(8,128)(2,1)S(1)}, bf16[128,512]{1,0:T(8,128)(2,1)}, u32[]{:S(2)}) copy-start(bf16[128,512]{1,0:T(8,128)(2,1)} %param.10) | copy-start | bytes 393220
  1.5 4.3 %collective-permute-start = (bf16[128,256]{1,0:T(8,128)(2,1)S(1)}, bf16[128,256]{1,0:T(8,128)(2,1)S(1)}, u32[]{:S(2)}, u32[]{:S(2)}) collective-permute-start(bf16[128,256]{1,0:T(8,128)(2,1)S(1)} %pad_maximum_fusion.4), channel_id=1, source_target_pairs={{0,1},{1,0},{2,3},{3,2},{4,5},{5,4},{6,7},{7,6},{8,9},{9,8},{10,11... | collective-permute-start | bytes 196616 | tf_op jit(solution)/shard_map/ppermute | solution.py:16
  4.0 6.4 %copy-start.18 = (f32[8]{0:T(128)}, f32[8]{0:T(128)S(1)}, u32[]{:S(2)}) copy-start(f32[8]{0:T(128)S(1)} %slice_reduce_fusion) | copy-start | bytes 100
  4.0 0.7 %copy-start.14 = (f32[128,8]{0,1:T(8,128)S(1)}, f32[128,8]{0,1:T(8,128)}, u32[]{:S(2)}) copy-start(f32[128,8]{0,1:T(8,128)} %param.15) | copy-start | bytes 12292
  4.7 6.3 %copy-start.21 = (f32[8]{0:T(128)}, f32[8]{0:T(128)S(1)}, u32[]{:S(2)}) copy-start(f32[8]{0:T(128)S(1)} %exp.29) | copy-start | bytes 100
  4.7 0.9 %copy-start.13 = (bf16[128,512]{1,0:T(8,128)(2,1)S(1)}, bf16[128,512]{1,0:T(8,128)(2,1)}, u32[]{:S(2)}) copy-start(bf16[128,512]{1,0:T(8,128)(2,1)} %param.11) | copy-start | bytes 393220
  5.8 0.8 %copy-start.5 = (bf16[128,128]{1,0:T(8,128)(2,1)S(1)}, bf16[128,128]{1,0:T(8,128)(2,1)}, u32[]{:S(2)}) copy-start(bf16[128,128]{1,0:T(8,128)(2,1)} %param.12) | copy-start | bytes 98308
  5.8 8.7 %copy-start.7 = (bf16[128,128]{1,0:T(8,128)(2,1)}, bf16[128,128]{1,0:T(8,128)(2,1)S(1)}, u32[]{:S(2)}) copy-start(bf16[128,128]{1,0:T(8,128)(2,1)S(1)} %get-tuple-element.84) | copy-start | bytes 98308
  5.8 8.7 %copy-start.2 = (bf16[128,128]{1,0:T(8,128)(2,1)}, bf16[128,128]{1,0:T(8,128)(2,1)S(1)}, u32[]{:S(2)}) copy-start(bf16[128,128]{1,0:T(8,128)(2,1)S(1)} %get-tuple-element.85) | copy-start | bytes 98308
  6.5 0.8 %copy-start.1 = (bf16[128,128]{1,0:T(8,128)(2,1)S(1)}, bf16[128,128]{1,0:T(8,128)(2,1)}, u32[]{:S(2)}) copy-start(bf16[128,128]{1,0:T(8,128)(2,1)} %param.13) | copy-start | bytes 98308
  7.7 2.7 %collective-permute-start.1 = (f32[9,256,64]{1,2,0:T(8,128)S(1)}, f32[9,256,64]{1,2,0:T(8,128)S(1)}, u32[]{:S(2)}, u32[]{:S(2)}) collective-permute-start(f32[9,256,64]{1,2,0:T(8,128)S(1)} %pad_maximum_fusion), channel_id=1, source_target_pairs={{0,4},{4,0},{8,12},{12,8},{16,20},{20,16},{24,28},{28,24},{1,5},{5... | collective-permute-start | bytes 1769480 | tf_op jit(solution)/shard_map/ppermute | solution.py:72
  10.4 0.5 %copy-start.25 = (f32[8]{0:T(128)}, f32[8]{0:T(128)S(1)}, u32[]{:S(2)}) copy-start(f32[8]{0:T(128)S(1)} %get-tuple-element.79) | copy-start | bytes 100
  11.2 6.9 %collective-permute-start.2 = (bf16[9,256,64]{1,2,0:T(8,128)(2,1)S(1)}, bf16[9,256,64]{1,2,0:T(8,128)(2,1)S(1)}, u32[]{:S(2)}, u32[]{:S(2)}) collective-permute-start(bf16[9,256,64]{1,2,0:T(8,128)(2,1)S(1)} %pad_maximum_fusion.1), channel_id=1, source_target_pairs={{4,12},{12,20},{20,28},{8,0},{16,8},{24,16},{5,13},{13,21},{21,29}... | collective-permute-start | bytes 884744 | tf_op jit(solution)/shard_map/ppermute | solution.py:90
  14.6 3.5 %copy-start.26 = (f32[8]{0:T(128)S(1)}, f32[8]{0:T(128)}, u32[]{:S(2)}) copy-start(f32[8]{0:T(128)} %copy-done.25) | copy-start | bytes 100
  18.1 6.7 %copy-start.15 = (f32[128,8]{0,1:T(8,128)S(1)}, f32[128,8]{0,1:T(8,128)}, u32[]{:S(2)}) copy-start(f32[128,8]{0,1:T(8,128)} %param.15) | copy-start | bytes 12292
  18.9 5.8 %copy-start.27 = (f32[8]{0:T(128)S(1)}, f32[8]{0:T(128)}, u32[]{:S(2)}) copy-start(f32[8]{0:T(128)} %param.16) | copy-start | bytes 100
  18.9 10.9 %collective-permute-start.3 = (bf16[8,256,64]{1,2,0:T(8,128)(2,1)}, bf16[8,256,64]{1,2,0:T(8,128)(2,1)S(1)}, u32[]{:S(2)}, u32[]{:S(2)}) collective-permute-start(bf16[8,256,64]{1,2,0:T(8,128)(2,1)} %fusion.24), channel_id=1, source_target_pairs={{4,20},{12,28},{16,0},{24,8},{5,21},{13,29},{17,1},{25,9},{6,22},{... | collective-permute-start | bytes 786440 | tf_op jit(solution)/shard_map/ppermute | solution.py:84
  26.9 1.1 %copy-start.16 = (f32[8,128]{1,0:T(8,128)}, f32[8,128]{1,0:T(8,128)S(1)}, u32[]{:S(2)}) copy-start(f32[8,128]{1,0:T(8,128)S(1)} %get-tuple-element.80) | copy-start | bytes 12292 | tf_op jit(solution)/shard_map/cond
  28.9 1.0 %copy-start.9 = (f32[128,256]{1,0:T(8,128)}, f32[128,256]{1,0:T(8,128)S(1)}, u32[]{:S(2)}) copy-start(f32[128,256]{1,0:T(8,128)S(1)} %get-tuple-element.68) | copy-start | bytes 393220
  29.0 1.0 %copy-start.11 = (f32[128,256]{1,0:T(8,128)}, f32[128,256]{1,0:T(8,128)S(1)}, u32[]{:S(2)}) copy-start(f32[128,256]{1,0:T(8,128)S(1)} %get-tuple-element.67) | copy-start | bytes 393220
  29.0 1.0 %copy-start.23 = (f32[128,8]{0,1:T(8,128)}, f32[128,8]{0,1:T(8,128)S(1)}, u32[]{:S(2)}) copy-start(f32[128,8]{0,1:T(8,128)S(1)} %get-tuple-element.69) | copy-start | bytes 12292
  30.0 3.7 %copy-start.20 = (f32[4,512]{1,0:T(4,128)S(1)}, f32[4,512]{1,0:T(4,128)}, u32[]{:S(2)}) copy-start(f32[4,512]{1,0:T(4,128)} %param.17) | copy-start | bytes 24580
  30.0 5.2 %collective-permute-start.4 = (f32[8,256,64]{1,2,0:T(8,128)S(1)}, f32[8,256,64]{1,2,0:T(8,128)S(1)}, u32[]{:S(2)}, u32[]{:S(2)}) collective-permute-start(f32[8,256,64]{1,2,0:T(8,128)S(1)} %convert_add_fusion), channel_id=1, source_target_pairs={{0,4},{4,0},{8,12},{12,8},{16,20},{20,16},{24,28},{28,24},{1,5},{5... | collective-permute-start | bytes 1572872 | tf_op jit(solution)/shard_map/ppermute | solution.py:99
  33.6 1.5 %copy-start.22 = (f32[8]{0:T(128)S(1)}, f32[8]{0:T(128)}, u32[]{:S(2)}) copy-start(f32[8]{0:T(128)} %copy-done.21) | copy-start | bytes 100
  33.7 1.9 %copy-start.6 = (bf16[128,128]{1,0:T(8,128)(2,1)S(1)}, bf16[128,128]{1,0:T(8,128)(2,1)}, u32[]{:S(2)}) copy-start(bf16[128,128]{1,0:T(8,128)(2,1)} %param.12) | copy-start | bytes 98308
  33.7 1.9 %copy-start.8 = (bf16[128,128]{1,0:T(8,128)(2,1)S(1)}, bf16[128,128]{1,0:T(8,128)(2,1)}, u32[]{:S(2)}) copy-start(bf16[128,128]{1,0:T(8,128)(2,1)} %copy-done.7) | copy-start | bytes 98308
  36.1 2.5 %copy-start.12 = (f32[128,256]{1,0:T(8,128)S(1)}, f32[128,256]{1,0:T(8,128)}, u32[]{:S(2)}) copy-start(f32[128,256]{1,0:T(8,128)} %copy-done.11) | copy-start | bytes 393220
  36.2 3.1 %copy-start.10 = (f32[128,256]{1,0:T(8,128)S(1)}, f32[128,256]{1,0:T(8,128)}, u32[]{:S(2)}) copy-start(f32[128,256]{1,0:T(8,128)} %copy-done.9) | copy-start | bytes 393220
  36.2 7.1 %collective-permute-start.5 = (f32[3,512]{1,0:T(4,128)S(1)}, f32[3,512]{1,0:T(4,128)S(1)}, u32[]{:S(2)}, u32[]{:S(2)}) collective-permute-start(f32[3,512]{1,0:T(4,128)S(1)} %slice.110), channel_id=1, source_target_pairs={{4,0},{8,4},{12,8},{16,12},{20,16},{24,20},{28,24},{5,1},{9,5},{13... | collective-permute-start | bytes 18440 | tf_op jit(solution)/shard_map/ppermute | solution.py:107
  39.9 1.2 %copy-start.3 = (bf16[128,128]{1,0:T(8,128)(2,1)S(1)}, bf16[128,128]{1,0:T(8,128)(2,1)}, u32[]{:S(2)}) copy-start(bf16[128,128]{1,0:T(8,128)(2,1)} %copy-done.2) | copy-start | bytes 98308
  39.9 4.1 %collective-permute-start.6 = (bf16[128,256]{1,0:T(8,128)(2,1)S(1)}, bf16[128,256]{1,0:T(8,128)(2,1)S(1)}, u32[]{:S(2)}, u32[]{:S(2)}) collective-permute-start(bf16[128,256]{1,0:T(8,128)(2,1)S(1)} %pad_maximum_fusion.6), channel_id=1, source_target_pairs={{0,1},{1,0},{2,3},{3,2},{4,5},{5,4},{6,7},{7,6},{8,9},{9,8},{10,11... | collective-permute-start | bytes 196616 | tf_op jit(solution)/shard_map/ppermute | solution.py:16
  41.1 0.7 %copy-start.24 = (f32[128,8]{0,1:T(8,128)S(1)}, f32[128,8]{0,1:T(8,128)}, u32[]{:S(2)}) copy-start(f32[128,8]{0,1:T(8,128)} %copy-done.23) | copy-start | bytes 12292
  41.8 0.8 %copy-start.17 = (f32[128,8]{0,1:T(8,128)S(1)}, f32[128,8]{0,1:T(8,128)}, u32[]{:S(2)}) copy-start(f32[128,8]{0,1:T(8,128)} %get-tuple-element.70) | copy-start | bytes 12292
  41.8 0.8 %copy-start.19 = (f32[8]{0:T(128)S(1)}, f32[8]{0:T(128)}, u32[]{:S(2)}) copy-start(f32[8]{0:T(128)} %copy-done.18) | copy-start | bytes 100

commit v12 on v11

--- a/solution.py
+++ b/solution.py
@@ -120,8 +120,10 @@
     parity = lax.axis_index("head") % 2
     own_first = parity == 0
     half = write_keys.shape[1]
-    both = swapped(jnp.concatenate([write_keys, read_queries], 1), "head", 0)
+    mine_both = lax.optimization_barrier(jnp.concatenate([write_keys, read_queries], 1))
+    both = swapped(mine_both, "head", 0)
     partner = (both[:, :half], both[:, half:])
+    write_keys, read_queries = mine_both[:, :half], mine_both[:, half:]
     keys_full = jnp.where(
         own_first,
         jnp.concatenate([write_keys, partner[0]], 1),

time: 45.3 us -> 47.2 us (1.042)
  local copies, waits for them, and re-layouts: 4 us -> 5.72 us
  other arithmetic: 6.65 us -> 7.82 us
  waiting for transfers between devices: 6.64 us -> 5.5 us
    ppermute x1, waiting for transfers between devices: 1.48 us -> 0.32 us  [paired_scan(): handed = lax.ppermute(passing, axis, swap)]
    unnamed x54 -> x64, local copies, waits for them, and re-layouts: 3.36 us -> 4.47 us
    slice x1, local copies, waits for them, and re-layouts: 0.01 us -> 0.61 us  [body(): conv_weight[offset][None, :] * extended[3 - offset:3 - offset + length]]
    convert_element_type x1, other arithmetic: 0.01 us -> 0.59 us  [body(): (lax.broadcasted_iota(jnp.int32, (length, 1), 0) == length - 1).astype(jn...]
    reduce_sum x1, other arithmetic: 0.35 us -> 0.92 us  [body(): jnp.sum(arriving * leaving, (1, 2))[None, :]]
    ppermute x2, starting transfers between devices: 3.25 us -> 3.8 us  [swapped(): return lax.ppermute(block, axis, route)]
    ppermute x1, starting transfers between devices: 3.22 us -> 3.75 us  [paired_scan(): far = lax.ppermute(packed(*window, jnp.bfloat16), axis, route)]
  transfers between devices with their start and end apart: 7 -> 7, of which waited for: 3 -> 3; matrix products, arithmetic and copies ran while one was open for 23% -> 24% of each run, Pallas kernels for 0% -> 0%
where the time goes in v12:
time: 47.2 us; the launch traced here: 46.7 us
  starting transfers between devices  19 us (40%)
  other arithmetic  7.82 us (17%)
  matrix products  7.44 us (16%)
  local copies, waits for them, and re-layouts  5.72 us (12%)
  waiting for transfers between devices  5.5 us (12%)
  between operations  1.14 us (2%)
    ppermute x1, starting transfers between devices, paired_scan(): far_s = lax.ppermute(window[1].astype(jnp.bfloat16), axis, route)  5.25 us
    unnamed x64, local copies, waits for them, and re-layouts  4.47 us
    ppermute x2, starting transfers between devices, swapped(): return lax.ppermute(block, axis, route)  3.8 us
    ppermute x1, starting transfers between devices, paired_scan(): far = lax.ppermute(packed(*window, jnp.bfloat16), axis, route)  3.75 us
    ppermute x1, waiting for transfers between devices, paired_scan(): far = lax.ppermute(packed(*window, jnp.bfloat16), axis, route)  3.54 us
    ppermute x1, starting transfers between devices, paired_scan(): handed = lax.ppermute(passing, axis, swap)  3.19 us
    ppermute x1, starting transfers between devices, shifted(): return lax.ppermute(block, axis, route)  2.02 us
    ppermute x1, waiting for transfers between devices, paired_scan(): mate = lax.ppermute(message, axis, swap)  1.63 us
  transfers between devices with their start and end apart: 7, of which 3 were waited for; matrix products, arithmetic and copies ran while one was open for 24% of the time, Pallas kernels for 0%

profile of v12, /device:TPU:1, one launch (start us, length us, event | category | flops | bytes accessed | tf_op | source)
XLA Modules:
  0.0 46.7 jit_solution(8597925638903724768)
XLA Ops:
  0.7 0.8 %pad_maximum_fusion.3 = bf16[128,256]{1,0:T(8,128)(2,1)S(1)} fusion(bf16[128,128]{1,0:T(8,128)(2,1)} %param.13, bf16[128,128]{1,0:T(8,128)(2,1)} %param.12), kind=kLoop, calls=%fused_computation.71 | loop fusion | flops 131072 | bytes 131072 | tf_op jit(solution)/shard_map/concatenate | solution.py:123
  1.5 2.1 %collective-permute-start = (bf16[128,256]{1,0:T(8,128)(2,1)S(1)}, bf16[128,256]{1,0:T(8,128)(2,1)S(1)}, u32[]{:S(2)}, u32[]{:S(2)}) collective-permute-start(bf16[128,256]{1,0:T(8,128)(2,1)S(1)} %pad_maximum_fusion.3), channel_id=1, source_target_pairs={{0,1},{1,0},{2,3},{3,2},{4,5},{5,4},{6,7},{7,6},{8,9},{9,8},{10,11... | collective-permute-start | bytes 196616 | tf_op jit(solution)/shard_map/ppermute | solution.py:16
  3.7 0.2 slice_reduce_fusion
  4.1 0.6 %copy-done.13 = f32[128,8]{0,1:T(8,128)S(1)} copy-done((f32[128,8]{0,1:T(8,128)S(1)}, f32[128,8]{0,1:T(8,128)}, u32[]{:S(2)}) %copy-start.13) | copy-done | bytes 4120
  4.9 0.8 %copy-done.12 = bf16[128,512]{1,0:T(8,128)(2,1)S(1)} copy-done((bf16[128,512]{1,0:T(8,128)(2,1)S(1)}, bf16[128,512]{1,0:T(8,128)(2,1)}, u32[]{:S(2)}) %copy-start.12) | copy-done | bytes 131096
  5.8 0.4 convolution_bitcast_fusion.2
  6.2 0.4 broadcast_select_fusion.2
  6.7 1.0 %collective-permute-start.1 = (f32[9,256,64]{1,2,0:T(8,128)S(1)}, f32[9,256,64]{1,2,0:T(8,128)S(1)}, u32[]{:S(2)}, u32[]{:S(2)}) collective-permute-start(f32[9,256,64]{1,2,0:T(8,128)S(1)} %pad_maximum_fusion), channel_id=1, source_target_pairs={{0,4},{4,0},{8,12},{12,8},{16,20},{20,16},{24,28},{28,24},{1,5},{5... | collective-permute-start | bytes 1769480 | tf_op jit(solution)/shard_map/ppermute | solution.py:72
  7.7 1.6 %collective-permute-done.1 = f32[9,256,64]{1,2,0:T(8,128)S(1)} collective-permute-done((f32[9,256,64]{1,2,0:T(8,128)S(1)}, f32[9,256,64]{1,2,0:T(8,128)S(1)}, u32[]{:S(2)}, u32[]{:S(2)}) %collective-permute-start.1) | collective-permute-done | bytes 589856 | tf_op jit(solution)/shard_map/ppermute | solution.py:72
  9.3 0.5 %copy-done.28 = f32[8]{0:T(128)} copy-done((f32[8]{0:T(128)}, f32[8]{0:T(128)S(1)}, u32[]{:S(2)}) %copy-start.28) | copy-done | bytes 56
  9.9 0.2 fusion.65
  10.2 3.7 %collective-permute-start.2 = (bf16[9,256,64]{1,2,0:T(8,128)(2,1)S(1)}, bf16[9,256,64]{1,2,0:T(8,128)(2,1)S(1)}, u32[]{:S(2)}, u32[]{:S(2)}) collective-permute-start(bf16[9,256,64]{1,2,0:T(8,128)(2,1)S(1)} %pad_maximum_fusion.1), channel_id=1, source_target_pairs={{4,12},{12,20},{20,28},{8,0},{16,8},{24,16},{5,13},{13,21},{21,29}... | collective-permute-start | bytes 884744 | tf_op jit(solution)/shard_map/ppermute | solution.py:90
  14.0 3.5 %collective-permute-done.2 = bf16[9,256,64]{1,2,0:T(8,128)(2,1)S(1)} collective-permute-done((bf16[9,256,64]{1,2,0:T(8,128)(2,1)S(1)}, bf16[9,256,64]{1,2,0:T(8,128)(2,1)S(1)}, u32[]{:S(2)}, u32[]{:S(2)}) %collective-permute-start.2) | collective-permute-done | bytes 294944 | tf_op jit(solution)/shard_map/ppermute | solution.py:90
  17.6 0.7 %copy-done.29 = f32[8]{0:T(128)S(1)} copy-done((f32[8]{0:T(128)S(1)}, f32[8]{0:T(128)}, u32[]{:S(2)}) %copy-start.29) | copy-done | bytes 56
  18.2 0.8 %fusion.24 = bf16[8,256,64]{1,2,0:T(8,128)(2,1)} fusion(f32[8,256,64]{1,2,0:T(8,128)S(1)} %get-tuple-element.77, f32[8]{0:T(128)S(1)} %copy-done.29, bf16[9,256,64]{1,2,0:T(8,128)(2,1)S(1)} %collective-permute-done.2), kind=kLoop, calls=%fused_computation.35 | loop fusion | flops 524288 | bytes 1048608 | tf_op jit(solution)/shard_map/convert_element_type | solution.py:84
  19.0 5.3 %collective-permute-start.3 = (bf16[8,256,64]{1,2,0:T(8,128)(2,1)}, bf16[8,256,64]{1,2,0:T(8,128)(2,1)S(1)}, u32[]{:S(2)}, u32[]{:S(2)}) collective-permute-start(bf16[8,256,64]{1,2,0:T(8,128)(2,1)} %fusion.24), channel_id=1, source_target_pairs={{4,20},{12,28},{16,0},{24,8},{5,21},{13,29},{17,1},{25,9},{6,22},{... | collective-permute-start | bytes 786440 | tf_op jit(solution)/shard_map/ppermute | solution.py:84
  24.3 0.6 %slice_convert_fusion = f32[1,256,1]{1,2,0:T(1,128)} fusion(bf16[9,256,64]{1,2,0:T(8,128)(2,1)S(1)} %collective-permute-done.2), kind=kLoop, calls=%fused_computation.99 | loop fusion | flops 256 | bytes 1536 | tf_op jit(solution)/shard_map/convert_element_type | solution.py:55
  24.9 4.2 %conditional.1 = (f32[128,8,64]{0,2,1:T(8,128)S(1)}, f32[128,8]{0,1:T(8,128)S(1)}, f32[128,8]{0,1:T(8,128)}, f32[128,256]{1,0:T(8,128)S(1)}, f32[128,256]{1,0:T(8,128)S(1)}, /*index=5*/f32[128,512]{1,0:T(8,128)S(1)}) conditional(s32[]{:T(128)} %convert_element_type.70, () %tuple.19, (f32[128,8]{0,1:T(8,128)S(1)}, f32[128,256]{1,0:T(8,128)S(1)}, ...), branch_computations={%region_0.1_spmd, %region_1.3_spmd} | conditional | flops 356844544 | bytes 4542572 | solution.py:189
  24.9 0.3 fusion.71
  25.2 0.8 %fusion = f32[128,8,64]{0,2,1:T(8,128)S(1)} fusion(f32[128,8,64]{0,2,1:T(8,128)S(1)} %get-tuple-element.20, f32[8,128]{1,0:T(8,128)S(1)} %bitcast.95, f32[128,128]{1,0:T(8,128)S(1)} %fusion.71, f32[8,128]{1,0:T(8,128)S(1)} %bitcast.91, pred[128,128]{1,0:T(8,128)(4,1)S(1)} %iota_compare_fusion, f32[8]{0:T(128)S(1)} %get-tuple-element.72), kind=kOutput, calls=%fused_computation.1 | convolution fusion | flops 101318656 | bytes 614432 | tf_op jit(solution)/shard_map/cond/branch_1_fun/hts,thp->shp/dot_general | solution.py:166
  26.0 1.1 %fusion.5 = (f32[8,128]{1,0:T(8,128)S(1)}, f32[8,128,128]{2,1,0:T(8,128)S(1)}) fusion(f32[128,128]{1,0:T(8,128)S(1)} %fusion.71, f32[8,128]{1,0:T(8,128)S(1)} %bitcast.92, pred[128,128]{1,0:T(8,128)(4,1)S(1)} %iota_compare_fusion, f32[128,8,64]{0,2,1:T(8,128)S(1)} %get-tuple-element.20, f32[128,8,64]{0,2,1:T(8,128)S(1)} %get-tuple-element.22), kind=kOutput, calls=%fused_computation.7 | convolution fusion | flops 101317632 | bytes 1138688 | tf_op jit(solution)/shard_map/cond/branch_1_fun/thp,shp->hts/dot_general | solution.py:163
  27.1 1.1 %fusion.6 = f32[8,1,128]{2,1,0:T(1,128)S(1)} fusion(f32[8,128,1]{1,2,0:T(1,128)S(1)} %bitcast.96, f32[8,128,128]{2,1,0:T(8,128)S(1)} %get-tuple-element.81, f32[128,128]{1,0:T(8,128)S(1)} %fusion.71, f32[8,128]{1,0:T(8,128)S(1)} %bitcast.93, pred[128,128]{1,0:T(8,128)(4,1)S(1)} %iota_compare_fusion), kind=kOutput, calls=%fused_computation.8 | convolution fusion | flops 2097152 | bytes 618496 | tf_op jit(solution)/shard_map/cond/branch_1_fun/hts,hs->th/dot_general | solution.py:170
  28.1 0.2 multiply_reduce_fusion
  28.4 0.3 fusion.72
  28.6 0.3 fusion.73
  29.1 0.8 %fusion.58 = f32[8]{0:T(128)S(1)} fusion(f32[1,256,1]{1,2,0:T(1,128)} %slice_convert_fusion), kind=kLoop, calls=%fused_computation.102 | loop fusion | flops 8 | bytes 96 | tf_op jit(solution)/shard_map/add | solution.py:56
  29.9 0.1 convert_add_fusion
  30.1 3.2 %collective-permute-start.4 = (f32[8,256,64]{1,2,0:T(8,128)S(1)}, f32[8,256,64]{1,2,0:T(8,128)S(1)}, u32[]{:S(2)}, u32[]{:S(2)}) collective-permute-start(f32[8,256,64]{1,2,0:T(8,128)S(1)} %convert_add_fusion), channel_id=1, source_target_pairs={{0,4},{4,0},{8,12},{12,8},{16,20},{20,16},{24,28},{28,24},{1,5},{5... | collective-permute-start | bytes 1572872 | tf_op jit(solution)/shard_map/ppermute | solution.py:99
  33.3 0.6 %compare_convert_fusion = f32[128]{0:T(128)} fusion(), kind=kLoop, calls=%fused_computation.95 | loop fusion | flops 256 | bytes 512 | tf_op jit(solution)/shard_map/convert_element_type | solution.py:216
  33.9 0.6 %fusion.70 = (f32[1,512]{1,0:T(1,128)}, f32[1,512]{1,0:T(1,128)}, f32[1,512]{1,0:T(1,128)}, f32[1,512]{1,0:T(1,128)}) fusion(f32[4,512]{1,0:T(4,128)S(1)} %copy-done.23), kind=kLoop, calls=%fused_computation.115 | loop fusion | bytes 16384 | tf_op jit(solution)/shard_map/slice | solution.py:240
  34.5 0.3 collective-permute-done.4
  34.8 0.3 copy-done.25
  35.1 0.9 %multiply_reduce_fusion.1 = (f32[8]{0:T(128)}, f32[8,256,64]{1,2,0:T(8,128)S(1)}, f32[8,256,64]{1,2,0:T(8,128)S(1)}) fusion(f32[8,256,64]{1,2,0:T(8,128)S(1)} %convolution_bitcast_fusion.2, f32[8]{0:T(128)S(1)} %copy-done.25, f32[8,256,64]{1,2,0:T(8,128)S(1)} %collective-permute-done.4, f32[8,256,64]{1,2,0:T(8,128)S(1)} %convert_add_fusion, ...), kind=kLoop, calls=%fused_computation.36 | loop fusion | flops 1048568 | bytes 3145825 | tf_op jit(solution)/shard_map/reduce_sum | solution.py:217
  36.0 0.4 multiply_reduce_fusion.2
  36.5 0.1 copy.19
  36.7 2.0 %collective-permute-start.5 = (f32[3,512]{1,0:T(4,128)S(1)}, f32[3,512]{1,0:T(4,128)S(1)}, u32[]{:S(2)}, u32[]{:S(2)}) collective-permute-start(f32[3,512]{1,0:T(4,128)S(1)} %slice.120), channel_id=1, source_target_pairs={{4,0},{8,4},{12,8},{16,12},{20,16},{24,20},{28,24},{5,1},{9,5},{13... | collective-permute-start | bytes 18440 | tf_op jit(solution)/shard_map/ppermute | solution.py:107
  38.7 0.6 %fusion.22 = f32[128,256]{1,0:T(8,128)S(1)} fusion(f32[128,256]{1,0:T(8,128)S(1)} %copy-done.9, f32[8,256,64]{1,2,0:T(8,128)S(1)} %get-tuple-element.74, f32[128,8,64]{0,2,1:T(8,128)S(1)} %bitcast.83, f32[128,8]{0,1:T(8,128)S(1)} %get-tuple-element.93), kind=kOutput, calls=%fused_computation.30 | convolution fusion | flops 201424896 | bytes 1052672 | tf_op jit(solution)/shard_map/lhp,hnp->ln/dot_general | solution.py:219
  39.3 0.2 copy-done.11
  39.6 0.6 %fusion.21 = f32[128,256]{1,0:T(8,128)S(1)} fusion(f32[128,256]{1,0:T(8,128)S(1)} %copy-done.11, f32[8,256,64]{1,2,0:T(8,128)S(1)} %get-tuple-element.75, f32[128,8,64]{0,2,1:T(8,128)S(1)} %bitcast.86, f32[128,8]{0,1:T(8,128)S(1)} %get-tuple-element.92), kind=kOutput, calls=%fused_computation.29 | convolution fusion | flops 201424896 | bytes 1052672 | tf_op jit(solution)/shard_map/lhp,hnp->ln/dot_general | solution.py:222
  40.3 1.7 %collective-permute-start.6 = (bf16[128,256]{1,0:T(8,128)(2,1)S(1)}, bf16[128,256]{1,0:T(8,128)(2,1)S(1)}, u32[]{:S(2)}, u32[]{:S(2)}) collective-permute-start(bf16[128,256]{1,0:T(8,128)(2,1)S(1)} %pad_maximum_fusion.4), channel_id=1, source_target_pairs={{0,1},{1,0},{2,3},{3,2},{4,5},{5,4},{6,7},{7,6},{8,9},{9,8},{10,11... | collective-permute-start | bytes 196616 | tf_op jit(solution)/shard_map/ppermute | solution.py:16
  42.0 0.4 multiply_reduce_fusion.3
  42.4 0.3 copy-done.27
  42.7 0.4 copy-done.30
  43.1 0.8 %fusion.45 = f32[128,8]{0,1:T(8,128)} fusion(f32[128,8]{0,1:T(8,128)S(1)} %get-tuple-element.92, f32[128,8]{0,1:T(8,128)S(1)} %get-tuple-element.96, f32[128,8]{0,1:T(8,128)S(1)} %copy-done.27, f32[128,8]{0,1:T(8,128)S(1)} %multiply_reduce_fusion.3, f32[8]{0:T(128)S(1)} %copy-done.30, f32[128]{0:T(128)S(1)} %copy-done.32, f32[128,8]{0,1:T(8,128)S(1)} %fusion.44), kind=kOutput, calls=%fused_computation.82 | convolution fusion | flops 1595392 | bytes 25120 | tf_op jit(solution)/shard_map/dot_general | solution.py:111
  43.9 0.7 %multiply_add_fusion.3 = f32[128,8]{0,1:T(8,128)} fusion(f32[128,8]{0,1:T(8,128)S(1)} %copy-done.16, f32[128,8]{0,1:T(8,128)S(1)} %get-tuple-element.96, f32[128,8]{0,1:T(8,128)S(1)} %fusion.44, f32[8]{0:T(128)S(1)} %copy-done.22), kind=kLoop, calls=%fused_computation.83 | loop fusion | flops 3072 | bytes 16416 | tf_op jit(solution)/shard_map/add | solution.py:208
  44.6 0.7 %copy-done.18 = f32[1,512]{1,0:T(1,128)S(1)} copy-done((f32[1,512]{1,0:T(1,128)S(1)}, f32[1,512]{1,0:T(1,128)}, u32[]{:S(2)}) %copy-start.18) | copy-done | bytes 2072
  45.2 0.8 %fusion.30 = bf16[128,512]{1,0:T(8,128)(2,1)} fusion(f32[128,512]{1,0:T(8,128)S(1)} %mul.207, f32[3,512]{1,0:T(4,128)S(1)} %collective-permute-done.5, f32[512]{0:T(512)S(1)} %bitcast.100, f32[512]{0:T(512)S(1)} %bitcast.101, f32[512]{0:T(512)S(1)} %bitcast.99, f32[512]{0:T(512)S(1)} %bitcast.98), kind=kLoop, calls=%fused_computation.49 | loop fusion | flops 720896 | bytes 407552 | tf_op jit(solution)/shard_map/convert_element_type | solution.py:242
  46.0 0.7 %slice_add_fusion = (f32[128,128]{1,0:T(8,128)}, f32[128,128]{1,0:T(8,128)}) fusion(f32[128,256]{1,0:T(8,128)S(1)} %convert_element_type.72, f32[128,256]{1,0:T(8,128)S(1)} %fusion.22, pred[]{:T(512)S(6)} %eq.21, f32[128,256]{1,0:T(8,128)S(1)} %fusion.21), kind=kLoop, calls=%fused_computation.69 | loop fusion | flops 65536 | bytes 524289 | tf_op jit(solution)/shard_map/add | solution.py:233
  (90 shorter events, 1.1 us)
Async XLA Ops:
  0.6 3.0 %copy-start = (f32[128,8]{0,1:T(8,128)S(1)}, f32[128,8]{0,1:T(8,128)}, u32[]{:S(2)}) copy-start(f32[128,8]{0,1:T(8,128)} %param.14) | copy-start | bytes 12292
  0.6 3.3 %copy-start.3 = (bf16[128,512]{1,0:T(8,128)(2,1)S(1)}, bf16[128,512]{1,0:T(8,128)(2,1)}, u32[]{:S(2)}) copy-start(bf16[128,512]{1,0:T(8,128)(2,1)} %param.10) | copy-start | bytes 393220
  1.5 4.3 %collective-permute-start = (bf16[128,256]{1,0:T(8,128)(2,1)S(1)}, bf16[128,256]{1,0:T(8,128)(2,1)S(1)}, u32[]{:S(2)}, u32[]{:S(2)}) collective-permute-start(bf16[128,256]{1,0:T(8,128)(2,1)S(1)} %pad_maximum_fusion.3), channel_id=1, source_target_pairs={{0,1},{1,0},{2,3},{3,2},{4,5},{5,4},{6,7},{7,6},{8,9},{9,8},{10,11... | collective-permute-start | bytes 196616 | tf_op jit(solution)/shard_map/ppermute | solution.py:16
  3.6 10.4 %copy-start.4 = (bf16[128,128]{1,0:T(8,128)(2,1)}, bf16[128,128]{1,0:T(8,128)(2,1)S(1)}, u32[]{:S(2)}) copy-start(bf16[128,128]{1,0:T(8,128)(2,1)S(1)} %get-tuple-element.84) | copy-start | bytes 98308
  4.0 5.3 %copy-start.21 = (f32[8]{0:T(128)}, f32[8]{0:T(128)S(1)}, u32[]{:S(2)}) copy-start(f32[8]{0:T(128)S(1)} %slice_reduce_fusion) | copy-start | bytes 100
  4.0 0.7 %copy-start.13 = (f32[128,8]{0,1:T(8,128)S(1)}, f32[128,8]{0,1:T(8,128)}, u32[]{:S(2)}) copy-start(f32[128,8]{0,1:T(8,128)} %param.15) | copy-start | bytes 12292
  4.8 5.2 %copy-start.24 = (f32[8]{0:T(128)}, f32[8]{0:T(128)S(1)}, u32[]{:S(2)}) copy-start(f32[8]{0:T(128)S(1)} %exp.29) | copy-start | bytes 100
  4.8 0.9 %copy-start.12 = (bf16[128,512]{1,0:T(8,128)(2,1)S(1)}, bf16[128,512]{1,0:T(8,128)(2,1)}, u32[]{:S(2)}) copy-start(bf16[128,512]{1,0:T(8,128)(2,1)} %param.11) | copy-start | bytes 393220
  5.8 8.1 %copy-start.1 = (bf16[128,128]{1,0:T(8,128)(2,1)}, bf16[128,128]{1,0:T(8,128)(2,1)S(1)}, u32[]{:S(2)}) copy-start(bf16[128,128]{1,0:T(8,128)(2,1)S(1)} %get-tuple-element.87) | copy-start | bytes 98308
  5.8 8.1 %copy-start.6 = (bf16[128,128]{1,0:T(8,128)(2,1)}, bf16[128,128]{1,0:T(8,128)(2,1)S(1)}, u32[]{:S(2)}) copy-start(bf16[128,128]{1,0:T(8,128)(2,1)S(1)} %get-tuple-element.86) | copy-start | bytes 98308
  6.7 2.7 %collective-permute-start.1 = (f32[9,256,64]{1,2,0:T(8,128)S(1)}, f32[9,256,64]{1,2,0:T(8,128)S(1)}, u32[]{:S(2)}, u32[]{:S(2)}) collective-permute-start(f32[9,256,64]{1,2,0:T(8,128)S(1)} %pad_maximum_fusion), channel_id=1, source_target_pairs={{0,4},{4,0},{8,12},{12,8},{16,20},{20,16},{24,28},{28,24},{1,5},{5... | collective-permute-start | bytes 1769480 | tf_op jit(solution)/shard_map/ppermute | solution.py:72
  9.3 0.5 %copy-start.28 = (f32[8]{0:T(128)}, f32[8]{0:T(128)S(1)}, u32[]{:S(2)}) copy-start(f32[8]{0:T(128)S(1)} %get-tuple-element.79) | copy-start | bytes 100
  10.2 7.4 %collective-permute-start.2 = (bf16[9,256,64]{1,2,0:T(8,128)(2,1)S(1)}, bf16[9,256,64]{1,2,0:T(8,128)(2,1)S(1)}, u32[]{:S(2)}, u32[]{:S(2)}) collective-permute-start(bf16[9,256,64]{1,2,0:T(8,128)(2,1)S(1)} %pad_maximum_fusion.1), channel_id=1, source_target_pairs={{4,12},{12,20},{20,28},{8,0},{16,8},{24,16},{5,13},{13,21},{21,29}... | collective-permute-start | bytes 884744 | tf_op jit(solution)/shard_map/ppermute | solution.py:90
  17.6 0.7 %copy-start.29 = (f32[8]{0:T(128)S(1)}, f32[8]{0:T(128)}, u32[]{:S(2)}) copy-start(f32[8]{0:T(128)} %copy-done.28) | copy-start | bytes 100
  18.2 6.7 %copy-start.14 = (f32[128,8]{0,1:T(8,128)S(1)}, f32[128,8]{0,1:T(8,128)}, u32[]{:S(2)}) copy-start(f32[128,8]{0,1:T(8,128)} %param.15) | copy-start | bytes 12292
  19.0 5.9 %copy-start.31 = (f32[8]{0:T(128)S(1)}, f32[8]{0:T(128)}, u32[]{:S(2)}) copy-start(f32[8]{0:T(128)} %param.16) | copy-start | bytes 100
  19.0 10.9 %collective-permute-start.3 = (bf16[8,256,64]{1,2,0:T(8,128)(2,1)}, bf16[8,256,64]{1,2,0:T(8,128)(2,1)S(1)}, u32[]{:S(2)}, u32[]{:S(2)}) collective-permute-start(bf16[8,256,64]{1,2,0:T(8,128)(2,1)} %fusion.24), channel_id=1, source_target_pairs={{4,20},{12,28},{16,0},{24,8},{5,21},{13,29},{17,1},{25,9},{6,22},{... | collective-permute-start | bytes 786440 | tf_op jit(solution)/shard_map/ppermute | solution.py:84
  27.1 1.1 %copy-start.15 = (f32[8,128]{1,0:T(8,128)}, f32[8,128]{1,0:T(8,128)S(1)}, u32[]{:S(2)}) copy-start(f32[8,128]{1,0:T(8,128)S(1)} %get-tuple-element.80) | copy-start | bytes 12292 | tf_op jit(solution)/shard_map/cond
  29.1 1.0 %copy-start.8 = (f32[128,256]{1,0:T(8,128)}, f32[128,256]{1,0:T(8,128)S(1)}, u32[]{:S(2)}) copy-start(f32[128,256]{1,0:T(8,128)S(1)} %get-tuple-element.68) | copy-start | bytes 393220
  29.1 1.0 %copy-start.10 = (f32[128,256]{1,0:T(8,128)}, f32[128,256]{1,0:T(8,128)S(1)}, u32[]{:S(2)}) copy-start(f32[128,256]{1,0:T(8,128)S(1)} %get-tuple-element.67) | copy-start | bytes 393220
  29.1 1.0 %copy-start.26 = (f32[128,8]{0,1:T(8,128)}, f32[128,8]{0,1:T(8,128)S(1)}, u32[]{:S(2)}) copy-start(f32[128,8]{0,1:T(8,128)S(1)} %get-tuple-element.69) | copy-start | bytes 12292
  30.1 3.8 %copy-start.23 = (f32[4,512]{1,0:T(4,128)S(1)}, f32[4,512]{1,0:T(4,128)}, u32[]{:S(2)}) copy-start(f32[4,512]{1,0:T(4,128)} %param.17) | copy-start | bytes 24580
  30.1 4.7 %collective-permute-start.4 = (f32[8,256,64]{1,2,0:T(8,128)S(1)}, f32[8,256,64]{1,2,0:T(8,128)S(1)}, u32[]{:S(2)}, u32[]{:S(2)}) collective-permute-start(f32[8,256,64]{1,2,0:T(8,128)S(1)} %convert_add_fusion), channel_id=1, source_target_pairs={{0,4},{4,0},{8,12},{12,8},{16,20},{20,16},{24,28},{28,24},{1,5},{5... | collective-permute-start | bytes 1572872 | tf_op jit(solution)/shard_map/ppermute | solution.py:99
  34.5 0.6 %copy-start.25 = (f32[8]{0:T(128)S(1)}, f32[8]{0:T(128)}, u32[]{:S(2)}) copy-start(f32[8]{0:T(128)} %copy-done.24) | copy-start | bytes 100
  34.5 1.5 %copy-start.5 = (bf16[128,128]{1,0:T(8,128)(2,1)S(1)}, bf16[128,128]{1,0:T(8,128)(2,1)}, u32[]{:S(2)}) copy-start(bf16[128,128]{1,0:T(8,128)(2,1)} %copy-done.4) | copy-start | bytes 98308
  34.5 1.5 %copy-start.7 = (bf16[128,128]{1,0:T(8,128)(2,1)S(1)}, bf16[128,128]{1,0:T(8,128)(2,1)}, u32[]{:S(2)}) copy-start(bf16[128,128]{1,0:T(8,128)(2,1)} %copy-done.6) | copy-start | bytes 98308
  36.6 2.1 %copy-start.9 = (f32[128,256]{1,0:T(8,128)S(1)}, f32[128,256]{1,0:T(8,128)}, u32[]{:S(2)}) copy-start(f32[128,256]{1,0:T(8,128)} %copy-done.8) | copy-start | bytes 393220
  36.7 7.9 %collective-permute-start.5 = (f32[3,512]{1,0:T(4,128)S(1)}, f32[3,512]{1,0:T(4,128)S(1)}, u32[]{:S(2)}, u32[]{:S(2)}) collective-permute-start(f32[3,512]{1,0:T(4,128)S(1)} %slice.120), channel_id=1, source_target_pairs={{4,0},{8,4},{12,8},{16,12},{20,16},{24,20},{28,24},{5,1},{9,5},{13... | collective-permute-start | bytes 18440 | tf_op jit(solution)/shard_map/ppermute | solution.py:107
  38.7 0.9 %copy-start.11 = (f32[128,256]{1,0:T(8,128)S(1)}, f32[128,256]{1,0:T(8,128)}, u32[]{:S(2)}) copy-start(f32[128,256]{1,0:T(8,128)} %copy-done.10) | copy-start | bytes 393220
  40.2 1.7 %copy-start.2 = (bf16[128,128]{1,0:T(8,128)(2,1)S(1)}, bf16[128,128]{1,0:T(8,128)(2,1)}, u32[]{:S(2)}) copy-start(bf16[128,128]{1,0:T(8,128)(2,1)} %copy-done.1) | copy-start | bytes 98308
  40.3 5.8 %collective-permute-start.6 = (bf16[128,256]{1,0:T(8,128)(2,1)S(1)}, bf16[128,256]{1,0:T(8,128)(2,1)S(1)}, u32[]{:S(2)}, u32[]{:S(2)}) collective-permute-start(bf16[128,256]{1,0:T(8,128)(2,1)S(1)} %pad_maximum_fusion.4), channel_id=1, source_target_pairs={{0,1},{1,0},{2,3},{3,2},{4,5},{5,4},{6,7},{7,6},{8,9},{9,8},{10,11... | collective-permute-start | bytes 196616 | tf_op jit(solution)/shard_map/ppermute | solution.py:16
  42.0 0.7 %copy-start.27 = (f32[128,8]{0,1:T(8,128)S(1)}, f32[128,8]{0,1:T(8,128)}, u32[]{:S(2)}) copy-start(f32[128,8]{0,1:T(8,128)} %copy-done.26) | copy-start | bytes 12292
  42.0 2.6 %copy-start.19 = (f32[1,512]{1,0:T(1,128)S(1)}, f32[1,512]{1,0:T(1,128)}, u32[]{:S(2)}) copy-start(f32[1,512]{1,0:T(1,128)} %get-tuple-element.90) | copy-start | bytes 6148
  42.0 2.6 %copy-start.20 = (f32[1,512]{1,0:T(1,128)S(1)}, f32[1,512]{1,0:T(1,128)}, u32[]{:S(2)}) copy-start(f32[1,512]{1,0:T(1,128)} %get-tuple-element.91) | copy-start | bytes 6148
  42.4 0.7 %copy-start.30 = (f32[8]{0:T(128)S(1)}, f32[8]{0:T(128)}, u32[]{:S(2)}) copy-start(f32[8]{0:T(128)} %get-tuple-element.73) | copy-start | bytes 100
  42.4 0.7 %copy-start.32 = (f32[128]{0:T(128)S(1)}, f32[128]{0:T(128)}, u32[]{:S(2)}) copy-start(f32[128]{0:T(128)} %compare_convert_fusion) | copy-start | bytes 1540
  43.1 0.8 %copy-start.16 = (f32[128,8]{0,1:T(8,128)S(1)}, f32[128,8]{0,1:T(8,128)}, u32[]{:S(2)}) copy-start(f32[128,8]{0,1:T(8,128)} %get-tuple-element.70) | copy-start | bytes 12292
  43.1 0.8 %copy-start.22 = (f32[8]{0:T(128)S(1)}, f32[8]{0:T(128)}, u32[]{:S(2)}) copy-start(f32[8]{0:T(128)} %copy-done.21) | copy-start | bytes 100
  44.6 0.7 %copy-start.18 = (f32[1,512]{1,0:T(1,128)S(1)}, f32[1,512]{1,0:T(1,128)}, u32[]{:S(2)}) copy-start(f32[1,512]{1,0:T(1,128)} %get-tuple-element.89) | copy-start | bytes 6148
  44.6 0.7 %copy-start.17 = (f32[1,512]{1,0:T(1,128)S(1)}, f32[1,512]{1,0:T(1,128)}, u32[]{:S(2)}) copy-start(f32[1,512]{1,0:T(1,128)} %get-tuple-element.88) | copy-start | bytes 6148

commit v13 on v11

--- a/solution.py
+++ b/solution.py
@@ -146,8 +146,17 @@
     from_start = jnp.exp(cumulative)
     weighted = values3 * (to_end * step_size)[:, :, None]
     seeded = upstream3 * from_start[:, :, None]
-    local_state = jnp.einsum("ln,lhp->hnp", keys_full, weighted, precision=precise)
-    local_grad = jnp.einsum("ln,lhp->hnp", queries_full, seeded, precision=precise)
+    def by_halves(own, other, mix):
+        own_block = jnp.einsum("ln,lhp->hnp", own.astype(jnp.float32), mix, precision=precise)
+        other_block = jnp.einsum("ln,lhp->hnp", other.astype(jnp.float32), mix, precision=precise)
+        return jnp.where(
+            own_first,
+            jnp.concatenate([own_block, other_block], 1),
+            jnp.concatenate([other_block, own_block], 1),
+        )
+
+    local_state = by_halves(write_keys, partner[0], weighted)
+    local_grad = by_halves(read_queries, partner[1], seeded)
     decay_total = jnp.exp(totals)
     def local_terms(keys_full, queries_full, values3, upstream3, cumulative, step_size, preact):
         scores = product(queries_full, keys_full.T)

time: 45.3 us -> 46.8 us (1.033)
  local copies, waits for them, and re-layouts: 4 us -> 5.55 us
  waiting for transfers between devices: 6.64 us -> 5.51 us
    unnamed x54 -> x58, local copies, waits for them, and re-layouts: 3.36 us -> 4.92 us
    add x1, other arithmetic: 0.14 us -> 1.09 us  [paired_scan(): near[1] + near[0][:, None, None] * far_s.astype(jnp.float32)]
    ppermute x2, starting transfers between devices: 3.25 us -> 2.37 us  [swapped(): return lax.ppermute(block, axis, route)]
    ppermute x1, waiting for transfers between devices: 1.63 us -> 0.88 us  [paired_scan(): mate = lax.ppermute(message, axis, swap)]
    add x1, other arithmetic: 0.81 us -> 0.07 us  [unpacked(): row[:heads] + row[heads:2 * heads]]
    convert_element_type x1, other arithmetic: 0.02 us -> 0.75 us  [body(): preact = conv_output.astype(jnp.float32)]
    ppermute x1, starting transfers between devices: 5.25 us -> 5.95 us  [paired_scan(): far_s = lax.ppermute(window[1].astype(jnp.bfloat16), axis, route)]
    convert_element_type x1, other arithmetic: 0.58 us -> 0.01 us  [unpacked(): row = message[heads, :, 0].astype(jnp.float32)]
  transfers between devices with their start and end apart: 7 -> 7, of which waited for: 3 -> 4; matrix products, arithmetic and copies ran while one was open for 23% -> 22% of each run, Pallas kernels for 0% -> 0%
where the time goes in v13:
time: 46.8 us; the launch traced here: 45.9 us
  starting transfers between devices  18.8 us (40%)
  matrix products  7.73 us (17%)
  other arithmetic  7.11 us (15%)
  local copies, waits for them, and re-layouts  5.55 us (12%)
  waiting for transfers between devices  5.51 us (12%)
  between operations  1.12 us (2%)
    ppermute x1, starting transfers between devices, paired_scan(): far_s = lax.ppermute(window[1].astype(jnp.bfloat16), axis, route)  5.95 us
    unnamed x58, local copies, waits for them, and re-layouts  4.92 us
    ppermute x1, starting transfers between devices, paired_scan(): handed = lax.ppermute(passing, axis, swap)  3.87 us
    ppermute x1, starting transfers between devices, paired_scan(): far = lax.ppermute(packed(*window, jnp.bfloat16), axis, route)  3.22 us
    ppermute x1, waiting for transfers between devices, paired_scan(): far = lax.ppermute(packed(*window, jnp.bfloat16), axis, route)  2.97 us
    ppermute x1, starting transfers between devices, shifted(): return lax.ppermute(block, axis, route)  2.41 us
    ppermute x2, starting transfers between devices, swapped(): return lax.ppermute(block, axis, route)  2.37 us
    ppermute x1, waiting for transfers between devices, paired_scan(): handed = lax.ppermute(passing, axis, swap)  1.49 us
  transfers between devices with their start and end apart: 7, of which 4 were waited for; matrix products, arithmetic and copies ran while one was open for 22% of the time, Pallas kernels for 0%

profile of v13, /device:TPU:1, one launch (start us, length us, event | category | flops | bytes accessed | tf_op | source)
XLA Modules:
  0.0 45.9 jit_solution(11719975450947329900)
XLA Ops:
  0.7 0.8 %pad_maximum_fusion.4 = bf16[128,256]{1,0:T(8,128)(2,1)S(1)} fusion(bf16[128,128]{1,0:T(8,128)(2,1)} %param.13, bf16[128,128]{1,0:T(8,128)(2,1)} %param.12), kind=kLoop, calls=%fused_computation.78 | loop fusion | flops 131072 | bytes 131072 | tf_op jit(solution)/shard_map/concatenate | solution.py:123
  1.5 2.1 %collective-permute-start = (bf16[128,256]{1,0:T(8,128)(2,1)S(1)}, bf16[128,256]{1,0:T(8,128)(2,1)S(1)}, u32[]{:S(2)}, u32[]{:S(2)}) collective-permute-start(bf16[128,256]{1,0:T(8,128)(2,1)S(1)} %pad_maximum_fusion.4), channel_id=1, source_target_pairs={{0,1},{1,0},{2,3},{3,2},{4,5},{5,4},{6,7},{7,6},{8,9},{9,8},{10,11... | collective-permute-start | bytes 196616 | tf_op jit(solution)/shard_map/ppermute | solution.py:16
  3.7 0.2 slice_reduce_fusion
  4.1 0.8 %copy-done.4 = bf16[128,512]{1,0:T(8,128)(2,1)S(1)} copy-done((bf16[128,512]{1,0:T(8,128)(2,1)S(1)}, bf16[128,512]{1,0:T(8,128)(2,1)}, u32[]{:S(2)}) %copy-start.4) | copy-done | bytes 131096
  5.1 0.5 %copy-done.16 = f32[128,8]{0,1:T(8,128)S(1)} copy-done((f32[128,8]{0,1:T(8,128)S(1)}, f32[128,8]{0,1:T(8,128)}, u32[]{:S(2)}) %copy-start.16) | copy-done | bytes 4120
  5.7 0.3 convolution_bitcast_fusion.2
  6.0 0.5 %copy-done.5 = bf16[128,128]{1,0:T(8,128)(2,1)S(1)} copy-done((bf16[128,128]{1,0:T(8,128)(2,1)S(1)}, bf16[128,128]{1,0:T(8,128)(2,1)}, u32[]{:S(2)}) %copy-start.5) | copy-done | bytes 32792
  6.5 0.3 convolution_bitcast_fusion.4
  6.8 0.5 %copy-done.24 = f32[8]{0:T(128)} copy-done((f32[8]{0:T(128)}, f32[8]{0:T(128)S(1)}, u32[]{:S(2)}) %copy-start.24) | copy-done | bytes 56
  7.4 0.3 convolution_bitcast_fusion.1
  7.6 0.3 convolution_bitcast_fusion.3
  8.0 1.0 %collective-permute-start.1 = (f32[9,256,64]{1,2,0:T(8,128)S(1)}, f32[9,256,64]{1,2,0:T(8,128)S(1)}, u32[]{:S(2)}, u32[]{:S(2)}) collective-permute-start(f32[9,256,64]{1,2,0:T(8,128)S(1)} %pad_maximum_fusion), channel_id=1, source_target_pairs={{0,4},{4,0},{8,12},{12,8},{16,20},{20,16},{24,28},{28,24},{1,5},{5... | collective-permute-start | bytes 1769480 | tf_op jit(solution)/shard_map/ppermute | solution.py:72
  9.1 0.7 %convert_element_type.63 = f32[128,512]{1,0:T(8,128)} convert(bf16[128,512]{1,0:T(8,128)(2,1)S(1)} %copy-done.4) | non-fusion elementwise | flops 65536 | bytes 393216 | tf_op jit(solution)/shard_map/convert_element_type | solution.py:136
  9.8 0.9 %collective-permute-done.1 = f32[9,256,64]{1,2,0:T(8,128)S(1)} collective-permute-done((f32[9,256,64]{1,2,0:T(8,128)S(1)}, f32[9,256,64]{1,2,0:T(8,128)S(1)}, u32[]{:S(2)}, u32[]{:S(2)}) %collective-permute-start.1) | collective-permute-done | bytes 589856 | tf_op jit(solution)/shard_map/ppermute | solution.py:72
  10.8 0.6 %copy-done.25 = f32[8]{0:T(128)S(1)} copy-done((f32[8]{0:T(128)S(1)}, f32[8]{0:T(128)}, u32[]{:S(2)}) %copy-start.25) | copy-done | bytes 56
  11.4 0.2 fusion.80
  11.6 3.2 %collective-permute-start.2 = (bf16[9,256,64]{1,2,0:T(8,128)(2,1)S(1)}, bf16[9,256,64]{1,2,0:T(8,128)(2,1)S(1)}, u32[]{:S(2)}, u32[]{:S(2)}) collective-permute-start(bf16[9,256,64]{1,2,0:T(8,128)(2,1)S(1)} %pad_maximum_fusion.1), channel_id=1, source_target_pairs={{4,12},{12,20},{20,28},{8,0},{16,8},{24,16},{5,13},{13,21},{21,29}... | collective-permute-start | bytes 884744 | tf_op jit(solution)/shard_map/ppermute | solution.py:90
  14.9 0.6 %copy-done.13 = bf16[128,128]{1,0:T(8,128)(2,1)} copy-done((bf16[128,128]{1,0:T(8,128)(2,1)}, bf16[128,128]{1,0:T(8,128)(2,1)S(1)}, u32[]{:S(2)}) %copy-start.13) | copy-done | bytes 32792
  15.5 3.0 %collective-permute-done.2 = bf16[9,256,64]{1,2,0:T(8,128)(2,1)S(1)} collective-permute-done((bf16[9,256,64]{1,2,0:T(8,128)(2,1)S(1)}, bf16[9,256,64]{1,2,0:T(8,128)(2,1)S(1)}, u32[]{:S(2)}, u32[]{:S(2)}) %collective-permute-start.2) | collective-permute-done | bytes 294944 | tf_op jit(solution)/shard_map/ppermute | solution.py:90
  18.5 0.8 %fusion.24 = bf16[8,256,64]{1,2,0:T(8,128)(2,1)} fusion(f32[8,256,64]{1,2,0:T(8,128)S(1)} %get-tuple-element.77, f32[8]{0:T(128)S(1)} %get-tuple-element.79, bf16[9,256,64]{1,2,0:T(8,128)(2,1)S(1)} %collective-permute-done.2), kind=kLoop, calls=%fused_computation.37 | loop fusion | flops 524288 | bytes 1048608 | tf_op jit(solution)/shard_map/convert_element_type | solution.py:84
  19.3 5.9 %collective-permute-start.3 = (bf16[8,256,64]{1,2,0:T(8,128)(2,1)}, bf16[8,256,64]{1,2,0:T(8,128)(2,1)}, u32[]{:S(2)}, u32[]{:S(2)}) collective-permute-start(bf16[8,256,64]{1,2,0:T(8,128)(2,1)} %fusion.24), channel_id=1, source_target_pairs={{4,20},{12,28},{16,0},{24,8},{5,21},{13,29},{17,1},{25,9},{6,22},{... | collective-permute-start | bytes 786440 | tf_op jit(solution)/shard_map/ppermute | solution.py:84
  25.3 4.2 %conditional.1 = (f32[128,8,64]{0,2,1:T(8,128)S(1)}, f32[128,8]{0,1:T(8,128)S(1)}, f32[128,8]{0,1:T(8,128)}, f32[128,256]{1,0:T(8,128)S(1)}, f32[128,256]{1,0:T(8,128)S(1)}, /*index=5*/f32[128,512]{1,0:T(8,128)S(1)}) conditional(s32[]{:T(128)} %convert_element_type.74, () %tuple.19, (f32[128,8]{0,1:T(8,128)S(1)}, f32[128,256]{1,0:T(8,128)S(1)}, ...), branch_computations={%region_0.1_spmd, %region_1.3_spmd} | conditional | flops 356844544 | bytes 4542572 | solution.py:196
  25.3 0.3 fusion.85
  25.6 0.8 %fusion = f32[128,8,64]{0,2,1:T(8,128)S(1)} fusion(f32[128,8,64]{0,2,1:T(8,128)S(1)} %get-tuple-element.20, f32[8,128]{1,0:T(8,128)S(1)} %bitcast.105, f32[128,128]{1,0:T(8,128)S(1)} %fusion.85, f32[8,128]{1,0:T(8,128)S(1)} %bitcast.101, pred[128,128]{1,0:T(8,128)(4,1)S(1)} %iota_compare_fusion, f32[8]{0:T(128)S(1)} %get-tuple-element.72), kind=kOutput, calls=%fused_computation.1 | convolution fusion | flops 101318656 | bytes 614432 | tf_op jit(solution)/shard_map/cond/branch_1_fun/hts,thp->shp/dot_general | solution.py:173
  26.4 1.1 %fusion.5 = (f32[8,128]{1,0:T(8,128)S(1)}, f32[8,128,128]{2,1,0:T(8,128)S(1)}) fusion(f32[128,128]{1,0:T(8,128)S(1)} %fusion.85, f32[8,128]{1,0:T(8,128)S(1)} %bitcast.102, pred[128,128]{1,0:T(8,128)(4,1)S(1)} %iota_compare_fusion, f32[128,8,64]{0,2,1:T(8,128)S(1)} %get-tuple-element.20, f32[128,8,64]{0,2,1:T(8,128)S(1)} %get-tuple-element.22), kind=kOutput, calls=%fused_computation.7 | convolution fusion | flops 101317632 | bytes 1138688 | tf_op jit(solution)/shard_map/cond/branch_1_fun/thp,shp->hts/dot_general | solution.py:170
  27.5 1.1 %fusion.6 = f32[8,1,128]{2,1,0:T(1,128)S(1)} fusion(f32[8,128,1]{1,2,0:T(1,128)S(1)} %bitcast.106, f32[8,128,128]{2,1,0:T(8,128)S(1)} %get-tuple-element.81, f32[128,128]{1,0:T(8,128)S(1)} %fusion.85, f32[8,128]{1,0:T(8,128)S(1)} %bitcast.103, pred[128,128]{1,0:T(8,128)(4,1)S(1)} %iota_compare_fusion), kind=kOutput, calls=%fused_computation.8 | convolution fusion | flops 2097152 | bytes 618496 | tf_op jit(solution)/shard_map/cond/branch_1_fun/hts,hs->th/dot_general | solution.py:177
  28.6 0.2 multiply_reduce_fusion
  28.8 0.3 fusion.86
  29.1 0.3 fusion.87
  29.6 0.5 %copy-done.27 = f32[128,8]{0,1:T(8,128)} copy-done((f32[128,8]{0,1:T(8,128)}, f32[128,8]{0,1:T(8,128)S(1)}, u32[]{:S(2)}) %copy-start.27) | copy-done | bytes 4120
  30.1 1.1 %convert_add_fusion = f32[8,256,64]{1,2,0:T(8,128)S(1)} fusion(bf16[8,256,64]{1,2,0:T(8,128)(2,1)} %collective-permute-done.3, f32[8]{0:T(128)S(1)} %fusion.73, bf16[9,256,64]{1,2,0:T(8,128)(2,1)S(1)} %copy-done.3), kind=kLoop, calls=%fused_computation.33 | loop fusion | flops 524288 | bytes 1048608 | tf_op jit(solution)/shard_map/add | solution.py:88
  31.2 3.9 %collective-permute-start.4 = (f32[8,256,64]{1,2,0:T(8,128)S(1)}, f32[8,256,64]{1,2,0:T(8,128)S(1)}, u32[]{:S(2)}, u32[]{:S(2)}) collective-permute-start(f32[8,256,64]{1,2,0:T(8,128)S(1)} %convert_add_fusion), channel_id=1, source_target_pairs={{0,4},{4,0},{8,12},{12,8},{16,20},{20,16},{24,28},{28,24},{1,5},{5... | collective-permute-start | bytes 1572872 | tf_op jit(solution)/shard_map/ppermute | solution.py:99
  35.1 1.5 %collective-permute-done.4 = f32[8,256,64]{1,2,0:T(8,128)S(1)} collective-permute-done((f32[8,256,64]{1,2,0:T(8,128)S(1)}, f32[8,256,64]{1,2,0:T(8,128)S(1)}, u32[]{:S(2)}, u32[]{:S(2)}) %collective-permute-start.4) | collective-permute-done | bytes 524320 | tf_op jit(solution)/shard_map/ppermute | solution.py:99
  36.6 0.4 multiply_reduce_fusion.1
  37.0 0.4 multiply_reduce_fusion.2
  37.4 0.1 copy.19
  37.6 2.4 %collective-permute-start.5 = (f32[3,512]{1,0:T(4,128)S(1)}, f32[3,512]{1,0:T(4,128)S(1)}, u32[]{:S(2)}, u32[]{:S(2)}) collective-permute-start(f32[3,512]{1,0:T(4,128)S(1)} %slice.110), channel_id=1, source_target_pairs={{4,0},{8,4},{12,8},{16,12},{20,16},{24,20},{28,24},{5,1},{9,5},{13... | collective-permute-start | bytes 18440 | tf_op jit(solution)/shard_map/ppermute | solution.py:107
  40.0 0.6 %fusion.21 = f32[128,256]{1,0:T(8,128)S(1)} fusion(f32[128,256]{1,0:T(8,128)S(1)} %copy-done.10, f32[8,256,64]{1,2,0:T(8,128)S(1)} %get-tuple-element.75, f32[128,8,64]{0,2,1:T(8,128)S(1)} %bitcast.96, f32[128,8]{0,1:T(8,128)S(1)} %get-tuple-element.90), kind=kOutput, calls=%fused_computation.31 | convolution fusion | flops 201424896 | bytes 1052672 | tf_op jit(solution)/shard_map/lhp,hnp->ln/dot_general | solution.py:229
  40.7 0.6 %fusion.22 = f32[128,256]{1,0:T(8,128)S(1)} fusion(f32[128,256]{1,0:T(8,128)S(1)} %copy-done.8, f32[8,256,64]{1,2,0:T(8,128)S(1)} %get-tuple-element.74, f32[128,8,64]{0,2,1:T(8,128)S(1)} %bitcast.92, f32[128,8]{0,1:T(8,128)S(1)} %get-tuple-element.91), kind=kOutput, calls=%fused_computation.32 | convolution fusion | flops 201424896 | bytes 1052672 | tf_op jit(solution)/shard_map/lhp,hnp->ln/dot_general | solution.py:226
  41.4 0.3 collective-permute-start.6
  41.6 0.5 %copy-done.12 = bf16[128,128]{1,0:T(8,128)(2,1)S(1)} copy-done((bf16[128,128]{1,0:T(8,128)(2,1)S(1)}, bf16[128,128]{1,0:T(8,128)(2,1)}, u32[]{:S(2)}) %copy-start.12) | copy-done | bytes 32792
  42.1 0.4 multiply_reduce_fusion.3
  42.5 0.3 copy-done.28
  42.8 0.8 %fusion.50 = f32[128,8]{0,1:T(8,128)} fusion(f32[128,8]{0,1:T(8,128)S(1)} %get-tuple-element.90, f32[128,8]{0,1:T(8,128)S(1)} %get-tuple-element.92, f32[128,8]{0,1:T(8,128)S(1)} %copy-done.28, f32[128,8]{0,1:T(8,128)S(1)} %multiply_reduce_fusion.3, f32[8]{0:T(128)S(1)} %get-tuple-element.73, f32[128]{0:T(128)S(1)} %compare_convert_fusion, ...), kind=kOutput, calls=%fused_computation.90 | convolution fusion | flops 1595392 | bytes 25120 | tf_op jit(solution)/shard_map/dot_general | solution.py:111
  43.6 0.7 %multiply_add_fusion.3 = f32[128,8]{0,1:T(8,128)} fusion(f32[128,8]{0,1:T(8,128)S(1)} %copy-done.19, f32[128,8]{0,1:T(8,128)S(1)} %get-tuple-element.92, f32[128,8]{0,1:T(8,128)S(1)} %fusion.49, f32[8]{0:T(128)S(1)} %copy-done.22), kind=kLoop, calls=%fused_computation.99 | loop fusion | flops 3072 | bytes 16416 | tf_op jit(solution)/shard_map/add | solution.py:215
  44.3 0.8 %fusion.31 = bf16[128,512]{1,0:T(8,128)(2,1)} fusion(f32[128,512]{1,0:T(8,128)S(1)} %mul.207, f32[3,512]{1,0:T(4,128)S(1)} %collective-permute-done.5, f32[512]{0:T(512)S(1)} %bitcast.110, f32[512]{0:T(512)S(1)} %bitcast.111, f32[512]{0:T(512)S(1)} %bitcast.109, f32[512]{0:T(512)S(1)} %bitcast.108), kind=kLoop, calls=%fused_computation.54 | loop fusion | flops 720896 | bytes 407552 | tf_op jit(solution)/shard_map/convert_element_type | solution.py:249
  45.1 0.2 collective-permute-done.6
  45.2 0.7 %slice_add_fusion = (f32[128,128]{1,0:T(8,128)}, f32[128,128]{1,0:T(8,128)}) fusion(f32[128,256]{1,0:T(8,128)S(1)} %convert_element_type.76, f32[128,256]{1,0:T(8,128)S(1)} %fusion.22, pred[]{:T(512)S(6)} %eq.21, f32[128,256]{1,0:T(8,128)S(1)} %fusion.21), kind=kLoop, calls=%fused_computation.82 | loop fusion | flops 65536 | bytes 524289 | tf_op jit(solution)/shard_map/add | solution.py:240
  (86 shorter events, 1.3 us)
Async XLA Ops:
  0.6 3.0 %copy-start = (f32[128,8]{0,1:T(8,128)S(1)}, f32[128,8]{0,1:T(8,128)}, u32[]{:S(2)}) copy-start(f32[128,8]{0,1:T(8,128)} %param.14) | copy-start | bytes 12292
  0.6 3.3 %copy-start.15 = (bf16[128,512]{1,0:T(8,128)(2,1)S(1)}, bf16[128,512]{1,0:T(8,128)(2,1)}, u32[]{:S(2)}) copy-start(bf16[128,512]{1,0:T(8,128)(2,1)} %param.11) | copy-start | bytes 393220
  1.5 5.9 %collective-permute-start = (bf16[128,256]{1,0:T(8,128)(2,1)S(1)}, bf16[128,256]{1,0:T(8,128)(2,1)S(1)}, u32[]{:S(2)}, u32[]{:S(2)}) collective-permute-start(bf16[128,256]{1,0:T(8,128)(2,1)S(1)} %pad_maximum_fusion.4), channel_id=1, source_target_pairs={{0,1},{1,0},{2,3},{3,2},{4,5},{5,4},{6,7},{7,6},{8,9},{9,8},{10,11... | collective-permute-start | bytes 196616 | tf_op jit(solution)/shard_map/ppermute | solution.py:16
  4.0 2.8 %copy-start.20 = (f32[8]{0:T(128)}, f32[8]{0:T(128)S(1)}, u32[]{:S(2)}) copy-start(f32[8]{0:T(128)S(1)} %slice_reduce_fusion) | copy-start | bytes 100
  4.0 0.9 %copy-start.4 = (bf16[128,512]{1,0:T(8,128)(2,1)S(1)}, bf16[128,512]{1,0:T(8,128)(2,1)}, u32[]{:S(2)}) copy-start(bf16[128,512]{1,0:T(8,128)(2,1)} %param.10) | copy-start | bytes 393220
  5.0 0.7 %copy-start.16 = (f32[128,8]{0,1:T(8,128)S(1)}, f32[128,8]{0,1:T(8,128)}, u32[]{:S(2)}) copy-start(f32[128,8]{0,1:T(8,128)} %param.15) | copy-start | bytes 12292
  5.0 0.8 %copy-start.6 = (bf16[128,128]{1,0:T(8,128)(2,1)S(1)}, bf16[128,128]{1,0:T(8,128)(2,1)}, u32[]{:S(2)}) copy-start(bf16[128,128]{1,0:T(8,128)(2,1)} %param.13) | copy-start | bytes 98308
  5.7 0.8 %copy-start.5 = (bf16[128,128]{1,0:T(8,128)(2,1)S(1)}, bf16[128,128]{1,0:T(8,128)(2,1)}, u32[]{:S(2)}) copy-start(bf16[128,128]{1,0:T(8,128)(2,1)} %param.12) | copy-start | bytes 98308
  6.8 0.6 %copy-start.24 = (f32[8]{0:T(128)}, f32[8]{0:T(128)S(1)}, u32[]{:S(2)}) copy-start(f32[8]{0:T(128)S(1)} %exp.29) | copy-start | bytes 100
  8.0 2.7 %collective-permute-start.1 = (f32[9,256,64]{1,2,0:T(8,128)S(1)}, f32[9,256,64]{1,2,0:T(8,128)S(1)}, u32[]{:S(2)}, u32[]{:S(2)}) collective-permute-start(f32[9,256,64]{1,2,0:T(8,128)S(1)} %pad_maximum_fusion), channel_id=1, source_target_pairs={{0,4},{4,0},{8,12},{12,8},{16,20},{20,16},{24,28},{28,24},{1,5},{5... | collective-permute-start | bytes 1769480 | tf_op jit(solution)/shard_map/ppermute | solution.py:72
  9.8 0.9 %copy-start.21 = (f32[8]{0:T(128)S(1)}, f32[8]{0:T(128)}, u32[]{:S(2)}) copy-start(f32[8]{0:T(128)} %copy-done.20) | copy-start | bytes 100
  10.7 0.7 %copy-start.25 = (f32[8]{0:T(128)S(1)}, f32[8]{0:T(128)}, u32[]{:S(2)}) copy-start(f32[8]{0:T(128)} %copy-done.24) | copy-start | bytes 100
  11.6 6.9 %collective-permute-start.2 = (bf16[9,256,64]{1,2,0:T(8,128)(2,1)S(1)}, bf16[9,256,64]{1,2,0:T(8,128)(2,1)S(1)}, u32[]{:S(2)}, u32[]{:S(2)}) collective-permute-start(bf16[9,256,64]{1,2,0:T(8,128)(2,1)S(1)} %pad_maximum_fusion.1), channel_id=1, source_target_pairs={{4,12},{12,20},{20,28},{8,0},{16,8},{24,16},{5,13},{13,21},{21,29}... | collective-permute-start | bytes 884744 | tf_op jit(solution)/shard_map/ppermute | solution.py:90
  14.9 0.6 %copy-start.13 = (bf16[128,128]{1,0:T(8,128)(2,1)}, bf16[128,128]{1,0:T(8,128)(2,1)S(1)}, u32[]{:S(2)}) copy-start(bf16[128,128]{1,0:T(8,128)(2,1)S(1)} %get-tuple-element.85) | copy-start | bytes 98308
  14.9 0.6 %copy-start.11 = (bf16[128,128]{1,0:T(8,128)(2,1)}, bf16[128,128]{1,0:T(8,128)(2,1)S(1)}, u32[]{:S(2)}) copy-start(bf16[128,128]{1,0:T(8,128)(2,1)S(1)} %get-tuple-element.84) | copy-start | bytes 98308
  18.5 6.8 %copy-start.2 = (bf16[9,256,64]{1,2,0:T(8,128)(2,1)}, bf16[9,256,64]{1,2,0:T(8,128)(2,1)S(1)}, u32[]{:S(2)}) copy-start(bf16[9,256,64]{1,2,0:T(8,128)(2,1)S(1)} %collective-permute-done.2) | copy-start | bytes 884740
  18.5 6.8 %copy-start.1 = (f32[128,512]{1,0:T(8,128)S(1)}, f32[128,512]{1,0:T(8,128)}, u32[]{:S(2)}) copy-start(f32[128,512]{1,0:T(8,128)} %convert_element_type.63) | copy-start | bytes 786436
  18.5 6.8 %copy-start.17 = (f32[128,8]{0,1:T(8,128)S(1)}, f32[128,8]{0,1:T(8,128)}, u32[]{:S(2)}) copy-start(f32[128,8]{0,1:T(8,128)} %param.15) | copy-start | bytes 12292
  19.3 6.0 %copy-start.29 = (f32[8]{0:T(128)S(1)}, f32[8]{0:T(128)}, u32[]{:S(2)}) copy-start(f32[8]{0:T(128)} %param.16) | copy-start | bytes 100
  19.3 10.3 %collective-permute-start.3 = (bf16[8,256,64]{1,2,0:T(8,128)(2,1)}, bf16[8,256,64]{1,2,0:T(8,128)(2,1)}, u32[]{:S(2)}, u32[]{:S(2)}) collective-permute-start(bf16[8,256,64]{1,2,0:T(8,128)(2,1)} %fusion.24), channel_id=1, source_target_pairs={{4,20},{12,28},{16,0},{24,8},{5,21},{13,29},{17,1},{25,9},{6,22},{... | collective-permute-start | bytes 786440 | tf_op jit(solution)/shard_map/ppermute | solution.py:84
  25.3 4.8 %copy-start.3 = (bf16[9,256,64]{1,2,0:T(8,128)(2,1)S(1)}, bf16[9,256,64]{1,2,0:T(8,128)(2,1)}, u32[]{:S(2)}) copy-start(bf16[9,256,64]{1,2,0:T(8,128)(2,1)} %copy-done.2) | copy-start | bytes 884740
  27.5 1.1 %copy-start.18 = (f32[8,128]{1,0:T(8,128)}, f32[8,128]{1,0:T(8,128)S(1)}, u32[]{:S(2)}) copy-start(f32[8,128]{1,0:T(8,128)S(1)} %get-tuple-element.80) | copy-start | bytes 12292 | tf_op jit(solution)/shard_map/cond
  29.5 0.6 %copy-start.27 = (f32[128,8]{0,1:T(8,128)}, f32[128,8]{0,1:T(8,128)S(1)}, u32[]{:S(2)}) copy-start(f32[128,8]{0,1:T(8,128)S(1)} %get-tuple-element.69) | copy-start | bytes 12292
  29.5 1.7 %copy-start.7 = (f32[128,256]{1,0:T(8,128)}, f32[128,256]{1,0:T(8,128)S(1)}, u32[]{:S(2)}) copy-start(f32[128,256]{1,0:T(8,128)S(1)} %get-tuple-element.68) | copy-start | bytes 393220
  29.5 1.7 %copy-start.9 = (f32[128,256]{1,0:T(8,128)}, f32[128,256]{1,0:T(8,128)S(1)}, u32[]{:S(2)}) copy-start(f32[128,256]{1,0:T(8,128)S(1)} %get-tuple-element.67) | copy-start | bytes 393220
  31.2 3.9 %copy-start.23 = (f32[4,512]{1,0:T(4,128)S(1)}, f32[4,512]{1,0:T(4,128)}, u32[]{:S(2)}) copy-start(f32[4,512]{1,0:T(4,128)} %param.17) | copy-start | bytes 24580
  31.2 5.4 %collective-permute-start.4 = (f32[8,256,64]{1,2,0:T(8,128)S(1)}, f32[8,256,64]{1,2,0:T(8,128)S(1)}, u32[]{:S(2)}, u32[]{:S(2)}) collective-permute-start(f32[8,256,64]{1,2,0:T(8,128)S(1)} %convert_add_fusion), channel_id=1, source_target_pairs={{0,4},{4,0},{8,12},{12,8},{16,20},{20,16},{24,28},{28,24},{1,5},{5... | collective-permute-start | bytes 1572872 | tf_op jit(solution)/shard_map/ppermute | solution.py:99
  35.1 1.5 %copy-start.26 = (f32[8]{0:T(128)S(1)}, f32[8]{0:T(128)}, u32[]{:S(2)}) copy-start(f32[8]{0:T(128)} %copy-done.24) | copy-start | bytes 100
  35.1 1.9 %copy-start.14 = (bf16[128,128]{1,0:T(8,128)(2,1)S(1)}, bf16[128,128]{1,0:T(8,128)(2,1)}, u32[]{:S(2)}) copy-start(bf16[128,128]{1,0:T(8,128)(2,1)} %copy-done.13) | copy-start | bytes 98308
  37.5 2.5 %copy-start.10 = (f32[128,256]{1,0:T(8,128)S(1)}, f32[128,256]{1,0:T(8,128)}, u32[]{:S(2)}) copy-start(f32[128,256]{1,0:T(8,128)} %copy-done.9) | copy-start | bytes 393220
  37.6 3.1 %copy-start.8 = (f32[128,256]{1,0:T(8,128)S(1)}, f32[128,256]{1,0:T(8,128)}, u32[]{:S(2)}) copy-start(f32[128,256]{1,0:T(8,128)} %copy-done.7) | copy-start | bytes 393220
  37.6 6.7 %collective-permute-start.5 = (f32[3,512]{1,0:T(4,128)S(1)}, f32[3,512]{1,0:T(4,128)S(1)}, u32[]{:S(2)}, u32[]{:S(2)}) collective-permute-start(f32[3,512]{1,0:T(4,128)S(1)} %slice.110), channel_id=1, source_target_pairs={{4,0},{8,4},{12,8},{16,12},{20,16},{24,20},{28,24},{5,1},{9,5},{13... | collective-permute-start | bytes 18440 | tf_op jit(solution)/shard_map/ppermute | solution.py:107
  41.3 0.8 %copy-start.12 = (bf16[128,128]{1,0:T(8,128)(2,1)S(1)}, bf16[128,128]{1,0:T(8,128)(2,1)}, u32[]{:S(2)}) copy-start(bf16[128,128]{1,0:T(8,128)(2,1)} %copy-done.11) | copy-start | bytes 98308
  41.4 3.9 %collective-permute-start.6 = (bf16[128,256]{1,0:T(8,128)(2,1)S(1)}, bf16[128,256]{1,0:T(8,128)(2,1)S(1)}, u32[]{:S(2)}, u32[]{:S(2)}) collective-permute-start(bf16[128,256]{1,0:T(8,128)(2,1)S(1)} %pad_maximum_fusion.6), channel_id=1, source_target_pairs={{0,1},{1,0},{2,3},{3,2},{4,5},{5,4},{6,7},{7,6},{8,9},{9,8},{10,11... | collective-permute-start | bytes 196616 | tf_op jit(solution)/shard_map/ppermute | solution.py:16
  42.1 0.7 %copy-start.28 = (f32[128,8]{0,1:T(8,128)S(1)}, f32[128,8]{0,1:T(8,128)}, u32[]{:S(2)}) copy-start(f32[128,8]{0,1:T(8,128)} %copy-done.27) | copy-start | bytes 12292
  42.8 0.8 %copy-start.19 = (f32[128,8]{0,1:T(8,128)S(1)}, f32[128,8]{0,1:T(8,128)}, u32[]{:S(2)}) copy-start(f32[128,8]{0,1:T(8,128)} %get-tuple-element.70) | copy-start | bytes 12292
  42.8 0.8 %copy-start.22 = (f32[8]{0:T(128)S(1)}, f32[8]{0:T(128)}, u32[]{:S(2)}) copy-start(f32[8]{0:T(128)} %copy-done.20) | copy-start | bytes 100

commit v14 on v11

--- a/solution.py
+++ b/solution.py
@@ -223,6 +223,7 @@
     key_other = jnp.where(own_first, key_part[:, half_width:], key_part[:, :half_width])
     query_mine = jnp.where(own_first, query_part[:, :half_width], query_part[:, half_width:])
     query_other = jnp.where(own_first, query_part[:, half_width:], query_part[:, :half_width])
+    key_mine, query_mine = lax.optimization_barrier((key_mine, query_mine))
     sent_back = swapped(
         jnp.concatenate([key_other, query_other], 1).astype(jnp.bfloat16), "head", 0
     ).astype(key_other.dtype)

time: 45.3 us -> 46.7 us (1.031)
  other arithmetic: 6.65 us -> 7.71 us
  local copies, waits for them, and re-layouts: 4 us -> 4.86 us
  waiting for transfers between devices: 6.64 us -> 6.13 us
    unnamed x54, local copies, waits for them, and re-layouts: 3.36 us -> 4.22 us
    reduce_sum x1, other arithmetic: 0.35 us -> 0.93 us  [body(): jnp.sum(arriving * leaving, (1, 2))[None, :]]
    convert_element_type x1, other arithmetic: 0.01 us -> 0.54 us  [body(): (lax.broadcasted_iota(jnp.int32, (length, 1), 0) == length - 1).astype(jn...]
    ppermute x1, waiting for transfers between devices: 1.48 us -> 0.95 us  [paired_scan(): handed = lax.ppermute(passing, axis, swap)]
  transfers between devices with their start and end apart: 7 -> 7, of which waited for: 3 -> 3; matrix products, arithmetic and copies ran while one was open for 23% -> 20% of each run, Pallas kernels for 0% -> 0%
where the time goes in v14:
time: 46.7 us; the launch traced here: 46.1 us
  starting transfers between devices  18.7 us (40%)
  other arithmetic  7.71 us (17%)
  matrix products  7.44 us (16%)
  waiting for transfers between devices  6.13 us (13%)
  local copies, waits for them, and re-layouts  4.86 us (10%)
  between operations  1.12 us (2%)
    ppermute x1, starting transfers between devices, paired_scan(): far_s = lax.ppermute(window[1].astype(jnp.bfloat16), axis, route)  5.25 us
    unnamed x54, local copies, waits for them, and re-layouts  4.22 us
    ppermute x1, starting transfers between devices, paired_scan(): handed = lax.ppermute(passing, axis, swap)  3.72 us
    ppermute x1, waiting for transfers between devices, paired_scan(): far = lax.ppermute(packed(*window, jnp.bfloat16), axis, route)  3.54 us
    ppermute x2, starting transfers between devices, swapped(): return lax.ppermute(block, axis, route)  3.25 us
    ppermute x1, starting transfers between devices, paired_scan(): far = lax.ppermute(packed(*window, jnp.bfloat16), axis, route)  3.22 us
    ppermute x1, starting transfers between devices, shifted(): return lax.ppermute(block, axis, route)  2.28 us
    ppermute x1, waiting for transfers between devices, paired_scan(): mate = lax.ppermute(message, axis, swap)  1.63 us
  transfers between devices with their start and end apart: 7, of which 3 were waited for; matrix products, arithmetic and copies ran while one was open for 20% of the time, Pallas kernels for 0%

profile of v14, /device:TPU:1, one launch (start us, length us, event | category | flops | bytes accessed | tf_op | source)
XLA Modules:
  0.0 46.1 jit_solution(8376475663370200261)
XLA Ops:
  0.7 0.8 %pad_maximum_fusion.4 = bf16[128,256]{1,0:T(8,128)(2,1)S(1)} fusion(bf16[128,128]{1,0:T(8,128)(2,1)} %param.13, bf16[128,128]{1,0:T(8,128)(2,1)} %param.12), kind=kLoop, calls=%fused_computation.70 | loop fusion | flops 131072 | bytes 131072 | tf_op jit(solution)/shard_map/concatenate | solution.py:123
  1.5 2.1 %collective-permute-start = (bf16[128,256]{1,0:T(8,128)(2,1)S(1)}, bf16[128,256]{1,0:T(8,128)(2,1)S(1)}, u32[]{:S(2)}, u32[]{:S(2)}) collective-permute-start(bf16[128,256]{1,0:T(8,128)(2,1)S(1)} %pad_maximum_fusion.4), channel_id=1, source_target_pairs={{0,1},{1,0},{2,3},{3,2},{4,5},{5,4},{6,7},{7,6},{8,9},{9,8},{10,11... | collective-permute-start | bytes 196616 | tf_op jit(solution)/shard_map/ppermute | solution.py:16
  3.6 0.1 fusion.46
  3.7 0.2 slice_reduce_fusion
  4.1 0.6 %copy-done.14 = f32[128,8]{0,1:T(8,128)S(1)} copy-done((f32[128,8]{0,1:T(8,128)S(1)}, f32[128,8]{0,1:T(8,128)}, u32[]{:S(2)}) %copy-start.14) | copy-done | bytes 4120
  4.7 0.1 copy.17
  4.9 0.8 %copy-done.13 = bf16[128,512]{1,0:T(8,128)(2,1)S(1)} copy-done((bf16[128,512]{1,0:T(8,128)(2,1)S(1)}, bf16[128,512]{1,0:T(8,128)(2,1)}, u32[]{:S(2)}) %copy-start.13) | copy-done | bytes 131096
  5.8 0.7 %copy-done.5 = bf16[128,128]{1,0:T(8,128)(2,1)S(1)} copy-done((bf16[128,128]{1,0:T(8,128)(2,1)S(1)}, bf16[128,128]{1,0:T(8,128)(2,1)}, u32[]{:S(2)}) %copy-start.5) | copy-done | bytes 32792
  6.5 0.4 convolution_bitcast_fusion.2
  6.9 0.4 copy-done.1
  7.3 0.4 broadcast_select_fusion.2
  7.7 1.0 %collective-permute-start.1 = (f32[9,256,64]{1,2,0:T(8,128)S(1)}, f32[9,256,64]{1,2,0:T(8,128)S(1)}, u32[]{:S(2)}, u32[]{:S(2)}) collective-permute-start(f32[9,256,64]{1,2,0:T(8,128)S(1)} %pad_maximum_fusion), channel_id=1, source_target_pairs={{0,4},{4,0},{8,12},{12,8},{16,20},{20,16},{24,28},{28,24},{1,5},{5... | collective-permute-start | bytes 1769480 | tf_op jit(solution)/shard_map/ppermute | solution.py:72
  8.8 1.6 %collective-permute-done.1 = f32[9,256,64]{1,2,0:T(8,128)S(1)} collective-permute-done((f32[9,256,64]{1,2,0:T(8,128)S(1)}, f32[9,256,64]{1,2,0:T(8,128)S(1)}, u32[]{:S(2)}, u32[]{:S(2)}) %collective-permute-start.1) | collective-permute-done | bytes 589856 | tf_op jit(solution)/shard_map/ppermute | solution.py:72
  10.5 0.2 fusion.73
  10.7 3.2 %collective-permute-start.2 = (bf16[9,256,64]{1,2,0:T(8,128)(2,1)S(1)}, bf16[9,256,64]{1,2,0:T(8,128)(2,1)S(1)}, u32[]{:S(2)}, u32[]{:S(2)}) collective-permute-start(bf16[9,256,64]{1,2,0:T(8,128)(2,1)S(1)} %pad_maximum_fusion.1), channel_id=1, source_target_pairs={{4,12},{12,20},{20,28},{8,0},{16,8},{24,16},{5,13},{13,21},{21,29}... | collective-permute-start | bytes 884744 | tf_op jit(solution)/shard_map/ppermute | solution.py:90
  14.0 3.5 %collective-permute-done.2 = bf16[9,256,64]{1,2,0:T(8,128)(2,1)S(1)} collective-permute-done((bf16[9,256,64]{1,2,0:T(8,128)(2,1)S(1)}, bf16[9,256,64]{1,2,0:T(8,128)(2,1)S(1)}, u32[]{:S(2)}, u32[]{:S(2)}) %collective-permute-start.2) | collective-permute-done | bytes 294944 | tf_op jit(solution)/shard_map/ppermute | solution.py:90
  17.6 0.8 %fusion.24 = bf16[8,256,64]{1,2,0:T(8,128)(2,1)} fusion(f32[8,256,64]{1,2,0:T(8,128)S(1)} %get-tuple-element.81, f32[8]{0:T(128)S(1)} %get-tuple-element.83, bf16[9,256,64]{1,2,0:T(8,128)(2,1)S(1)} %collective-permute-done.2), kind=kLoop, calls=%fused_computation.35 | loop fusion | flops 524288 | bytes 1048608 | tf_op jit(solution)/shard_map/convert_element_type | solution.py:84
  18.4 5.3 %collective-permute-start.3 = (bf16[8,256,64]{1,2,0:T(8,128)(2,1)}, bf16[8,256,64]{1,2,0:T(8,128)(2,1)S(1)}, u32[]{:S(2)}, u32[]{:S(2)}) collective-permute-start(bf16[8,256,64]{1,2,0:T(8,128)(2,1)} %fusion.24), channel_id=1, source_target_pairs={{4,20},{12,28},{16,0},{24,8},{5,21},{13,29},{17,1},{25,9},{6,22},{... | collective-permute-start | bytes 786440 | tf_op jit(solution)/shard_map/ppermute | solution.py:84
  23.7 0.5 %slice_convert_fusion = f32[1,256,1]{1,2,0:T(1,128)} fusion(bf16[9,256,64]{1,2,0:T(8,128)(2,1)S(1)} %collective-permute-done.2), kind=kLoop, calls=%fused_computation.103 | loop fusion | flops 256 | bytes 1536 | tf_op jit(solution)/shard_map/convert_element_type | solution.py:55
  24.2 4.2 %conditional.1 = (f32[128,8,64]{0,2,1:T(8,128)S(1)}, f32[128,8]{0,1:T(8,128)S(1)}, f32[128,8]{0,1:T(8,128)}, f32[128,256]{1,0:T(8,128)S(1)}, f32[128,256]{1,0:T(8,128)S(1)}, /*index=5*/f32[128,512]{1,0:T(8,128)S(1)}) conditional(s32[]{:T(128)} %convert_element_type.70, () %tuple.20, (f32[128,8]{0,1:T(8,128)S(1)}, f32[128,256]{1,0:T(8,128)S(1)}, ...), branch_computations={%region_0.1_spmd, %region_1.3_spmd} | conditional | flops 356844544 | bytes 4542572 | solution.py:187
  24.2 0.3 fusion.78
  24.5 0.8 %fusion = f32[128,8,64]{0,2,1:T(8,128)S(1)} fusion(f32[128,8,64]{0,2,1:T(8,128)S(1)} %get-tuple-element.20, f32[8,128]{1,0:T(8,128)S(1)} %bitcast.95, f32[128,128]{1,0:T(8,128)S(1)} %fusion.78, f32[8,128]{1,0:T(8,128)S(1)} %bitcast.91, pred[128,128]{1,0:T(8,128)(4,1)S(1)} %iota_compare_fusion, f32[8]{0:T(128)S(1)} %get-tuple-element.76), kind=kOutput, calls=%fused_computation.1 | convolution fusion | flops 101318656 | bytes 614432 | tf_op jit(solution)/shard_map/cond/branch_1_fun/hts,thp->shp/dot_general | solution.py:164
  25.3 1.1 %fusion.5 = (f32[8,128]{1,0:T(8,128)S(1)}, f32[8,128,128]{2,1,0:T(8,128)S(1)}) fusion(f32[128,128]{1,0:T(8,128)S(1)} %fusion.78, f32[8,128]{1,0:T(8,128)S(1)} %bitcast.92, pred[128,128]{1,0:T(8,128)(4,1)S(1)} %iota_compare_fusion, f32[128,8,64]{0,2,1:T(8,128)S(1)} %get-tuple-element.20, f32[128,8,64]{0,2,1:T(8,128)S(1)} %get-tuple-element.22), kind=kOutput, calls=%fused_computation.7 | convolution fusion | flops 101317632 | bytes 1138688 | tf_op jit(solution)/shard_map/cond/branch_1_fun/thp,shp->hts/dot_general | solution.py:161
  26.4 1.1 %fusion.6 = f32[8,1,128]{2,1,0:T(1,128)S(1)} fusion(f32[8,128,1]{1,2,0:T(1,128)S(1)} %bitcast.96, f32[8,128,128]{2,1,0:T(8,128)S(1)} %get-tuple-element.85, f32[128,128]{1,0:T(8,128)S(1)} %fusion.78, f32[8,128]{1,0:T(8,128)S(1)} %bitcast.93, pred[128,128]{1,0:T(8,128)(4,1)S(1)} %iota_compare_fusion), kind=kOutput, calls=%fused_computation.8 | convolution fusion | flops 2097152 | bytes 618496 | tf_op jit(solution)/shard_map/cond/branch_1_fun/hts,hs->th/dot_general | solution.py:168
  27.5 0.2 multiply_reduce_fusion
  27.7 0.3 fusion.79
  28.0 0.3 fusion.80
  28.4 0.8 %fusion.60 = f32[8]{0:T(128)S(1)} fusion(f32[1,256,1]{1,2,0:T(1,128)} %slice_convert_fusion), kind=kLoop, calls=%fused_computation.106 | loop fusion | flops 8 | bytes 96 | tf_op jit(solution)/shard_map/add | solution.py:56
  29.2 0.1 convert_add_fusion
  29.4 3.7 %collective-permute-start.4 = (f32[8,256,64]{1,2,0:T(8,128)S(1)}, f32[8,256,64]{1,2,0:T(8,128)S(1)}, u32[]{:S(2)}, u32[]{:S(2)}) collective-permute-start(f32[8,256,64]{1,2,0:T(8,128)S(1)} %convert_add_fusion), channel_id=1, source_target_pairs={{0,4},{4,0},{8,12},{12,8},{16,20},{20,16},{24,28},{28,24},{1,5},{5... | collective-permute-start | bytes 1572872 | tf_op jit(solution)/shard_map/ppermute | solution.py:99
  33.1 0.5 %compare_convert_fusion = f32[128]{0:T(128)} fusion(), kind=kLoop, calls=%fused_computation.99 | loop fusion | flops 256 | bytes 512 | tf_op jit(solution)/shard_map/convert_element_type | solution.py:214
  33.7 1.0 %collective-permute-done.4 = f32[8,256,64]{1,2,0:T(8,128)S(1)} collective-permute-done((f32[8,256,64]{1,2,0:T(8,128)S(1)}, f32[8,256,64]{1,2,0:T(8,128)S(1)}, u32[]{:S(2)}, u32[]{:S(2)}) %collective-permute-start.4) | collective-permute-done | bytes 524320 | tf_op jit(solution)/shard_map/ppermute | solution.py:99
  34.6 0.9 %multiply_reduce_fusion.1 = (f32[8]{0:T(128)}, f32[8,256,64]{1,2,0:T(8,128)S(1)}, f32[8,256,64]{1,2,0:T(8,128)S(1)}) fusion(f32[8,256,64]{1,2,0:T(8,128)S(1)} %convolution_bitcast_fusion.2, f32[8]{0:T(128)S(1)} %copy-done.22, f32[8,256,64]{1,2,0:T(8,128)S(1)} %collective-permute-done.4, f32[8,256,64]{1,2,0:T(8,128)S(1)} %convert_add_fusion, ...), kind=kLoop, calls=%fused_computation.36 | loop fusion | flops 1048568 | bytes 3145825 | tf_op jit(solution)/shard_map/reduce_sum | solution.py:215
  35.6 0.6 %fusion.22 = f32[128,256]{1,0:T(8,128)S(1)} fusion(f32[128,256]{1,0:T(8,128)S(1)} %copy-done.10, f32[8,256,64]{1,2,0:T(8,128)S(1)} %get-tuple-element.78, f32[128,8,64]{0,2,1:T(8,128)S(1)} %bitcast.83, f32[128,8]{0,1:T(8,128)S(1)} %get-tuple-element.95), kind=kOutput, calls=%fused_computation.30 | convolution fusion | flops 201424896 | bytes 1052672 | tf_op jit(solution)/shard_map/lhp,hnp->ln/dot_general | solution.py:217
  36.2 0.3 copy-done.12
  36.5 0.6 %fusion.21 = f32[128,256]{1,0:T(8,128)S(1)} fusion(f32[128,256]{1,0:T(8,128)S(1)} %copy-done.12, f32[8,256,64]{1,2,0:T(8,128)S(1)} %get-tuple-element.79, f32[128,8,64]{0,2,1:T(8,128)S(1)} %bitcast.86, f32[128,8]{0,1:T(8,128)S(1)} %get-tuple-element.94), kind=kOutput, calls=%fused_computation.29 | convolution fusion | flops 201424896 | bytes 1052672 | tf_op jit(solution)/shard_map/lhp,hnp->ln/dot_general | solution.py:220
  37.2 0.7 %copy-done.6 = bf16[128,128]{1,0:T(8,128)(2,1)S(1)} copy-done((bf16[128,128]{1,0:T(8,128)(2,1)S(1)}, bf16[128,128]{1,0:T(8,128)(2,1)}, u32[]{:S(2)}) %copy-start.6) | copy-done | bytes 32792
  37.9 0.4 multiply_reduce_fusion.2
  38.4 0.1 copy.19
  38.5 2.3 %collective-permute-start.5 = (f32[3,512]{1,0:T(4,128)S(1)}, f32[3,512]{1,0:T(4,128)S(1)}, u32[]{:S(2)}, u32[]{:S(2)}) collective-permute-start(f32[3,512]{1,0:T(4,128)S(1)} %slice.110), channel_id=1, source_target_pairs={{4,0},{8,4},{12,8},{16,12},{20,16},{24,20},{28,24},{5,1},{9,5},{13... | collective-permute-start | bytes 18440 | tf_op jit(solution)/shard_map/ppermute | solution.py:107
  40.9 1.2 %collective-permute-start.6 = (bf16[128,256]{1,0:T(8,128)(2,1)S(1)}, bf16[128,256]{1,0:T(8,128)(2,1)S(1)}, u32[]{:S(2)}, u32[]{:S(2)}) collective-permute-start(bf16[128,256]{1,0:T(8,128)(2,1)S(1)} %pad_maximum_fusion.6), channel_id=1, source_target_pairs={{0,1},{1,0},{2,3},{3,2},{4,5},{5,4},{6,7},{7,6},{8,9},{9,8},{10,11... | collective-permute-start | bytes 196616 | tf_op jit(solution)/shard_map/ppermute | solution.py:16
  42.0 0.4 multiply_reduce_fusion.3
  42.4 0.3 copy-done.24
  42.7 0.4 copy-done.25
  43.1 0.8 %fusion.47 = f32[128,8]{0,1:T(8,128)} fusion(f32[128,8]{0,1:T(8,128)S(1)} %get-tuple-element.94, f32[128,8]{0,1:T(8,128)S(1)} %get-tuple-element.98, f32[128,8]{0,1:T(8,128)S(1)} %copy-done.24, f32[128,8]{0,1:T(8,128)S(1)} %multiply_reduce_fusion.3, f32[8]{0:T(128)S(1)} %copy-done.25, f32[128]{0:T(128)S(1)} %copy-done.27, f32[128,8]{0,1:T(8,128)S(1)} %fusion.46), kind=kOutput, calls=%fused_computation.84 | convolution fusion | flops 1595392 | bytes 25120 | tf_op jit(solution)/shard_map/dot_general | solution.py:111
  43.9 0.7 %multiply_add_fusion.3 = f32[128,8]{0,1:T(8,128)} fusion(f32[128,8]{0,1:T(8,128)S(1)} %copy-done.17, f32[128,8]{0,1:T(8,128)S(1)} %get-tuple-element.98, f32[128,8]{0,1:T(8,128)S(1)} %fusion.46, f32[8]{0:T(128)S(1)} %copy-done.19), kind=kLoop, calls=%fused_computation.87 | loop fusion | flops 3072 | bytes 16416 | tf_op jit(solution)/shard_map/add | solution.py:206
  44.6 0.8 %fusion.30 = bf16[128,512]{1,0:T(8,128)(2,1)} fusion(f32[128,512]{1,0:T(8,128)S(1)} %mul.207, f32[3,512]{1,0:T(4,128)S(1)} %collective-permute-done.5, f32[512]{0:T(512)S(1)} %bitcast.100, f32[512]{0:T(512)S(1)} %bitcast.101, f32[512]{0:T(512)S(1)} %bitcast.99, f32[512]{0:T(512)S(1)} %bitcast.98), kind=kLoop, calls=%fused_computation.49 | loop fusion | flops 720896 | bytes 407552 | tf_op jit(solution)/shard_map/convert_element_type | solution.py:241
  45.4 0.7 %slice_add_fusion = (f32[128,128]{1,0:T(8,128)}, f32[128,128]{1,0:T(8,128)}) fusion(f32[128,128]{1,0:T(8,128)S(1)} %get-tuple-element.72, f32[128,256]{1,0:T(8,128)S(1)} %convert_element_type.72, f32[128,128]{1,0:T(8,128)S(1)} %get-tuple-element.71), kind=kLoop, calls=%fused_computation.74 | loop fusion | flops 32768 | bytes 393216 | tf_op jit(solution)/shard_map/add | solution.py:232
  (80 shorter events, 0.9 us)
Async XLA Ops:
  0.6 3.0 %copy-start = (f32[128,8]{0,1:T(8,128)S(1)}, f32[128,8]{0,1:T(8,128)}, u32[]{:S(2)}) copy-start(f32[128,8]{0,1:T(8,128)} %param.14) | copy-start | bytes 12292
  0.6 3.3 %copy-start.4 = (bf16[128,512]{1,0:T(8,128)(2,1)S(1)}, bf16[128,512]{1,0:T(8,128)(2,1)}, u32[]{:S(2)}) copy-start(bf16[128,512]{1,0:T(8,128)(2,1)} %param.10) | copy-start | bytes 393220
  1.5 4.3 %collective-permute-start = (bf16[128,256]{1,0:T(8,128)(2,1)S(1)}, bf16[128,256]{1,0:T(8,128)(2,1)S(1)}, u32[]{:S(2)}, u32[]{:S(2)}) collective-permute-start(bf16[128,256]{1,0:T(8,128)(2,1)S(1)} %pad_maximum_fusion.4), channel_id=1, source_target_pairs={{0,1},{1,0},{2,3},{3,2},{4,5},{5,4},{6,7},{7,6},{8,9},{9,8},{10,11... | collective-permute-start | bytes 196616 | tf_op jit(solution)/shard_map/ppermute | solution.py:16
  4.0 6.4 %copy-start.18 = (f32[8]{0:T(128)}, f32[8]{0:T(128)S(1)}, u32[]{:S(2)}) copy-start(f32[8]{0:T(128)S(1)} %slice_reduce_fusion) | copy-start | bytes 100
  4.0 0.7 %copy-start.14 = (f32[128,8]{0,1:T(8,128)S(1)}, f32[128,8]{0,1:T(8,128)}, u32[]{:S(2)}) copy-start(f32[128,8]{0,1:T(8,128)} %param.15) | copy-start | bytes 12292
  4.7 5.7 %copy-start.21 = (f32[8]{0:T(128)}, f32[8]{0:T(128)S(1)}, u32[]{:S(2)}) copy-start(f32[8]{0:T(128)S(1)} %exp.29) | copy-start | bytes 100
  4.7 0.9 %copy-start.13 = (bf16[128,512]{1,0:T(8,128)(2,1)S(1)}, bf16[128,512]{1,0:T(8,128)(2,1)}, u32[]{:S(2)}) copy-start(bf16[128,512]{1,0:T(8,128)(2,1)} %param.11) | copy-start | bytes 393220
  5.8 0.8 %copy-start.5 = (bf16[128,128]{1,0:T(8,128)(2,1)S(1)}, bf16[128,128]{1,0:T(8,128)(2,1)}, u32[]{:S(2)}) copy-start(bf16[128,128]{1,0:T(8,128)(2,1)} %param.12) | copy-start | bytes 98308
  5.8 8.2 %copy-start.7 = (bf16[128,128]{1,0:T(8,128)(2,1)}, bf16[128,128]{1,0:T(8,128)(2,1)S(1)}, u32[]{:S(2)}) copy-start(bf16[128,128]{1,0:T(8,128)(2,1)S(1)} %get-tuple-element.88) | copy-start | bytes 98308
  5.8 8.2 %copy-start.2 = (bf16[128,128]{1,0:T(8,128)(2,1)}, bf16[128,128]{1,0:T(8,128)(2,1)S(1)}, u32[]{:S(2)}) copy-start(bf16[128,128]{1,0:T(8,128)(2,1)S(1)} %get-tuple-element.89) | copy-start | bytes 98308
  6.5 0.8 %copy-start.1 = (bf16[128,128]{1,0:T(8,128)(2,1)S(1)}, bf16[128,128]{1,0:T(8,128)(2,1)}, u32[]{:S(2)}) copy-start(bf16[128,128]{1,0:T(8,128)(2,1)} %param.13) | copy-start | bytes 98308
  7.7 2.7 %collective-permute-start.1 = (f32[9,256,64]{1,2,0:T(8,128)S(1)}, f32[9,256,64]{1,2,0:T(8,128)S(1)}, u32[]{:S(2)}, u32[]{:S(2)}) collective-permute-start(f32[9,256,64]{1,2,0:T(8,128)S(1)} %pad_maximum_fusion), channel_id=1, source_target_pairs={{0,4},{4,0},{8,12},{12,8},{16,20},{20,16},{24,28},{28,24},{1,5},{5... | collective-permute-start | bytes 1769480 | tf_op jit(solution)/shard_map/ppermute | solution.py:72
  10.7 6.9 %collective-permute-start.2 = (bf16[9,256,64]{1,2,0:T(8,128)(2,1)S(1)}, bf16[9,256,64]{1,2,0:T(8,128)(2,1)S(1)}, u32[]{:S(2)}, u32[]{:S(2)}) collective-permute-start(bf16[9,256,64]{1,2,0:T(8,128)(2,1)S(1)} %pad_maximum_fusion.1), channel_id=1, source_target_pairs={{4,12},{12,20},{20,28},{8,0},{16,8},{24,16},{5,13},{13,21},{21,29}... | collective-permute-start | bytes 884744 | tf_op jit(solution)/shard_map/ppermute | solution.py:90
  17.6 6.6 %copy-start.15 = (f32[128,8]{0,1:T(8,128)S(1)}, f32[128,8]{0,1:T(8,128)}, u32[]{:S(2)}) copy-start(f32[128,8]{0,1:T(8,128)} %param.15) | copy-start | bytes 12292
  18.4 5.8 %copy-start.26 = (f32[8]{0:T(128)S(1)}, f32[8]{0:T(128)}, u32[]{:S(2)}) copy-start(f32[8]{0:T(128)} %param.16) | copy-start | bytes 100
  18.4 10.8 %collective-permute-start.3 = (bf16[8,256,64]{1,2,0:T(8,128)(2,1)}, bf16[8,256,64]{1,2,0:T(8,128)(2,1)S(1)}, u32[]{:S(2)}, u32[]{:S(2)}) collective-permute-start(bf16[8,256,64]{1,2,0:T(8,128)(2,1)} %fusion.24), channel_id=1, source_target_pairs={{4,20},{12,28},{16,0},{24,8},{5,21},{13,29},{17,1},{25,9},{6,22},{... | collective-permute-start | bytes 786440 | tf_op jit(solution)/shard_map/ppermute | solution.py:84
  26.4 1.1 %copy-start.16 = (f32[8,128]{1,0:T(8,128)}, f32[8,128]{1,0:T(8,128)S(1)}, u32[]{:S(2)}) copy-start(f32[8,128]{1,0:T(8,128)S(1)} %get-tuple-element.84) | copy-start | bytes 12292 | tf_op jit(solution)/shard_map/cond
  28.4 1.0 %copy-start.9 = (f32[128,256]{1,0:T(8,128)}, f32[128,256]{1,0:T(8,128)S(1)}, u32[]{:S(2)}) copy-start(f32[128,256]{1,0:T(8,128)S(1)} %get-tuple-element.70) | copy-start | bytes 393220
  28.4 1.0 %copy-start.11 = (f32[128,256]{1,0:T(8,128)}, f32[128,256]{1,0:T(8,128)S(1)}, u32[]{:S(2)}) copy-start(f32[128,256]{1,0:T(8,128)S(1)} %get-tuple-element.69) | copy-start | bytes 393220
  28.4 1.0 %copy-start.23 = (f32[128,8]{0,1:T(8,128)}, f32[128,8]{0,1:T(8,128)S(1)}, u32[]{:S(2)}) copy-start(f32[128,8]{0,1:T(8,128)S(1)} %get-tuple-element.73) | copy-start | bytes 12292
  29.4 4.3 %copy-start.20 = (f32[4,512]{1,0:T(4,128)S(1)}, f32[4,512]{1,0:T(4,128)}, u32[]{:S(2)}) copy-start(f32[4,512]{1,0:T(4,128)} %param.17) | copy-start | bytes 24580
  29.4 5.3 %collective-permute-start.4 = (f32[8,256,64]{1,2,0:T(8,128)S(1)}, f32[8,256,64]{1,2,0:T(8,128)S(1)}, u32[]{:S(2)}, u32[]{:S(2)}) collective-permute-start(f32[8,256,64]{1,2,0:T(8,128)S(1)} %convert_add_fusion), channel_id=1, source_target_pairs={{0,4},{4,0},{8,12},{12,8},{16,20},{20,16},{24,28},{28,24},{1,5},{5... | collective-permute-start | bytes 1572872 | tf_op jit(solution)/shard_map/ppermute | solution.py:99
  33.7 1.0 %copy-start.22 = (f32[8]{0:T(128)S(1)}, f32[8]{0:T(128)}, u32[]{:S(2)}) copy-start(f32[8]{0:T(128)} %copy-done.21) | copy-start | bytes 100
  33.7 1.9 %copy-start.10 = (f32[128,256]{1,0:T(8,128)S(1)}, f32[128,256]{1,0:T(8,128)}, u32[]{:S(2)}) copy-start(f32[128,256]{1,0:T(8,128)} %copy-done.9) | copy-start | bytes 393220
  35.6 0.9 %copy-start.12 = (f32[128,256]{1,0:T(8,128)S(1)}, f32[128,256]{1,0:T(8,128)}, u32[]{:S(2)}) copy-start(f32[128,256]{1,0:T(8,128)} %copy-done.11) | copy-start | bytes 393220
  37.1 0.8 %copy-start.6 = (bf16[128,128]{1,0:T(8,128)(2,1)S(1)}, bf16[128,128]{1,0:T(8,128)(2,1)}, u32[]{:S(2)}) copy-start(bf16[128,128]{1,0:T(8,128)(2,1)} %param.12) | copy-start | bytes 98308
  37.2 0.8 %copy-start.8 = (bf16[128,128]{1,0:T(8,128)(2,1)S(1)}, bf16[128,128]{1,0:T(8,128)(2,1)}, u32[]{:S(2)}) copy-start(bf16[128,128]{1,0:T(8,128)(2,1)} %copy-done.7) | copy-start | bytes 98308
  38.5 6.0 %collective-permute-start.5 = (f32[3,512]{1,0:T(4,128)S(1)}, f32[3,512]{1,0:T(4,128)S(1)}, u32[]{:S(2)}, u32[]{:S(2)}) collective-permute-start(f32[3,512]{1,0:T(4,128)S(1)} %slice.110), channel_id=1, source_target_pairs={{4,0},{8,4},{12,8},{16,12},{20,16},{24,20},{28,24},{5,1},{9,5},{13... | collective-permute-start | bytes 18440 | tf_op jit(solution)/shard_map/ppermute | solution.py:107
  40.8 1.2 %copy-start.3 = (bf16[128,128]{1,0:T(8,128)(2,1)S(1)}, bf16[128,128]{1,0:T(8,128)(2,1)}, u32[]{:S(2)}) copy-start(bf16[128,128]{1,0:T(8,128)(2,1)} %copy-done.2) | copy-start | bytes 98308
  40.9 4.5 %collective-permute-start.6 = (bf16[128,256]{1,0:T(8,128)(2,1)S(1)}, bf16[128,256]{1,0:T(8,128)(2,1)S(1)}, u32[]{:S(2)}, u32[]{:S(2)}) collective-permute-start(bf16[128,256]{1,0:T(8,128)(2,1)S(1)} %pad_maximum_fusion.6), channel_id=1, source_target_pairs={{0,1},{1,0},{2,3},{3,2},{4,5},{5,4},{6,7},{7,6},{8,9},{9,8},{10,11... | collective-permute-start | bytes 196616 | tf_op jit(solution)/shard_map/ppermute | solution.py:16
  42.0 0.7 %copy-start.24 = (f32[128,8]{0,1:T(8,128)S(1)}, f32[128,8]{0,1:T(8,128)}, u32[]{:S(2)}) copy-start(f32[128,8]{0,1:T(8,128)} %copy-done.23) | copy-start | bytes 12292
  42.4 0.7 %copy-start.25 = (f32[8]{0:T(128)S(1)}, f32[8]{0:T(128)}, u32[]{:S(2)}) copy-start(f32[8]{0:T(128)} %get-tuple-element.77) | copy-start | bytes 100
  42.4 0.7 %copy-start.27 = (f32[128]{0:T(128)S(1)}, f32[128]{0:T(128)}, u32[]{:S(2)}) copy-start(f32[128]{0:T(128)} %compare_convert_fusion) | copy-start | bytes 1540
  43.1 0.8 %copy-start.17 = (f32[128,8]{0,1:T(8,128)S(1)}, f32[128,8]{0,1:T(8,128)}, u32[]{:S(2)}) copy-start(f32[128,8]{0,1:T(8,128)} %get-tuple-element.74) | copy-start | bytes 12292
  43.1 0.8 %copy-start.19 = (f32[8]{0:T(128)S(1)}, f32[8]{0:T(128)}, u32[]{:S(2)}) copy-start(f32[8]{0:T(128)} %copy-done.18) | copy-start | bytes 100

commit v15 on v11

--- a/solution.py
+++ b/solution.py
@@ -70,6 +70,9 @@
         message, rider_inputs = lax.optimization_barrier((message, rider_inputs))
         riders = rider_fn(*rider_inputs)
     mate = lax.ppermute(message, axis, swap)
+    if peers > 2:
+        mate, rider_inputs = lax.optimization_barrier((mate, rider_inputs))
+        riders = rider_fn(*rider_inputs)
     if peers == 2:
         mate, riders = lax.optimization_barrier((mate, riders))
     mate_a, mate_s = unpacked(mate)
@@ -83,14 +86,12 @@
         if 2 * distance >= peers:
             far_s = lax.ppermute(window[1].astype(jnp.bfloat16), axis, route)
             if distance == 2:
-                far_s, rider_inputs = lax.optimization_barrier((far_s, rider_inputs))
-                riders = rider_fn(*rider_inputs)
+                far_s, riders = lax.optimization_barrier((far_s, riders))
             near = (near[0], near[1] + near[0][:, None, None] * far_s.astype(jnp.float32))
         else:
             far = lax.ppermute(packed(*window, jnp.bfloat16), axis, route)
             if distance == 2:
-                far, rider_inputs = lax.optimization_barrier((far, rider_inputs))
-                riders = rider_fn(*rider_inputs)
+                far, riders = lax.optimization_barrier((far, riders))
             far_a, far_s = unpacked(far)
             near = (near[0] * far_a, near[1] + near[0][:, None, None] * far_s)
             window = (window[0] * far_a, window[1] + window[0][:, None, None] * far_s)

time: 45.3 us -> 48.8 us (1.077)
  local copies, waits for them, and re-layouts: 4 us -> 6.82 us
  waiting for transfers between devices: 6.64 us -> 8.21 us
  other arithmetic: 6.65 us -> 5.3 us
    ppermute x1, waiting for transfers between devices: 3.53 us -> 0.01 us  [paired_scan(): far = lax.ppermute(packed(*window, jnp.bfloat16), axis, route)]
    ppermute x1, waiting for transfers between devices: 0.01 us -> 3.24 us  [paired_scan(): far_s = lax.ppermute(window[1].astype(jnp.bfloat16), axis, route)]
    ppermute x2, waiting for transfers between devices: 0.01 us -> 1.93 us  [swapped(): return lax.ppermute(block, axis, route)]
    unnamed x54 -> x50, local copies, waits for them, and re-layouts: 3.36 us -> 4.85 us
    cond x2 -> x6, local copies, waits for them, and re-layouts: 0.01 us -> 1.34 us
    ppermute x1, starting transfers between devices: 3.64 us -> 4.9 us  [paired_scan(): handed = lax.ppermute(passing, axis, swap)]
    ppermute x1, starting transfers between devices: 5.25 us -> 4.22 us  [paired_scan(): far_s = lax.ppermute(window[1].astype(jnp.bfloat16), axis, route)]
    add x1, other arithmetic: 0.81 us -> 0.07 us  [unpacked(): row[:heads] + row[heads:2 * heads]]
  transfers between devices with their start and end apart: 7 -> 7, of which waited for: 3 -> 4; matrix products, arithmetic and copies ran while one was open for 23% -> 15% of each run, Pallas kernels for 0% -> 0%
where the time goes in v15:
time: 48.8 us; the launch traced here: 47.8 us
  starting transfers between devices  18.9 us (39%)
  waiting for transfers between devices  8.21 us (17%)
  matrix products  7.44 us (15%)
  local copies, waits for them, and re-layouts  6.82 us (14%)
  other arithmetic  5.3 us (11%)
  between operations  1.11 us (2%)
    ppermute x1, starting transfers between devices, paired_scan(): handed = lax.ppermute(passing, axis, swap)  4.9 us
    unnamed x50, local copies, waits for them, and re-layouts  4.85 us
    ppermute x1, starting transfers between devices, paired_scan(): far_s = lax.ppermute(window[1].astype(jnp.bfloat16), axis, route)  4.22 us
    ppermute x2, starting transfers between devices, swapped(): return lax.ppermute(block, axis, route)  3.25 us
    ppermute x1, waiting for transfers between devices, paired_scan(): far_s = lax.ppermute(window[1].astype(jnp.bfloat16), axis, route)  3.24 us
    ppermute x1, starting transfers between devices, paired_scan(): far = lax.ppermute(packed(*window, jnp.bfloat16), axis, route)  3.21 us
    ppermute x1, starting transfers between devices, shifted(): return lax.ppermute(block, axis, route)  2.28 us
    ppermute x2, waiting for transfers between devices, swapped(): return lax.ppermute(block, axis, route)  1.93 us
  transfers between devices with their start and end apart: 7, of which 4 were waited for; matrix products, arithmetic and copies ran while one was open for 15% of the time, Pallas kernels for 0%

profile of v15, /device:TPU:1, one launch (start us, length us, event | category | flops | bytes accessed | tf_op | source)
XLA Modules:
  0.0 47.8 jit_solution(9244672716724746312)
XLA Ops:
  0.7 0.8 %pad_maximum_fusion.4 = bf16[128,256]{1,0:T(8,128)(2,1)S(1)} fusion(bf16[128,128]{1,0:T(8,128)(2,1)} %param.13, bf16[128,128]{1,0:T(8,128)(2,1)} %param.12), kind=kLoop, calls=%fused_computation.70 | loop fusion | flops 131072 | bytes 131072 | tf_op jit(solution)/shard_map/concatenate | solution.py:124
  1.5 2.1 %collective-permute-start = (bf16[128,256]{1,0:T(8,128)(2,1)S(1)}, bf16[128,256]{1,0:T(8,128)(2,1)S(1)}, u32[]{:S(2)}, u32[]{:S(2)}) collective-permute-start(bf16[128,256]{1,0:T(8,128)(2,1)S(1)} %pad_maximum_fusion.4), channel_id=1, source_target_pairs={{0,1},{1,0},{2,3},{3,2},{4,5},{5,4},{6,7},{7,6},{8,9},{9,8},{10,11... | collective-permute-start | bytes 196616 | tf_op jit(solution)/shard_map/ppermute | solution.py:16
  3.7 0.2 slice_reduce_fusion
  4.1 0.6 %copy-done.14 = f32[128,8]{0,1:T(8,128)S(1)} copy-done((f32[128,8]{0,1:T(8,128)S(1)}, f32[128,8]{0,1:T(8,128)}, u32[]{:S(2)}) %copy-start.14) | copy-done | bytes 4120
  4.9 0.8 %copy-done.13 = bf16[128,512]{1,0:T(8,128)(2,1)S(1)} copy-done((bf16[128,512]{1,0:T(8,128)(2,1)S(1)}, bf16[128,512]{1,0:T(8,128)(2,1)}, u32[]{:S(2)}) %copy-start.13) | copy-done | bytes 131096
  5.8 0.7 %copy-done.5 = bf16[128,128]{1,0:T(8,128)(2,1)S(1)} copy-done((bf16[128,128]{1,0:T(8,128)(2,1)S(1)}, bf16[128,128]{1,0:T(8,128)(2,1)}, u32[]{:S(2)}) %copy-start.5) | copy-done | bytes 32792
  6.5 0.4 convolution_bitcast_fusion.2
  6.9 0.4 copy-done.1
  7.3 0.4 broadcast_select_fusion.2
  7.7 1.0 %collective-permute-start.1 = (f32[9,256,64]{1,2,0:T(8,128)S(1)}, f32[9,256,64]{1,2,0:T(8,128)S(1)}, u32[]{:S(2)}, u32[]{:S(2)}) collective-permute-start(f32[9,256,64]{1,2,0:T(8,128)S(1)} %pad_maximum_fusion), channel_id=1, source_target_pairs={{0,4},{4,0},{8,12},{12,8},{16,20},{20,16},{24,28},{28,24},{1,5},{5... | collective-permute-start | bytes 1769480 | tf_op jit(solution)/shard_map/ppermute | solution.py:72
  8.8 1.6 %collective-permute-done.1 = f32[9,256,64]{1,2,0:T(8,128)S(1)} collective-permute-done((f32[9,256,64]{1,2,0:T(8,128)S(1)}, f32[9,256,64]{1,2,0:T(8,128)S(1)}, u32[]{:S(2)}, u32[]{:S(2)}) %collective-permute-start.1) | collective-permute-done | bytes 589856 | tf_op jit(solution)/shard_map/ppermute | solution.py:72
  10.4 0.5 %copy-done.25 = f32[8]{0:T(128)} copy-done((f32[8]{0:T(128)}, f32[8]{0:T(128)S(1)}, u32[]{:S(2)}) %copy-start.25) | copy-done | bytes 56
  10.9 0.2 fusion.73
  11.2 0.7 %pad_maximum_fusion.1 = bf16[9,256,64]{1,2,0:T(8,128)(2,1)} fusion(bf16[1,256,64]{1,2,0:T(8,128)(2,1)S(1)} %broadcast_in_dim.17, bf16[8,256,64]{1,2,0:T(8,128)(2,1)S(1)} %get-tuple-element.90), kind=kLoop, calls=%fused_computation.41 | loop fusion | flops 147456 | bytes 589824 | tf_op jit(solution)/shard_map/concatenate | solution.py:50
  11.9 3.2 %collective-permute-start.2 = (bf16[9,256,64]{1,2,0:T(8,128)(2,1)}, bf16[9,256,64]{1,2,0:T(8,128)(2,1)S(1)}, u32[]{:S(2)}, u32[]{:S(2)}) collective-permute-start(bf16[9,256,64]{1,2,0:T(8,128)(2,1)} %pad_maximum_fusion.1), channel_id=1, source_target_pairs={{4,12},{12,20},{20,28},{8,0},{16,8},{24,16},{5,13},{13,21},{21,29}... | collective-permute-start | bytes 884744 | tf_op jit(solution)/shard_map/ppermute | solution.py:92
  15.2 5.5 %conditional.1 = (f32[128,8,64]{0,2,1:T(8,128)S(1)}, f32[128,8]{0,1:T(8,128)S(1)}, f32[128,8]{0,1:T(8,128)}, f32[128,256]{1,0:T(8,128)S(1)}, f32[128,256]{1,0:T(8,128)S(1)}, /*index=5*/f32[128,512]{1,0:T(8,128)S(1)}) conditional(s32[]{:T(128)} %convert_element_type.66, () %tuple.20, (f32[128,8]{0,1:T(8,128)S(1)}, f32[128,256]{1,0:T(8,128)S(1)}, ...), branch_computations={%region_0.1_spmd, %region_1.3_spmd} | conditional | flops 356844544 | bytes 4559140 | solution.py:188
  15.2 0.3 fusion.78
  15.5 1.1 %fusion.5 = (f32[8,128]{1,0:T(8,128)S(1)}, f32[8,128,128]{2,1,0:T(8,128)S(1)}) fusion(f32[128,128]{1,0:T(8,128)S(1)} %fusion.78, f32[8,128]{1,0:T(8,128)S(1)} %bitcast.91, pred[128,128]{1,0:T(8,128)(4,1)S(1)} %iota_compare_fusion, f32[128,8,64]{0,2,1:T(8,128)S(1)} %get-tuple-element.20, f32[128,8,64]{0,2,1:T(8,128)S(1)} %get-tuple-element.22), kind=kOutput, calls=%fused_computation.7 | convolution fusion | flops 101317632 | bytes 1138688 | tf_op jit(solution)/shard_map/cond/branch_1_fun/thp,shp->hts/dot_general | solution.py:162
  16.6 0.7 %copy-done.15 = f32[128,8]{0,1:T(8,128)S(1)} copy-done((f32[128,8]{0,1:T(8,128)S(1)}, f32[128,8]{0,1:T(8,128)}, u32[]{:S(2)}) %copy-start.15) | copy-done | bytes 4120 | tf_op jit(solution)/shard_map/cond
  17.3 1.1 %fusion.6 = f32[8,1,128]{2,1,0:T(1,128)S(1)} fusion(f32[8,128,1]{1,2,0:T(1,128)S(1)} %bitcast.95, f32[8,128,128]{2,1,0:T(8,128)S(1)} %get-tuple-element.95, f32[128,128]{1,0:T(8,128)S(1)} %fusion.78, f32[8,128]{1,0:T(8,128)S(1)} %bitcast.92, pred[128,128]{1,0:T(8,128)(4,1)S(1)} %iota_compare_fusion), kind=kOutput, calls=%fused_computation.8 | convolution fusion | flops 2097152 | bytes 618496 | tf_op jit(solution)/shard_map/cond/branch_1_fun/hts,hs->th/dot_general | solution.py:169
  18.3 0.2 multiply_reduce_fusion
  18.6 0.3 fusion.79
  18.8 0.3 fusion.80
  19.2 0.6 %copy-done.27 = f32[8]{0:T(128)S(1)} copy-done((f32[8]{0:T(128)S(1)}, f32[8]{0:T(128)}, u32[]{:S(2)}) %copy-start.27) | copy-done | bytes 56 | tf_op jit(solution)/shard_map/cond
  19.8 0.8 %fusion = f32[128,8,64]{0,2,1:T(8,128)S(1)} fusion(f32[128,8,64]{0,2,1:T(8,128)S(1)} %get-tuple-element.20, f32[8,128]{1,0:T(8,128)S(1)} %bitcast.96, f32[128,128]{1,0:T(8,128)S(1)} %fusion.78, f32[8,128]{1,0:T(8,128)S(1)} %bitcast.94, pred[128,128]{1,0:T(8,128)(4,1)S(1)} %iota_compare_fusion, f32[8]{0:T(128)S(1)} %copy-done.27), kind=kOutput, calls=%fused_computation.1 | convolution fusion | flops 101318656 | bytes 614432 | tf_op jit(solution)/shard_map/cond/branch_1_fun/hts,thp->shp/dot_general | solution.py:165
  20.7 0.6 %copy-done.26 = f32[8]{0:T(128)S(1)} copy-done((f32[8]{0:T(128)S(1)}, f32[8]{0:T(128)}, u32[]{:S(2)}) %copy-start.26) | copy-done | bytes 56
  21.4 0.1 fusion.24
  21.5 4.2 %collective-permute-start.3 = (bf16[8,256,64]{1,2,0:T(8,128)(2,1)S(1)}, bf16[8,256,64]{1,2,0:T(8,128)(2,1)S(1)}, u32[]{:S(2)}, u32[]{:S(2)}) collective-permute-start(bf16[8,256,64]{1,2,0:T(8,128)(2,1)S(1)} %fusion.24), channel_id=1, source_target_pairs={{4,20},{12,28},{16,0},{24,8},{5,21},{13,29},{17,1},{25,9},{6,22},{... | collective-permute-start | bytes 786440 | tf_op jit(solution)/shard_map/ppermute | solution.py:87
  25.8 3.2 %collective-permute-done.3 = bf16[8,256,64]{1,2,0:T(8,128)(2,1)S(1)} collective-permute-done((bf16[8,256,64]{1,2,0:T(8,128)(2,1)S(1)}, bf16[8,256,64]{1,2,0:T(8,128)(2,1)S(1)}, u32[]{:S(2)}, u32[]{:S(2)}) %collective-permute-start.3) | collective-permute-done | bytes 262176 | tf_op jit(solution)/shard_map/ppermute | solution.py:87
  29.1 0.1 convert_add_fusion
  29.2 4.9 %collective-permute-start.4 = (f32[8,256,64]{1,2,0:T(8,128)S(1)}, f32[8,256,64]{1,2,0:T(8,128)S(1)}, u32[]{:S(2)}, u32[]{:S(2)}) collective-permute-start(f32[8,256,64]{1,2,0:T(8,128)S(1)} %convert_add_fusion), channel_id=1, source_target_pairs={{0,4},{4,0},{8,12},{12,8},{16,20},{20,16},{24,28},{28,24},{1,5},{5... | collective-permute-start | bytes 1572872 | tf_op jit(solution)/shard_map/ppermute | solution.py:100
  34.2 1.5 %collective-permute-done.4 = f32[8,256,64]{1,2,0:T(8,128)S(1)} collective-permute-done((f32[8,256,64]{1,2,0:T(8,128)S(1)}, f32[8,256,64]{1,2,0:T(8,128)S(1)}, u32[]{:S(2)}, u32[]{:S(2)}) %collective-permute-start.4) | collective-permute-done | bytes 524320 | tf_op jit(solution)/shard_map/ppermute | solution.py:100
  35.7 0.3 multiply_reduce_fusion.1
  36.0 0.4 multiply_reduce_fusion.2
  36.4 0.4 copy-done.3
  36.7 0.4 multiply_reduce_fusion.3
  37.1 0.5 %copy-done.12 = f32[128,256]{1,0:T(8,128)S(1)} copy-done((f32[128,256]{1,0:T(8,128)S(1)}, f32[128,256]{1,0:T(8,128)}, u32[]{:S(2)}) %copy-start.12) | copy-done | bytes 131096
  37.6 0.6 %fusion.21 = f32[128,256]{1,0:T(8,128)S(1)} fusion(f32[128,256]{1,0:T(8,128)S(1)} %copy-done.12, f32[8,256,64]{1,2,0:T(8,128)S(1)} %get-tuple-element.89, f32[128,8,64]{0,2,1:T(8,128)S(1)} %bitcast.86, f32[128,8]{0,1:T(8,128)S(1)} %get-tuple-element.104), kind=kOutput, calls=%fused_computation.29 | convolution fusion | flops 201424896 | bytes 1052672 | tf_op jit(solution)/shard_map/lhp,hnp->ln/dot_general | solution.py:221
  38.3 0.3 copy-done.10
  38.5 0.6 %fusion.22 = f32[128,256]{1,0:T(8,128)S(1)} fusion(f32[128,256]{1,0:T(8,128)S(1)} %copy-done.10, f32[8,256,64]{1,2,0:T(8,128)S(1)} %get-tuple-element.88, f32[128,8,64]{0,2,1:T(8,128)S(1)} %bitcast.83, f32[128,8]{0,1:T(8,128)S(1)} %get-tuple-element.105), kind=kOutput, calls=%fused_computation.30 | convolution fusion | flops 201424896 | bytes 1052672 | tf_op jit(solution)/shard_map/lhp,hnp->ln/dot_general | solution.py:218
  39.2 0.1 copy.19
  39.5 2.3 %collective-permute-start.5 = (f32[3,512]{1,0:T(4,128)S(1)}, f32[3,512]{1,0:T(4,128)S(1)}, u32[]{:S(2)}, u32[]{:S(2)}) collective-permute-start(f32[3,512]{1,0:T(4,128)S(1)} %slice.108), channel_id=1, source_target_pairs={{4,0},{8,4},{12,8},{16,12},{20,16},{24,20},{28,24},{5,1},{9,5},{13... | collective-permute-start | bytes 18440 | tf_op jit(solution)/shard_map/ppermute | solution.py:108
  41.8 0.7 %multiply_add_fusion.3 = f32[128,8]{0,1:T(8,128)} fusion(f32[128,8]{0,1:T(8,128)S(1)} %copy-done.17, f32[128,8]{0,1:T(8,128)S(1)} %get-tuple-element.108, f32[128,8]{0,1:T(8,128)S(1)} %fusion.46, f32[8]{0:T(128)S(1)} %copy-done.19), kind=kLoop, calls=%fused_computation.85 | loop fusion | flops 3072 | bytes 16416 | tf_op jit(solution)/shard_map/add | solution.py:207
  42.5 0.8 %fusion.47 = f32[128,8]{0,1:T(8,128)} fusion(f32[128,8]{0,1:T(8,128)S(1)} %get-tuple-element.104, f32[128,8]{0,1:T(8,128)S(1)} %get-tuple-element.108, f32[128,8]{0,1:T(8,128)S(1)} %copy-done.24, f32[128,8]{0,1:T(8,128)S(1)} %multiply_reduce_fusion.3, f32[8]{0:T(128)S(1)} %get-tuple-element.87, f32[128]{0:T(128)S(1)} %compare_convert_fusion, ...), kind=kOutput, calls=%fused_computation.84 | convolution fusion | flops 1595392 | bytes 25120 | tf_op jit(solution)/shard_map/dot_general | solution.py:112
  43.3 1.1 %collective-permute-start.6 = (bf16[128,256]{1,0:T(8,128)(2,1)S(1)}, bf16[128,256]{1,0:T(8,128)(2,1)S(1)}, u32[]{:S(2)}, u32[]{:S(2)}) collective-permute-start(bf16[128,256]{1,0:T(8,128)(2,1)S(1)} %pad_maximum_fusion.6), channel_id=1, source_target_pairs={{0,1},{1,0},{2,3},{3,2},{4,5},{5,4},{6,7},{7,6},{8,9},{9,8},{10,11... | collective-permute-start | bytes 196616 | tf_op jit(solution)/shard_map/ppermute | solution.py:16
  44.4 0.8 %fusion.30 = bf16[128,512]{1,0:T(8,128)(2,1)} fusion(f32[128,512]{1,0:T(8,128)S(1)} %mul.207, f32[3,512]{1,0:T(4,128)S(1)} %collective-permute-done.5, f32[512]{0:T(512)S(1)} %bitcast.100, f32[512]{0:T(512)S(1)} %bitcast.101, f32[512]{0:T(512)S(1)} %bitcast.99, f32[512]{0:T(512)S(1)} %bitcast.98), kind=kLoop, calls=%fused_computation.49 | loop fusion | flops 720896 | bytes 407552 | tf_op jit(solution)/shard_map/convert_element_type | solution.py:241
  45.2 1.9 %collective-permute-done.6 = bf16[128,256]{1,0:T(8,128)(2,1)S(1)} collective-permute-done((bf16[128,256]{1,0:T(8,128)(2,1)S(1)}, bf16[128,256]{1,0:T(8,128)(2,1)S(1)}, u32[]{:S(2)}, u32[]{:S(2)}) %collective-permute-start.6) | collective-permute-done | bytes 65568 | tf_op jit(solution)/shard_map/ppermute | solution.py:16
  47.2 0.7 %slice_add_fusion = (f32[128,128]{1,0:T(8,128)}, f32[128,128]{1,0:T(8,128)}) fusion(f32[128,256]{1,0:T(8,128)S(1)} %convert_element_type.72, f32[128,256]{1,0:T(8,128)S(1)} %fusion.22, pred[]{:T(512)S(6)} %eq.21, f32[128,256]{1,0:T(8,128)S(1)} %fusion.21), kind=kLoop, calls=%fused_computation.74 | loop fusion | flops 65536 | bytes 524289 | tf_op jit(solution)/shard_map/add | solution.py:232
  (79 shorter events, 1.2 us)
Async XLA Ops:
  0.6 3.0 %copy-start = (f32[128,8]{0,1:T(8,128)S(1)}, f32[128,8]{0,1:T(8,128)}, u32[]{:S(2)}) copy-start(f32[128,8]{0,1:T(8,128)} %param.14) | copy-start | bytes 12292
  0.6 3.3 %copy-start.4 = (bf16[128,512]{1,0:T(8,128)(2,1)S(1)}, bf16[128,512]{1,0:T(8,128)(2,1)}, u32[]{:S(2)}) copy-start(bf16[128,512]{1,0:T(8,128)(2,1)} %param.10) | copy-start | bytes 393220
  1.5 4.3 %collective-permute-start = (bf16[128,256]{1,0:T(8,128)(2,1)S(1)}, bf16[128,256]{1,0:T(8,128)(2,1)S(1)}, u32[]{:S(2)}, u32[]{:S(2)}) collective-permute-start(bf16[128,256]{1,0:T(8,128)(2,1)S(1)} %pad_maximum_fusion.4), channel_id=1, source_target_pairs={{0,1},{1,0},{2,3},{3,2},{4,5},{5,4},{6,7},{7,6},{8,9},{9,8},{10,11... | collective-permute-start | bytes 196616 | tf_op jit(solution)/shard_map/ppermute | solution.py:16
  4.0 6.4 %copy-start.18 = (f32[8]{0:T(128)}, f32[8]{0:T(128)S(1)}, u32[]{:S(2)}) copy-start(f32[8]{0:T(128)S(1)} %slice_reduce_fusion) | copy-start | bytes 100
  4.0 0.7 %copy-start.14 = (f32[128,8]{0,1:T(8,128)S(1)}, f32[128,8]{0,1:T(8,128)}, u32[]{:S(2)}) copy-start(f32[128,8]{0,1:T(8,128)} %param.15) | copy-start | bytes 12292
  4.7 6.2 %copy-start.21 = (f32[8]{0:T(128)}, f32[8]{0:T(128)S(1)}, u32[]{:S(2)}) copy-start(f32[8]{0:T(128)S(1)} %exp.29) | copy-start | bytes 100
  4.7 0.9 %copy-start.13 = (bf16[128,512]{1,0:T(8,128)(2,1)S(1)}, bf16[128,512]{1,0:T(8,128)(2,1)}, u32[]{:S(2)}) copy-start(bf16[128,512]{1,0:T(8,128)(2,1)} %param.11) | copy-start | bytes 393220
  5.8 0.8 %copy-start.5 = (bf16[128,128]{1,0:T(8,128)(2,1)S(1)}, bf16[128,128]{1,0:T(8,128)(2,1)}, u32[]{:S(2)}) copy-start(bf16[128,128]{1,0:T(8,128)(2,1)} %param.12) | copy-start | bytes 98308
  5.8 3.0 %copy-start.2 = (bf16[128,128]{1,0:T(8,128)(2,1)}, bf16[128,128]{1,0:T(8,128)(2,1)S(1)}, u32[]{:S(2)}) copy-start(bf16[128,128]{1,0:T(8,128)(2,1)S(1)} %get-tuple-element.99) | copy-start | bytes 98308
  5.8 3.0 %copy-start.7 = (bf16[128,128]{1,0:T(8,128)(2,1)}, bf16[128,128]{1,0:T(8,128)(2,1)S(1)}, u32[]{:S(2)}) copy-start(bf16[128,128]{1,0:T(8,128)(2,1)S(1)} %get-tuple-element.98) | copy-start | bytes 98308
  6.5 0.8 %copy-start.1 = (bf16[128,128]{1,0:T(8,128)(2,1)S(1)}, bf16[128,128]{1,0:T(8,128)(2,1)}, u32[]{:S(2)}) copy-start(bf16[128,128]{1,0:T(8,128)(2,1)} %param.13) | copy-start | bytes 98308
  7.7 2.7 %collective-permute-start.1 = (f32[9,256,64]{1,2,0:T(8,128)S(1)}, f32[9,256,64]{1,2,0:T(8,128)S(1)}, u32[]{:S(2)}, u32[]{:S(2)}) collective-permute-start(f32[9,256,64]{1,2,0:T(8,128)S(1)} %pad_maximum_fusion), channel_id=1, source_target_pairs={{0,4},{4,0},{8,12},{12,8},{16,20},{20,16},{24,28},{28,24},{1,5},{5... | collective-permute-start | bytes 1769480 | tf_op jit(solution)/shard_map/ppermute | solution.py:72
  10.4 0.5 %copy-start.25 = (f32[8]{0:T(128)}, f32[8]{0:T(128)S(1)}, u32[]{:S(2)}) copy-start(f32[8]{0:T(128)S(1)} %get-tuple-element.93) | copy-start | bytes 100
  11.9 8.8 %collective-permute-start.2 = (bf16[9,256,64]{1,2,0:T(8,128)(2,1)}, bf16[9,256,64]{1,2,0:T(8,128)(2,1)S(1)}, u32[]{:S(2)}, u32[]{:S(2)}) collective-permute-start(bf16[9,256,64]{1,2,0:T(8,128)(2,1)} %pad_maximum_fusion.1), channel_id=1, source_target_pairs={{4,12},{12,20},{20,28},{8,0},{16,8},{24,16},{5,13},{13,21},{21,29}... | collective-permute-start | bytes 884744 | tf_op jit(solution)/shard_map/ppermute | solution.py:92
  16.6 1.8 %copy-start.16 = (f32[8,128]{1,0:T(8,128)}, f32[8,128]{1,0:T(8,128)S(1)}, u32[]{:S(2)}) copy-start(f32[8,128]{1,0:T(8,128)S(1)} %get-tuple-element.94) | copy-start | bytes 12292 | tf_op jit(solution)/shard_map/cond
  16.6 0.7 %copy-start.15 = (f32[128,8]{0,1:T(8,128)S(1)}, f32[128,8]{0,1:T(8,128)}, u32[]{:S(2)}) copy-start(f32[128,8]{0,1:T(8,128)} %get-tuple-element.19) | copy-start | bytes 12292 | tf_op jit(solution)/shard_map/cond
  19.2 0.7 %copy-start.27 = (f32[8]{0:T(128)S(1)}, f32[8]{0:T(128)}, u32[]{:S(2)}) copy-start(f32[8]{0:T(128)} %get-tuple-element.86) | copy-start | bytes 100 | tf_op jit(solution)/shard_map/cond
  20.7 0.8 %copy-start.9 = (f32[128,256]{1,0:T(8,128)}, f32[128,256]{1,0:T(8,128)S(1)}, u32[]{:S(2)}) copy-start(f32[128,256]{1,0:T(8,128)S(1)} %get-tuple-element.82) | copy-start | bytes 393220
  20.7 0.8 %copy-start.11 = (f32[128,256]{1,0:T(8,128)}, f32[128,256]{1,0:T(8,128)S(1)}, u32[]{:S(2)}) copy-start(f32[128,256]{1,0:T(8,128)S(1)} %get-tuple-element.81) | copy-start | bytes 393220
  20.7 0.8 %copy-start.23 = (f32[128,8]{0,1:T(8,128)}, f32[128,8]{0,1:T(8,128)S(1)}, u32[]{:S(2)}) copy-start(f32[128,8]{0,1:T(8,128)S(1)} %get-tuple-element.83) | copy-start | bytes 12292
  20.7 0.6 %copy-start.26 = (f32[8]{0:T(128)S(1)}, f32[8]{0:T(128)}, u32[]{:S(2)}) copy-start(f32[8]{0:T(128)} %copy-done.25) | copy-start | bytes 100
  21.5 7.6 %collective-permute-start.3 = (bf16[8,256,64]{1,2,0:T(8,128)(2,1)S(1)}, bf16[8,256,64]{1,2,0:T(8,128)(2,1)S(1)}, u32[]{:S(2)}, u32[]{:S(2)}) collective-permute-start(bf16[8,256,64]{1,2,0:T(8,128)(2,1)S(1)} %fusion.24), channel_id=1, source_target_pairs={{4,20},{12,28},{16,0},{24,8},{5,21},{13,29},{17,1},{25,9},{6,22},{... | collective-permute-start | bytes 786440 | tf_op jit(solution)/shard_map/ppermute | solution.py:87
  25.8 8.3 %copy-start.20 = (f32[4,512]{1,0:T(4,128)S(1)}, f32[4,512]{1,0:T(4,128)}, u32[]{:S(2)}) copy-start(f32[4,512]{1,0:T(4,128)} %param.17) | copy-start | bytes 24580
  29.2 6.4 %collective-permute-start.4 = (f32[8,256,64]{1,2,0:T(8,128)S(1)}, f32[8,256,64]{1,2,0:T(8,128)S(1)}, u32[]{:S(2)}, u32[]{:S(2)}) collective-permute-start(f32[8,256,64]{1,2,0:T(8,128)S(1)} %convert_add_fusion), channel_id=1, source_target_pairs={{0,4},{4,0},{8,12},{12,8},{16,20},{20,16},{24,28},{28,24},{1,5},{5... | collective-permute-start | bytes 1572872 | tf_op jit(solution)/shard_map/ppermute | solution.py:100
  34.1 1.5 %copy-start.22 = (f32[8]{0:T(128)S(1)}, f32[8]{0:T(128)}, u32[]{:S(2)}) copy-start(f32[8]{0:T(128)} %copy-done.21) | copy-start | bytes 100
  34.1 1.8 %copy-start.6 = (bf16[128,128]{1,0:T(8,128)(2,1)S(1)}, bf16[128,128]{1,0:T(8,128)(2,1)}, u32[]{:S(2)}) copy-start(bf16[128,128]{1,0:T(8,128)(2,1)} %param.12) | copy-start | bytes 98308
  34.2 1.8 %copy-start.8 = (bf16[128,128]{1,0:T(8,128)(2,1)S(1)}, bf16[128,128]{1,0:T(8,128)(2,1)}, u32[]{:S(2)}) copy-start(bf16[128,128]{1,0:T(8,128)(2,1)} %copy-done.7) | copy-start | bytes 98308
  36.0 0.8 %copy-start.3 = (bf16[128,128]{1,0:T(8,128)(2,1)S(1)}, bf16[128,128]{1,0:T(8,128)(2,1)}, u32[]{:S(2)}) copy-start(bf16[128,128]{1,0:T(8,128)(2,1)} %copy-done.2) | copy-start | bytes 98308
  36.7 0.9 %copy-start.12 = (f32[128,256]{1,0:T(8,128)S(1)}, f32[128,256]{1,0:T(8,128)}, u32[]{:S(2)}) copy-start(f32[128,256]{1,0:T(8,128)} %copy-done.11) | copy-start | bytes 393220
  37.6 0.9 %copy-start.10 = (f32[128,256]{1,0:T(8,128)S(1)}, f32[128,256]{1,0:T(8,128)}, u32[]{:S(2)}) copy-start(f32[128,256]{1,0:T(8,128)} %copy-done.9) | copy-start | bytes 393220
  39.4 2.3 %copy-start.17 = (f32[128,8]{0,1:T(8,128)S(1)}, f32[128,8]{0,1:T(8,128)}, u32[]{:S(2)}) copy-start(f32[128,8]{0,1:T(8,128)} %get-tuple-element.84) | copy-start | bytes 12292
  39.4 2.3 %copy-start.19 = (f32[8]{0:T(128)S(1)}, f32[8]{0:T(128)}, u32[]{:S(2)}) copy-start(f32[8]{0:T(128)} %copy-done.18) | copy-start | bytes 100
  39.5 5.0 %collective-permute-start.5 = (f32[3,512]{1,0:T(4,128)S(1)}, f32[3,512]{1,0:T(4,128)S(1)}, u32[]{:S(2)}, u32[]{:S(2)}) collective-permute-start(f32[3,512]{1,0:T(4,128)S(1)} %slice.108), channel_id=1, source_target_pairs={{4,0},{8,4},{12,8},{16,12},{20,16},{24,20},{28,24},{5,1},{9,5},{13... | collective-permute-start | bytes 18440 | tf_op jit(solution)/shard_map/ppermute | solution.py:108
  41.8 0.7 %copy-start.24 = (f32[128,8]{0,1:T(8,128)S(1)}, f32[128,8]{0,1:T(8,128)}, u32[]{:S(2)}) copy-start(f32[128,8]{0,1:T(8,128)} %copy-done.23) | copy-start | bytes 12292
  43.3 3.9 %collective-permute-start.6 = (bf16[128,256]{1,0:T(8,128)(2,1)S(1)}, bf16[128,256]{1,0:T(8,128)(2,1)S(1)}, u32[]{:S(2)}, u32[]{:S(2)}) collective-permute-start(bf16[128,256]{1,0:T(8,128)(2,1)S(1)} %pad_maximum_fusion.6), channel_id=1, source_target_pairs={{0,1},{1,0},{2,3},{3,2},{4,5},{5,4},{6,7},{7,6},{8,9},{9,8},{10,11... | collective-permute-start | bytes 196616 | tf_op jit(solution)/shard_map/ppermute | solution.py:16
